TPU v7x, 32 devices: a whole 2x2x4 slice. The times are simulated.
32 devices in a mesh: seq: 16 (over z, y, core), dp: 2 (over x).
Axes of the slice: x: 2, y: 2, z: 4, core: 2. Of those that a mesh axis runs over, the one named last changes fastest.
Arguments:
- query_rows: bfloat16 [2, 4096, 768], P('dp', 'seq'), may hold values from -40 to 40
- key_rows: bfloat16 [2, 4096, 768], P('dp', 'seq'), may hold values from -40 to 40
- value_rows: bfloat16 [2, 4096, 768], P('dp', 'seq'), may hold values from -6 to 6
- out_grad: bfloat16 [2, 4096, 1536], P('dp', 'seq'), may hold values from -6 to 6
- lengths: int32 [2, 8], P('dp'), may hold values from 1 to 1024, 4096 in all within a row
- out_weight: bfloat16 [768, 1536], P('seq', 'dp'), may hold values from -0.21875 to 0.21875
Outputs:
- mixed_out: bfloat16 [2, 4096, 1536], P('dp', 'seq')
- query_grad: bfloat16 [2, 4096, 768], P('dp', 'seq')
- key_grad: bfloat16 [2, 4096, 768], P('dp', 'seq')
- value_grad: bfloat16 [2, 4096, 768], P('dp', 'seq')
- weight_grad: float32 [768, 1536], P('seq', 'dp')
Inputs may be any that keep to these rules, and one draw needn't show every extreme that they name: Each row holds the lengths of the 8 utterances of one group in packing order; they sum to 4096 and the longest is exactly 1024.
All inputs are finite; a program needn't handle non-finite values.
Results may differ from a plain program's by a relative error of at most 0.022.
Values may be sent and summed in bfloat16 or wider, within the bound.
No kernel may reach another device: no remote copies, remote signals or barrier semaphores. Data moves between devices by JAX's collectives and lax.ppermute only.
A program may use at most 64 MiB of HBM per device.

v0:
```python
import jax
import jax.numpy as jnp
from jax import lax
from jax.sharding import PartitionSpec as P

HEADS = 12
HEAD_DIM = 64
STRETCH = 128
MOST = 1024


MASKED_SCORE = -1e30


def from_behind(block, axis, distance):
    devices = range(lax.axis_size(axis))
    route = [(i - distance, i) for i in devices if i - distance in devices]
    return lax.ppermute(block, axis, route)


def from_behind_2(value, axis, by):
    count = lax.axis_size(axis)
    return lax.ppermute(value, axis, [(i, (i + by) % count) for i in range(count)])


def frame_labels(utt_lengths, source, tok_rows, seq_count):
    positions = source * tok_rows + jnp.arange(tok_rows, dtype=jnp.int32)
    utt_ends = jnp.cumsum(utt_lengths)
    utt_index = jnp.sum((positions[:, None] >= utt_ends[None, :]).astype(jnp.int32), axis=1)
    outside = (positions < 0) | (positions >= seq_count * tok_rows)
    return (jnp.where(outside, -1, utt_index), positions // STRETCH)


def visible_pairs(query_utt, query_stretch, key_utt, key_stretch):
    return (query_utt[:, None] == key_utt[None, :]) & (
        key_stretch[None, :] <= query_stretch[:, None]
    )


def masked_scores(query_heads, key_block, visible):
    scores = jnp.einsum(
        "qhe,khe->hqk", query_heads, key_block, preferred_element_type=jnp.float32
    ) * HEAD_DIM ** (-0.5)
    return jnp.where(visible[None], scores, MASKED_SCORE)


def max_step(row_max, key_block, query_heads, query_utt, query_stretch, key_utt, key_stretch):
    visible = visible_pairs(query_utt, query_stretch, key_utt, key_stretch)

    def max_update(current):
        return jnp.maximum(current, jnp.max(masked_scores(query_heads, key_block, visible), axis=2))

    return lax.cond(jnp.any(visible), max_update, lambda unchanged: unchanged, row_max)


def sum_step(
    carried,
    top_score,
    key_block,
    value_block,
    query_heads,
    query_utt,
    query_stretch,
    key_utt,
    key_stretch,
):
    visible = visible_pairs(query_utt, query_stretch, key_utt, key_stretch)

    def sum_update(state):
        row_total, weighted = state
        scores = masked_scores(query_heads, key_block, visible)
        expo_full = jnp.where(visible[None], jnp.exp(scores - top_score[:, :, None]), 0.0)
        product = jnp.einsum(
            "hqk,khe->hqe",
            expo_full.astype(jnp.bfloat16),
            value_block,
            preferred_element_type=jnp.float32,
        )
        return (row_total + jnp.sum(expo_full, axis=2), weighted + product)

    return lax.cond(jnp.any(visible), sum_update, lambda unchanged: unchanged, carried)


def grad_block(
    query_heads,
    grad_heads,
    log_sum,
    delta_rows,
    query_utt,
    query_stretch,
    key_heads,
    value_heads,
    key_utt,
    key_stretch,
):
    visible = visible_pairs(query_utt, query_stretch, key_utt, key_stretch)
    score_scale = HEAD_DIM ** (-0.5)
    zero_query = jnp.zeros(query_heads.shape, jnp.float32)
    zero_key = jnp.zeros(key_heads.shape, jnp.float32)

    def compute(unused):
        scores = (
            jnp.einsum("qhe,khe->hqk", query_heads, key_heads, preferred_element_type=jnp.float32)
            * score_scale
        )
        prob_full = jnp.where(visible[None], jnp.exp(scores - log_sum[:, :, None]), 0.0)
        prob_back = prob_full.astype(jnp.bfloat16)
        prob_grad = jnp.einsum(
            "qhe,khe->hqk", grad_heads, value_heads, preferred_element_type=jnp.float32
        )
        score_grad = (prob_full * (prob_grad - delta_rows[:, :, None])).astype(jnp.bfloat16)
        query_part = (
            jnp.einsum("hqk,khe->qhe", score_grad, key_heads, preferred_element_type=jnp.float32)
            * score_scale
        )
        key_part = (
            jnp.einsum("hqk,qhe->khe", score_grad, query_heads, preferred_element_type=jnp.float32)
            * score_scale
        )
        value_part = jnp.einsum(
            "hqk,qhe->khe", prob_back, grad_heads, preferred_element_type=jnp.float32
        )
        return (query_part, key_part, value_part)

    return lax.cond(jnp.any(visible), compute, lambda unused: (zero_query, zero_key, zero_key), 0)


def local(query_rows, key_rows, value_rows, out_grad, lengths, out_weight):
    seq_count = lax.axis_size("seq")
    device = lax.axis_index("seq")
    tok_rows = query_rows.shape[1]
    feature_width = query_rows.shape[2]
    reach_steps = min(-(-MOST // tok_rows), seq_count - 1)
    utt_lengths = lengths[0]
    query_heads = query_rows[0].reshape(tok_rows, HEADS, HEAD_DIM)
    key_heads = key_rows[0].reshape(tok_rows, HEADS, HEAD_DIM)
    value_heads = value_rows[0].reshape(tok_rows, HEADS, HEAD_DIM)
    query_utt, query_stretch = frame_labels(utt_lengths, device, tok_rows, seq_count)
    start_max = jnp.full((HEADS, tok_rows), MASKED_SCORE, jnp.float32)
    start_max = max_step(
        start_max, key_heads, query_heads, query_utt, query_stretch, query_utt, query_stretch
    )
    empty_stack = jnp.zeros((reach_steps, tok_rows, HEADS, HEAD_DIM), key_heads.dtype)

    def forward_turn(turn_index, carried):
        row_max, key_block, value_block, key_stack, value_stack = carried
        key_block, value_block = from_behind((key_block, value_block), "seq", 1)
        key_utt, key_stretch = frame_labels(utt_lengths, device - turn_index, tok_rows, seq_count)
        row_max = max_step(
            row_max, key_block, query_heads, query_utt, query_stretch, key_utt, key_stretch
        )
        key_stack = lax.dynamic_update_index_in_dim(key_stack, key_block, turn_index - 1, 0)
        value_stack = lax.dynamic_update_index_in_dim(value_stack, value_block, turn_index - 1, 0)
        return (row_max, key_block, value_block, key_stack, value_stack)

    top_score, unused_keys, unused_values, key_stack, value_stack = lax.fori_loop(
        1,
        reach_steps + 1,
        forward_turn,
        (start_max, key_heads, value_heads, empty_stack, empty_stack),
    )
    start_sums = (
        jnp.zeros((HEADS, tok_rows), jnp.float32),
        jnp.zeros((HEADS, tok_rows, HEAD_DIM), jnp.float32),
    )
    start_sums = sum_step(
        start_sums,
        top_score,
        key_heads,
        value_heads,
        query_heads,
        query_utt,
        query_stretch,
        query_utt,
        query_stretch,
    )

    def summing_turn(turn_index, carried):
        key_block = lax.dynamic_index_in_dim(key_stack, turn_index - 1, 0, keepdims=False)
        value_block = lax.dynamic_index_in_dim(value_stack, turn_index - 1, 0, keepdims=False)
        key_utt, key_stretch = frame_labels(utt_lengths, device - turn_index, tok_rows, seq_count)
        return sum_step(
            carried,
            top_score,
            key_block,
            value_block,
            query_heads,
            query_utt,
            query_stretch,
            key_utt,
            key_stretch,
        )

    row_total, weighted = lax.fori_loop(1, reach_steps + 1, summing_turn, start_sums)
    attended = (
        jnp.transpose(weighted / row_total[:, :, None], (1, 0, 2))
        .reshape(tok_rows, feature_width)
        .astype(jnp.bfloat16)
    )
    log_sum = top_score + jnp.log(row_total)
    weight_cols = lax.all_gather(out_weight, "dp", axis=1, tiled=True)
    weight_full = lax.all_gather(weight_cols, "seq", axis=0, tiled=True)
    mixed_out = jnp.dot(attended, weight_full, preferred_element_type=jnp.float32).astype(
        jnp.bfloat16
    )
    upstream = out_grad[0]
    att_grad = lax.dot_general(
        upstream, weight_full, (((1,), (1,)), ((), ())), preferred_element_type=jnp.float32
    ).astype(jnp.bfloat16)
    grad_heads = att_grad.reshape(tok_rows, HEADS, HEAD_DIM)
    delta_rows = jnp.transpose(
        jnp.sum(
            grad_heads.astype(jnp.float32)
            * attended.reshape(tok_rows, HEADS, HEAD_DIM).astype(jnp.float32),
            axis=2,
        )
    )
    query_acc, key_own, value_own = grad_block(
        query_heads,
        grad_heads,
        log_sum,
        delta_rows,
        query_utt,
        query_stretch,
        key_heads,
        value_heads,
        query_utt,
        query_stretch,
    )

    def kept_turn(turn_index, carried):
        query_acc, key_acc, value_acc = carried
        key_acc, value_acc = from_behind_2((key_acc, value_acc), "seq", 1)
        key_block = lax.dynamic_index_in_dim(key_stack, turn_index - 1, 0, keepdims=False)
        value_block = lax.dynamic_index_in_dim(value_stack, turn_index - 1, 0, keepdims=False)
        key_utt, key_stretch = frame_labels(utt_lengths, device - turn_index, tok_rows, seq_count)
        query_part, key_part, value_part = grad_block(
            query_heads,
            grad_heads,
            log_sum,
            delta_rows,
            query_utt,
            query_stretch,
            key_block,
            value_block,
            key_utt,
            key_stretch,
        )
        return (query_acc + query_part, key_acc + key_part, value_acc + value_part)

    query_acc, key_acc, value_acc = lax.fori_loop(
        1, reach_steps + 1, kept_turn, (query_acc, key_own, value_own)
    )
    key_acc, value_acc = from_behind_2((key_acc, value_acc), "seq", -reach_steps)
    query_grad = query_acc.reshape(tok_rows, feature_width).astype(jnp.bfloat16)
    key_grad = key_acc.reshape(tok_rows, feature_width).astype(jnp.bfloat16)
    value_grad = value_acc.reshape(tok_rows, feature_width).astype(jnp.bfloat16)
    row_share = lax.psum_scatter(
        lax.dot_general(
            attended, upstream, (((0,), (0,)), ((), ())), preferred_element_type=jnp.float32
        ),
        "seq",
        scatter_dimension=0,
        tiled=True,
    )
    weight_grad = lax.psum_scatter(row_share, "dp", scatter_dimension=1, tiled=True)
    return (mixed_out[None], query_grad[None], key_grad[None], value_grad[None], weight_grad)


def solution(mesh):
    return jax.shard_map(
        local,
        mesh=mesh,
        in_specs=(
            P("dp", "seq", None),
            P("dp", "seq", None),
            P("dp", "seq", None),
            P("dp", "seq", None),
            P("dp", None),
            P("seq", "dp"),
        ),
        out_specs=(
            P("dp", "seq", None),
            P("dp", "seq", None),
            P("dp", "seq", None),
            P("dp", "seq", None),
            P("seq", "dp"),
        ),
        check_vma=False,
    )
```

profile of v0, /device:TPU:4, one launch (start us, length us, event | category | flops | bytes accessed | tf_op | source)
XLA Modules:
  0.0 330.8 jit_solution(18214105469658841321)
XLA Ops:
  7.2 6.4 %all_gather.6 = bf16[48,1536]{1,0:T(8,128)(2,1)} all-gather(bf16[48,768]{1,0:T(8,128)(2,1)} %param.29), channel_id=1, replica_groups=mesh['seq'=16,'dp'=2] {'dp'}, dimensions={1}, use_global_device_ids=true | all-gather | bytes 221184 | tf_op jit(solution)/shard_map/all_gather | solution.py:201
  22.8 71.5 %while.74 = (s32[]{:T(128)}, f32[12,256]{1,0:T(8,128)S(1)}, bf16[256,12,64]{0,2,1:T(8,128)(2,1)}, bf16[256,12,64]{0,2,1:T(8,128)(2,1)}, bf16[4,256,12,64]{1,3,2,...) while((s32[]{:T(128)}, f32[12,256]{1,0:T(8,128)S(1)}, ...), condition=%wide.region_13.14_spmd.clone, body=%wide.region_7.0_spmd.clone.sunk | while | flops 103299840 | bytes 7269711 | solution.py:156
  24.8 3.5 %collective-permute-start = (bf16[256,12,64]{0,2,1:T(8,128)(2,1)}, bf16[256,12,64]{0,2,1:T(8,128)(2,1)S(1)}, u32[]{:S(2)}, u32[]{:S(2)}) collective-permute-start(bf16[256,12,64]{0,2,1:T(8,128)(2,1)} %get-tuple-element.2182), channel_id=1, source_target_pairs={{0,2},{2,4},{4,6},{6,8},{8,10},{10,12},{12,14},{14,16},{16,18},{18... | collective-permute-start | bytes 1179656 | tf_op jit(solution)/shard_map/while/body/eval_jaxpr/ppermute | solution.py:18
  29.8 6.5 %collective-permute-done = bf16[256,12,64]{0,2,1:T(8,128)(2,1)S(1)} collective-permute-done((bf16[256,12,64]{0,2,1:T(8,128)(2,1)}, bf16[256,12,64]{0,2,1:T(8,128)(2,1)S(1)}, u32[]{:S(2)}, u32[]{:S(2)}) %collective-permute-start) | collective-permute-done | bytes 393248 | tf_op jit(solution)/shard_map/while/body/eval_jaxpr/ppermute | solution.py:18
  40.1 3.7 %collective-permute-start.1 = (bf16[256,12,64]{0,2,1:T(8,128)(2,1)}, bf16[256,12,64]{0,2,1:T(8,128)(2,1)S(1)}, u32[]{:S(2)}, u32[]{:S(2)}) collective-permute-start(bf16[256,12,64]{0,2,1:T(8,128)(2,1)} %get-tuple-element.2183), channel_id=1, source_target_pairs={{0,2},{2,4},{4,6},{6,8},{8,10},{10,12},{12,14},{14,16},{16,18},{18... | collective-permute-start | bytes 1179656 | tf_op jit(solution)/shard_map/while/body/eval_jaxpr/ppermute | solution.py:18
  43.8 5.2 %collective-permute-start = (bf16[256,12,64]{0,2,1:T(8,128)(2,1)}, bf16[256,12,64]{0,2,1:T(8,128)(2,1)S(1)}, u32[]{:S(2)}, u32[]{:S(2)}) collective-permute-start(bf16[256,12,64]{0,2,1:T(8,128)(2,1)} %get-tuple-element.2182), channel_id=1, source_target_pairs={{0,2},{2,4},{4,6},{6,8},{8,10},{10,12},{12,14},{14,16},{16,18},{18... | collective-permute-start | bytes 1179656 | tf_op jit(solution)/shard_map/while/body/eval_jaxpr/ppermute | solution.py:18
  50.6 4.6 %collective-permute-done = bf16[256,12,64]{0,2,1:T(8,128)(2,1)S(1)} collective-permute-done((bf16[256,12,64]{0,2,1:T(8,128)(2,1)}, bf16[256,12,64]{0,2,1:T(8,128)(2,1)S(1)}, u32[]{:S(2)}, u32[]{:S(2)}) %collective-permute-start) | collective-permute-done | bytes 393248 | tf_op jit(solution)/shard_map/while/body/eval_jaxpr/ppermute | solution.py:18
  58.9 5.6 %collective-permute-start.1 = (bf16[256,12,64]{0,2,1:T(8,128)(2,1)}, bf16[256,12,64]{0,2,1:T(8,128)(2,1)S(1)}, u32[]{:S(2)}, u32[]{:S(2)}) collective-permute-start(bf16[256,12,64]{0,2,1:T(8,128)(2,1)} %get-tuple-element.2183), channel_id=1, source_target_pairs={{0,2},{2,4},{4,6},{6,8},{8,10},{10,12},{12,14},{14,16},{16,18},{18... | collective-permute-start | bytes 1179656 | tf_op jit(solution)/shard_map/while/body/eval_jaxpr/ppermute | solution.py:18
  64.5 5.2 %collective-permute-start = (bf16[256,12,64]{0,2,1:T(8,128)(2,1)}, bf16[256,12,64]{0,2,1:T(8,128)(2,1)S(1)}, u32[]{:S(2)}, u32[]{:S(2)}) collective-permute-start(bf16[256,12,64]{0,2,1:T(8,128)(2,1)} %get-tuple-element.2182), channel_id=1, source_target_pairs={{0,2},{2,4},{4,6},{6,8},{8,10},{10,12},{12,14},{14,16},{16,18},{18... | collective-permute-start | bytes 1179656 | tf_op jit(solution)/shard_map/while/body/eval_jaxpr/ppermute | solution.py:18
  71.2 2.6 collective-permute-done
  76.8 5.1 %collective-permute-start.1 = (bf16[256,12,64]{0,2,1:T(8,128)(2,1)}, bf16[256,12,64]{0,2,1:T(8,128)(2,1)S(1)}, u32[]{:S(2)}, u32[]{:S(2)}) collective-permute-start(bf16[256,12,64]{0,2,1:T(8,128)(2,1)} %get-tuple-element.2183), channel_id=1, source_target_pairs={{0,2},{2,4},{4,6},{6,8},{8,10},{10,12},{12,14},{14,16},{16,18},{18... | collective-permute-start | bytes 1179656 | tf_op jit(solution)/shard_map/while/body/eval_jaxpr/ppermute | solution.py:18
  81.9 5.2 %collective-permute-start = (bf16[256,12,64]{0,2,1:T(8,128)(2,1)}, bf16[256,12,64]{0,2,1:T(8,128)(2,1)S(1)}, u32[]{:S(2)}, u32[]{:S(2)}) collective-permute-start(bf16[256,12,64]{0,2,1:T(8,128)(2,1)} %get-tuple-element.2182), channel_id=1, source_target_pairs={{0,2},{2,4},{4,6},{6,8},{8,10},{10,12},{12,14},{14,16},{16,18},{18... | collective-permute-start | bytes 1179656 | tf_op jit(solution)/shard_map/while/body/eval_jaxpr/ppermute | solution.py:18
  88.7 2.6 collective-permute-done
  94.3 2.2 conditional.7
  96.5 14.6 %while.75 = (s32[]{:T(128)}, f32[12,256]{1,0:T(8,128)S(1)}, f32[12,256,64]{1,2,0:T(8,128)S(1)}, s32[256]{0:T(256)S(1)}, s32[]{:T(128)}, /*index=5*/s32[1,8]{1,0:...) while((s32[]{:T(128)}, f32[12,256]{1,0:T(8,128)S(1)}, ...), condition=%wide.region_23.24_spmd.clone, body=%wide.region_17.23_spmd.clone.sunk | while | flops 209664768 | bytes 9325921 | solution.py:194
  98.1 4.1 %conditional.16 = ((f32[12,256]{1,0:T(8,128)S(1)}, f32[12,256,64]{1,2,0:T(8,128)S(1)})) conditional(s32[]{:T(128)} %convert_element_type.243, (f32[12,256]{1,0:T(8,128)S(1)}, f32[12,256,64]{1,2,0:T(8,128)S(1)}) %tuple.285, (pred[256,256]{0,1:T(8,128)(4,1)S(1)}, s32[]{:T(128)}, bf16[4,256,12,64]{1,3,2,0:T(8,128)(2,1)}, ...), branch_computations={%region_20.20_spmd, %region_21.22_spmd} | conditional | flops 209387520 | bytes 9248834 | solution.py:81
  103.7 4.1 %conditional.16 = ((f32[12,256]{1,0:T(8,128)S(1)}, f32[12,256,64]{1,2,0:T(8,128)S(1)})) conditional(s32[]{:T(128)} %convert_element_type.243, (f32[12,256]{1,0:T(8,128)S(1)}, f32[12,256,64]{1,2,0:T(8,128)S(1)}) %tuple.285, (pred[256,256]{0,1:T(8,128)(4,1)S(1)}, s32[]{:T(128)}, bf16[4,256,12,64]{1,3,2,0:T(8,128)(2,1)}, ...), branch_computations={%region_20.20_spmd, %region_21.22_spmd} | conditional | flops 209387520 | bytes 9248834 | solution.py:81
  111.1 2.5 convolution_convert_fusion.1
  116.2 2.9 fusion.75
  119.8 8.7 %conditional.8 = (f32[256,12,64]{0,2,1:T(8,128)}, f32[256,12,64]{0,2,1:T(8,128)}, f32[256,12,64]{0,2,1:T(8,128)}) conditional(s32[]{:T(128)} %convert_element_type.186, () %tuple.199, (pred[256,256]{1,0:T(8,128)(4,1)S(1)}, bf16[256,12,64]{0,2,1:T(8,128)(2,1)S(1)}, bf16[256,12,64]{0,2,1:T(8,128)(2,1)S(1)}, f32[12,256]{1,0:T(8,128)S(1)}, ...), branch_computations={%region_25.26_spmd, %region_26.27_spmd} | conditional | flops 511574016 | bytes 21270608 | solution.py:125
  120.6 2.7 fusion.42
  123.3 2.5 multiply_convert_fusion
  128.5 79.9 %reduce-scatter.3.cloned.1.call-done = f32[48,1536]{1,0:T(8,128)} async-done(((f32[768,1536]{1,0:T(8,128)}), f32[48,1536]{1,0:T(8,128)}) %reduce-scatter.3.cloned.1.call-update) | async-done | bytes 294928 | tf_op jit(solution)/shard_map/reduce_scatter | solution.py:258
  208.5 89.4 %while.76 = (s32[]{:T(128)}, f32[256,12,64]{0,2,1:T(8,128)}, f32[256,12,64]{0,2,1:T(8,128)}, f32[256,12,64]{0,2,1:T(8,128)}, s32[256]{0:T(256)S(1)}, /*index=5*/...) while((s32[]{:T(128)}, f32[256,12,64]{0,2,1:T(8,128)}, ...), condition=%wide.region_32.33_spmd.clone, body=%wide.region_27.32_spmd.clone.sunk | while | flops 512441088 | bytes 33291828 | solution.py:251
  212.4 7.7 %conditional.17 = (f32[256,12,64]{0,2,1:T(8,128)S(1)}, f32[256,12,64]{0,2,1:T(8,128)S(1)}, f32[256,12,64]{0,2,1:T(8,128)S(1)}) conditional(s32[]{:T(128)} %convert_element_type.245, () %tuple.290, (pred[256,256]{0,1:T(8,128)(4,1)}, s32[]{:T(128)}, bf16[4,256,12,64]{1,3,2,0:T(8,128)(2,1)}, bf16[256,12,64]{0,2,1:T(8,128)(2,1)S(1)}, ...), branch_computations={%region_30.30_spmd, %region_31.31_spmd} | conditional | flops 511574016 | bytes 19697762 | solution.py:125
  214.1 2.2 fusion.49
  220.1 2.1 add.723
  222.2 2.2 add.725
  224.4 4.3 %collective-permute-done.2 = f32[256,12,64]{0,2,1:T(8,128)} collective-permute-done((f32[256,12,64]{0,2,1:T(8,128)}, f32[256,12,64]{0,2,1:T(8,128)}, u32[]{:S(2)}, u32[]{:S(2)}) %collective-permute-start.2) | collective-permute-done | bytes 786464 | tf_op jit(solution)/shard_map/while/body/eval_jaxpr/ppermute | solution.py:23
  228.7 2.1 add.724
  230.9 2.6 collective-permute-start.2
  235.7 7.7 %conditional.17 = (f32[256,12,64]{0,2,1:T(8,128)S(1)}, f32[256,12,64]{0,2,1:T(8,128)S(1)}, f32[256,12,64]{0,2,1:T(8,128)S(1)}) conditional(s32[]{:T(128)} %convert_element_type.245, () %tuple.290, (pred[256,256]{0,1:T(8,128)(4,1)}, s32[]{:T(128)}, bf16[4,256,12,64]{1,3,2,0:T(8,128)(2,1)}, bf16[256,12,64]{0,2,1:T(8,128)(2,1)S(1)}, ...), branch_computations={%region_30.30_spmd, %region_31.31_spmd} | conditional | flops 511574016 | bytes 19697762 | solution.py:125
  237.4 2.2 fusion.49
  245.5 2.1 add.725
  247.6 3.4 %collective-permute-done.2 = f32[256,12,64]{0,2,1:T(8,128)} collective-permute-done((f32[256,12,64]{0,2,1:T(8,128)}, f32[256,12,64]{0,2,1:T(8,128)}, u32[]{:S(2)}, u32[]{:S(2)}) %collective-permute-start.2) | collective-permute-done | bytes 786464 | tf_op jit(solution)/shard_map/while/body/eval_jaxpr/ppermute | solution.py:23
  251.1 2.1 add.724
  253.4 3.4 %collective-permute-start.2 = (f32[256,12,64]{0,2,1:T(8,128)}, f32[256,12,64]{0,2,1:T(8,128)}, u32[]{:S(2)}, u32[]{:S(2)}) collective-permute-start(f32[256,12,64]{0,2,1:T(8,128)} %get-tuple-element.2273), channel_id=1, source_target_pairs={{0,2},{2,4},{4,6},{6,8},{8,10},{10,12},{12,14},{14,16},{16,18},{18... | collective-permute-start | bytes 2359304 | tf_op jit(solution)/shard_map/while/body/eval_jaxpr/ppermute | solution.py:23
  261.3 3.7 %collective-permute-done.3 = f32[256,12,64]{0,2,1:T(8,128)} collective-permute-done((f32[256,12,64]{0,2,1:T(8,128)}, f32[256,12,64]{0,2,1:T(8,128)}, u32[]{:S(2)}, u32[]{:S(2)}) %collective-permute-start.3) | collective-permute-done | bytes 786464 | tf_op jit(solution)/shard_map/while/body/eval_jaxpr/ppermute | solution.py:23
  265.0 2.1 add.725
  267.1 6.3 %collective-permute-done.2 = f32[256,12,64]{0,2,1:T(8,128)} collective-permute-done((f32[256,12,64]{0,2,1:T(8,128)}, f32[256,12,64]{0,2,1:T(8,128)}, u32[]{:S(2)}, u32[]{:S(2)}) %collective-permute-start.2) | collective-permute-done | bytes 786464 | tf_op jit(solution)/shard_map/while/body/eval_jaxpr/ppermute | solution.py:23
  273.4 2.1 add.724
  276.7 3.4 %collective-permute-start.2 = (f32[256,12,64]{0,2,1:T(8,128)}, f32[256,12,64]{0,2,1:T(8,128)}, u32[]{:S(2)}, u32[]{:S(2)}) collective-permute-start(f32[256,12,64]{0,2,1:T(8,128)} %get-tuple-element.2273), channel_id=1, source_target_pairs={{0,2},{2,4},{4,6},{6,8},{8,10},{10,12},{12,14},{14,16},{16,18},{18... | collective-permute-start | bytes 2359304 | tf_op jit(solution)/shard_map/while/body/eval_jaxpr/ppermute | solution.py:23
  284.6 2.8 collective-permute-done.3
  287.4 2.1 add.725
  289.5 6.3 %collective-permute-done.2 = f32[256,12,64]{0,2,1:T(8,128)} collective-permute-done((f32[256,12,64]{0,2,1:T(8,128)}, f32[256,12,64]{0,2,1:T(8,128)}, u32[]{:S(2)}, u32[]{:S(2)}) %collective-permute-start.2) | collective-permute-done | bytes 786464 | tf_op jit(solution)/shard_map/while/body/eval_jaxpr/ppermute | solution.py:23
  295.8 2.1 add.724
  311.1 3.6 %collective-permute-done.4 = bf16[256,12,64]{0,2,1:T(8,128)(2,1)} collective-permute-done((bf16[256,12,64]{0,2,1:T(8,128)(2,1)}, bf16[256,12,64]{0,2,1:T(8,128)(2,1)}, u32[]{:S(2)}, u32[]{:S(2)}) %collective-permute-start.4) | collective-permute-done | bytes 393248 | tf_op jit(solution)/shard_map/ppermute | solution.py:23
  316.6 5.7 %collective-permute-done.5 = bf16[256,12,64]{0,2,1:T(8,128)(2,1)} collective-permute-done((bf16[256,12,64]{0,2,1:T(8,128)(2,1)}, bf16[256,12,64]{0,2,1:T(8,128)(2,1)}, u32[]{:S(2)}, u32[]{:S(2)}) %collective-permute-start.5) | collective-permute-done | bytes 393248 | tf_op jit(solution)/shard_map/ppermute | solution.py:23
  (208 shorter events, 94.6 us)
Async XLA Ops:
  7.2 103.9 %copy-start = (bf16[1,256,1536]{2,1,0:T(8,128)(2,1)S(1)}, bf16[1,256,1536]{2,1,0:T(8,128)(2,1)}, u32[]{:S(2)}) copy-start(bf16[1,256,1536]{2,1,0:T(8,128)(2,1)} %param.27) | copy-start | bytes 2359300
  7.2 103.9 %all-gather.2.cloned.1.call-start = ((), (), s32[]{:S(2)}) async-start(), calls=%async_computation.2 | async-start | bytes 2506752 | tf_op jit(solution)/shard_map/all_gather | solution.py:202
  13.7 194.8 %reduce-scatter.3.cloned.1.call-start = ((), (), s32[]{:S(2)}) async-start(), calls=%async_computation.3 | async-start | bytes 5013504 | tf_op jit(solution)/shard_map/reduce_scatter | solution.py:258
  22.8 15.0 %collective-permute-start.1 = (bf16[256,12,64]{0,2,1:T(8,128)(2,1)}, bf16[256,12,64]{0,2,1:T(8,128)(2,1)S(1)}, u32[]{:S(2)}, u32[]{:S(2)}) collective-permute-start(bf16[256,12,64]{0,2,1:T(8,128)(2,1)} %get-tuple-element.2183), channel_id=1, source_target_pairs={{0,2},{2,4},{4,6},{6,8},{8,10},{10,12},{12,14},{14,16},{16,18},{18... | collective-permute-start | bytes 1179656 | tf_op jit(solution)/shard_map/while/body/eval_jaxpr/ppermute | solution.py:18
  24.8 11.6 %collective-permute-start = (bf16[256,12,64]{0,2,1:T(8,128)(2,1)}, bf16[256,12,64]{0,2,1:T(8,128)(2,1)S(1)}, u32[]{:S(2)}, u32[]{:S(2)}) collective-permute-start(bf16[256,12,64]{0,2,1:T(8,128)(2,1)} %get-tuple-element.2182), channel_id=1, source_target_pairs={{0,2},{2,4},{4,6},{6,8},{8,10},{10,12},{12,14},{14,16},{16,18},{18... | collective-permute-start | bytes 1179656 | tf_op jit(solution)/shard_map/while/body/eval_jaxpr/ppermute | solution.py:18
  40.1 16.5 %collective-permute-start.1 = (bf16[256,12,64]{0,2,1:T(8,128)(2,1)}, bf16[256,12,64]{0,2,1:T(8,128)(2,1)S(1)}, u32[]{:S(2)}, u32[]{:S(2)}) collective-permute-start(bf16[256,12,64]{0,2,1:T(8,128)(2,1)} %get-tuple-element.2183), channel_id=1, source_target_pairs={{0,2},{2,4},{4,6},{6,8},{8,10},{10,12},{12,14},{14,16},{16,18},{18... | collective-permute-start | bytes 1179656 | tf_op jit(solution)/shard_map/while/body/eval_jaxpr/ppermute | solution.py:18
  43.8 11.3 %collective-permute-start = (bf16[256,12,64]{0,2,1:T(8,128)(2,1)}, bf16[256,12,64]{0,2,1:T(8,128)(2,1)S(1)}, u32[]{:S(2)}, u32[]{:S(2)}) collective-permute-start(bf16[256,12,64]{0,2,1:T(8,128)(2,1)} %get-tuple-element.2182), channel_id=1, source_target_pairs={{0,2},{2,4},{4,6},{6,8},{8,10},{10,12},{12,14},{14,16},{16,18},{18... | collective-permute-start | bytes 1179656 | tf_op jit(solution)/shard_map/while/body/eval_jaxpr/ppermute | solution.py:18
  58.9 15.6 %collective-permute-start.1 = (bf16[256,12,64]{0,2,1:T(8,128)(2,1)}, bf16[256,12,64]{0,2,1:T(8,128)(2,1)S(1)}, u32[]{:S(2)}, u32[]{:S(2)}) collective-permute-start(bf16[256,12,64]{0,2,1:T(8,128)(2,1)} %get-tuple-element.2183), channel_id=1, source_target_pairs={{0,2},{2,4},{4,6},{6,8},{8,10},{10,12},{12,14},{14,16},{16,18},{18... | collective-permute-start | bytes 1179656 | tf_op jit(solution)/shard_map/while/body/eval_jaxpr/ppermute | solution.py:18
  64.5 9.3 %collective-permute-start = (bf16[256,12,64]{0,2,1:T(8,128)(2,1)}, bf16[256,12,64]{0,2,1:T(8,128)(2,1)S(1)}, u32[]{:S(2)}, u32[]{:S(2)}) collective-permute-start(bf16[256,12,64]{0,2,1:T(8,128)(2,1)} %get-tuple-element.2182), channel_id=1, source_target_pairs={{0,2},{2,4},{4,6},{6,8},{8,10},{10,12},{12,14},{14,16},{16,18},{18... | collective-permute-start | bytes 1179656 | tf_op jit(solution)/shard_map/while/body/eval_jaxpr/ppermute | solution.py:18
  76.8 15.2 %collective-permute-start.1 = (bf16[256,12,64]{0,2,1:T(8,128)(2,1)}, bf16[256,12,64]{0,2,1:T(8,128)(2,1)S(1)}, u32[]{:S(2)}, u32[]{:S(2)}) collective-permute-start(bf16[256,12,64]{0,2,1:T(8,128)(2,1)} %get-tuple-element.2183), channel_id=1, source_target_pairs={{0,2},{2,4},{4,6},{6,8},{8,10},{10,12},{12,14},{14,16},{16,18},{18... | collective-permute-start | bytes 1179656 | tf_op jit(solution)/shard_map/while/body/eval_jaxpr/ppermute | solution.py:18
  81.9 9.3 %collective-permute-start = (bf16[256,12,64]{0,2,1:T(8,128)(2,1)}, bf16[256,12,64]{0,2,1:T(8,128)(2,1)S(1)}, u32[]{:S(2)}, u32[]{:S(2)}) collective-permute-start(bf16[256,12,64]{0,2,1:T(8,128)(2,1)} %get-tuple-element.2182), channel_id=1, source_target_pairs={{0,2},{2,4},{4,6},{6,8},{8,10},{10,12},{12,14},{14,16},{16,18},{18... | collective-permute-start | bytes 1179656 | tf_op jit(solution)/shard_map/while/body/eval_jaxpr/ppermute | solution.py:18
  116.2 2.9 copy-start.1
  119.1 0.7 copy-start.7
  119.1 205.1 %reduce-scatter.5.cloned.1.call-start = ((), (), s32[]{:S(2)}) async-start(), calls=%async_computation.4 | async-start | bytes 442368 | tf_op jit(solution)/shard_map/reduce_scatter | solution.py:266
  119.8 0.7 copy-start.5
  119.8 0.8 copy-start.6
  208.5 3.9 %copy-start.9 = (f32[12,256]{1,0:T(8,128)}, f32[12,256]{1,0:T(8,128)S(1)}, u32[]{:S(2)}) copy-start(f32[12,256]{1,0:T(8,128)S(1)} %get-tuple-element.2296) | copy-start | bytes 36868 | tf_op jit(solution)/shard_map/while
  208.5 13.7 %collective-permute-start.3 = (f32[256,12,64]{0,2,1:T(8,128)}, f32[256,12,64]{0,2,1:T(8,128)}, u32[]{:S(2)}, u32[]{:S(2)}) collective-permute-start(f32[256,12,64]{0,2,1:T(8,128)} %get-tuple-element.2274), channel_id=1, source_target_pairs={{0,2},{2,4},{4,6},{6,8},{8,10},{10,12},{12,14},{14,16},{16,18},{18... | collective-permute-start | bytes 2359304 | tf_op jit(solution)/shard_map/while/body/eval_jaxpr/ppermute | solution.py:23
  208.6 20.1 %collective-permute-start.2 = (f32[256,12,64]{0,2,1:T(8,128)}, f32[256,12,64]{0,2,1:T(8,128)}, u32[]{:S(2)}, u32[]{:S(2)}) collective-permute-start(f32[256,12,64]{0,2,1:T(8,128)} %get-tuple-element.2273), channel_id=1, source_target_pairs={{0,2},{2,4},{4,6},{6,8},{8,10},{10,12},{12,14},{14,16},{16,18},{18... | collective-permute-start | bytes 2359304 | tf_op jit(solution)/shard_map/while/body/eval_jaxpr/ppermute | solution.py:23
  212.5 1.7 copy-start.4
  222.2 8.6 %copy-start.8 = (f32[256,12]{0,1:T(8,128)S(1)}, f32[256,12]{0,1:T(8,128)}, u32[]{:S(2)}) copy-start(f32[256,12]{0,1:T(8,128)} %get-tuple-element.2344) | copy-start | bytes 36868 | tf_op jit(solution)/shard_map/while
  222.2 8.6 %copy-start.10 = (f32[12,256]{1,0:T(8,128)S(1)}, f32[12,256]{1,0:T(8,128)}, u32[]{:S(2)}) copy-start(f32[12,256]{1,0:T(8,128)} %copy-done.9) | copy-start | bytes 36868 | tf_op jit(solution)/shard_map/while
  230.9 4.8 %copy-start.9 = (f32[12,256]{1,0:T(8,128)}, f32[12,256]{1,0:T(8,128)S(1)}, u32[]{:S(2)}) copy-start(f32[12,256]{1,0:T(8,128)S(1)} %get-tuple-element.2296) | copy-start | bytes 36868 | tf_op jit(solution)/shard_map/while
  230.9 14.6 %collective-permute-start.3 = (f32[256,12,64]{0,2,1:T(8,128)}, f32[256,12,64]{0,2,1:T(8,128)}, u32[]{:S(2)}, u32[]{:S(2)}) collective-permute-start(f32[256,12,64]{0,2,1:T(8,128)} %get-tuple-element.2274), channel_id=1, source_target_pairs={{0,2},{2,4},{4,6},{6,8},{8,10},{10,12},{12,14},{14,16},{16,18},{18... | collective-permute-start | bytes 2359304 | tf_op jit(solution)/shard_map/while/body/eval_jaxpr/ppermute | solution.py:23
  230.9 20.1 %collective-permute-start.2 = (f32[256,12,64]{0,2,1:T(8,128)}, f32[256,12,64]{0,2,1:T(8,128)}, u32[]{:S(2)}, u32[]{:S(2)}) collective-permute-start(f32[256,12,64]{0,2,1:T(8,128)} %get-tuple-element.2273), channel_id=1, source_target_pairs={{0,2},{2,4},{4,6},{6,8},{8,10},{10,12},{12,14},{14,16},{16,18},{18... | collective-permute-start | bytes 2359304 | tf_op jit(solution)/shard_map/while/body/eval_jaxpr/ppermute | solution.py:23
  235.7 1.7 copy-start.4
  245.5 7.7 %copy-start.8 = (f32[256,12]{0,1:T(8,128)S(1)}, f32[256,12]{0,1:T(8,128)}, u32[]{:S(2)}) copy-start(f32[256,12]{0,1:T(8,128)} %get-tuple-element.2344) | copy-start | bytes 36868 | tf_op jit(solution)/shard_map/while
  245.5 7.7 %copy-start.10 = (f32[12,256]{1,0:T(8,128)S(1)}, f32[12,256]{1,0:T(8,128)}, u32[]{:S(2)}) copy-start(f32[12,256]{1,0:T(8,128)} %copy-done.9) | copy-start | bytes 36868 | tf_op jit(solution)/shard_map/while
  253.2 5.7 %copy-start.9 = (f32[12,256]{1,0:T(8,128)}, f32[12,256]{1,0:T(8,128)S(1)}, u32[]{:S(2)}) copy-start(f32[12,256]{1,0:T(8,128)S(1)} %get-tuple-element.2296) | copy-start | bytes 36868 | tf_op jit(solution)/shard_map/while
  253.2 11.8 %collective-permute-start.3 = (f32[256,12,64]{0,2,1:T(8,128)}, f32[256,12,64]{0,2,1:T(8,128)}, u32[]{:S(2)}, u32[]{:S(2)}) collective-permute-start(f32[256,12,64]{0,2,1:T(8,128)} %get-tuple-element.2274), channel_id=1, source_target_pairs={{0,2},{2,4},{4,6},{6,8},{8,10},{10,12},{12,14},{14,16},{16,18},{18... | collective-permute-start | bytes 2359304 | tf_op jit(solution)/shard_map/while/body/eval_jaxpr/ppermute | solution.py:23
  253.4 20.0 %collective-permute-start.2 = (f32[256,12,64]{0,2,1:T(8,128)}, f32[256,12,64]{0,2,1:T(8,128)}, u32[]{:S(2)}, u32[]{:S(2)}) collective-permute-start(f32[256,12,64]{0,2,1:T(8,128)} %get-tuple-element.2273), channel_id=1, source_target_pairs={{0,2},{2,4},{4,6},{6,8},{8,10},{10,12},{12,14},{14,16},{16,18},{18... | collective-permute-start | bytes 2359304 | tf_op jit(solution)/shard_map/while/body/eval_jaxpr/ppermute | solution.py:23
  261.3 14.3 %copy-start.8 = (f32[256,12]{0,1:T(8,128)S(1)}, f32[256,12]{0,1:T(8,128)}, u32[]{:S(2)}) copy-start(f32[256,12]{0,1:T(8,128)} %get-tuple-element.2344) | copy-start | bytes 36868 | tf_op jit(solution)/shard_map/while
  261.3 14.3 %copy-start.10 = (f32[12,256]{1,0:T(8,128)S(1)}, f32[12,256]{1,0:T(8,128)}, u32[]{:S(2)}) copy-start(f32[12,256]{1,0:T(8,128)} %copy-done.9) | copy-start | bytes 36868 | tf_op jit(solution)/shard_map/while
  275.6 6.6 %copy-start.9 = (f32[12,256]{1,0:T(8,128)}, f32[12,256]{1,0:T(8,128)S(1)}, u32[]{:S(2)}) copy-start(f32[12,256]{1,0:T(8,128)S(1)} %get-tuple-element.2296) | copy-start | bytes 36868 | tf_op jit(solution)/shard_map/while
  275.6 11.8 %collective-permute-start.3 = (f32[256,12,64]{0,2,1:T(8,128)}, f32[256,12,64]{0,2,1:T(8,128)}, u32[]{:S(2)}, u32[]{:S(2)}) collective-permute-start(f32[256,12,64]{0,2,1:T(8,128)} %get-tuple-element.2274), channel_id=1, source_target_pairs={{0,2},{2,4},{4,6},{6,8},{8,10},{10,12},{12,14},{14,16},{16,18},{18... | collective-permute-start | bytes 2359304 | tf_op jit(solution)/shard_map/while/body/eval_jaxpr/ppermute | solution.py:23
  276.7 19.1 %collective-permute-start.2 = (f32[256,12,64]{0,2,1:T(8,128)}, f32[256,12,64]{0,2,1:T(8,128)}, u32[]{:S(2)}, u32[]{:S(2)}) collective-permute-start(f32[256,12,64]{0,2,1:T(8,128)} %get-tuple-element.2273), channel_id=1, source_target_pairs={{0,2},{2,4},{4,6},{6,8},{8,10},{10,12},{12,14},{14,16},{16,18},{18... | collective-permute-start | bytes 2359304 | tf_op jit(solution)/shard_map/while/body/eval_jaxpr/ppermute | solution.py:23
  284.6 13.4 %copy-start.8 = (f32[256,12]{0,1:T(8,128)S(1)}, f32[256,12]{0,1:T(8,128)}, u32[]{:S(2)}) copy-start(f32[256,12]{0,1:T(8,128)} %get-tuple-element.2344) | copy-start | bytes 36868 | tf_op jit(solution)/shard_map/while
  284.6 13.4 %copy-start.10 = (f32[12,256]{1,0:T(8,128)S(1)}, f32[12,256]{1,0:T(8,128)}, u32[]{:S(2)}) copy-start(f32[12,256]{1,0:T(8,128)} %copy-done.9) | copy-start | bytes 36868 | tf_op jit(solution)/shard_map/while
  297.9 11.5 %copy-start.2 = (bf16[12,256,64]{1,2,0:T(8,128)(2,1)S(1)}, bf16[12,256,64]{1,2,0:T(8,128)(2,1)}, u32[]{:S(2)}) copy-start(bf16[12,256,64]{1,2,0:T(8,128)(2,1)} %copy-done.1) | copy-start | bytes 1179652
  297.9 11.5 %copy-start.3 = (bf16[768,1536]{1,0:T(8,128)(2,1)S(1)}, bf16[768,1536]{1,0:T(8,128)(2,1)}, u32[]{:S(2)}) copy-start(bf16[768,1536]{1,0:T(8,128)(2,1)} %all-gather.2.cloned.1.call-done) | copy-start | bytes 7077892
  300.0 14.7 %collective-permute-start.4 = (bf16[256,12,64]{0,2,1:T(8,128)(2,1)}, bf16[256,12,64]{0,2,1:T(8,128)(2,1)}, u32[]{:S(2)}, u32[]{:S(2)}) collective-permute-start(bf16[256,12,64]{0,2,1:T(8,128)(2,1)} %convert.9), channel_id=1, source_target_pairs={{0,24},{2,26},{4,28},{6,30},{8,0},{10,2},{12,4},{14,6},{16,8},{18,... | collective-permute-start | bytes 1179656 | tf_op jit(solution)/shard_map/ppermute | solution.py:23
  303.8 18.5 %collective-permute-start.5 = (bf16[256,12,64]{0,2,1:T(8,128)(2,1)}, bf16[256,12,64]{0,2,1:T(8,128)(2,1)}, u32[]{:S(2)}, u32[]{:S(2)}) collective-permute-start(bf16[256,12,64]{0,2,1:T(8,128)(2,1)} %convert.10), channel_id=1, source_target_pairs={{0,24},{2,26},{4,28},{6,30},{8,0},{10,2},{12,4},{14,6},{16,8},{18,... | collective-permute-start | bytes 1179656 | tf_op jit(solution)/shard_map/ppermute | solution.py:23
Sparse Core Ops, SparseCore 0:
  13.8 42.0 all-gather.1
  119.3 89.1 reduce-scatter.2
  211.4 11.7 reduce-scatter.4
where the time goes:
time: 336 us; the launch traced here: 331 us
  waiting for transfers between devices  132 us (39%)
  starting transfers between devices  51.4 us (15%)
  other arithmetic  49 us (15%)
  matrix products  42.8 us (13%)
  local copies, waits for them, and re-layouts  25.5 us (8%)
  between operations  14.5 us (4%)
  loops' own time  8.61 us (3%)
  blocking collectives  6.42 us (2%)
    reduce_scatter x1, waiting for transfers between devices, local(): lax.psum_scatter(lax.dot_general(attended, upstream, (((0,), (0,)), ((),...  79.9 us
    ppermute x10, waiting for transfers between devices, from_behind_2(): lax.ppermute(value, axis, [(i, (i + by) % count) for i in range(count)])  36.2 us
    ppermute x8, starting transfers between devices, from_behind(): return lax.ppermute(block, axis, route)  35.3 us
    add x12, other arithmetic, kept_turn(): return (query_acc + query_part, key_acc + key_part, value_acc + value_part)  25.6 us
    ppermute x8, waiting for transfers between devices, from_behind(): return lax.ppermute(block, axis, route)  16.2 us
    ppermute x10, starting transfers between devices, from_behind_2(): lax.ppermute(value, axis, [(i, (i + by) % count) for i in range(count)])  16 us
    unnamed x18, local copies, waits for them, and re-layouts  11.4 us
    dot_general x6, matrix products, masked_scores(): jnp.einsum('qhe,khe->hqk', query_heads, key_block, preferred_element_type...  7.33 us
  transfers between devices with their start and end apart: 21, of which 13 were waited for; matrix products, arithmetic and copies ran while one was open for 33% of the time, Pallas kernels for 0%

commit v1 on v0

v1 whole, which is shorter than its diff:
```python
import jax
import jax.numpy as jnp
from jax import lax
from jax.sharding import PartitionSpec as P

HEADS = 12
HEAD_DIM = 64
STRETCH = 128
MOST = 1024


MASKED_SCORE = -1e30


def shift_up(block, axis, distance):
    devices = range(lax.axis_size(axis))
    route = [(i - distance, i) for i in devices if i - distance in devices]
    return lax.ppermute(block, axis, route)


def frame_labels(utt_lengths, first_frame, frame_count, total_frames):
    positions = first_frame + jnp.arange(frame_count, dtype=jnp.int32)
    utt_ends = jnp.cumsum(utt_lengths)
    utt_index = jnp.sum((positions[:, None] >= utt_ends[None, :]).astype(jnp.int32), axis=1)
    outside = (positions < 0) | (positions >= total_frames)
    return (jnp.where(outside, -1, utt_index), positions // STRETCH)


def local(query_rows, key_rows, value_rows, out_grad, lengths, out_weight):
    seq_count = lax.axis_size("seq")
    device = lax.axis_index("seq")
    tok_rows = query_rows.shape[1]
    feature_width = query_rows.shape[2]
    total_frames = seq_count * tok_rows
    reach = min(-(-MOST // tok_rows), seq_count - 1)
    window = (reach + 1) * tok_rows
    score_scale = HEAD_DIM ** (-0.5)
    utt_lengths = lengths[0]

    weight_cols = lax.all_gather(out_weight, "dp", axis=1, tiled=True)
    weight_full = lax.all_gather(weight_cols, "seq", axis=0, tiled=True)

    query_heads = query_rows[0].reshape(tok_rows, HEADS, HEAD_DIM)
    key_value = jnp.concatenate([key_rows[0], value_rows[0]], axis=1)

    held = [key_value]
    for _ in range(reach):
        held.append(shift_up(held[-1], "seq", 1))
    kv_window = jnp.concatenate(held[::-1], axis=0)
    key_window = kv_window[:, :feature_width].reshape(window, HEADS, HEAD_DIM)
    value_window = kv_window[:, feature_width:].reshape(window, HEADS, HEAD_DIM)

    query_utt, query_stretch = frame_labels(utt_lengths, device * tok_rows, tok_rows, total_frames)
    key_utt, key_stretch = frame_labels(
        utt_lengths, (device - reach) * tok_rows, window, total_frames
    )
    visible = (query_utt[:, None] == key_utt[None, :]) & (
        key_stretch[None, :] <= query_stretch[:, None]
    )

    scores = (
        jnp.einsum("qhe,khe->hqk", query_heads, key_window, preferred_element_type=jnp.float32)
        * score_scale
    )
    masked = jnp.where(visible[None], scores, MASKED_SCORE)
    top_score = jnp.max(masked, axis=2)
    expo_full = jnp.where(visible[None], jnp.exp(masked - top_score[:, :, None]), 0.0)
    row_sum = jnp.sum(expo_full, axis=2)
    weighted = jnp.einsum(
        "hqk,khe->qhe",
        expo_full.astype(jnp.bfloat16),
        value_window,
        preferred_element_type=jnp.float32,
    )
    attended = (
        (weighted / jnp.transpose(row_sum)[:, :, None])
        .reshape(tok_rows, feature_width)
        .astype(jnp.bfloat16)
    )
    log_sum = top_score + jnp.log(row_sum)

    mixed_out = jnp.dot(attended, weight_full, preferred_element_type=jnp.float32).astype(
        jnp.bfloat16
    )
    upstream = out_grad[0]
    att_grad = lax.dot_general(
        upstream, weight_full, (((1,), (1,)), ((), ())), preferred_element_type=jnp.float32
    ).astype(jnp.bfloat16)

    partial_weight = lax.dot_general(
        attended, upstream, (((0,), (0,)), ((), ())), preferred_element_type=jnp.float32
    )
    col_share = lax.psum_scatter(partial_weight, "dp", scatter_dimension=1, tiled=True)
    weight_grad = lax.psum_scatter(col_share, "seq", scatter_dimension=0, tiled=True)

    grad_heads = att_grad.reshape(tok_rows, HEADS, HEAD_DIM)
    delta_rows = jnp.sum(
        grad_heads.astype(jnp.float32)
        * attended.reshape(tok_rows, HEADS, HEAD_DIM).astype(jnp.float32),
        axis=2,
    )

    query_acc = jnp.zeros((tok_rows, HEADS, HEAD_DIM), jnp.float32)
    carried = None
    for back in range(reach, -1, -1):
        rows = slice((reach - back) * tok_rows, (reach - back + 1) * tok_rows)
        key_block = key_window[rows]
        value_block = value_window[rows]
        block_visible = visible[:, rows]
        block_scores = (
            jnp.einsum("qhe,khe->hqk", query_heads, key_block, preferred_element_type=jnp.float32)
            * score_scale
        )
        prob_full = jnp.where(
            block_visible[None], jnp.exp(block_scores - log_sum[:, :, None]), 0.0
        )
        prob_back = prob_full.astype(jnp.bfloat16)
        prob_grad = jnp.einsum(
            "qhe,khe->hqk", grad_heads, value_block, preferred_element_type=jnp.float32
        )
        score_grad = (prob_full * (prob_grad - jnp.transpose(delta_rows)[:, :, None])).astype(
            jnp.bfloat16
        )
        query_acc = query_acc + jnp.einsum(
            "hqk,khe->qhe", score_grad, key_block, preferred_element_type=jnp.float32
        )
        key_part = (
            jnp.einsum("hqk,qhe->khe", score_grad, query_heads, preferred_element_type=jnp.float32)
            * score_scale
        )
        value_part = jnp.einsum(
            "hqk,qhe->khe", prob_back, grad_heads, preferred_element_type=jnp.float32
        )
        part = jnp.concatenate(
            [key_part.reshape(tok_rows, feature_width), value_part.reshape(tok_rows, feature_width)],
            axis=1,
        )
        if carried is None:
            carried = part
        else:
            carried = shift_up(carried, "seq", -1) + part

    query_grad = (query_acc * score_scale).reshape(tok_rows, feature_width).astype(jnp.bfloat16)
    key_grad = carried[:, :feature_width].astype(jnp.bfloat16)
    value_grad = carried[:, feature_width:].astype(jnp.bfloat16)
    return (mixed_out[None], query_grad[None], key_grad[None], value_grad[None], weight_grad)


def solution(mesh):
    return jax.shard_map(
        local,
        mesh=mesh,
        in_specs=(
            P("dp", "seq", None),
            P("dp", "seq", None),
            P("dp", "seq", None),
            P("dp", "seq", None),
            P("dp", None),
            P("seq", "dp"),
        ),
        out_specs=(
            P("dp", "seq", None),
            P("dp", "seq", None),
            P("dp", "seq", None),
            P("dp", "seq", None),
            P("seq", "dp"),
        ),
        check_vma=False,
    )
```

time: 336 us -> 280 us (0.83)
  waiting for transfers between devices: 132 us -> 86 us
  matrix products: 42.8 us -> 74.7 us
  starting transfers between devices: 51.4 us -> 21.1 us
  other arithmetic: 49 us -> 25.6 us
  local copies, waits for them, and re-layouts: 25.5 us -> 48.9 us
  loops' own time: 8.61 us -> 0 us
    reduce_scatter x2, waiting for transfers between devices: 79.9 us -> 32.2 us  [the longest x1 32.2 us: local(): lax.psum_scatter(col_share, 'seq', scatter_dimension=0, tiled=True)]
    ppermute x18 -> x8, starting transfers between devices: 51.3 us -> 20.8 us  [shift_up(): return lax.ppermute(block, axis, route)]
    dot_general x24 -> x27, matrix products: 35.8 us -> 65.9 us  [the longest x5 15.6 us: local(): jnp.einsum('hqk,qhe->khe', prob_back, grad_heads, preferred_element_type=...]
    reshape x0 -> x10, local copies, waits for them, and re-layouts: none -> 21.1 us  [the longest x5 11.6 us: local(): value_part.reshape(tok_rows, feature_width)]
    add x28 -> x6, other arithmetic: 25.7 us -> 9.01 us  [the longest x3 9 us: local(): carried = shift_up(carried, 'seq', -1) + part]
    slice x0 -> x16, local copies, waits for them, and re-layouts: none -> 13.5 us  [the longest x2 5.55 us: local(): key_window = kv_window[:, :feature_width].reshape(window, HEADS, HEAD_DIM)]
    reduce_or x12 -> x0, other arithmetic: 11.8 us -> none  [the longest x4 5.67 us: grad_block(): jnp.any(visible)]
    another operation x18 -> x0, loops' own time: 8.61 us -> none  [the longest x1 2.79 us: local(): lax.fori_loop(1, reach_steps + 1, forward_turn, (start_max, key_heads, va...]
  transfers between devices with their start and end apart: 21 -> 11, of which waited for: 13 -> 8; matrix products, arithmetic and copies ran while one was open for 33% -> 46% of each run, Pallas kernels for 0% -> 0%
where the time goes in v1:
time: 280 us; the launch traced here: 277 us
  waiting for transfers between devices  86 us (31%)
  matrix products  74.7 us (27%)
  local copies, waits for them, and re-layouts  48.9 us (17%)
  other arithmetic  25.6 us (9%)
  starting transfers between devices  21.1 us (8%)
  between operations  14.4 us (5%)
  blocking collectives  6.32 us (2%)
    ppermute x8, waiting for transfers between devices, shift_up(): return lax.ppermute(block, axis, route)  53.8 us
    reduce_scatter x1, waiting for transfers between devices, local(): lax.psum_scatter(col_share, 'seq', scatter_dimension=0, tiled=True)  32.2 us
    ppermute x8, starting transfers between devices, shift_up(): return lax.ppermute(block, axis, route)  20.8 us
    dot_general x5, matrix products, local(): jnp.einsum('hqk,qhe->khe', prob_back, grad_heads, preferred_element_type=...  15.6 us
    reshape x5, local copies, waits for them, and re-layouts, local(): value_part.reshape(tok_rows, feature_width)  11.6 us
    dot_general x5, matrix products, local(): jnp.einsum('qhe,khe->hqk', grad_heads, value_block, preferred_element_typ...  10.1 us
    dot_general x1, matrix products, local(): jnp.einsum('hqk,khe->qhe', expo_full.astype(jnp.bfloat16), value_window,...  9.96 us
    unnamed x90, local copies, waits for them, and re-layouts  9.59 us
  transfers between devices with their start and end apart: 11, of which 8 were waited for; matrix products, arithmetic and copies ran while one was open for 46% of the time, Pallas kernels for 0%

profile of v1, /device:TPU:4, one launch (start us, length us, event | category | flops | bytes accessed | tf_op | source)
XLA Modules:
  0.0 277.1 jit_solution(4228232559934887295)
XLA Ops:
  8.5 1.9 collective-permute-start
  10.4 11.4 %collective-permute-done = bf16[256,1536]{1,0:T(8,128)(2,1)S(1)} collective-permute-done((bf16[256,1536]{1,0:T(8,128)(2,1)S(1)}, bf16[256,1536]{1,0:T(8,128)(2,1)S(1)}, u32[]{:S(2)}, u32[]{:S(2)}) %collective-permute-start) | collective-permute-done | bytes 786464 | tf_op jit(solution)/shard_map/ppermute | solution.py:18
  23.7 11.4 %collective-permute-done.1 = bf16[256,1536]{1,0:T(8,128)(2,1)S(1)} collective-permute-done((bf16[256,1536]{1,0:T(8,128)(2,1)S(1)}, bf16[256,1536]{1,0:T(8,128)(2,1)S(1)}, u32[]{:S(2)}, u32[]{:S(2)}) %collective-permute-start.1) | collective-permute-done | bytes 786464 | tf_op jit(solution)/shard_map/ppermute | solution.py:18
  35.1 2.0 collective-permute-start.2
  37.0 6.3 %all_gather.6 = bf16[48,1536]{1,0:T(8,128)(2,1)} all-gather(bf16[48,768]{1,0:T(8,128)(2,1)} %param.11), channel_id=1, replica_groups=mesh['seq'=16,'dp'=2] {'dp'}, dimensions={1}, use_global_device_ids=true | all-gather | bytes 221184 | tf_op jit(solution)/shard_map/all_gather | solution.py:40
  44.4 4.0 %collective-permute-done.2 = bf16[256,1536]{1,0:T(8,128)(2,1)S(1)} collective-permute-done((bf16[256,1536]{1,0:T(8,128)(2,1)S(1)}, bf16[256,1536]{1,0:T(8,128)(2,1)S(1)}, u32[]{:S(2)}, u32[]{:S(2)}) %collective-permute-start.2) | collective-permute-done | bytes 786464 | tf_op jit(solution)/shard_map/ppermute | solution.py:18
  48.4 2.9 %collective-permute-start.3 = (bf16[256,1536]{1,0:T(8,128)(2,1)S(1)}, bf16[256,1536]{1,0:T(8,128)(2,1)}, u32[]{:S(2)}, u32[]{:S(2)}) collective-permute-start(bf16[256,1536]{1,0:T(8,128)(2,1)S(1)} %collective-permute-done.2), channel_id=1, source_target_pairs={{0,2},{2,4},{4,6},{6,8},{8,10},{10,12},{12,14},{14,16},{16,18},{18... | collective-permute-start | bytes 2359304 | tf_op jit(solution)/shard_map/ppermute | solution.py:18
  53.4 9.9 %collective-permute-done.3 = bf16[256,1536]{1,0:T(8,128)(2,1)} collective-permute-done((bf16[256,1536]{1,0:T(8,128)(2,1)S(1)}, bf16[256,1536]{1,0:T(8,128)(2,1)}, u32[]{:S(2)}, u32[]{:S(2)}) %collective-permute-start.3) | collective-permute-done | bytes 786464 | tf_op jit(solution)/shard_map/ppermute | solution.py:18
  66.4 4.0 %copy.117 = bf16[1280,768]{0,1:T(8,128)(2,1)} copy(bf16[1280,768]{1,0:T(8,128)(2,1)} %get-tuple-element.20) | data formatting | bytes 3932160 | tf_op jit(solution)/shard_map/slice | solution.py:50
  70.4 2.3 copy.116
  72.7 9.5 %fusion = (f32[12,256]{1,0:T(8,128)S(1)}, f32[12,1280,256]{2,1,0:T(8,128)}) fusion(pred[256,1280]{0,1:T(8,128)(4,1)S(1)} %compare_and_fusion, bf16[1280,12,64]{0,2,1:T(8,128)(2,1)} %bitcast.189, bf16[256,12,64]{0,2,1:T(8,128)(2,1)S(1)} %bitcast.178), kind=kOutput, calls=%fused_computation.2 | convolution fusion | flops 515109888 | bytes 18427904 | tf_op jit(solution)/shard_map/qhe,khe->hqk/dot_general | solution.py:62
  82.2 9.3 %fusion.1 = f32[12,256]{1,0:T(8,128)S(1)} fusion(f32[12,1280,256]{2,1,0:T(8,128)} %get-tuple-element.38, f32[12,256]{1,0:T(8,128)S(1)} %get-tuple-element.37, pred[256,1280]{0,1:T(8,128)(4,1)S(1)} %compare_and_fusion), kind=kLoop, calls=%fused_computation.3 | loop fusion | flops 19657728 | bytes 16080896 | tf_op jit(solution)/shard_map/reduce_sum | solution.py:68
  91.5 2.5 convolution_convert_fusion.1
  94.2 10.0 %multiply_reduce_fusion = (f32[256,12]{0,1:T(8,128)S(1)}, bf16[256,12,64]{0,2,1:T(8,128)(2,1)S(1)}) fusion(bf16[256,12,64]{0,2,1:T(8,128)(2,1)S(1)} %bitcast.194, f32[256,12]{0,1:T(8,128)S(1)} %bitcast.234, bf16[1280,12,64]{0,2,1:T(8,128)(2,1)} %bitcast.223, f32[12,1280,256]{2,1,0:T(8,128)} %get-tuple-element.38, f32[12,256]{1,0:T(8,128)S(1)} %get-tuple-element.37, ...), kind=kOutput, calls=%fused_computation.75 | convolution fusion | flops 524153856 | bytes 18845696 | tf_op jit(solution)/shard_map/hqk,khe->qhe/dot_general | solution.py:69
  104.9 2.9 %fusion.54 = f32[768,1536]{1,0:T(8,128)} fusion(bf16[256,768]{0,1:T(8,128)(2,1)S(1)} %bitcast.221, bf16[1,256,1536]{2,1,0:T(8,128)(2,1)S(1)} %copy-done), kind=kOutput, calls=%fused_computation.72 | convolution fusion | flops 603979776 | bytes 5898240 | tf_op jit(solution)/shard_map/dot_general | solution.py:90
  112.5 2.3 fusion.86
  116.0 2.3 fusion.84
  123.7 3.5 %fusion.17 = f32[12,64,256]{2,1,0:T(8,128)} fusion(bf16[256,12,64]{0,2,1:T(8,128)(2,1)S(1)} %bitcast.196, f32[12,256,256]{2,1,0:T(8,128)} %copy-done.27, f32[12,256]{1,0:T(8,128)S(1)} %log_add_fusion, pred[256,256]{0,1:T(8,128)(4,1)} %copy-done.37), kind=kOutput, calls=%fused_computation.27 | convolution fusion | flops 103809024 | bytes 4403200 | tf_op jit(solution)/shard_map/hqk,qhe->khe/dot_general | solution.py:131
  127.2 2.4 copy.145
  129.5 2.5 pad_maximum_fusion
  136.1 2.1 multiply_convert_fusion.3
  139.7 2.3 copy.148
  142.0 3.6 %fusion.15 = f32[12,64,256]{2,1,0:T(8,128)} fusion(bf16[256,12,64]{0,2,1:T(8,128)(2,1)S(1)} %bitcast.198, f32[12,256,256]{2,1,0:T(8,128)} %copy-done.28, f32[12,256]{1,0:T(8,128)S(1)} %log_add_fusion, pred[256,256]{0,1:T(8,128)(4,1)} %get-tuple-element.36), kind=kOutput, calls=%fused_computation.26 | convolution fusion | flops 103809024 | bytes 4403200 | tf_op jit(solution)/shard_map/hqk,qhe->khe/dot_general | solution.py:131
  145.6 2.4 copy.149
  147.9 4.2 %collective-permute-done.4 = f32[256,1536]{1,0:T(8,128)} collective-permute-done((f32[256,1536]{1,0:T(8,128)}, f32[256,1536]{1,0:T(8,128)}, u32[]{:S(2)}, u32[]{:S(2)}) %collective-permute-start.4) | collective-permute-done | bytes 1572896 | tf_op jit(solution)/shard_map/ppermute | solution.py:18
  152.2 3.3 %maximum_add_fusion = f32[256,1536]{1,0:T(8,128)} fusion(f32[256,1536]{1,0:T(8,128)} %collective-permute-done.4, f32[256,768]{1,0:T(8,128)} %copy.149, f32[256,768]{1,0:T(8,128)} %copy.148), kind=kLoop, calls=%fused_computation.30 | loop fusion | flops 786432 | bytes 4718592 | tf_op jit(solution)/shard_map/add | solution.py:141
  155.4 4.4 %collective-permute-start.5 = (f32[256,1536]{1,0:T(8,128)}, f32[256,1536]{1,0:T(8,128)}, u32[]{:S(2)}, u32[]{:S(2)}) collective-permute-start(f32[256,1536]{1,0:T(8,128)} %maximum_add_fusion), channel_id=1, source_target_pairs={{2,0},{4,2},{6,4},{8,6},{10,8},{12,10},{14,12},{16,14},{18,16},{20... | collective-permute-start | bytes 4718600 | tf_op jit(solution)/shard_map/ppermute | solution.py:18
  159.8 2.4 subtract_exponential_fusion
  162.2 3.6 %copy.138 = f32[12,256,256]{1,2,0:T(8,128)} copy(f32[12,256,256]{2,1,0:T(8,128)} %subtract_exponential_fusion) | data formatting | bytes 6291456 | tf_op jit(solution)/shard_map/exp | solution.py:115
  165.8 3.1 %multiply_convert_fusion.2 = bf16[12,256,256]{1,2,0:T(8,128)(2,1)S(1)} fusion(f32[12,256,256]{2,1,0:T(8,128)} %fusion.84, bf16[256,12,64]{0,2,1:T(8,128)(2,1)S(1)} %bitcast.199, bf16[256,12,64]{0,2,1:T(8,128)(2,1)} %bitcast.231, f32[12,256]{1,0:T(8,128)} %bitcast.237, f32[12,256]{1,0:T(8,128)S(1)} %log_add_fusion, pred[256,256]{0,1:T(8,128)(4,1)} %get-tuple-element.35), kind=kOutput, calls=%fused_computation.14 | convolution fusion | flops 105381888 | bytes 5595136 | tf_op jit(solution)/shard_map/qhe,khe->hqk/dot_general | solution.py:118
  171.6 2.3 copy.152
  173.9 3.5 %fusion.13 = f32[12,64,256]{2,1,0:T(8,128)} fusion(bf16[256,12,64]{0,2,1:T(8,128)(2,1)S(1)} %bitcast.200, f32[12,256,256]{2,1,0:T(8,128)} %fusion.84, f32[12,256]{1,0:T(8,128)S(1)} %log_add_fusion, pred[256,256]{0,1:T(8,128)(4,1)} %get-tuple-element.35), kind=kOutput, calls=%fused_computation.25 | convolution fusion | flops 103809024 | bytes 4403200 | tf_op jit(solution)/shard_map/hqk,qhe->khe/dot_general | solution.py:131
  177.3 2.3 copy.153
  179.6 3.5 %fusion.19 = f32[12,64,256]{2,1,0:T(8,128)} fusion(bf16[256,12,64]{0,2,1:T(8,128)(2,1)S(1)} %bitcast.201, f32[12,256,256]{1,2,0:T(8,128)} %copy.138, pred[256,256]{0,1:T(8,128)(4,1)} %get-tuple-element.33), kind=kOutput, calls=%fused_computation.28 | convolution fusion | flops 101449728 | bytes 4390912 | tf_op jit(solution)/shard_map/hqk,qhe->khe/dot_general | solution.py:131
  183.2 2.9 %maximum_add_fusion.1 = f32[256,1536]{1,0:T(8,128)} fusion(f32[256,1536]{1,0:T(8,128)} %collective-permute-done.5, f32[256,768]{1,0:T(8,128)S(1)} %copy-done.18, f32[256,768]{1,0:T(8,128)S(1)} %copy-done.17), kind=kLoop, calls=%fused_computation.31 | loop fusion | flops 786432 | bytes 4718592 | tf_op jit(solution)/shard_map/add | solution.py:141
  186.1 2.1 collective-permute-start.6
  193.8 2.3 copy.156
  196.1 2.3 copy.157
  198.4 2.8 %multiply_convert_fusion = bf16[12,256,256]{1,2,0:T(8,128)(2,1)S(1)} fusion(f32[12,256,256]{1,2,0:T(8,128)} %copy.138, bf16[256,12,64]{0,2,1:T(8,128)(2,1)S(1)} %bitcast.204, bf16[256,12,64]{0,2,1:T(8,128)(2,1)} %bitcast.224, f32[12,256]{1,0:T(8,128)S(1)} %bitcast.239, pred[256,256]{0,1:T(8,128)(4,1)} %get-tuple-element.33), kind=kOutput, calls=%fused_computation.11 | convolution fusion | flops 103809024 | bytes 5582848 | tf_op jit(solution)/shard_map/qhe,khe->hqk/dot_general | solution.py:118
  201.2 5.3 %collective-permute-done.6 = f32[256,1536]{1,0:T(8,128)} collective-permute-done((f32[256,1536]{1,0:T(8,128)}, f32[256,1536]{1,0:T(8,128)}, u32[]{:S(2)}, u32[]{:S(2)}) %collective-permute-start.6) | collective-permute-done | bytes 1572896 | tf_op jit(solution)/shard_map/ppermute | solution.py:18
  206.4 2.8 %maximum_add_fusion.2 = f32[256,1536]{1,0:T(8,128)} fusion(f32[256,1536]{1,0:T(8,128)} %collective-permute-done.6, f32[256,768]{1,0:T(8,128)S(1)} %copy-done.16, f32[256,768]{1,0:T(8,128)S(1)} %copy-done.15), kind=kLoop, calls=%fused_computation.32 | loop fusion | flops 786432 | bytes 4718592 | tf_op jit(solution)/shard_map/add | solution.py:141
  209.2 3.8 %collective-permute-start.7 = (f32[256,1536]{1,0:T(8,128)}, f32[256,1536]{1,0:T(8,128)}, u32[]{:S(2)}, u32[]{:S(2)}) collective-permute-start(f32[256,1536]{1,0:T(8,128)} %maximum_add_fusion.2), channel_id=1, source_target_pairs={{2,0},{4,2},{6,4},{8,6},{10,8},{12,10},{14,12},{16,14},{18,16},{20... | collective-permute-start | bytes 4718600 | tf_op jit(solution)/shard_map/ppermute | solution.py:18
  214.6 2.3 copy.160
  216.9 2.3 copy.161
  221.1 1.9 fusion.87
  224.8 3.4 %fusion.6 = bf16[1,256,1536]{2,1,0:T(8,128)(2,1)} fusion(bf16[256,768]{0,1:T(8,128)(2,1)S(1)} %bitcast.222, bf16[768,1536]{1,0:T(8,128)(2,1)} %all-gather.2.cloned.1.call-done), kind=kOutput, calls=%fused_computation.19 | convolution fusion | flops 604372992 | bytes 3538944 | tf_op jit(solution)/shard_map/dot_general | solution.py:82
  228.2 7.6 %collective-permute-done.7 = f32[256,1536]{1,0:T(8,128)} collective-permute-done((f32[256,1536]{1,0:T(8,128)}, f32[256,1536]{1,0:T(8,128)}, u32[]{:S(2)}, u32[]{:S(2)}) %collective-permute-start.7) | collective-permute-done | bytes 1572896 | tf_op jit(solution)/shard_map/ppermute | solution.py:18
  238.3 32.2 %reduce-scatter.5.cloned.1.call-done = f32[48,768]{1,0:T(8,128)} async-done(((f32[768,768]{1,0:T(8,128)}), f32[48,768]{1,0:T(8,128)}) %reduce-scatter.5.cloned.1.call-update) | async-done | bytes 147472 | tf_op jit(solution)/shard_map/reduce_scatter | solution.py:94
  (144 shorter events, 42.8 us)
Async XLA Ops:
  7.2 84.4 %copy-start = (bf16[1,256,1536]{2,1,0:T(8,128)(2,1)S(1)}, bf16[1,256,1536]{2,1,0:T(8,128)(2,1)}, u32[]{:S(2)}) copy-start(bf16[1,256,1536]{2,1,0:T(8,128)(2,1)} %param.9) | copy-start | bytes 2359300
  7.2 84.3 %all-gather.2.cloned.1.call-start = ((), (), s32[]{:S(2)}) async-start(), calls=%async_computation.2 | async-start | bytes 2506752 | tf_op jit(solution)/shard_map/all_gather | solution.py:41
  8.5 13.3 %collective-permute-start = (bf16[256,1536]{1,0:T(8,128)(2,1)S(1)}, bf16[256,1536]{1,0:T(8,128)(2,1)S(1)}, u32[]{:S(2)}, u32[]{:S(2)}) collective-permute-start(bf16[256,1536]{1,0:T(8,128)(2,1)S(1)} %pad_maximum_fusion.1), channel_id=1, source_target_pairs={{0,2},{2,4},{4,6},{6,8},{8,10},{10,12},{12,14},{14,16},{16,18},{18... | collective-permute-start | bytes 2359304 | tf_op jit(solution)/shard_map/ppermute | solution.py:18
  21.8 13.3 %copy-start.23 = (bf16[256,1536]{1,0:T(8,128)(2,1)}, bf16[256,1536]{1,0:T(8,128)(2,1)S(1)}, u32[]{:S(2)}) copy-start(bf16[256,1536]{1,0:T(8,128)(2,1)S(1)} %collective-permute-done) | copy-start | bytes 2359300
  21.8 13.3 %collective-permute-start.1 = (bf16[256,1536]{1,0:T(8,128)(2,1)S(1)}, bf16[256,1536]{1,0:T(8,128)(2,1)S(1)}, u32[]{:S(2)}, u32[]{:S(2)}) collective-permute-start(bf16[256,1536]{1,0:T(8,128)(2,1)S(1)} %collective-permute-done), channel_id=1, source_target_pairs={{0,2},{2,4},{4,6},{6,8},{8,10},{10,12},{12,14},{14,16},{16,18},{18... | collective-permute-start | bytes 2359304 | tf_op jit(solution)/shard_map/ppermute | solution.py:18
  35.1 29.6 %copy-start.21 = (bf16[256,1536]{1,0:T(8,128)(2,1)}, bf16[256,1536]{1,0:T(8,128)(2,1)S(1)}, u32[]{:S(2)}) copy-start(bf16[256,1536]{1,0:T(8,128)(2,1)S(1)} %collective-permute-done.1) | copy-start | bytes 2359300
  35.1 13.3 %collective-permute-start.2 = (bf16[256,1536]{1,0:T(8,128)(2,1)S(1)}, bf16[256,1536]{1,0:T(8,128)(2,1)S(1)}, u32[]{:S(2)}, u32[]{:S(2)}) collective-permute-start(bf16[256,1536]{1,0:T(8,128)(2,1)S(1)} %collective-permute-done.1), channel_id=1, source_target_pairs={{0,2},{2,4},{4,6},{6,8},{8,10},{10,12},{12,14},{14,16},{16,18},{18... | collective-permute-start | bytes 2359304 | tf_op jit(solution)/shard_map/ppermute | solution.py:18
  43.4 148.9 %reduce-scatter.3.cloned.1.call-start = ((), (), s32[]{:S(2)}) async-start(), calls=%async_computation.3 | async-start | bytes 7077888 | tf_op jit(solution)/shard_map/reduce_scatter | solution.py:93
  48.4 16.4 %copy-start.19 = (bf16[256,1536]{1,0:T(8,128)(2,1)}, bf16[256,1536]{1,0:T(8,128)(2,1)S(1)}, u32[]{:S(2)}) copy-start(bf16[256,1536]{1,0:T(8,128)(2,1)S(1)} %collective-permute-done.2) | copy-start | bytes 2359300
  48.4 15.0 %collective-permute-start.3 = (bf16[256,1536]{1,0:T(8,128)(2,1)S(1)}, bf16[256,1536]{1,0:T(8,128)(2,1)}, u32[]{:S(2)}, u32[]{:S(2)}) collective-permute-start(bf16[256,1536]{1,0:T(8,128)(2,1)S(1)} %collective-permute-done.2), channel_id=1, source_target_pairs={{0,2},{2,4},{4,6},{6,8},{8,10},{10,12},{12,14},{14,16},{16,18},{18... | collective-permute-start | bytes 2359304 | tf_op jit(solution)/shard_map/ppermute | solution.py:18
  52.5 12.2 %copy-start.24 = (bf16[256,1536]{1,0:T(8,128)(2,1)S(1)}, bf16[256,1536]{1,0:T(8,128)(2,1)}, u32[]{:S(2)}) copy-start(bf16[256,1536]{1,0:T(8,128)(2,1)} %copy-done.23) | copy-start | bytes 2359300
  53.4 11.3 %copy-start.6 = (bf16[1,256,768]{2,1,0:T(8,128)(2,1)S(1)}, bf16[1,256,768]{2,1,0:T(8,128)(2,1)}, u32[]{:S(2)}) copy-start(bf16[1,256,768]{2,1,0:T(8,128)(2,1)} %param.7) | copy-start | bytes 1179652
  53.4 11.3 %copy-start.8 = (bf16[1,256,768]{2,1,0:T(8,128)(2,1)S(1)}, bf16[1,256,768]{2,1,0:T(8,128)(2,1)}, u32[]{:S(2)}) copy-start(bf16[1,256,768]{2,1,0:T(8,128)(2,1)} %param.8) | copy-start | bytes 1179652
  104.2 16.3 %copy-start.38 = (f32[256,12]{0,1:T(8,128)}, f32[256,12]{0,1:T(8,128)S(1)}, u32[]{:S(2)}) copy-start(f32[256,12]{0,1:T(8,128)S(1)} %get-tuple-element.39) | copy-start | bytes 36868
  107.8 1.9 copy-start.9
  107.8 3.5 %copy-start.25 = (bf16[256,1536]{1,0:T(8,128)(2,1)S(1)}, bf16[256,1536]{1,0:T(8,128)(2,1)}, u32[]{:S(2)}) copy-start(bf16[256,1536]{1,0:T(8,128)(2,1)} %copy-done.23) | copy-start | bytes 2359300
  107.9 162.7 %reduce-scatter.5.cloned.1.call-start = ((), (), s32[]{:S(2)}) async-start(), calls=%async_computation.4 | async-start | bytes 2506752 | tf_op jit(solution)/shard_map/reduce_scatter | solution.py:94
  111.4 9.1 %copy-start.37 = (pred[256,256]{0,1:T(8,128)(4,1)}, pred[256,256]{0,1:T(8,128)(4,1)S(1)}, u32[]{:S(2)}) copy-start(pred[256,256]{0,1:T(8,128)(4,1)S(1)} %get-tuple-element.32) | copy-start | bytes 196612
  111.4 3.4 %copy-start.22 = (bf16[256,1536]{1,0:T(8,128)(2,1)S(1)}, bf16[256,1536]{1,0:T(8,128)(2,1)}, u32[]{:S(2)}) copy-start(bf16[256,1536]{1,0:T(8,128)(2,1)} %copy-done.21) | copy-start | bytes 2359300
  119.7 2.0 copy-start.13
  120.5 2.9 %copy-start.27 = (f32[12,256,256]{2,1,0:T(8,128)}, f32[12,256,256]{2,1,0:T(8,128)S(1)}, u32[]{:S(2)}) copy-start(f32[12,256,256]{2,1,0:T(8,128)S(1)} %fusion.81) | copy-start | bytes 9437188
  127.2 6.8 %copy-start.20 = (bf16[256,1536]{1,0:T(8,128)(2,1)S(1)}, bf16[256,1536]{1,0:T(8,128)(2,1)}, u32[]{:S(2)}) copy-start(bf16[256,1536]{1,0:T(8,128)(2,1)} %copy-done.19) | copy-start | bytes 2359300
  132.0 20.1 %collective-permute-start.4 = (f32[256,1536]{1,0:T(8,128)}, f32[256,1536]{1,0:T(8,128)}, u32[]{:S(2)}, u32[]{:S(2)}) collective-permute-start(f32[256,1536]{1,0:T(8,128)} %pad_maximum_fusion), channel_id=1, source_target_pairs={{2,0},{4,2},{6,4},{8,6},{10,8},{12,10},{14,12},{16,14},{18,16},{20... | collective-permute-start | bytes 4718600 | tf_op jit(solution)/shard_map/ppermute | solution.py:18
  134.2 4.0 %copy-start.11 = (bf16[256,768]{0,1:T(8,128)(2,1)}, bf16[256,768]{0,1:T(8,128)(2,1)S(1)}, u32[]{:S(2)}) copy-start(bf16[256,768]{0,1:T(8,128)(2,1)S(1)} %copy.125) | copy-start | bytes 1179652
  135.7 4.0 %copy-start.28 = (f32[12,256,256]{2,1,0:T(8,128)}, f32[12,256,256]{2,1,0:T(8,128)S(1)}, u32[]{:S(2)}) copy-start(f32[12,256,256]{2,1,0:T(8,128)S(1)} %fusion.82) | copy-start | bytes 9437188
  145.6 14.2 %copy-start.10 = (bf16[1,256,768]{1,2,0:T(8,128)(2,1)S(1)}, bf16[1,256,768]{1,2,0:T(8,128)(2,1)}, u32[]{:S(2)}) copy-start(bf16[1,256,768]{1,2,0:T(8,128)(2,1)} %copy.137) | copy-start | bytes 1179652
  155.4 27.7 %collective-permute-start.5 = (f32[256,1536]{1,0:T(8,128)}, f32[256,1536]{1,0:T(8,128)}, u32[]{:S(2)}, u32[]{:S(2)}) collective-permute-start(f32[256,1536]{1,0:T(8,128)} %maximum_add_fusion), channel_id=1, source_target_pairs={{2,0},{4,2},{6,4},{8,6},{10,8},{12,10},{14,12},{16,14},{18,16},{20... | collective-permute-start | bytes 4718600 | tf_op jit(solution)/shard_map/ppermute | solution.py:18
  168.9 1.2 copy-start.4
  179.6 3.5 %copy-start.17 = (f32[256,768]{1,0:T(8,128)S(1)}, f32[256,768]{1,0:T(8,128)}, u32[]{:S(2)}) copy-start(f32[256,768]{1,0:T(8,128)} %copy.152) | copy-start | bytes 2359300
  179.6 3.5 %copy-start.18 = (f32[256,768]{1,0:T(8,128)S(1)}, f32[256,768]{1,0:T(8,128)}, u32[]{:S(2)}) copy-start(f32[256,768]{1,0:T(8,128)} %copy.153) | copy-start | bytes 2359300
  183.2 5.0 %copy-start.12 = (bf16[256,768]{0,1:T(8,128)(2,1)S(1)}, bf16[256,768]{0,1:T(8,128)(2,1)}, u32[]{:S(2)}) copy-start(bf16[256,768]{0,1:T(8,128)(2,1)} %copy-done.11) | copy-start | bytes 1179652
  183.2 6.3 %copy-start.26 = (f32[12,256,256]{2,1,0:T(8,128)S(1)}, f32[12,256,256]{2,1,0:T(8,128)}, u32[]{:S(2)}) copy-start(f32[12,256,256]{2,1,0:T(8,128)} %fusion.86) | copy-start | bytes 9437188
  183.2 6.3 %copy-start.36 = (pred[256,256]{0,1:T(8,128)(4,1)S(1)}, pred[256,256]{0,1:T(8,128)(4,1)}, u32[]{:S(2)}) copy-start(pred[256,256]{0,1:T(8,128)(4,1)} %get-tuple-element.34) | copy-start | bytes 196612
  186.1 5.0 %copy-start.34 = (bf16[256,768]{0,1:T(8,128)(2,1)S(1)}, bf16[256,768]{0,1:T(8,128)(2,1)}, u32[]{:S(2)}) copy-start(bf16[256,768]{0,1:T(8,128)(2,1)} %copy.134) | copy-start | bytes 1179652
  186.1 5.0 %copy-start.39 = (f32[256,12]{0,1:T(8,128)S(1)}, f32[256,12]{0,1:T(8,128)}, u32[]{:S(2)}) copy-start(f32[256,12]{0,1:T(8,128)} %copy-done.38) | copy-start | bytes 36868
  186.1 20.3 %collective-permute-start.6 = (f32[256,1536]{1,0:T(8,128)}, f32[256,1536]{1,0:T(8,128)}, u32[]{:S(2)}, u32[]{:S(2)}) collective-permute-start(f32[256,1536]{1,0:T(8,128)} %maximum_add_fusion.1), channel_id=1, source_target_pairs={{2,0},{4,2},{6,4},{8,6},{10,8},{12,10},{14,12},{16,14},{18,16},{20... | collective-permute-start | bytes 4718600 | tf_op jit(solution)/shard_map/ppermute | solution.py:18
  192.3 3.8 %copy-start.5 = (bf16[12,256,256]{1,2,0:T(8,128)(2,1)}, bf16[12,256,256]{1,2,0:T(8,128)(2,1)S(1)}, u32[]{:S(2)}) copy-start(bf16[12,256,256]{1,2,0:T(8,128)(2,1)S(1)} %multiply_convert_fusion.1) | copy-start | bytes 4718596
  192.3 6.1 %copy-start.40 = (f32[256,12]{0,1:T(8,128)S(1)}, f32[256,12]{0,1:T(8,128)}, u32[]{:S(2)}) copy-start(f32[256,12]{0,1:T(8,128)} %copy-done.38) | copy-start | bytes 36868
  198.4 8.1 %copy-start.15 = (f32[256,768]{1,0:T(8,128)S(1)}, f32[256,768]{1,0:T(8,128)}, u32[]{:S(2)}) copy-start(f32[256,768]{1,0:T(8,128)} %copy.156) | copy-start | bytes 2359300
  198.4 8.1 %copy-start.16 = (f32[256,768]{1,0:T(8,128)S(1)}, f32[256,768]{1,0:T(8,128)}, u32[]{:S(2)}) copy-start(f32[256,768]{1,0:T(8,128)} %copy.157) | copy-start | bytes 2359300
  209.2 26.6 %collective-permute-start.7 = (f32[256,1536]{1,0:T(8,128)}, f32[256,1536]{1,0:T(8,128)}, u32[]{:S(2)}, u32[]{:S(2)}) collective-permute-start(f32[256,1536]{1,0:T(8,128)} %maximum_add_fusion.2), channel_id=1, source_target_pairs={{2,0},{4,2},{6,4},{8,6},{10,8},{12,10},{14,12},{16,14},{18,16},{20... | collective-permute-start | bytes 4718600 | tf_op jit(solution)/shard_map/ppermute | solution.py:18
  221.0 2.4 copy-start.3
  221.0 2.4 copy-start.14
  221.1 2.4 copy-start.31
  223.4 1.4 copy-start.33
  223.9 12.0 %copy-start.29 = (f32[256,768]{1,0:T(8,128)S(1)}, f32[256,768]{1,0:T(8,128)}, u32[]{:S(2)}) copy-start(f32[256,768]{1,0:T(8,128)} %copy.160) | copy-start | bytes 2359300
  223.9 12.0 %copy-start.30 = (f32[256,768]{1,0:T(8,128)S(1)}, f32[256,768]{1,0:T(8,128)}, u32[]{:S(2)}) copy-start(f32[256,768]{1,0:T(8,128)} %copy.161) | copy-start | bytes 2359300
  224.8 45.7 %copy-start.1 = (bf16[1,256,1536]{2,1,0:T(8,128)(2,1)S(1)}, bf16[1,256,1536]{2,1,0:T(8,128)(2,1)}, u32[]{:S(2)}) copy-start(bf16[1,256,1536]{2,1,0:T(8,128)(2,1)} %param.9) | copy-start | bytes 2359300
  (4 other events, 3.9 us)
Sparse Core Ops, SparseCore 0:
  43.5 43.7 all-gather.1
  108.0 65.5 reduce-scatter.2
  192.4 78.0 reduce-scatter.4

commit v2 on v1

v2 whole, which is shorter than its diff:
```python
import jax
import jax.numpy as jnp
from jax import lax
from jax.sharding import PartitionSpec as P

HEADS = 12
HEAD_DIM = 64
STRETCH = 128
MOST = 1024


MASKED_SCORE = -1e30


def shift_up(block, axis, distance):
    devices = range(lax.axis_size(axis))
    route = [(i - distance, i) for i in devices if i - distance in devices]
    return lax.ppermute(block, axis, route)


def swap_partner(block, axis):
    count = lax.axis_size(axis)
    return lax.ppermute(block, axis, [(i, i ^ 1) for i in range(count)])


def frame_labels(utt_lengths, first_frame, frame_count, total_frames):
    positions = first_frame + jnp.arange(frame_count, dtype=jnp.int32)
    utt_ends = jnp.cumsum(utt_lengths)
    utt_index = jnp.sum((positions[:, None] >= utt_ends[None, :]).astype(jnp.int32), axis=1)
    outside = (positions < 0) | (positions >= total_frames)
    return (jnp.where(outside, -1, utt_index), positions // STRETCH)


def head_major(rows, tok_rows):
    return jnp.transpose(rows.reshape(tok_rows, HEADS, HEAD_DIM), (1, 0, 2))


def row_major(heads, tok_rows):
    return jnp.transpose(heads, (1, 0, 2)).reshape(tok_rows, HEADS * HEAD_DIM)


def gather_behind(own, reach, paired, core):
    if not paired:
        held = [own]
        for _ in range(reach):
            held.append(shift_up(held[-1], "seq", 1))
        return held
    evens = {0: own}
    for dist in range(2, reach + 2, 2):
        evens[dist] = shift_up(own, "seq", dist)
    odds = list(range(1, reach + 1, 2))
    payload = [jnp.where(core == 0, evens[s - 1], evens[s + 1]) for s in odds]
    received = swap_partner(payload, "seq")
    held = []
    for dist in range(reach + 1):
        held.append(evens[dist] if dist % 2 == 0 else received[(dist - 1) // 2])
    return held


def return_behind(parts, reach, paired, core):
    if not paired:
        carried = parts[reach]
        for dist in range(reach - 1, -1, -1):
            carried = shift_up(carried.astype(jnp.bfloat16), "seq", -1).astype(jnp.float32) + parts[dist]
        return carried
    odds = list(range(1, reach + 1, 2))
    received = swap_partner([parts[s] for s in odds], "seq")
    total = None
    for dist in range(0, reach + 2, 2):
        zero = jnp.zeros_like(parts[0])
        from_core1 = received[dist // 2] if dist // 2 < len(odds) else zero
        from_core0 = received[dist // 2 - 1] if dist >= 2 and dist // 2 - 1 < len(odds) else zero
        own = parts[dist] if dist <= reach else zero
        summed = own + jnp.where(core == 0, from_core1, from_core0)
        if dist == 0:
            total = summed
        else:
            total = total + shift_up(summed.astype(jnp.bfloat16), "seq", -dist).astype(jnp.float32)
    return total


def local(query_rows, key_rows, value_rows, out_grad, lengths, out_weight):
    seq_count = lax.axis_size("seq")
    device = lax.axis_index("seq")
    core = device % 2
    paired = seq_count % 2 == 0
    tok_rows = query_rows.shape[1]
    feature_width = query_rows.shape[2]
    total_frames = seq_count * tok_rows
    reach = min(-(-MOST // tok_rows), seq_count - 1)
    score_scale = HEAD_DIM ** (-0.5)
    utt_lengths = lengths[0]

    weight_cols = lax.all_gather(out_weight, "dp", axis=1, tiled=True)
    weight_full = lax.all_gather(weight_cols, "seq", axis=0, tiled=True)

    query_heads = head_major(query_rows[0], tok_rows)
    own_kv = jnp.stack([head_major(key_rows[0], tok_rows), head_major(value_rows[0], tok_rows)])
    held = gather_behind(own_kv, reach, paired, core)

    query_utt, query_stretch = frame_labels(utt_lengths, device * tok_rows, tok_rows, total_frames)
    block_visible = []
    for dist in range(reach + 1):
        key_utt, key_stretch = frame_labels(
            utt_lengths, (device - dist) * tok_rows, tok_rows, total_frames
        )
        block_visible.append(
            (query_utt[:, None] == key_utt[None, :]) & (key_stretch[None, :] <= query_stretch[:, None])
        )

    block_scores = []
    top_score = None
    for dist in range(reach + 1):
        scores = (
            jnp.einsum("hqe,hke->hqk", query_heads, held[dist][0], preferred_element_type=jnp.float32)
            * score_scale
        )
        scores = jnp.where(block_visible[dist][None], scores, MASKED_SCORE)
        block_scores.append(scores)
        block_top = jnp.max(scores, axis=2)
        top_score = block_top if top_score is None else jnp.maximum(top_score, block_top)
    row_sum = None
    weighted = None
    for dist in range(reach + 1):
        expo_full = jnp.where(
            block_visible[dist][None], jnp.exp(block_scores[dist] - top_score[:, :, None]), 0.0
        )
        part_sum = jnp.sum(expo_full, axis=2)
        product = jnp.einsum(
            "hqk,hke->hqe",
            expo_full.astype(jnp.bfloat16),
            held[dist][1],
            preferred_element_type=jnp.float32,
        )
        row_sum = part_sum if row_sum is None else row_sum + part_sum
        weighted = product if weighted is None else weighted + product
    attended_heads = (weighted / row_sum[:, :, None]).astype(jnp.bfloat16)
    attended = row_major(attended_heads, tok_rows)
    log_sum = top_score + jnp.log(row_sum)

    mixed_out = jnp.dot(attended, weight_full, preferred_element_type=jnp.float32).astype(
        jnp.bfloat16
    )
    upstream = out_grad[0]
    att_grad = lax.dot_general(
        upstream, weight_full, (((1,), (1,)), ((), ())), preferred_element_type=jnp.float32
    ).astype(jnp.bfloat16)

    partial_weight = lax.dot_general(
        attended, upstream, (((0,), (0,)), ((), ())), preferred_element_type=jnp.float32
    )
    row_share = lax.psum_scatter(
        partial_weight.astype(jnp.bfloat16), "seq", scatter_dimension=0, tiled=True
    )
    weight_grad = lax.psum_scatter(
        row_share.astype(jnp.float32), "dp", scatter_dimension=1, tiled=True
    )

    grad_heads = head_major(att_grad, tok_rows)
    delta_rows = jnp.sum(
        grad_heads.astype(jnp.float32) * attended_heads.astype(jnp.float32), axis=2
    )

    query_acc = None
    parts = [None] * (reach + 1)
    order = [d for d in range(reach, -1, -1) if d % 2 == 1] + [
        d for d in range(reach, -1, -1) if d % 2 == 0
    ]
    for dist in order:
        key_block = held[dist][0]
        value_block = held[dist][1]
        scores = (
            jnp.einsum("hqe,hke->hqk", query_heads, key_block, preferred_element_type=jnp.float32)
            * score_scale
        )
        prob_full = jnp.where(
            block_visible[dist][None], jnp.exp(scores - log_sum[:, :, None]), 0.0
        )
        prob_back = prob_full.astype(jnp.bfloat16)
        prob_grad = jnp.einsum(
            "hqe,hke->hqk", grad_heads, value_block, preferred_element_type=jnp.float32
        )
        score_grad = (prob_full * (prob_grad - delta_rows[:, :, None])).astype(jnp.bfloat16)
        query_part = jnp.einsum(
            "hqk,hke->hqe", score_grad, key_block, preferred_element_type=jnp.float32
        )
        query_acc = query_part if query_acc is None else query_acc + query_part
        key_part = (
            jnp.einsum("hqk,hqe->hke", score_grad, query_heads, preferred_element_type=jnp.float32)
            * score_scale
        )
        value_part = jnp.einsum(
            "hqk,hqe->hke", prob_back, grad_heads, preferred_element_type=jnp.float32
        )
        parts[dist] = jnp.stack([key_part, value_part])

    kv_grad = return_behind(parts, reach, paired, core)
    query_grad = row_major(query_acc * score_scale, tok_rows).astype(jnp.bfloat16)
    key_grad = row_major(kv_grad[0], tok_rows).astype(jnp.bfloat16)
    value_grad = row_major(kv_grad[1], tok_rows).astype(jnp.bfloat16)
    return (mixed_out[None], query_grad[None], key_grad[None], value_grad[None], weight_grad)


def solution(mesh):
    return jax.shard_map(
        local,
        mesh=mesh,
        in_specs=(
            P("dp", "seq", None),
            P("dp", "seq", None),
            P("dp", "seq", None),
            P("dp", "seq", None),
            P("dp", None),
            P("seq", "dp"),
        ),
        out_specs=(
            P("dp", "seq", None),
            P("dp", "seq", None),
            P("dp", "seq", None),
            P("dp", "seq", None),
            P("seq", "dp"),
        ),
        check_vma=False,
    )
```

time: 280 us -> 182 us (0.65)
  matrix products: 74.7 us -> 34.3 us
  local copies, waits for them, and re-layouts: 48.9 us -> 12 us
  starting transfers between devices: 21.1 us -> 11.5 us
  other arithmetic: 25.6 us -> 16.8 us
    dot_general x27 -> x30, matrix products: 65.9 us -> 27.2 us  [the longest x5 6.48 us: local(): jnp.einsum('hqk,hqe->hke', prob_back, grad_heads, preferred_element_type=...]
    ppermute x8 -> x4, waiting for transfers between devices: 53.8 us -> 29.1 us  [shift_up(): return lax.ppermute(block, axis, route)]
    reduce_scatter x2, waiting for transfers between devices: 32.2 us -> 56.8 us  [the longest x1 50.2 us: local(): lax.psum_scatter(partial_weight.astype(jnp.bfloat16), 'seq', scatter_dime...]
    reshape x10 -> x0, local copies, waits for them, and re-layouts: 21.1 us -> none  [the longest x5 11.6 us: local(): value_part.reshape(tok_rows, feature_width)]
    slice x16 -> x1, local copies, waits for them, and re-layouts: 13.5 us -> 0.07 us  [local(): value_grad = row_major(kv_grad[1], tok_rows).astype(jnp.bfloat16)]
    ppermute x8 -> x4, starting transfers between devices: 20.8 us -> 10.1 us  [shift_up(): return lax.ppermute(block, axis, route)]
    add x3 -> x0, other arithmetic: 9 us -> none  [local(): carried = shift_up(carried, 'seq', -1) + part]
    reduce_sum x1 -> x2, other arithmetic: 9.28 us -> 4.09 us  [the longest x1 3.92 us: local(): part_sum = jnp.sum(expo_full, axis=2)]
  transfers between devices with their start and end apart: 11 -> 11, of which waited for: 8 -> 5; matrix products, arithmetic and copies ran while one was open for 46% -> 31% of each run, Pallas kernels for 0% -> 0%
where the time goes in v2:
time: 182 us; the launch traced here: 180 us
  waiting for transfers between devices  86.1 us (47%)
  matrix products  34.3 us (19%)
  other arithmetic  16.8 us (9%)
  between operations  14.5 us (8%)
  local copies, waits for them, and re-layouts  12 us (7%)
  starting transfers between devices  11.5 us (6%)
  blocking collectives  5.14 us (3%)
    reduce_scatter x1, waiting for transfers between devices, local(): lax.psum_scatter(partial_weight.astype(jnp.bfloat16), 'seq', scatter_dime...  50.2 us
    ppermute x4, waiting for transfers between devices, shift_up(): return lax.ppermute(block, axis, route)  29.1 us
    unnamed x92, local copies, waits for them, and re-layouts  10.8 us
    ppermute x4, starting transfers between devices, shift_up(): return lax.ppermute(block, axis, route)  10.1 us
    reduce_scatter x1, waiting for transfers between devices, local(): lax.psum_scatter(row_share.astype(jnp.float32), 'dp', scatter_dimension=1...  6.6 us
    dot_general x5, matrix products, local(): jnp.einsum('hqk,hqe->hke', prob_back, grad_heads, preferred_element_type=...  6.48 us
    dot_general x5, matrix products, local(): jnp.einsum('hqe,hke->hqk', grad_heads, value_block, preferred_element_typ...  5.47 us
    dot_general x5, matrix products, local(): jnp.einsum('hqk,hke->hqe', expo_full.astype(jnp.bfloat16), held[dist][1],...  5.3 us
  transfers between devices with their start and end apart: 11, of which 5 were waited for; matrix products, arithmetic and copies ran while one was open for 31% of the time, Pallas kernels for 0%

profile of v2, /device:TPU:4, one launch (start us, length us, event | category | flops | bytes accessed | tf_op | source)
XLA Modules:
  0.0 180.3 jit_solution(8619392349483098166)
XLA Ops:
  7.2 1.2 copy.80
  8.5 1.2 copy.78
  9.7 0.9 pad_maximum_fusion.2
  10.6 3.4 %collective-permute-start = (bf16[2,12,256,64]{2,3,1,0:T(8,128)(2,1)}, bf16[2,12,256,64]{2,3,1,0:T(8,128)(2,1)S(1)}, u32[]{:S(2)}, u32[]{:S(2)}) collective-permute-start(bf16[2,12,256,64]{2,3,1,0:T(8,128)(2,1)} %pad_maximum_fusion.2), channel_id=1, source_target_pairs={{0,4},{2,6},{4,8},{6,10},{8,12},{10,14},{12,16},{14,18},{16,20},{1... | collective-permute-start | bytes 2359304 | tf_op jit(solution)/shard_map/ppermute | solution.py:18
  14.0 3.5 %collective-permute-start.2 = (bf16[2,12,256,64]{2,3,1,0:T(8,128)(2,1)}, bf16[2,12,256,64]{2,3,1,0:T(8,128)(2,1)S(1)}, u32[]{:S(2)}, u32[]{:S(2)}) collective-permute-start(bf16[2,12,256,64]{2,3,1,0:T(8,128)(2,1)} %pad_maximum_fusion.2), channel_id=1, source_target_pairs={{0,8},{2,10},{4,12},{6,14},{8,16},{10,18},{12,20},{14,22},{16,24},... | collective-permute-start | bytes 2359304 | tf_op jit(solution)/shard_map/ppermute | solution.py:18
  17.6 5.1 %all_gather.6 = bf16[48,1536]{1,0:T(8,128)(2,1)} all-gather(bf16[48,768]{1,0:T(8,128)(2,1)S(1)} %copy-done.39), channel_id=1, replica_groups=mesh['seq'=16,'dp'=2] {'dp'}, dimensions={1}, use_global_device_ids=true | all-gather | bytes 221184 | tf_op jit(solution)/shard_map/all_gather | solution.py:94
  24.3 1.2 copy.77
  25.5 0.7 and_select_fusion.3
  26.2 0.7 and_select_fusion.4
  26.9 1.3 compare_and_fusion.3
  28.2 5.3 %collective-permute-done = bf16[2,12,256,64]{2,3,1,0:T(8,128)(2,1)S(1)} collective-permute-done((bf16[2,12,256,64]{2,3,1,0:T(8,128)(2,1)}, bf16[2,12,256,64]{2,3,1,0:T(8,128)(2,1)S(1)}, u32[]{:S(2)}, u32[]{:S(2)}) %collective-permute-start) | collective-permute-done | bytes 786464 | tf_op jit(solution)/shard_map/ppermute | solution.py:18
  33.5 23.8 %collective-permute-done.2 = bf16[2,12,256,64]{2,3,1,0:T(8,128)(2,1)S(1)} collective-permute-done((bf16[2,12,256,64]{2,3,1,0:T(8,128)(2,1)}, bf16[2,12,256,64]{2,3,1,0:T(8,128)(2,1)S(1)}, u32[]{:S(2)}, u32[]{:S(2)}) %collective-permute-start.2) | collective-permute-done | bytes 786464 | tf_op jit(solution)/shard_map/ppermute | solution.py:18
  59.4 0.7 fusion.9
  61.7 3.9 %fusion.20 = (f32[12,256]{1,0:T(8,128)S(1)}, f32[12,256]{1,0:T(8,128)S(1)}, f32[12,256]{1,0:T(8,128)S(1)}, f32[12,256]{1,0:T(8,128)S(1)}, f32[12,256]{1,0:T(8,128)S(1)}) fusion(f32[12,256,256]{2,1,0:T(8,128)S(1)} %get-tuple-element.52, f32[12,256]{1,0:T(8,128)S(1)} %maximum_maximum_fusion, pred[256,256]{0,1:T(8,128)(4,1)S(1)} %get-tuple-element.38, ...), kind=kLoop, calls=%fused_computation.42 | loop fusion | flops 19645440 | bytes 16130048 | tf_op jit(solution)/shard_map/reduce_sum | solution.py:128
  66.2 0.9 fusion.66
  67.1 0.9 fusion.62
  68.0 0.9 fusion.60
  68.9 0.9 fusion.58
  69.7 1.9 %fusion.117 = (bf16[256,12,64]{0,2,1:T(8,128)(2,1)S(1)}, f32[12,256,64]{1,2,0:T(8,128)}) fusion(f32[256,12]{0,1:T(8,128)S(1)} %bitcast.280, f32[12,256,64]{1,2,0:T(8,128)S(1)} %fusion.58, f32[12,256,64]{1,2,0:T(8,128)S(1)} %fusion.60, f32[12,256,64]{1,2,0:T(8,128)S(1)} %fusion.62, f32[12,256,64]{1,2,0:T(8,128)S(1)} %fusion.66, ...), kind=kOutput, calls=%fused_computation.125 | convolution fusion | flops 105775104 | bytes 7962624 | tf_op jit(solution)/shard_map/hqk,hke->hqe/dot_general | solution.py:129
  71.6 0.7 copy-done.18
  72.4 2.2 %convolution_convert_fusion = bf16[768,1536]{1,0:T(8,128)(2,1)} fusion(bf16[256,768]{0,1:T(8,128)(2,1)S(1)} %bitcast.264, bf16[1,256,1536]{2,1,0:T(8,128)(2,1)S(1)} %copy-done), kind=kOutput, calls=%fused_computation | convolution fusion | flops 605159424 | bytes 3538944 | tf_op jit(solution)/shard_map/dot_general | solution.py:149
  74.8 3.2 %convolution_convert_fusion.2 = bf16[256,768]{1,0:T(8,128)(2,1)} fusion(bf16[768,1536]{1,0:T(8,128)(2,1)} %all-gather.2.cloned.1.call-done, bf16[1,256,1536]{2,1,0:T(8,128)(2,1)S(1)} %copy-done), kind=kOutput, calls=%fused_computation.120 | convolution fusion | flops 604176384 | bytes 3538944 | tf_op jit(solution)/shard_map/dot_general | solution.py:145
  78.0 1.2 copy.86
  79.2 2.8 %fusion.81 = f32[1,12,256,64]{2,3,1,0:T(8,128)S(1)} fusion(bf16[12,256,64]{1,2,0:T(8,128)(2,1)S(1)} %bitcast.266, f32[12,256,256]{2,1,0:T(8,128)} %copy-done.10, f32[12,256]{1,0:T(8,128)} %get-tuple-element.30, pred[256,256]{0,1:T(8,128)(4,1)} %copy-done.37), kind=kOutput, calls=%fused_computation.96 | convolution fusion | flops 103809024 | bytes 4403200 | tf_op jit(solution)/shard_map/hqk,hqe->hke/dot_general | solution.py:192
  82.2 0.7 fusion.87
  83.5 0.8 copy-done.11
  84.6 1.1 multiply_convert_fusion.3
  86.9 1.1 multiply_convert_fusion.4
  89.1 1.0 copy-done.5
  90.1 1.1 multiply_convert_fusion.2
  91.8 1.1 multiply_convert_fusion.1
  93.7 1.1 multiply_convert_fusion
  96.8 0.7 fusion.84
  97.5 0.7 fusion.90
  98.2 1.6 fusion.78
  99.8 2.1 %fusion.41 = (bf16[2,12,256,64]{2,3,1,0:T(8,128)(2,1)}, bf16[2,12,256,64]{2,3,1,0:T(8,128)(2,1)}) fusion(f32[1,12,256,64]{2,3,1,0:T(8,128)S(1)} %fusion.84, f32[1,12,256,64]{2,3,1,0:T(8,128)S(1)} %fusion.96, f32[2,12,256,64]{2,3,1,0:T(8,128)S(1)} %collective-permute-done.5, f32[2,12,256,64]{2,3,1,0:T(8,128)S(1)} %collective-permute-done.4, pred[]{:T(512)S(6)} %eq.91, ...), kind=kLoop, calls=%fused_computation.61 | loop fusion | flops 3145728 | bytes 7864321 | tf_op jit(solution)/shard_map/convert_element_type | solution.py:78
  102.0 1.9 %collective-permute-start.6 = (bf16[2,12,256,64]{2,3,1,0:T(8,128)(2,1)}, bf16[2,12,256,64]{2,3,1,0:T(8,128)(2,1)}, u32[]{:S(2)}, u32[]{:S(2)}) collective-permute-start(bf16[2,12,256,64]{2,3,1,0:T(8,128)(2,1)} %get-tuple-element.32), channel_id=1, source_target_pairs={{4,0},{6,2},{8,4},{10,6},{12,8},{14,10},{16,12},{18,14},{20,16},{2... | collective-permute-start | bytes 2359304 | tf_op jit(solution)/shard_map/ppermute | solution.py:18
  103.9 1.3 collective-permute-start.7
  105.2 1.7 fusion.12
  106.9 1.2 fusion.114
  108.1 50.2 %reduce-scatter.3.cloned.1.call-done = bf16[48,1536]{1,0:T(8,128)(2,1)} async-done(((bf16[768,1536]{1,0:T(8,128)(2,1)}), bf16[48,1536]{1,0:T(8,128)(2,1)}) %reduce-scatter.3.cloned.1.call-update) | async-done | bytes 147472 | tf_op jit(solution)/shard_map/reduce_scatter | solution.py:152
  158.3 1.7 convert_element_type.183
  160.0 1.5 fusion.98
  161.4 0.9 copy.107
  162.4 2.9 %fusion.40 = bf16[2,12,256,64]{2,3,1,0:T(8,128)(2,1)S(1)} fusion(f32[1,12,256,64]{2,3,1,0:T(8,128)} %fusion.78, f32[1,12,256,64]{2,3,1,0:T(8,128)} %fusion.98, bf16[2,12,256,64]{2,3,1,0:T(8,128)(2,1)} %collective-permute-done.7, bf16[2,12,256,64]{2,3,1,0:T(8,128)(2,1)} %collective-permute-done.6, f32[2,12,256,64]{2,3,1,0:T(8,128)} %copy-done.12, pred[]{:T(512)S(6)} %eq.91), kind=kLoop, calls=%fused_computation.58 | loop fusion | flops 3145728 | bytes 5505025 | tf_op jit(solution)/shard_map/convert.1
  165.3 0.9 copy.108
  166.2 0.9 copy.109
  167.2 6.6 %reduce-scatter.5.cloned.1.call-done = f32[48,768]{1,0:T(8,128)} async-done(((f32[48,1536]{1,0:T(8,128)}), f32[48,768]{1,0:T(8,128)}) %reduce-scatter.5.cloned.1.call-update) | async-done | bytes 147472 | tf_op jit(solution)/shard_map/reduce_scatter | solution.py:155
  (129 shorter events, 12.8 us)
Async XLA Ops:
  7.2 65.2 %copy-start = (bf16[1,256,1536]{2,1,0:T(8,128)(2,1)S(1)}, bf16[1,256,1536]{2,1,0:T(8,128)(2,1)}, u32[]{:S(2)}) copy-start(bf16[1,256,1536]{2,1,0:T(8,128)(2,1)} %param.9) | copy-start | bytes 2359300
  7.2 10.4 %copy-start.39 = (bf16[48,768]{1,0:T(8,128)(2,1)S(1)}, bf16[48,768]{1,0:T(8,128)(2,1)}, u32[]{:S(2)}) copy-start(bf16[48,768]{1,0:T(8,128)(2,1)} %param.11) | copy-start | bytes 221188
  7.2 15.7 %copy-start.42 = (s32[1,8]{1,0:T(1,128)S(1)}, s32[1,8]{1,0:T(1,128)}, u32[]{:S(2)}) copy-start(s32[1,8]{1,0:T(1,128)} %param.10) | copy-start | bytes 100
  7.2 67.6 %all-gather.2.cloned.1.call-start = ((), (), s32[]{:S(2)}) async-start(), calls=%async_computation.2 | async-start | bytes 2506752 | tf_op jit(solution)/shard_map/all_gather | solution.py:95
  10.6 22.9 %collective-permute-start = (bf16[2,12,256,64]{2,3,1,0:T(8,128)(2,1)}, bf16[2,12,256,64]{2,3,1,0:T(8,128)(2,1)S(1)}, u32[]{:S(2)}, u32[]{:S(2)}) collective-permute-start(bf16[2,12,256,64]{2,3,1,0:T(8,128)(2,1)} %pad_maximum_fusion.2), channel_id=1, source_target_pairs={{0,4},{2,6},{4,8},{6,10},{8,12},{10,14},{12,16},{14,18},{16,20},{1... | collective-permute-start | bytes 2359304 | tf_op jit(solution)/shard_map/ppermute | solution.py:18
  14.0 43.3 %collective-permute-start.2 = (bf16[2,12,256,64]{2,3,1,0:T(8,128)(2,1)}, bf16[2,12,256,64]{2,3,1,0:T(8,128)(2,1)S(1)}, u32[]{:S(2)}, u32[]{:S(2)}) collective-permute-start(bf16[2,12,256,64]{2,3,1,0:T(8,128)(2,1)} %pad_maximum_fusion.2), channel_id=1, source_target_pairs={{0,8},{2,10},{4,12},{6,14},{8,16},{10,18},{12,20},{14,22},{16,24},... | collective-permute-start | bytes 2359304 | tf_op jit(solution)/shard_map/ppermute | solution.py:18
  22.7 135.5 %reduce-scatter.3.cloned.1.call-start = ((), (), s32[]{:S(2)}) async-start(), calls=%async_computation.3 | async-start | bytes 2506752 | tf_op jit(solution)/shard_map/reduce_scatter | solution.py:152
  28.1 38.1 %copy-start.28 = (pred[256,256]{0,1:T(8,128)(4,1)}, pred[256,256]{0,1:T(8,128)(4,1)S(1)}, u32[]{:S(2)}) copy-start(pred[256,256]{0,1:T(8,128)(4,1)S(1)} %get-tuple-element.42) | copy-start | bytes 196612
  28.2 38.9 %copy-start.32 = (pred[256,256]{0,1:T(8,128)(4,1)}, pred[256,256]{0,1:T(8,128)(4,1)S(1)}, u32[]{:S(2)}) copy-start(pred[256,256]{0,1:T(8,128)(4,1)S(1)} %get-tuple-element.39) | copy-start | bytes 196612
  28.2 39.8 %copy-start.34 = (pred[256,256]{0,1:T(8,128)(4,1)}, pred[256,256]{0,1:T(8,128)(4,1)S(1)}, u32[]{:S(2)}) copy-start(pred[256,256]{0,1:T(8,128)(4,1)S(1)} %get-tuple-element.40) | copy-start | bytes 196612
  28.2 40.7 %copy-start.30 = (pred[256,256]{0,1:T(8,128)(4,1)}, pred[256,256]{0,1:T(8,128)(4,1)S(1)}, u32[]{:S(2)}) copy-start(pred[256,256]{0,1:T(8,128)(4,1)S(1)} %get-tuple-element.41) | copy-start | bytes 196612
  28.2 41.5 %copy-start.37 = (pred[256,256]{0,1:T(8,128)(4,1)}, pred[256,256]{0,1:T(8,128)(4,1)S(1)}, u32[]{:S(2)}) copy-start(pred[256,256]{0,1:T(8,128)(4,1)S(1)} %get-tuple-element.38) | copy-start | bytes 196612
  33.5 58.3 %copy-start.13 = (bf16[2,12,256,64]{2,3,1,0:T(8,128)(2,1)}, bf16[2,12,256,64]{2,3,1,0:T(8,128)(2,1)S(1)}, u32[]{:S(2)}) copy-start(bf16[2,12,256,64]{2,3,1,0:T(8,128)(2,1)S(1)} %collective-permute-done) | copy-start | bytes 2359300
  57.3 31.8 %copy-start.15 = (bf16[2,12,256,64]{2,3,1,0:T(8,128)(2,1)}, bf16[2,12,256,64]{2,3,1,0:T(8,128)(2,1)S(1)}, u32[]{:S(2)}) copy-start(bf16[2,12,256,64]{2,3,1,0:T(8,128)(2,1)S(1)} %collective-permute-done.2) | copy-start | bytes 2359300
  57.4 2.7 %collective-permute-start.3 = (bf16[2,12,256,64]{2,3,1,0:T(8,128)(2,1)S(1)}, bf16[2,12,256,64]{2,3,1,0:T(8,128)(2,1)S(1)}, u32[]{:S(2)}, u32[]{:S(2)}) collective-permute-start(bf16[2,12,256,64]{2,3,1,0:T(8,128)(2,1)S(1)} %get-tuple-element.37), channel_id=1, source_target_pairs={{0,2},{2,0},{4,6},{6,4},{8,10},{10,8},{12,14},{14,12},{16,18},{18,... | collective-permute-start | bytes 2359304 | tf_op jit(solution)/shard_map/ppermute | solution.py:23
  58.2 8.0 %copy-start.2 = (f32[12,256,256]{1,2,0:T(8,128)}, f32[12,256,256]{1,2,0:T(8,128)S(1)}, u32[]{:S(2)}) copy-start(f32[12,256,256]{1,2,0:T(8,128)S(1)} %get-tuple-element.50) | copy-start | bytes 9437188
  58.2 2.8 %collective-permute-start.1 = (bf16[2,12,256,64]{2,3,1,0:T(8,128)(2,1)S(1)}, bf16[2,12,256,64]{2,3,1,0:T(8,128)(2,1)S(1)}, u32[]{:S(2)}, u32[]{:S(2)}) collective-permute-start(bf16[2,12,256,64]{2,3,1,0:T(8,128)(2,1)S(1)} %get-tuple-element.36), channel_id=1, source_target_pairs={{0,2},{2,0},{4,6},{6,4},{8,10},{10,8},{12,14},{14,12},{16,18},{18,... | collective-permute-start | bytes 2359304 | tf_op jit(solution)/shard_map/ppermute | solution.py:23
  59.4 9.4 %copy-start.4 = (f32[12,256,256]{2,1,0:T(8,128)}, f32[12,256,256]{2,1,0:T(8,128)S(1)}, u32[]{:S(2)}) copy-start(f32[12,256,256]{2,1,0:T(8,128)S(1)} %get-tuple-element.44) | copy-start | bytes 9437188
  60.1 6.9 %copy-start.6 = (f32[12,256,256]{2,1,0:T(8,128)}, f32[12,256,256]{2,1,0:T(8,128)S(1)}, u32[]{:S(2)}) copy-start(f32[12,256,256]{2,1,0:T(8,128)S(1)} %get-tuple-element.48) | copy-start | bytes 9437188
  60.2 7.8 %copy-start.26 = (bf16[2,12,256,64]{2,3,1,0:T(8,128)(2,1)}, bf16[2,12,256,64]{2,3,1,0:T(8,128)(2,1)S(1)}, u32[]{:S(2)}) copy-start(bf16[2,12,256,64]{2,3,1,0:T(8,128)(2,1)S(1)} %collective-permute-done.3) | copy-start | bytes 2359300
  60.9 7.1 %copy-start.8 = (f32[12,256,256]{2,1,0:T(8,128)}, f32[12,256,256]{2,1,0:T(8,128)S(1)}, u32[]{:S(2)}) copy-start(f32[12,256,256]{2,1,0:T(8,128)S(1)} %get-tuple-element.46) | copy-start | bytes 9437188
  61.0 8.8 %copy-start.24 = (bf16[2,12,256,64]{2,3,1,0:T(8,128)(2,1)}, bf16[2,12,256,64]{2,3,1,0:T(8,128)(2,1)S(1)}, u32[]{:S(2)}) copy-start(bf16[2,12,256,64]{2,3,1,0:T(8,128)(2,1)S(1)} %collective-permute-done.1) | copy-start | bytes 2359300
  61.6 8.1 %copy-start.10 = (f32[12,256,256]{2,1,0:T(8,128)}, f32[12,256,256]{2,1,0:T(8,128)S(1)}, u32[]{:S(2)}) copy-start(f32[12,256,256]{2,1,0:T(8,128)S(1)} %get-tuple-element.52) | copy-start | bytes 9437188
  74.5 99.2 %reduce-scatter.5.cloned.1.call-start = ((), (), s32[]{:S(2)}) async-start(), calls=%async_computation.4 | async-start | bytes 442368 | tf_op jit(solution)/shard_map/reduce_scatter | solution.py:155
  78.0 4.0 %copy-start.35 = (pred[256,256]{0,1:T(8,128)(4,1)S(1)}, pred[256,256]{0,1:T(8,128)(4,1)}, u32[]{:S(2)}) copy-start(pred[256,256]{0,1:T(8,128)(4,1)} %copy-done.34) | copy-start | bytes 196612
  78.0 4.0 %copy-start.40 = (f32[12,256]{1,0:T(8,128)S(1)}, f32[12,256]{1,0:T(8,128)}, u32[]{:S(2)}) copy-start(f32[12,256]{1,0:T(8,128)} %get-tuple-element.30) | copy-start | bytes 36868
  79.2 4.3 %copy-start.20 = (bf16[256,768]{0,1:T(8,128)(2,1)}, bf16[256,768]{0,1:T(8,128)(2,1)S(1)}, u32[]{:S(2)}) copy-start(bf16[256,768]{0,1:T(8,128)(2,1)S(1)} %copy.86) | copy-start | bytes 1179652
  79.2 3.0 %copy-start.9 = (f32[12,256,256]{2,1,0:T(8,128)S(1)}, f32[12,256,256]{2,1,0:T(8,128)}, u32[]{:S(2)}) copy-start(f32[12,256,256]{2,1,0:T(8,128)} %copy-done.8) | copy-start | bytes 9437188
  82.2 2.1 %copy-start.11 = (f32[12,256,256]{2,1,0:T(8,128)S(1)}, f32[12,256,256]{2,1,0:T(8,128)}, u32[]{:S(2)}) copy-start(f32[12,256,256]{2,1,0:T(8,128)} %copy-done.10) | copy-start | bytes 9437188
  82.2 2.3 %copy-start.25 = (bf16[2,12,256,64]{2,3,1,0:T(8,128)(2,1)S(1)}, bf16[2,12,256,64]{2,3,1,0:T(8,128)(2,1)}, u32[]{:S(2)}) copy-start(bf16[2,12,256,64]{2,3,1,0:T(8,128)(2,1)} %copy-done.24) | copy-start | bytes 2359300
  82.2 2.3 %copy-start.38 = (pred[256,256]{0,1:T(8,128)(4,1)S(1)}, pred[256,256]{0,1:T(8,128)(4,1)}, u32[]{:S(2)}) copy-start(pred[256,256]{0,1:T(8,128)(4,1)} %copy-done.37) | copy-start | bytes 196612
  85.7 1.2 copy-start.27
  85.7 1.2 copy-start.36
  86.5 13.4 %collective-permute-start.4 = (f32[2,12,256,64]{2,3,1,0:T(8,128)S(1)}, f32[2,12,256,64]{2,3,1,0:T(8,128)S(1)}, u32[]{:S(2)}, u32[]{:S(2)}) collective-permute-start(f32[2,12,256,64]{2,3,1,0:T(8,128)S(1)} %pad_maximum_fusion), channel_id=1, source_target_pairs={{0,2},{2,0},{4,6},{6,4},{8,10},{10,8},{12,14},{14,12},{16,18},{18,... | collective-permute-start | bytes 4718600 | tf_op jit(solution)/shard_map/ppermute | solution.py:23
  88.1 2.0 %copy-start.5 = (f32[12,256,256]{2,1,0:T(8,128)S(1)}, f32[12,256,256]{2,1,0:T(8,128)}, u32[]{:S(2)}) copy-start(f32[12,256,256]{2,1,0:T(8,128)} %copy-done.4) | copy-start | bytes 9437188
  88.1 2.0 %copy-start.31 = (pred[256,256]{0,1:T(8,128)(4,1)S(1)}, pred[256,256]{0,1:T(8,128)(4,1)}, u32[]{:S(2)}) copy-start(pred[256,256]{0,1:T(8,128)(4,1)} %copy-done.30) | copy-start | bytes 196612
  88.8 3.0 %copy-start.7 = (f32[12,256,256]{2,1,0:T(8,128)S(1)}, f32[12,256,256]{2,1,0:T(8,128)}, u32[]{:S(2)}) copy-start(f32[12,256,256]{2,1,0:T(8,128)} %copy-done.6) | copy-start | bytes 9437188
  88.8 3.0 %copy-start.33 = (pred[256,256]{0,1:T(8,128)(4,1)S(1)}, pred[256,256]{0,1:T(8,128)(4,1)}, u32[]{:S(2)}) copy-start(pred[256,256]{0,1:T(8,128)(4,1)} %copy-done.32) | copy-start | bytes 196612
  88.9 11.0 %collective-permute-start.5 = (f32[2,12,256,64]{2,3,1,0:T(8,128)S(1)}, f32[2,12,256,64]{2,3,1,0:T(8,128)S(1)}, u32[]{:S(2)}, u32[]{:S(2)}) collective-permute-start(f32[2,12,256,64]{2,3,1,0:T(8,128)S(1)} %pad_maximum_fusion.1), channel_id=1, source_target_pairs={{0,2},{2,0},{4,6},{6,4},{8,10},{10,8},{12,14},{14,12},{16,18},{18,... | collective-permute-start | bytes 4718600 | tf_op jit(solution)/shard_map/ppermute | solution.py:23
  91.8 1.9 %copy-start.3 = (f32[12,256,256]{1,2,0:T(8,128)S(1)}, f32[12,256,256]{1,2,0:T(8,128)}, u32[]{:S(2)}) copy-start(f32[12,256,256]{1,2,0:T(8,128)} %copy-done.2) | copy-start | bytes 9437188
  91.8 1.9 %copy-start.29 = (pred[256,256]{0,1:T(8,128)(4,1)S(1)}, pred[256,256]{0,1:T(8,128)(4,1)}, u32[]{:S(2)}) copy-start(pred[256,256]{0,1:T(8,128)(4,1)} %copy-done.28) | copy-start | bytes 196612
  99.8 5.4 %copy-start.17 = (bf16[768,1536]{1,0:T(8,128)(2,1)S(1)}, bf16[768,1536]{1,0:T(8,128)(2,1)}, u32[]{:S(2)}) copy-start(bf16[768,1536]{1,0:T(8,128)(2,1)} %all-gather.2.cloned.1.call-done) | copy-start | bytes 7077892
  99.8 5.4 %copy-start.19 = (bf16[256,12,64]{0,2,1:T(8,128)(2,1)S(1)}, bf16[256,12,64]{0,2,1:T(8,128)(2,1)}, u32[]{:S(2)}) copy-start(bf16[256,12,64]{0,2,1:T(8,128)(2,1)} %copy-done.18) | copy-start | bytes 1179652
  99.8 2.1 %copy-start.12 = (f32[2,12,256,64]{2,3,1,0:T(8,128)}, f32[2,12,256,64]{2,3,1,0:T(8,128)S(1)}, u32[]{:S(2)}) copy-start(f32[2,12,256,64]{2,3,1,0:T(8,128)S(1)} %collective-permute-done.4) | copy-start | bytes 4718596
  102.0 60.4 %collective-permute-start.6 = (bf16[2,12,256,64]{2,3,1,0:T(8,128)(2,1)}, bf16[2,12,256,64]{2,3,1,0:T(8,128)(2,1)}, u32[]{:S(2)}, u32[]{:S(2)}) collective-permute-start(bf16[2,12,256,64]{2,3,1,0:T(8,128)(2,1)} %get-tuple-element.32), channel_id=1, source_target_pairs={{4,0},{6,2},{8,4},{10,6},{12,8},{14,10},{16,12},{18,14},{20,16},{2... | collective-permute-start | bytes 2359304 | tf_op jit(solution)/shard_map/ppermute | solution.py:18
  103.9 58.5 %collective-permute-start.7 = (bf16[2,12,256,64]{2,3,1,0:T(8,128)(2,1)}, bf16[2,12,256,64]{2,3,1,0:T(8,128)(2,1)}, u32[]{:S(2)}, u32[]{:S(2)}) collective-permute-start(bf16[2,12,256,64]{2,3,1,0:T(8,128)(2,1)} %get-tuple-element.33), channel_id=1, source_target_pairs={{8,0},{10,2},{12,4},{14,6},{16,8},{18,10},{20,12},{22,14},{24,16},... | collective-permute-start | bytes 2359304 | tf_op jit(solution)/shard_map/ppermute | solution.py:18
  108.1 53.4 %copy-start.22 = (bf16[12,256,64]{1,2,0:T(8,128)(2,1)S(1)}, bf16[12,256,64]{1,2,0:T(8,128)(2,1)}, u32[]{:S(2)}) copy-start(bf16[12,256,64]{1,2,0:T(8,128)(2,1)} %fusion.114) | copy-start | bytes 1179652
  161.4 12.3 %copy-start.1 = (bf16[1,256,1536]{2,1,0:T(8,128)(2,1)S(1)}, bf16[1,256,1536]{2,1,0:T(8,128)(2,1)}, u32[]{:S(2)}) copy-start(bf16[1,256,1536]{2,1,0:T(8,128)(2,1)} %param.9) | copy-start | bytes 2359300
  (6 other events, 6.5 us)
Sparse Core Ops, SparseCore 0:
  22.9 43.0 all-gather.1
  74.7 83.5 reduce-scatter.2
  161.2 12.5 reduce-scatter.4

commit v3 on v2

--- a/solution.py
+++ b/solution.py
@@ -21,6 +21,26 @@
 def swap_partner(block, axis):
     count = lax.axis_size(axis)
     return lax.ppermute(block, axis, [(i, i ^ 1) for i in range(count)])
+
+
+def halving_scatter(total, axis, dim, sends_narrow):
+    count = lax.axis_size(axis)
+    if count & (count - 1):
+        return lax.psum_scatter(total, axis, scatter_dimension=dim, tiled=True)
+    me = lax.axis_index(axis)
+    bits = count.bit_length() - 1
+    moved = jnp.moveaxis(total, dim, 0)
+    rest = moved.shape[1:]
+    blocks = moved.reshape((2,) * bits + (moved.shape[0] // count,) + rest)
+    for step in range(bits):
+        own_bit = (me >> step) % 2
+        keep = lax.dynamic_index_in_dim(blocks, own_bit, blocks.ndim - len(rest) - 2, keepdims=False)
+        give = lax.dynamic_index_in_dim(blocks, 1 - own_bit, blocks.ndim - len(rest) - 2, keepdims=False)
+        if sends_narrow[step]:
+            give = give.astype(jnp.bfloat16)
+        got = lax.ppermute(give, axis, [(i, i ^ (1 << step)) for i in range(count)])
+        blocks = keep + got.astype(keep.dtype)
+    return jnp.moveaxis(blocks, 0, dim)
 
 
 def frame_labels(utt_lengths, first_frame, frame_count, total_frames):
@@ -149,12 +169,11 @@
     partial_weight = lax.dot_general(
         attended, upstream, (((0,), (0,)), ((), ())), preferred_element_type=jnp.float32
     )
-    row_share = lax.psum_scatter(
-        partial_weight.astype(jnp.bfloat16), "seq", scatter_dimension=0, tiled=True
-    )
-    weight_grad = lax.psum_scatter(
-        row_share.astype(jnp.float32), "dp", scatter_dimension=1, tiled=True
-    )
+    seq_bits = max(seq_count.bit_length() - 1, 1)
+    row_share = halving_scatter(
+        partial_weight, "seq", 0, [step > 0 for step in range(seq_bits)]
+    )
+    weight_grad = halving_scatter(row_share, "dp", 1, [False] * 8)
 
     grad_heads = head_major(att_grad, tok_rows)
     delta_rows = jnp.sum(

time: 182 us -> 201 us (1.10)
  waiting for transfers between devices: 86.1 us -> 65.4 us
  starting transfers between devices: 11.5 us -> 23.9 us
  matrix products: 34.3 us -> 43.6 us
  other arithmetic: 16.8 us -> 26.1 us
  local copies, waits for them, and re-layouts: 12 us -> 21.2 us
    reduce_scatter x2 -> x0, waiting for transfers between devices: 56.8 us -> none  [the longest x1 50.2 us: local(): lax.psum_scatter(partial_weight.astype(jnp.bfloat16), 'seq', scatter_dime...]
    ppermute x4, waiting for transfers between devices: 29.1 us -> 56.8 us  [shift_up(): return lax.ppermute(block, axis, route)]
    ppermute x0 -> x5, starting transfers between devices: none -> 12.6 us  [halving_scatter(): got = lax.ppermute(give, axis, [(i, i ^ 1 << step) for i in range(count)])]
    ppermute x0 -> x5, waiting for transfers between devices: none -> 8.57 us  [halving_scatter(): got = lax.ppermute(give, axis, [(i, i ^ 1 << step) for i in range(count)])]
    unnamed x92 -> x93, local copies, waits for them, and re-layouts: 10.8 us -> 17.2 us
    add x0 -> x3, other arithmetic: none -> 4.98 us  [halving_scatter(): blocks = keep + got.astype(keep.dtype)]
    dot_general x5, matrix products: 3.38 us -> 7.37 us  [local(): jnp.einsum('hqe,hke->hqk', query_heads, held[dist][0], preferred_element_...]
    another operation x2, other arithmetic: 0.28 us -> 2.74 us  [local(): parts[dist] = jnp.stack([key_part, value_part])]
  transfers between devices with their start and end apart: 11 -> 14, of which waited for: 5 -> 7; matrix products, arithmetic and copies ran while one was open for 31% -> 37% of each run, Pallas kernels for 0% -> 0%
where the time goes in v3:
time: 201 us; the launch traced here: 200 us
  waiting for transfers between devices  65.4 us (33%)
  matrix products  43.6 us (22%)
  other arithmetic  26.1 us (13%)
  starting transfers between devices  23.9 us (12%)
  local copies, waits for them, and re-layouts  21.2 us (11%)
  between operations  14.7 us (7%)
  blocking collectives  5.14 us (3%)
    ppermute x4, waiting for transfers between devices, shift_up(): return lax.ppermute(block, axis, route)  56.8 us
    unnamed x93, local copies, waits for them, and re-layouts  17.2 us
    ppermute x5, starting transfers between devices, halving_scatter(): got = lax.ppermute(give, axis, [(i, i ^ 1 << step) for i in range(count)])  12.6 us
    ppermute x4, starting transfers between devices, shift_up(): return lax.ppermute(block, axis, route)  10.2 us
    ppermute x5, waiting for transfers between devices, halving_scatter(): got = lax.ppermute(give, axis, [(i, i ^ 1 << step) for i in range(count)])  8.57 us
    dot_general x5, matrix products, local(): jnp.einsum('hqk,hqe->hke', prob_back, grad_heads, preferred_element_type=...  8.29 us
    dot_general x5, matrix products, local(): jnp.einsum('hqe,hke->hqk', query_heads, held[dist][0], preferred_element_...  7.37 us
    dot_general x5, matrix products, local(): jnp.einsum('hqe,hke->hqk', grad_heads, value_block, preferred_element_typ...  6.92 us
  transfers between devices with their start and end apart: 14, of which 7 were waited for; matrix products, arithmetic and copies ran while one was open for 37% of the time, Pallas kernels for 0%

profile of v3, /device:TPU:4, one launch (start us, length us, event | category | flops | bytes accessed | tf_op | source)
XLA Modules:
  0.0 200.2 jit_solution(3423447739439646486)
XLA Ops:
  7.2 1.2 copy.113
  8.5 1.2 copy.111
  10.6 3.5 %collective-permute-start.2 = (bf16[2,12,256,64]{2,3,1,0:T(8,128)(2,1)}, bf16[2,12,256,64]{2,3,1,0:T(8,128)(2,1)S(1)}, u32[]{:S(2)}, u32[]{:S(2)}) collective-permute-start(bf16[2,12,256,64]{2,3,1,0:T(8,128)(2,1)} %pad_maximum_fusion.2), channel_id=1, source_target_pairs={{0,8},{2,10},{4,12},{6,14},{8,16},{10,18},{12,20},{14,22},{16,24},... | collective-permute-start | bytes 2359304 | tf_op jit(solution)/shard_map/ppermute | solution.py:18
  14.1 3.4 %collective-permute-start = (bf16[2,12,256,64]{2,3,1,0:T(8,128)(2,1)}, bf16[2,12,256,64]{2,3,1,0:T(8,128)(2,1)S(1)}, u32[]{:S(2)}, u32[]{:S(2)}) collective-permute-start(bf16[2,12,256,64]{2,3,1,0:T(8,128)(2,1)} %pad_maximum_fusion.2), channel_id=1, source_target_pairs={{0,4},{2,6},{4,8},{6,10},{8,12},{10,14},{12,16},{14,18},{16,20},{1... | collective-permute-start | bytes 2359304 | tf_op jit(solution)/shard_map/ppermute | solution.py:18
  17.5 5.1 %all_gather.6 = bf16[48,1536]{1,0:T(8,128)(2,1)} all-gather(bf16[48,768]{1,0:T(8,128)(2,1)S(1)} %copy-done.41), channel_id=1, replica_groups=mesh['seq'=16,'dp'=2] {'dp'}, dimensions={1}, use_global_device_ids=true | all-gather | bytes 221184 | tf_op jit(solution)/shard_map/all_gather | solution.py:114
  24.2 1.2 copy.110
  26.8 1.9 compare_and_fusion.3
  28.6 4.9 %collective-permute-done.2 = bf16[2,12,256,64]{2,3,1,0:T(8,128)(2,1)S(1)} collective-permute-done((bf16[2,12,256,64]{2,3,1,0:T(8,128)(2,1)}, bf16[2,12,256,64]{2,3,1,0:T(8,128)(2,1)S(1)}, u32[]{:S(2)}, u32[]{:S(2)}) %collective-permute-start.2) | collective-permute-done | bytes 786464 | tf_op jit(solution)/shard_map/ppermute | solution.py:18
  33.6 23.9 %collective-permute-done = bf16[2,12,256,64]{2,3,1,0:T(8,128)(2,1)S(1)} collective-permute-done((bf16[2,12,256,64]{2,3,1,0:T(8,128)(2,1)}, bf16[2,12,256,64]{2,3,1,0:T(8,128)(2,1)S(1)}, u32[]{:S(2)}, u32[]{:S(2)}) %collective-permute-start) | collective-permute-done | bytes 786464 | tf_op jit(solution)/shard_map/ppermute | solution.py:18
  57.5 1.4 broadcast_select_fusion.1
  58.9 2.3 %select_reduce_fusion = (f32[12,256]{1,0:T(8,128)S(1)}, f32[12,256,256]{1,2,0:T(8,128)}) fusion(pred[256,256]{0,1:T(8,128)(4,1)S(1)} %get-tuple-element.49, bf16[12,256,64]{1,2,0:T(8,128)(2,1)S(1)} %bitcast.285, bf16[12,256,64]{1,2,0:T(8,128)(2,1)S(1)} %bitcast.297), kind=kOutput, calls=%fused_computation.31 | convolution fusion | flops 103019520 | bytes 4009984 | tf_op jit(solution)/shard_map/hqe,hke->hqk/dot_general | solution.py:135
  61.7 1.6 fusion.11
  64.1 2.1 %fusion.10 = (f32[12,256]{1,0:T(8,128)S(1)}, f32[12,256,256]{2,1,0:T(8,128)S(1)}) fusion(pred[256,256]{0,1:T(8,128)(4,1)S(1)} %copy-done.35, bf16[12,256,64]{1,2,0:T(8,128)(2,1)S(1)} %bitcast.288, bf16[2,12,256,64]{2,3,1,0:T(8,128)(2,1)} %collective-permute-done.3), kind=kOutput, calls=%fused_computation.29 | convolution fusion | flops 103019520 | bytes 4009984 | tf_op jit(solution)/shard_map/hqe,hke->hqk/dot_general | solution.py:135
  67.0 1.7 copy-done.3
  69.5 4.1 %fusion.20 = (f32[12,256]{1,0:T(8,128)S(1)}, f32[12,256]{1,0:T(8,128)S(1)}, f32[12,256]{1,0:T(8,128)S(1)}, f32[12,256]{1,0:T(8,128)S(1)}, f32[12,256]{1,0:T(8,128)S(1)}) fusion(f32[12,256,256]{2,1,0:T(8,128)S(1)} %get-tuple-element.59, f32[12,256]{1,0:T(8,128)S(1)} %maximum_maximum_fusion, pred[256,256]{0,1:T(8,128)(4,1)S(1)} %copy-done.33, ...), kind=kLoop, calls=%fused_computation.43 | loop fusion | flops 19645440 | bytes 16130048 | tf_op jit(solution)/shard_map/reduce_sum | solution.py:148
  74.5 1.9 fusion.60
  79.1 2.1 %copy-done.2 = f32[2,2,2,2,48,1536]{5,4,3,2,1,0:T(8,128)} copy-done((f32[2,2,2,2,48,1536]{5,4,3,2,1,0:T(8,128)}, f32[2,2,2,2,48,1536]{5,4,3,2,1,0:T(8,128)S(1)}, u32[]{:S(2)}) %copy-start.2) | copy-done | bytes 4718616
  81.2 1.7 dynamic-slice_bitcast_fusion
  82.9 4.9 %collective-permute-done.8 = f32[2,2,2,48,1536]{4,3,2,1,0:T(8,128)} collective-permute-done((f32[2,2,2,48,1536]{4,3,2,1,0:T(8,128)}, f32[2,2,2,48,1536]{4,3,2,1,0:T(8,128)}, u32[]{:S(2)}, u32[]{:S(2)}) %collective-permute-start.8) | collective-permute-done | bytes 2359328 | tf_op jit(solution)/shard_map/ppermute | solution.py:41
  87.8 2.8 %bitcast_add_fusion = f32[2,2,2,48,1536]{4,3,2,1,0:T(8,128)S(1)} fusion(f32[2,2,2,48,1536]{4,3,2,1,0:T(8,128)} %collective-permute-done.8, f32[2,2,2,2,48,1536]{5,4,3,2,1,0:T(8,128)} %copy-done.2, s32[]{:T(128)S(6)} %select_n.250), kind=kLoop, calls=%fused_computation.39 | loop fusion | flops 589824 | bytes 7077892 | tf_op jit(solution)/shard_map/add | solution.py:42
  90.6 1.4 copy-done.13
  92.9 2.5 %convolution_convert_fusion.1 = bf16[256,768]{1,0:T(8,128)(2,1)S(1)} fusion(bf16[768,1536]{1,0:T(8,128)(2,1)} %all-gather.2.cloned.1.call-done, bf16[1,256,1536]{2,1,0:T(8,128)(2,1)S(1)} %copy-done), kind=kOutput, calls=%fused_computation.121 | convolution fusion | flops 604176384 | bytes 3538944 | tf_op jit(solution)/shard_map/dot_general | solution.py:165
  95.6 3.7 %fusion.78 = f32[1,12,256,64]{2,3,1,0:T(8,128)} fusion(bf16[12,256,64]{1,2,0:T(8,128)(2,1)S(1)} %bitcast.305, f32[12,256,256]{1,2,0:T(8,128)} %get-tuple-element.57, f32[12,256]{1,0:T(8,128)S(1)} %get-tuple-element.35, pred[256,256]{0,1:T(8,128)(4,1)S(1)} %copy-done.39), kind=kOutput, calls=%fused_computation.96 | convolution fusion | flops 103809024 | bytes 4403200 | tf_op jit(solution)/shard_map/hqk,hqe->hke/dot_general | solution.py:211
  99.3 1.6 fusion.84
  102.1 1.2 copy-done.10
  104.0 1.2 copy-done.6
  105.2 1.6 fusion.90
  108.9 2.2 %multiply_convert_fusion.4 = bf16[12,256,256]{1,2,0:T(8,128)(2,1)S(1)} fusion(f32[12,256,256]{2,1,0:T(8,128)S(1)} %copy-done.12, bf16[12,256,64]{1,2,0:T(8,128)(2,1)} %bitcast.312, f32[12,256]{1,0:T(8,128)S(1)} %multiply_reduce_fusion, f32[12,256]{1,0:T(8,128)S(1)} %get-tuple-element.35, pred[256,256]{0,1:T(8,128)(4,1)S(1)} %copy-done.36, ...), kind=kOutput, calls=%fused_computation.21 | convolution fusion | flops 105381888 | bytes 5595136 | tf_op jit(solution)/shard_map/hqe,hke->hqk/dot_general | solution.py:199
  111.8 1.3 pad_maximum_fusion.1
  113.2 1.3 multiply_convert_fusion.3
  115.2 1.4 pad_maximum_fusion
  117.0 1.1 multiply_convert_fusion.1
  120.4 1.6 fusion.96
  122.0 2.4 %fusion.114 = bf16[12,256,64]{1,2,0:T(8,128)(2,1)} fusion(f32[12,256,64]{1,2,0:T(8,128)S(1)} %fusion.157, f32[12,256,64]{1,2,0:T(8,128)S(1)} %fusion.122, f32[12,256,64]{1,2,0:T(8,128)S(1)} %fusion.125, f32[12,256,64]{1,2,0:T(8,128)S(1)} %fusion.120, bf16[12,256,256]{1,2,0:T(8,128)(2,1)S(1)} %multiply_convert_fusion.4, ...), kind=kOutput, calls=%fused_computation.120 | convolution fusion | flops 101842944 | bytes 5505024 | tf_op jit(solution)/shard_map/hqk,hke->hqe/dot_general | solution.py:203
  124.4 1.2 bitcast_add_fusion.1
  127.4 4.5 %collective-permute-start.10 = (bf16[2,48,1536]{2,1,0:T(8,128)(2,1)}, bf16[2,48,1536]{2,1,0:T(8,128)(2,1)}, u32[]{:S(2)}, u32[]{:S(2)}) collective-permute-start(bf16[2,48,1536]{2,1,0:T(8,128)(2,1)} %fusion.127), channel_id=1, source_target_pairs={{0,8},{2,10},{4,12},{6,14},{8,0},{10,2},{12,4},{14,6},{16,24},{18,... | collective-permute-start | bytes 884744 | tf_op jit(solution)/shard_map/ppermute | solution.py:41
  131.9 1.5 fusion.94
  133.4 2.0 copy.140
  135.4 3.6 %fusion.12 = bf16[1,256,1536]{2,1,0:T(8,128)(2,1)} fusion(bf16[256,768]{0,1:T(8,128)(2,1)} %bitcast.304, bf16[768,1536]{1,0:T(8,128)(2,1)} %all-gather.2.cloned.1.call-done), kind=kOutput, calls=%fused_computation.33 | convolution fusion | flops 604372992 | bytes 3538944 | tf_op jit(solution)/shard_map/dot_general | solution.py:161
  140.6 6.6 %collective-permute-start.11 = (bf16[48,1536]{1,0:T(8,128)(2,1)S(1)}, bf16[48,1536]{1,0:T(8,128)(2,1)S(1)}, u32[]{:S(2)}, u32[]{:S(2)}) collective-permute-start(bf16[48,1536]{1,0:T(8,128)(2,1)S(1)} %fusion.129), channel_id=1, source_target_pairs={{0,16},{2,18},{4,20},{6,22},{8,24},{10,26},{12,28},{14,30},{16,0},... | collective-permute-start | bytes 442376 | tf_op jit(solution)/shard_map/ppermute | solution.py:41
  147.2 3.7 %fusion.41 = (bf16[2,12,256,64]{2,3,1,0:T(8,128)(2,1)}, bf16[2,12,256,64]{2,3,1,0:T(8,128)(2,1)}) fusion(f32[1,12,256,64]{2,3,1,0:T(8,128)} %fusion.84, f32[1,12,256,64]{2,3,1,0:T(8,128)S(1)} %copy-done.21, f32[2,12,256,64]{2,3,1,0:T(8,128)} %collective-permute-done.5, f32[2,12,256,64]{2,3,1,0:T(8,128)} %collective-permute-done.4, pred[]{:T(512)S(6)} %eq.96, ...), kind=kLoop, calls=%fused_computation.62 | loop fusion | flops 3145728 | bytes 7864321 | tf_op jit(solution)/shard_map/convert_element_type | solution.py:98
  150.9 1.3 collective-permute-start.7
  152.2 2.0 %collective-permute-start.6 = (bf16[2,12,256,64]{2,3,1,0:T(8,128)(2,1)}, bf16[2,12,256,64]{2,3,1,0:T(8,128)(2,1)}, u32[]{:S(2)}, u32[]{:S(2)}) collective-permute-start(bf16[2,12,256,64]{2,3,1,0:T(8,128)(2,1)} %get-tuple-element.37), channel_id=1, source_target_pairs={{4,0},{6,2},{8,4},{10,6},{12,8},{14,10},{16,12},{18,14},{20,16},{2... | collective-permute-start | bytes 2359304 | tf_op jit(solution)/shard_map/ppermute | solution.py:18
  154.8 1.6 collective-permute-start.12
  156.9 3.2 %collective-permute-done.12 = f32[768,48]{0,1:T(8,128)S(1)} collective-permute-done((f32[768,48]{0,1:T(8,128)S(1)}, f32[768,48]{0,1:T(8,128)S(1)}, u32[]{:S(2)}, u32[]{:S(2)}) %collective-permute-start.12) | collective-permute-done | bytes 147488 | tf_op jit(solution)/shard_map/ppermute | solution.py:41
  160.8 11.4 %collective-permute-done.7 = bf16[2,12,256,64]{2,3,1,0:T(8,128)(2,1)} collective-permute-done((bf16[2,12,256,64]{2,3,1,0:T(8,128)(2,1)}, bf16[2,12,256,64]{2,3,1,0:T(8,128)(2,1)}, u32[]{:S(2)}, u32[]{:S(2)}) %collective-permute-start.7) | collective-permute-done | bytes 786464 | tf_op jit(solution)/shard_map/ppermute | solution.py:18
  172.2 16.6 %collective-permute-done.6 = bf16[2,12,256,64]{2,3,1,0:T(8,128)(2,1)} collective-permute-done((bf16[2,12,256,64]{2,3,1,0:T(8,128)(2,1)}, bf16[2,12,256,64]{2,3,1,0:T(8,128)(2,1)}, u32[]{:S(2)}, u32[]{:S(2)}) %collective-permute-start.6) | collective-permute-done | bytes 786464 | tf_op jit(solution)/shard_map/ppermute | solution.py:18
  188.8 2.6 %fusion.40 = bf16[2,12,256,64]{2,3,1,0:T(8,128)(2,1)S(1)} fusion(f32[1,12,256,64]{2,3,1,0:T(8,128)} %fusion.78, f32[1,12,256,64]{2,3,1,0:T(8,128)S(1)} %fusion.98, bf16[2,12,256,64]{2,3,1,0:T(8,128)(2,1)} %collective-permute-done.7, bf16[2,12,256,64]{2,3,1,0:T(8,128)(2,1)} %collective-permute-done.6, f32[2,12,256,64]{2,3,1,0:T(8,128)} %collective-permute-done.4, ...), kind=kLoop, calls=%fused_computation.59 | loop fusion | flops 3145728 | bytes 5505025 | tf_op jit(solution)/shard_map/convert.1
  (144 shorter events, 26.4 us)
Async XLA Ops:
  7.2 71.1 %copy-start = (bf16[1,256,1536]{2,1,0:T(8,128)(2,1)S(1)}, bf16[1,256,1536]{2,1,0:T(8,128)(2,1)}, u32[]{:S(2)}) copy-start(bf16[1,256,1536]{2,1,0:T(8,128)(2,1)} %param.9) | copy-start | bytes 2359300
  7.2 10.3 %copy-start.41 = (bf16[48,768]{1,0:T(8,128)(2,1)S(1)}, bf16[48,768]{1,0:T(8,128)(2,1)}, u32[]{:S(2)}) copy-start(bf16[48,768]{1,0:T(8,128)(2,1)} %param.11) | copy-start | bytes 221188
  7.2 15.6 %copy-start.42 = (s32[1,8]{1,0:T(1,128)S(1)}, s32[1,8]{1,0:T(1,128)}, u32[]{:S(2)}) copy-start(s32[1,8]{1,0:T(1,128)} %param.10) | copy-start | bytes 100
  7.2 85.7 %all-gather.2.cloned.1.call-start = ((), (), s32[]{:S(2)}) async-start(), calls=%async_computation | async-start | bytes 2506752 | tf_op jit(solution)/shard_map/all_gather | solution.py:115
  10.6 23.0 %collective-permute-start.2 = (bf16[2,12,256,64]{2,3,1,0:T(8,128)(2,1)}, bf16[2,12,256,64]{2,3,1,0:T(8,128)(2,1)S(1)}, u32[]{:S(2)}, u32[]{:S(2)}) collective-permute-start(bf16[2,12,256,64]{2,3,1,0:T(8,128)(2,1)} %pad_maximum_fusion.2), channel_id=1, source_target_pairs={{0,8},{2,10},{4,12},{6,14},{8,16},{10,18},{12,20},{14,22},{16,24},... | collective-permute-start | bytes 2359304 | tf_op jit(solution)/shard_map/ppermute | solution.py:18
  14.1 43.3 %collective-permute-start = (bf16[2,12,256,64]{2,3,1,0:T(8,128)(2,1)}, bf16[2,12,256,64]{2,3,1,0:T(8,128)(2,1)S(1)}, u32[]{:S(2)}, u32[]{:S(2)}) collective-permute-start(bf16[2,12,256,64]{2,3,1,0:T(8,128)(2,1)} %pad_maximum_fusion.2), channel_id=1, source_target_pairs={{0,4},{2,6},{4,8},{6,10},{8,12},{10,14},{12,16},{14,18},{16,20},{1... | collective-permute-start | bytes 2359304 | tf_op jit(solution)/shard_map/ppermute | solution.py:18
  28.6 30.2 %copy-start.37 = (pred[256,256]{0,1:T(8,128)(4,1)}, pred[256,256]{0,1:T(8,128)(4,1)S(1)}, u32[]{:S(2)}) copy-start(pred[256,256]{0,1:T(8,128)(4,1)S(1)} %get-tuple-element.49) | copy-start | bytes 196612
  33.6 40.0 %copy-start.17 = (bf16[2,12,256,64]{2,3,1,0:T(8,128)(2,1)}, bf16[2,12,256,64]{2,3,1,0:T(8,128)(2,1)S(1)}, u32[]{:S(2)}) copy-start(bf16[2,12,256,64]{2,3,1,0:T(8,128)(2,1)S(1)} %collective-permute-done.2) | copy-start | bytes 2359300
  57.5 18.9 %copy-start.19 = (bf16[2,12,256,64]{2,3,1,0:T(8,128)(2,1)}, bf16[2,12,256,64]{2,3,1,0:T(8,128)(2,1)S(1)}, u32[]{:S(2)}) copy-start(bf16[2,12,256,64]{2,3,1,0:T(8,128)(2,1)S(1)} %collective-permute-done) | copy-start | bytes 2359300
  58.9 5.2 %collective-permute-start.3 = (bf16[2,12,256,64]{2,3,1,0:T(8,128)(2,1)}, bf16[2,12,256,64]{2,3,1,0:T(8,128)(2,1)}, u32[]{:S(2)}, u32[]{:S(2)}) collective-permute-start(bf16[2,12,256,64]{2,3,1,0:T(8,128)(2,1)} %get-tuple-element.42), channel_id=1, source_target_pairs={{0,2},{2,0},{4,6},{6,4},{8,10},{10,8},{12,14},{14,12},{16,18},{18,... | collective-permute-start | bytes 2359304 | tf_op jit(solution)/shard_map/ppermute | solution.py:23
  61.2 2.1 %copy-start.30 = (pred[256,256]{0,1:T(8,128)(4,1)S(1)}, pred[256,256]{0,1:T(8,128)(4,1)}, u32[]{:S(2)}) copy-start(pred[256,256]{0,1:T(8,128)(4,1)} %get-tuple-element.46) | copy-start | bytes 196612
  61.2 5.0 %collective-permute-start.1 = (bf16[2,12,256,64]{2,3,1,0:T(8,128)(2,1)}, bf16[2,12,256,64]{2,3,1,0:T(8,128)(2,1)S(1)}, u32[]{:S(2)}, u32[]{:S(2)}) collective-permute-start(bf16[2,12,256,64]{2,3,1,0:T(8,128)(2,1)} %get-tuple-element.41), channel_id=1, source_target_pairs={{0,2},{2,0},{4,6},{6,4},{8,10},{10,8},{12,14},{14,12},{16,18},{18,... | collective-permute-start | bytes 2359304 | tf_op jit(solution)/shard_map/ppermute | solution.py:23
  61.7 2.3 %copy-start.35 = (pred[256,256]{0,1:T(8,128)(4,1)S(1)}, pred[256,256]{0,1:T(8,128)(4,1)}, u32[]{:S(2)}) copy-start(pred[256,256]{0,1:T(8,128)(4,1)} %get-tuple-element.47) | copy-start | bytes 196612
  63.3 10.3 %copy-start.5 = (f32[12,256,256]{2,1,0:T(8,128)}, f32[12,256,256]{2,1,0:T(8,128)S(1)}, u32[]{:S(2)}) copy-start(f32[12,256,256]{2,1,0:T(8,128)S(1)} %get-tuple-element.51) | copy-start | bytes 9437188
  63.3 2.9 %copy-start.33 = (pred[256,256]{0,1:T(8,128)(4,1)S(1)}, pred[256,256]{0,1:T(8,128)(4,1)}, u32[]{:S(2)}) copy-start(pred[256,256]{0,1:T(8,128)(4,1)} %get-tuple-element.45) | copy-start | bytes 196612
  64.0 12.3 %copy-start.7 = (f32[12,256,256]{2,1,0:T(8,128)}, f32[12,256,256]{2,1,0:T(8,128)S(1)}, u32[]{:S(2)}) copy-start(f32[12,256,256]{2,1,0:T(8,128)S(1)} %get-tuple-element.55) | copy-start | bytes 9437188
  64.0 4.6 %copy-start.3 = (f32[12,256,256]{1,2,0:T(8,128)S(1)}, f32[12,256,256]{1,2,0:T(8,128)}, u32[]{:S(2)}) copy-start(f32[12,256,256]{1,2,0:T(8,128)} %get-tuple-element.57) | copy-start | bytes 9437188
  64.0 4.6 %copy-start.38 = (pred[256,256]{0,1:T(8,128)(4,1)S(1)}, pred[256,256]{0,1:T(8,128)(4,1)}, u32[]{:S(2)}) copy-start(pred[256,256]{0,1:T(8,128)(4,1)} %copy-done.37) | copy-start | bytes 196612
  66.2 8.3 %copy-start.11 = (f32[12,256,256]{2,1,0:T(8,128)}, f32[12,256,256]{2,1,0:T(8,128)S(1)}, u32[]{:S(2)}) copy-start(f32[12,256,256]{2,1,0:T(8,128)S(1)} %get-tuple-element.53) | copy-start | bytes 9437188
  66.2 11.0 %copy-start.26 = (bf16[2,12,256,64]{2,3,1,0:T(8,128)(2,1)}, bf16[2,12,256,64]{2,3,1,0:T(8,128)(2,1)S(1)}, u32[]{:S(2)}) copy-start(bf16[2,12,256,64]{2,3,1,0:T(8,128)(2,1)S(1)} %collective-permute-done.1) | copy-start | bytes 2359300
  66.9 10.3 %copy-start.9 = (f32[12,256,256]{2,1,0:T(8,128)}, f32[12,256,256]{2,1,0:T(8,128)S(1)}, u32[]{:S(2)}) copy-start(f32[12,256,256]{2,1,0:T(8,128)S(1)} %get-tuple-element.59) | copy-start | bytes 9437188
  66.9 2.5 %copy-start.28 = (pred[256,256]{0,1:T(8,128)(4,1)S(1)}, pred[256,256]{0,1:T(8,128)(4,1)}, u32[]{:S(2)}) copy-start(pred[256,256]{0,1:T(8,128)(4,1)} %get-tuple-element.48) | copy-start | bytes 196612
  78.2 4.7 %copy-start.23 = (bf16[256,12,64]{0,2,1:T(8,128)(2,1)}, bf16[256,12,64]{0,2,1:T(8,128)(2,1)S(1)}, u32[]{:S(2)}) copy-start(bf16[256,12,64]{0,2,1:T(8,128)(2,1)S(1)} %get-tuple-element.60) | copy-start | bytes 1179652
  79.0 2.1 %copy-start.2 = (f32[2,2,2,2,48,1536]{5,4,3,2,1,0:T(8,128)}, f32[2,2,2,2,48,1536]{5,4,3,2,1,0:T(8,128)S(1)}, u32[]{:S(2)}) copy-start(f32[2,2,2,2,48,1536]{5,4,3,2,1,0:T(8,128)S(1)} %fusion.115) | copy-start | bytes 14155780
  82.9 4.9 %collective-permute-start.8 = (f32[2,2,2,48,1536]{4,3,2,1,0:T(8,128)}, f32[2,2,2,48,1536]{4,3,2,1,0:T(8,128)}, u32[]{:S(2)}, u32[]{:S(2)}) collective-permute-start(f32[2,2,2,48,1536]{4,3,2,1,0:T(8,128)} %dynamic-slice_bitcast_fusion), channel_id=1, source_target_pairs={{0,2},{2,0},{4,6},{6,4},{8,10},{10,8},{12,14},{14,12},{16,18},{18,... | collective-permute-start | bytes 7077896 | tf_op jit(solution)/shard_map/ppermute | solution.py:41
  92.0 3.6 %copy-start.39 = (pred[256,256]{0,1:T(8,128)(4,1)S(1)}, pred[256,256]{0,1:T(8,128)(4,1)}, u32[]{:S(2)}) copy-start(pred[256,256]{0,1:T(8,128)(4,1)} %copy-done.37) | copy-start | bytes 196612
  92.9 31.5 %collective-permute-start.9 = (bf16[2,2,48,1536]{3,2,1,0:T(8,128)(2,1)}, bf16[2,2,48,1536]{3,2,1,0:T(8,128)(2,1)}, u32[]{:S(2)}, u32[]{:S(2)}) collective-permute-start(bf16[2,2,48,1536]{3,2,1,0:T(8,128)(2,1)} %fusion.119), channel_id=1, source_target_pairs={{0,4},{2,6},{4,0},{6,2},{8,12},{10,14},{12,8},{14,10},{16,20},{18,... | collective-permute-start | bytes 1769480 | tf_op jit(solution)/shard_map/ppermute | solution.py:41
  95.4 3.9 %copy-start.31 = (pred[256,256]{0,1:T(8,128)(4,1)S(1)}, pred[256,256]{0,1:T(8,128)(4,1)}, u32[]{:S(2)}) copy-start(pred[256,256]{0,1:T(8,128)(4,1)} %get-tuple-element.46) | copy-start | bytes 196612
  95.5 11.4 %copy-start.24 = (bf16[256,768]{0,1:T(8,128)(2,1)}, bf16[256,768]{0,1:T(8,128)(2,1)S(1)}, u32[]{:S(2)}) copy-start(bf16[256,768]{0,1:T(8,128)(2,1)S(1)} %copy.119) | copy-start | bytes 1179652
  95.6 3.7 %copy-start.8 = (f32[12,256,256]{2,1,0:T(8,128)S(1)}, f32[12,256,256]{2,1,0:T(8,128)}, u32[]{:S(2)}) copy-start(f32[12,256,256]{2,1,0:T(8,128)} %copy-done.7) | copy-start | bytes 9437188
  99.2 2.2 %copy-start.12 = (f32[12,256,256]{2,1,0:T(8,128)S(1)}, f32[12,256,256]{2,1,0:T(8,128)}, u32[]{:S(2)}) copy-start(f32[12,256,256]{2,1,0:T(8,128)} %copy-done.11) | copy-start | bytes 9437188
  99.2 2.2 %copy-start.36 = (pred[256,256]{0,1:T(8,128)(4,1)S(1)}, pred[256,256]{0,1:T(8,128)(4,1)}, u32[]{:S(2)}) copy-start(pred[256,256]{0,1:T(8,128)(4,1)} %get-tuple-element.47) | copy-start | bytes 196612
  105.2 2.2 %copy-start.4 = (f32[12,256,256]{1,2,0:T(8,128)S(1)}, f32[12,256,256]{1,2,0:T(8,128)}, u32[]{:S(2)}) copy-start(f32[12,256,256]{1,2,0:T(8,128)} %get-tuple-element.57) | copy-start | bytes 9437188
  105.2 2.2 %copy-start.40 = (pred[256,256]{0,1:T(8,128)(4,1)S(1)}, pred[256,256]{0,1:T(8,128)(4,1)}, u32[]{:S(2)}) copy-start(pred[256,256]{0,1:T(8,128)(4,1)} %copy-done.37) | copy-start | bytes 196612
  113.1 34.1 %collective-permute-start.5 = (f32[2,12,256,64]{2,3,1,0:T(8,128)}, f32[2,12,256,64]{2,3,1,0:T(8,128)}, u32[]{:S(2)}, u32[]{:S(2)}) collective-permute-start(f32[2,12,256,64]{2,3,1,0:T(8,128)} %pad_maximum_fusion.1), channel_id=1, source_target_pairs={{0,2},{2,0},{4,6},{6,4},{8,10},{10,8},{12,14},{14,12},{16,18},{18,... | collective-permute-start | bytes 4718600 | tf_op jit(solution)/shard_map/ppermute | solution.py:23
  114.5 2.4 %copy-start.20 = (bf16[2,12,256,64]{2,3,1,0:T(8,128)(2,1)S(1)}, bf16[2,12,256,64]{2,3,1,0:T(8,128)(2,1)}, u32[]{:S(2)}) copy-start(bf16[2,12,256,64]{2,3,1,0:T(8,128)(2,1)} %copy-done.19) | copy-start | bytes 2359300
  114.6 2.4 %copy-start.32 = (pred[256,256]{0,1:T(8,128)(4,1)S(1)}, pred[256,256]{0,1:T(8,128)(4,1)}, u32[]{:S(2)}) copy-start(pred[256,256]{0,1:T(8,128)(4,1)} %get-tuple-element.46) | copy-start | bytes 196612
  116.6 30.6 %collective-permute-start.4 = (f32[2,12,256,64]{2,3,1,0:T(8,128)}, f32[2,12,256,64]{2,3,1,0:T(8,128)}, u32[]{:S(2)}, u32[]{:S(2)}) collective-permute-start(f32[2,12,256,64]{2,3,1,0:T(8,128)} %pad_maximum_fusion), channel_id=1, source_target_pairs={{0,2},{2,0},{4,6},{6,4},{8,10},{10,8},{12,14},{14,12},{16,18},{18,... | collective-permute-start | bytes 4718600 | tf_op jit(solution)/shard_map/ppermute | solution.py:23
  122.0 2.4 %copy-start.14 = (f32[2,2,2,48,1536]{4,3,2,1,0:T(8,128)S(1)}, f32[2,2,2,48,1536]{4,3,2,1,0:T(8,128)}, u32[]{:S(2)}) copy-start(f32[2,2,2,48,1536]{4,3,2,1,0:T(8,128)} %copy-done.13) | copy-start | bytes 7077892
  127.4 12.1 %collective-permute-start.10 = (bf16[2,48,1536]{2,1,0:T(8,128)(2,1)}, bf16[2,48,1536]{2,1,0:T(8,128)(2,1)}, u32[]{:S(2)}, u32[]{:S(2)}) collective-permute-start(bf16[2,48,1536]{2,1,0:T(8,128)(2,1)} %fusion.127), channel_id=1, source_target_pairs={{0,8},{2,10},{4,12},{6,14},{8,0},{10,2},{12,4},{14,6},{16,24},{18,... | collective-permute-start | bytes 884744 | tf_op jit(solution)/shard_map/ppermute | solution.py:41
  133.4 13.7 %copy-start.21 = (f32[1,12,256,64]{2,3,1,0:T(8,128)S(1)}, f32[1,12,256,64]{2,3,1,0:T(8,128)}, u32[]{:S(2)}) copy-start(f32[1,12,256,64]{2,3,1,0:T(8,128)} %fusion.96) | copy-start | bytes 2359300
  135.4 4.1 %copy-start.16 = (f32[2,2,48,1536]{3,2,1,0:T(8,128)S(1)}, f32[2,2,48,1536]{3,2,1,0:T(8,128)}, u32[]{:S(2)}) copy-start(f32[2,2,48,1536]{3,2,1,0:T(8,128)} %copy-done.15) | copy-start | bytes 3538948
  135.4 11.7 %copy-start.22 = (f32[1,12,256,64]{2,3,1,0:T(8,128)S(1)}, f32[1,12,256,64]{2,3,1,0:T(8,128)}, u32[]{:S(2)}) copy-start(f32[1,12,256,64]{2,3,1,0:T(8,128)} %fusion.94) | copy-start | bytes 2359300
  140.6 13.7 %collective-permute-start.11 = (bf16[48,1536]{1,0:T(8,128)(2,1)S(1)}, bf16[48,1536]{1,0:T(8,128)(2,1)S(1)}, u32[]{:S(2)}, u32[]{:S(2)}) collective-permute-start(bf16[48,1536]{1,0:T(8,128)(2,1)S(1)} %fusion.129), channel_id=1, source_target_pairs={{0,16},{2,18},{4,20},{6,22},{8,24},{10,26},{12,28},{14,30},{16,0},... | collective-permute-start | bytes 442376 | tf_op jit(solution)/shard_map/ppermute | solution.py:41
  150.9 21.3 %collective-permute-start.7 = (bf16[2,12,256,64]{2,3,1,0:T(8,128)(2,1)}, bf16[2,12,256,64]{2,3,1,0:T(8,128)(2,1)}, u32[]{:S(2)}, u32[]{:S(2)}) collective-permute-start(bf16[2,12,256,64]{2,3,1,0:T(8,128)(2,1)} %get-tuple-element.38), channel_id=1, source_target_pairs={{8,0},{10,2},{12,4},{14,6},{16,8},{18,10},{20,12},{22,14},{24,16},... | collective-permute-start | bytes 2359304 | tf_op jit(solution)/shard_map/ppermute | solution.py:18
  152.2 36.6 %collective-permute-start.6 = (bf16[2,12,256,64]{2,3,1,0:T(8,128)(2,1)}, bf16[2,12,256,64]{2,3,1,0:T(8,128)(2,1)}, u32[]{:S(2)}, u32[]{:S(2)}) collective-permute-start(bf16[2,12,256,64]{2,3,1,0:T(8,128)(2,1)} %get-tuple-element.37), channel_id=1, source_target_pairs={{4,0},{6,2},{8,4},{10,6},{12,8},{14,10},{16,12},{18,14},{20,16},{2... | collective-permute-start | bytes 2359304 | tf_op jit(solution)/shard_map/ppermute | solution.py:18
  154.8 5.4 %collective-permute-start.12 = (f32[768,48]{0,1:T(8,128)S(1)}, f32[768,48]{0,1:T(8,128)S(1)}, u32[]{:S(2)}, u32[]{:S(2)}) collective-permute-start(f32[768,48]{0,1:T(8,128)S(1)} %bitcast.319), channel_id=1, source_target_pairs={{0,1},{1,0},{2,3},{3,2},{4,5},{5,4},{6,7},{7,6},{8,9},{9,8},{10,11... | collective-permute-start | bytes 442376 | tf_op jit(solution)/shard_map/ppermute | solution.py:41
  160.1 33.2 %copy-start.1 = (bf16[1,256,1536]{2,1,0:T(8,128)(2,1)S(1)}, bf16[1,256,1536]{2,1,0:T(8,128)(2,1)}, u32[]{:S(2)}) copy-start(bf16[1,256,1536]{2,1,0:T(8,128)(2,1)} %param.9) | copy-start | bytes 2359300
  (9 other events, 15.7 us)
Sparse Core Ops, SparseCore 0:
  22.8 43.1 all-gather.1

commit v4 on v3

--- a/solution.py
+++ b/solution.py
@@ -169,11 +169,10 @@
     partial_weight = lax.dot_general(
         attended, upstream, (((0,), (0,)), ((), ())), preferred_element_type=jnp.float32
     )
-    seq_bits = max(seq_count.bit_length() - 1, 1)
-    row_share = halving_scatter(
-        partial_weight, "seq", 0, [step > 0 for step in range(seq_bits)]
-    )
-    weight_grad = halving_scatter(row_share, "dp", 1, [False] * 8)
+    col_share = halving_scatter(partial_weight, "dp", 1, [False] * 8)
+    weight_grad = lax.psum_scatter(
+        col_share.astype(jnp.bfloat16), "seq", scatter_dimension=0, tiled=True
+    ).astype(jnp.float32)
 
     grad_heads = head_major(att_grad, tok_rows)
     delta_rows = jnp.sum(

time: 201 us -> 247 us (1.23); the launches traced: 200 us -> 243 us
  waiting for transfers between devices: 65.4 us -> 118 us
  starting transfers between devices: 23.9 us -> 13.1 us
  local copies, waits for them, and re-layouts: 21.2 us -> 27.8 us
  other arithmetic: 26.1 us -> 22.5 us
    ppermute x5 -> x1, waiting for transfers between devices: 8.57 us -> 51.6 us  [halving_scatter(): got = lax.ppermute(give, axis, [(i, i ^ 1 << step) for i in range(count)])]
    reduce_scatter x0 -> x1, waiting for transfers between devices: none -> 26.6 us  [local(): lax.psum_scatter(col_share.astype(jnp.bfloat16), 'seq', scatter_dimension...]
    ppermute x4, waiting for transfers between devices: 56.8 us -> 39.5 us  [shift_up(): return lax.ppermute(block, axis, route)]
    ppermute x5 -> x1, starting transfers between devices: 12.6 us -> 1.55 us  [halving_scatter(): got = lax.ppermute(give, axis, [(i, i ^ 1 << step) for i in range(count)])]
    dynamic_slice x1, local copies, waits for them, and re-layouts: 0.26 us -> 8.63 us  [halving_scatter(): lax.dynamic_index_in_dim(blocks, own_bit, blocks.ndim - len(rest) - 2, ke...]
    reshape x1, local copies, waits for them, and re-layouts: 0.19 us -> 6.63 us  [halving_scatter(): blocks = moved.reshape((2,) * bits + (moved.shape[0] // count,) + rest)]
    add x3 -> x0, other arithmetic: 4.98 us -> none  [halving_scatter(): blocks = keep + got.astype(keep.dtype)]
    unnamed x93 -> x101, local copies, waits for them, and re-layouts: 17.2 us -> 12.3 us
  transfers between devices with their start and end apart: 14 -> 11, of which waited for: 7 -> 5; matrix products, arithmetic and copies ran while one was open for 37% -> 32% of each run, Pallas kernels for 0% -> 0%
where the time goes in v4:
time: 247 us; the launch traced here: 243 us
  waiting for transfers between devices  118 us (48%)
  matrix products  42 us (17%)
  local copies, waits for them, and re-layouts  27.8 us (11%)
  other arithmetic  22.5 us (9%)
  between operations  14.8 us (6%)
  starting transfers between devices  13.1 us (5%)
  blocking collectives  5.14 us (2%)
    ppermute x1, waiting for transfers between devices, halving_scatter(): got = lax.ppermute(give, axis, [(i, i ^ 1 << step) for i in range(count)])  51.6 us
    ppermute x4, waiting for transfers between devices, shift_up(): return lax.ppermute(block, axis, route)  39.5 us
    reduce_scatter x1, waiting for transfers between devices, local(): lax.psum_scatter(col_share.astype(jnp.bfloat16), 'seq', scatter_dimension...  26.6 us
    unnamed x101, local copies, waits for them, and re-layouts  12.3 us
    ppermute x4, starting transfers between devices, shift_up(): return lax.ppermute(block, axis, route)  10.5 us
    dynamic_slice x1, local copies, waits for them, and re-layouts, halving_scatter(): lax.dynamic_index_in_dim(blocks, own_bit, blocks.ndim - len(rest) - 2, ke...  8.63 us
    dot_general x5, matrix products, local(): jnp.einsum('hqe,hke->hqk', query_heads, held[dist][0], preferred_element_...  7.34 us
    dot_general x5, matrix products, local(): jnp.einsum('hqk,hqe->hke', score_grad, query_heads, preferred_element_typ...  6.89 us
  transfers between devices with their start and end apart: 11, of which 5 were waited for; matrix products, arithmetic and copies ran while one was open for 32% of the time, Pallas kernels for 0%

profile of v4, /device:TPU:4, one launch (start us, length us, event | category | flops | bytes accessed | tf_op | source)
XLA Modules:
  0.0 243.1 jit_solution(13316027785868684042)
XLA Ops:
  7.2 1.2 copy.80
  8.5 1.2 copy.78
  9.7 0.9 pad_maximum_fusion.2
  10.6 3.5 %collective-permute-start.2 = (bf16[2,12,256,64]{2,3,1,0:T(8,128)(2,1)}, bf16[2,12,256,64]{2,3,1,0:T(8,128)(2,1)S(1)}, u32[]{:S(2)}, u32[]{:S(2)}) collective-permute-start(bf16[2,12,256,64]{2,3,1,0:T(8,128)(2,1)} %pad_maximum_fusion.2), channel_id=1, source_target_pairs={{0,8},{2,10},{4,12},{6,14},{8,16},{10,18},{12,20},{14,22},{16,24},... | collective-permute-start | bytes 2359304 | tf_op jit(solution)/shard_map/ppermute | solution.py:18
  14.1 3.4 %collective-permute-start = (bf16[2,12,256,64]{2,3,1,0:T(8,128)(2,1)}, bf16[2,12,256,64]{2,3,1,0:T(8,128)(2,1)S(1)}, u32[]{:S(2)}, u32[]{:S(2)}) collective-permute-start(bf16[2,12,256,64]{2,3,1,0:T(8,128)(2,1)} %pad_maximum_fusion.2), channel_id=1, source_target_pairs={{0,4},{2,6},{4,8},{6,10},{8,12},{10,14},{12,16},{14,18},{16,20},{1... | collective-permute-start | bytes 2359304 | tf_op jit(solution)/shard_map/ppermute | solution.py:18
  17.5 5.1 %all_gather.6 = bf16[48,1536]{1,0:T(8,128)(2,1)} all-gather(bf16[48,768]{1,0:T(8,128)(2,1)S(1)} %copy-done.45), channel_id=1, replica_groups=mesh['seq'=16,'dp'=2] {'dp'}, dimensions={1}, use_global_device_ids=true | all-gather | bytes 221184 | tf_op jit(solution)/shard_map/all_gather | solution.py:114
  24.3 1.2 copy.77
  26.8 1.9 compare_and_fusion.3
  28.7 4.9 %collective-permute-done.2 = bf16[2,12,256,64]{2,3,1,0:T(8,128)(2,1)S(1)} collective-permute-done((bf16[2,12,256,64]{2,3,1,0:T(8,128)(2,1)}, bf16[2,12,256,64]{2,3,1,0:T(8,128)(2,1)S(1)}, u32[]{:S(2)}, u32[]{:S(2)}) %collective-permute-start.2) | collective-permute-done | bytes 786464 | tf_op jit(solution)/shard_map/ppermute | solution.py:18
  33.6 23.9 %collective-permute-done = bf16[2,12,256,64]{2,3,1,0:T(8,128)(2,1)S(1)} collective-permute-done((bf16[2,12,256,64]{2,3,1,0:T(8,128)(2,1)}, bf16[2,12,256,64]{2,3,1,0:T(8,128)(2,1)S(1)}, u32[]{:S(2)}, u32[]{:S(2)}) %collective-permute-start) | collective-permute-done | bytes 786464 | tf_op jit(solution)/shard_map/ppermute | solution.py:18
  57.4 1.4 broadcast_select_fusion.1
  58.8 2.3 select_reduce_fusion
  61.7 1.6 fusion.11
  64.0 2.1 fusion.10
  66.9 1.7 copy-done.2
  69.5 3.9 %fusion.21 = (f32[12,256]{1,0:T(8,128)S(1)}, f32[12,256]{1,0:T(8,128)S(1)}, f32[12,256]{1,0:T(8,128)S(1)}, f32[12,256]{1,0:T(8,128)S(1)}, f32[12,256]{1,0:T(8,128)S(1)}) fusion(f32[12,256,256]{2,1,0:T(8,128)S(1)} %get-tuple-element.54, f32[12,256]{1,0:T(8,128)S(1)} %maximum_maximum_fusion, pred[256,256]{0,1:T(8,128)(4,1)S(1)} %copy-done.39, ...), kind=kLoop, calls=%fused_computation.45 | loop fusion | flops 19645440 | bytes 16130048 | tf_op jit(solution)/shard_map/reduce_sum | solution.py:148
  74.3 1.9 fusion.61
  78.8 2.9 %convolution_bitcast_fusion = f32[1536,768]{0,1:T(8,128)} fusion(bf16[256,768]{0,1:T(8,128)(2,1)S(1)} %bitcast.279, bf16[1,256,1536]{2,1,0:T(8,128)(2,1)S(1)} %copy-done), kind=kOutput, calls=%fused_computation | convolution fusion | flops 603979776 | bytes 5898240 | tf_op jit(solution)/shard_map/dot_general | solution.py:169
  81.7 6.6 %reshape.585 = f32[2,768,768]{1,0,2:T(2,128)} reshape(f32[1536,768]{0,1:T(8,128)} %convolution_bitcast_fusion) | data formatting | bytes 9437184 | tf_op jit(solution)/shard_map/reshape | solution.py:34
  88.3 8.6 %constant_dynamic-slice_fusion.1 = (f32[1,768,768]{1,0,2:T(1,128)S(1)}, f32[1,768,768]{1,0,2:T(1,128)S(1)}) fusion(f32[2,768,768]{1,0,2:T(2,128)} %reshape.585, s32[]{:T(128)S(6)} %select_n.206, s32[]{:T(128)S(6)} %select_n.207), kind=kLoop, calls=%fused_computation.193 | loop fusion | bytes 9437192 | tf_op jit(solution)/shard_map/jit(dynamic_index_in_dim)/dynamic_slice | solution.py:37
  97.1 1.6 collective-permute-start.8
  98.6 51.6 %collective-permute-done.8 = f32[768,768]{0,1:T(8,128)S(1)} collective-permute-done((f32[768,768]{0,1:T(8,128)S(1)}, f32[768,768]{0,1:T(8,128)S(1)}, u32[]{:S(2)}, u32[]{:S(2)}) %collective-permute-start.8) | collective-permute-done | bytes 2359328 | tf_op jit(solution)/shard_map/ppermute | solution.py:41
  150.3 1.2 fusion.116
  151.6 2.5 %convolution_convert_fusion.1 = bf16[256,768]{1,0:T(8,128)(2,1)S(1)} fusion(bf16[768,1536]{1,0:T(8,128)(2,1)} %all-gather.2.cloned.1.call-done, bf16[1,256,1536]{2,1,0:T(8,128)(2,1)S(1)} %copy-done), kind=kOutput, calls=%fused_computation.123 | convolution fusion | flops 604176384 | bytes 3538944 | tf_op jit(solution)/shard_map/dot_general | solution.py:165
  154.3 2.8 %fusion.88 = f32[1,12,256,64]{2,3,1,0:T(8,128)S(1)} fusion(bf16[12,256,64]{1,2,0:T(8,128)(2,1)S(1)} %bitcast.282, f32[12,256,256]{2,1,0:T(8,128)} %copy-done.13, f32[12,256]{1,0:T(8,128)S(1)} %get-tuple-element.30, pred[256,256]{0,1:T(8,128)(4,1)S(1)} %copy-done.43), kind=kOutput, calls=%fused_computation.101 | convolution fusion | flops 103809024 | bytes 4403200 | tf_op jit(solution)/shard_map/hqk,hqe->hke/dot_general | solution.py:210
  158.1 1.0 copy-done.3
  159.1 1.1 multiply_convert_fusion
  161.0 2.1 multiply_convert_fusion.4
  163.8 1.3 pad_maximum_fusion.1
  165.1 1.1 multiply_convert_fusion.3
  166.9 1.4 pad_maximum_fusion
  168.9 1.3 multiply_convert_fusion.1
  170.5 1.1 multiply_convert_fusion.2
  172.8 1.5 fusion.115
  174.3 0.9 copy.107
  175.2 2.2 fusion.97
  177.4 2.0 fusion.95
  180.2 1.2 copy-done.7
  182.1 3.4 %fusion.42 = (bf16[2,12,256,64]{2,3,1,0:T(8,128)(2,1)}, bf16[2,12,256,64]{2,3,1,0:T(8,128)(2,1)}) fusion(f32[1,12,256,64]{2,3,1,0:T(8,128)S(1)} %fusion.85, f32[1,12,256,64]{2,3,1,0:T(8,128)S(1)} %fusion.97, f32[2,12,256,64]{2,3,1,0:T(8,128)} %collective-permute-done.5, f32[2,12,256,64]{2,3,1,0:T(8,128)} %collective-permute-done.4, pred[]{:T(512)S(6)} %eq.92, ...), kind=kLoop, calls=%fused_computation.64 | loop fusion | flops 3145728 | bytes 7864321 | tf_op jit(solution)/shard_map/convert_element_type | solution.py:98
  185.5 1.4 collective-permute-start.7
  186.9 2.2 collective-permute-start.6
  189.1 1.5 fusion.99
  190.6 1.7 fusion.12
  193.0 26.6 %reduce-scatter.2.cloned.1.call-done = bf16[48,768]{1,0:T(8,128)(2,1)} async-done(((bf16[768,768]{1,0:T(8,128)(2,1)}), bf16[48,768]{1,0:T(8,128)(2,1)}) %reduce-scatter.2.cloned.1.call-update) | async-done | bytes 73744 | tf_op jit(solution)/shard_map/reduce_scatter | solution.py:173
  219.6 1.6 convert_element_type.187
  221.2 10.8 %collective-permute-done.6 = bf16[2,12,256,64]{2,3,1,0:T(8,128)(2,1)} collective-permute-done((bf16[2,12,256,64]{2,3,1,0:T(8,128)(2,1)}, bf16[2,12,256,64]{2,3,1,0:T(8,128)(2,1)}, u32[]{:S(2)}, u32[]{:S(2)}) %collective-permute-start.6) | collective-permute-done | bytes 786464 | tf_op jit(solution)/shard_map/ppermute | solution.py:18
  232.0 2.4 fusion.41
  234.5 0.9 copy.108
  (140 shorter events, 17.8 us)
Async XLA Ops:
  7.2 71.6 %copy-start = (bf16[1,256,1536]{2,1,0:T(8,128)(2,1)S(1)}, bf16[1,256,1536]{2,1,0:T(8,128)(2,1)}, u32[]{:S(2)}) copy-start(bf16[1,256,1536]{2,1,0:T(8,128)(2,1)} %param.9) | copy-start | bytes 2359300
  7.2 10.3 %copy-start.45 = (bf16[48,768]{1,0:T(8,128)(2,1)S(1)}, bf16[48,768]{1,0:T(8,128)(2,1)}, u32[]{:S(2)}) copy-start(bf16[48,768]{1,0:T(8,128)(2,1)} %param.11) | copy-start | bytes 221188
  7.2 15.6 %copy-start.46 = (s32[1,8]{1,0:T(1,128)S(1)}, s32[1,8]{1,0:T(1,128)}, u32[]{:S(2)}) copy-start(s32[1,8]{1,0:T(1,128)} %param.10) | copy-start | bytes 100
  7.2 144.4 %all-gather.2.cloned.1.call-start = ((), (), s32[]{:S(2)}) async-start(), calls=%async_computation.1 | async-start | bytes 2506752 | tf_op jit(solution)/shard_map/all_gather | solution.py:115
  10.6 23.0 %collective-permute-start.2 = (bf16[2,12,256,64]{2,3,1,0:T(8,128)(2,1)}, bf16[2,12,256,64]{2,3,1,0:T(8,128)(2,1)S(1)}, u32[]{:S(2)}, u32[]{:S(2)}) collective-permute-start(bf16[2,12,256,64]{2,3,1,0:T(8,128)(2,1)} %pad_maximum_fusion.2), channel_id=1, source_target_pairs={{0,8},{2,10},{4,12},{6,14},{8,16},{10,18},{12,20},{14,22},{16,24},... | collective-permute-start | bytes 2359304 | tf_op jit(solution)/shard_map/ppermute | solution.py:18
  14.1 43.3 %collective-permute-start = (bf16[2,12,256,64]{2,3,1,0:T(8,128)(2,1)}, bf16[2,12,256,64]{2,3,1,0:T(8,128)(2,1)S(1)}, u32[]{:S(2)}, u32[]{:S(2)}) collective-permute-start(bf16[2,12,256,64]{2,3,1,0:T(8,128)(2,1)} %pad_maximum_fusion.2), channel_id=1, source_target_pairs={{0,4},{2,6},{4,8},{6,10},{8,12},{10,14},{12,16},{14,18},{16,20},{1... | collective-permute-start | bytes 2359304 | tf_op jit(solution)/shard_map/ppermute | solution.py:18
  22.7 196.9 %reduce-scatter.2.cloned.1.call-start = ((), (), s32[]{:S(2)}) async-start(), calls=%async_computation.2 | async-start | bytes 1253376 | tf_op jit(solution)/shard_map/reduce_scatter | solution.py:173
  28.7 30.1 %copy-start.29 = (pred[256,256]{0,1:T(8,128)(4,1)}, pred[256,256]{0,1:T(8,128)(4,1)S(1)}, u32[]{:S(2)}) copy-start(pred[256,256]{0,1:T(8,128)(4,1)S(1)} %get-tuple-element.44) | copy-start | bytes 196612
  33.6 39.9 %copy-start.18 = (bf16[2,12,256,64]{2,3,1,0:T(8,128)(2,1)}, bf16[2,12,256,64]{2,3,1,0:T(8,128)(2,1)S(1)}, u32[]{:S(2)}) copy-start(bf16[2,12,256,64]{2,3,1,0:T(8,128)(2,1)S(1)} %collective-permute-done.2) | copy-start | bytes 2359300
  57.4 18.7 %copy-start.20 = (bf16[2,12,256,64]{2,3,1,0:T(8,128)(2,1)}, bf16[2,12,256,64]{2,3,1,0:T(8,128)(2,1)S(1)}, u32[]{:S(2)}) copy-start(bf16[2,12,256,64]{2,3,1,0:T(8,128)(2,1)S(1)} %collective-permute-done) | copy-start | bytes 2359300
  58.8 5.1 %collective-permute-start.3 = (bf16[2,12,256,64]{2,3,1,0:T(8,128)(2,1)}, bf16[2,12,256,64]{2,3,1,0:T(8,128)(2,1)}, u32[]{:S(2)}, u32[]{:S(2)}) collective-permute-start(bf16[2,12,256,64]{2,3,1,0:T(8,128)(2,1)} %get-tuple-element.39), channel_id=1, source_target_pairs={{0,2},{2,0},{4,6},{6,4},{8,10},{10,8},{12,14},{14,12},{16,18},{18,... | collective-permute-start | bytes 2359304 | tf_op jit(solution)/shard_map/ppermute | solution.py:23
  61.2 2.1 copy-start.36
  61.2 5.0 %collective-permute-start.1 = (bf16[2,12,256,64]{2,3,1,0:T(8,128)(2,1)}, bf16[2,12,256,64]{2,3,1,0:T(8,128)(2,1)S(1)}, u32[]{:S(2)}, u32[]{:S(2)}) collective-permute-start(bf16[2,12,256,64]{2,3,1,0:T(8,128)(2,1)} %get-tuple-element.38), channel_id=1, source_target_pairs={{0,2},{2,0},{4,6},{6,4},{8,10},{10,8},{12,14},{14,12},{16,18},{18,... | collective-permute-start | bytes 2359304 | tf_op jit(solution)/shard_map/ppermute | solution.py:23
  61.7 2.3 copy-start.42
  63.2 10.2 %copy-start.5 = (f32[12,256,256]{2,1,0:T(8,128)}, f32[12,256,256]{2,1,0:T(8,128)S(1)}, u32[]{:S(2)}) copy-start(f32[12,256,256]{2,1,0:T(8,128)S(1)} %get-tuple-element.46) | copy-start | bytes 9437188
  63.3 2.9 %copy-start.39 = (pred[256,256]{0,1:T(8,128)(4,1)S(1)}, pred[256,256]{0,1:T(8,128)(4,1)}, u32[]{:S(2)}) copy-start(pred[256,256]{0,1:T(8,128)(4,1)} %get-tuple-element.40) | copy-start | bytes 196612
  64.0 12.2 %copy-start.8 = (f32[12,256,256]{2,1,0:T(8,128)}, f32[12,256,256]{2,1,0:T(8,128)S(1)}, u32[]{:S(2)}) copy-start(f32[12,256,256]{2,1,0:T(8,128)S(1)} %get-tuple-element.50) | copy-start | bytes 9437188
  64.0 4.6 %copy-start.2 = (f32[12,256,256]{1,2,0:T(8,128)S(1)}, f32[12,256,256]{1,2,0:T(8,128)}, u32[]{:S(2)}) copy-start(f32[12,256,256]{1,2,0:T(8,128)} %get-tuple-element.52) | copy-start | bytes 9437188
  64.0 4.6 %copy-start.30 = (pred[256,256]{0,1:T(8,128)(4,1)S(1)}, pred[256,256]{0,1:T(8,128)(4,1)}, u32[]{:S(2)}) copy-start(pred[256,256]{0,1:T(8,128)(4,1)} %copy-done.29) | copy-start | bytes 196612
  66.1 8.2 %copy-start.13 = (f32[12,256,256]{2,1,0:T(8,128)}, f32[12,256,256]{2,1,0:T(8,128)S(1)}, u32[]{:S(2)}) copy-start(f32[12,256,256]{2,1,0:T(8,128)S(1)} %get-tuple-element.48) | copy-start | bytes 9437188
  66.2 10.9 %copy-start.27 = (bf16[2,12,256,64]{2,3,1,0:T(8,128)(2,1)}, bf16[2,12,256,64]{2,3,1,0:T(8,128)(2,1)S(1)}, u32[]{:S(2)}) copy-start(bf16[2,12,256,64]{2,3,1,0:T(8,128)(2,1)S(1)} %collective-permute-done.1) | copy-start | bytes 2359300
  66.9 10.2 %copy-start.11 = (f32[12,256,256]{2,1,0:T(8,128)}, f32[12,256,256]{2,1,0:T(8,128)S(1)}, u32[]{:S(2)}) copy-start(f32[12,256,256]{2,1,0:T(8,128)S(1)} %get-tuple-element.54) | copy-start | bytes 9437188
  66.9 2.6 %copy-start.33 = (pred[256,256]{0,1:T(8,128)(4,1)S(1)}, pred[256,256]{0,1:T(8,128)(4,1)}, u32[]{:S(2)}) copy-start(pred[256,256]{0,1:T(8,128)(4,1)} %get-tuple-element.43) | copy-start | bytes 196612
  97.1 53.2 %collective-permute-start.8 = (f32[768,768]{0,1:T(8,128)S(1)}, f32[768,768]{0,1:T(8,128)S(1)}, u32[]{:S(2)}, u32[]{:S(2)}) collective-permute-start(f32[768,768]{0,1:T(8,128)S(1)} %bitcast.281), channel_id=1, source_target_pairs={{0,1},{1,0},{2,3},{3,2},{4,5},{5,4},{6,7},{7,6},{8,9},{9,8},{10,11... | collective-permute-start | bytes 7077896 | tf_op jit(solution)/shard_map/ppermute | solution.py:41
  151.5 2.7 %copy-start.43 = (pred[256,256]{0,1:T(8,128)(4,1)S(1)}, pred[256,256]{0,1:T(8,128)(4,1)}, u32[]{:S(2)}) copy-start(pred[256,256]{0,1:T(8,128)(4,1)} %get-tuple-element.42) | copy-start | bytes 196612
  154.0 3.0 %copy-start.40 = (pred[256,256]{0,1:T(8,128)(4,1)S(1)}, pred[256,256]{0,1:T(8,128)(4,1)}, u32[]{:S(2)}) copy-start(pred[256,256]{0,1:T(8,128)(4,1)} %get-tuple-element.40) | copy-start | bytes 196612
  154.2 6.4 %copy-start.25 = (bf16[256,768]{0,1:T(8,128)(2,1)}, bf16[256,768]{0,1:T(8,128)(2,1)S(1)}, u32[]{:S(2)}) copy-start(bf16[256,768]{0,1:T(8,128)(2,1)S(1)} %copy.86) | copy-start | bytes 1179652
  154.2 3.0 %copy-start.12 = (f32[12,256,256]{2,1,0:T(8,128)S(1)}, f32[12,256,256]{2,1,0:T(8,128)}, u32[]{:S(2)}) copy-start(f32[12,256,256]{2,1,0:T(8,128)} %copy-done.11) | copy-start | bytes 9437188
  163.1 2.0 copy-start.26
  163.1 2.0 copy-start.28
  165.1 17.0 %collective-permute-start.5 = (f32[2,12,256,64]{2,3,1,0:T(8,128)}, f32[2,12,256,64]{2,3,1,0:T(8,128)}, u32[]{:S(2)}, u32[]{:S(2)}) collective-permute-start(f32[2,12,256,64]{2,3,1,0:T(8,128)} %pad_maximum_fusion.1), channel_id=1, source_target_pairs={{0,2},{2,0},{4,6},{6,4},{8,10},{10,8},{12,14},{14,12},{16,18},{18,... | collective-permute-start | bytes 4718600 | tf_op jit(solution)/shard_map/ppermute | solution.py:23
  166.2 2.5 %copy-start.9 = (f32[12,256,256]{2,1,0:T(8,128)S(1)}, f32[12,256,256]{2,1,0:T(8,128)}, u32[]{:S(2)}) copy-start(f32[12,256,256]{2,1,0:T(8,128)} %copy-done.8) | copy-start | bytes 9437188
  166.2 2.7 %copy-start.21 = (bf16[2,12,256,64]{2,3,1,0:T(8,128)(2,1)S(1)}, bf16[2,12,256,64]{2,3,1,0:T(8,128)(2,1)}, u32[]{:S(2)}) copy-start(bf16[2,12,256,64]{2,3,1,0:T(8,128)(2,1)} %copy-done.20) | copy-start | bytes 2359300
  166.3 2.7 %copy-start.37 = (pred[256,256]{0,1:T(8,128)(4,1)S(1)}, pred[256,256]{0,1:T(8,128)(4,1)}, u32[]{:S(2)}) copy-start(pred[256,256]{0,1:T(8,128)(4,1)} %get-tuple-element.41) | copy-start | bytes 196612
  168.3 2.1 copy-start.6
  168.3 2.2 copy-start.19
  168.3 2.2 copy-start.34
  168.3 13.8 %collective-permute-start.4 = (f32[2,12,256,64]{2,3,1,0:T(8,128)}, f32[2,12,256,64]{2,3,1,0:T(8,128)}, u32[]{:S(2)}, u32[]{:S(2)}) collective-permute-start(f32[2,12,256,64]{2,3,1,0:T(8,128)} %pad_maximum_fusion), channel_id=1, source_target_pairs={{0,2},{2,0},{4,6},{6,4},{8,10},{10,8},{12,14},{14,12},{16,18},{18,... | collective-permute-start | bytes 4718600 | tf_op jit(solution)/shard_map/ppermute | solution.py:23
  175.2 4.2 %copy-start.10 = (f32[12,256,256]{2,1,0:T(8,128)S(1)}, f32[12,256,256]{2,1,0:T(8,128)}, u32[]{:S(2)}) copy-start(f32[12,256,256]{2,1,0:T(8,128)} %copy-done.8) | copy-start | bytes 9437188
  175.2 4.2 %copy-start.38 = (pred[256,256]{0,1:T(8,128)(4,1)S(1)}, pred[256,256]{0,1:T(8,128)(4,1)}, u32[]{:S(2)}) copy-start(pred[256,256]{0,1:T(8,128)(4,1)} %get-tuple-element.41) | copy-start | bytes 196612
  182.1 8.5 %copy-start.23 = (bf16[256,12,64]{0,2,1:T(8,128)(2,1)S(1)}, bf16[256,12,64]{0,2,1:T(8,128)(2,1)}, u32[]{:S(2)}) copy-start(bf16[256,12,64]{0,2,1:T(8,128)(2,1)} %copy-done.22) | copy-start | bytes 1179652
  185.5 5.1 %copy-start.24 = (bf16[768,1536]{1,0:T(8,128)(2,1)S(1)}, bf16[768,1536]{1,0:T(8,128)(2,1)}, u32[]{:S(2)}) copy-start(bf16[768,1536]{1,0:T(8,128)(2,1)} %all-gather.2.cloned.1.call-done) | copy-start | bytes 7077892
  185.5 35.7 %collective-permute-start.7 = (bf16[2,12,256,64]{2,3,1,0:T(8,128)(2,1)}, bf16[2,12,256,64]{2,3,1,0:T(8,128)(2,1)}, u32[]{:S(2)}, u32[]{:S(2)}) collective-permute-start(bf16[2,12,256,64]{2,3,1,0:T(8,128)(2,1)} %get-tuple-element.35), channel_id=1, source_target_pairs={{8,0},{10,2},{12,4},{14,6},{16,8},{18,10},{20,12},{22,14},{24,16},... | collective-permute-start | bytes 2359304 | tf_op jit(solution)/shard_map/ppermute | solution.py:18
  186.9 5.4 %copy-start.4 = (f32[12,256,256]{1,2,0:T(8,128)S(1)}, f32[12,256,256]{1,2,0:T(8,128)}, u32[]{:S(2)}) copy-start(f32[12,256,256]{1,2,0:T(8,128)} %get-tuple-element.52) | copy-start | bytes 9437188
  186.9 5.4 %copy-start.32 = (pred[256,256]{0,1:T(8,128)(4,1)S(1)}, pred[256,256]{0,1:T(8,128)(4,1)}, u32[]{:S(2)}) copy-start(pred[256,256]{0,1:T(8,128)(4,1)} %copy-done.29) | copy-start | bytes 196612
  186.9 45.1 %collective-permute-start.6 = (bf16[2,12,256,64]{2,3,1,0:T(8,128)(2,1)}, bf16[2,12,256,64]{2,3,1,0:T(8,128)(2,1)}, u32[]{:S(2)}, u32[]{:S(2)}) collective-permute-start(bf16[2,12,256,64]{2,3,1,0:T(8,128)(2,1)} %get-tuple-element.34), channel_id=1, source_target_pairs={{4,0},{6,2},{8,4},{10,6},{12,8},{14,10},{16,12},{18,14},{20,16},{2... | collective-permute-start | bytes 2359304 | tf_op jit(solution)/shard_map/ppermute | solution.py:18
  192.3 39.7 %copy-start.17 = (f32[1,12,256,64]{2,3,1,0:T(8,128)S(1)}, f32[1,12,256,64]{2,3,1,0:T(8,128)}, u32[]{:S(2)}) copy-start(f32[1,12,256,64]{2,3,1,0:T(8,128)} %fusion.99) | copy-start | bytes 2359300
  219.6 16.7 %copy-start.1 = (bf16[1,256,1536]{2,1,0:T(8,128)(2,1)S(1)}, bf16[1,256,1536]{2,1,0:T(8,128)(2,1)}, u32[]{:S(2)}) copy-start(bf16[1,256,1536]{2,1,0:T(8,128)(2,1)} %param.9) | copy-start | bytes 2359300
  (10 other events, 16.8 us)
Sparse Core Ops, SparseCore 0:
  22.8 43.1 all-gather.1
  151.7 67.8 reduce-scatter.1

commit v5 on v2

--- a/solution.py
+++ b/solution.py
@@ -12,15 +12,26 @@
 MASKED_SCORE = -1e30
 
 
+SEQ = ("chip", "core")
+
+
+def axis_count(axis):
+    if isinstance(axis, tuple):
+        count = 1
+        for name in axis:
+            count *= lax.axis_size(name)
+        return count
+    return lax.axis_size(axis)
+
+
 def shift_up(block, axis, distance):
-    devices = range(lax.axis_size(axis))
+    devices = range(axis_count(axis))
     route = [(i - distance, i) for i in devices if i - distance in devices]
     return lax.ppermute(block, axis, route)
 
 
 def swap_partner(block, axis):
-    count = lax.axis_size(axis)
-    return lax.ppermute(block, axis, [(i, i ^ 1) for i in range(count)])
+    return lax.ppermute(block, "core", [(0, 1), (1, 0)])
 
 
 def frame_labels(utt_lengths, first_frame, frame_count, total_frames):
@@ -43,14 +54,14 @@
     if not paired:
         held = [own]
         for _ in range(reach):
-            held.append(shift_up(held[-1], "seq", 1))
+            held.append(shift_up(held[-1], SEQ, 1))
         return held
     evens = {0: own}
     for dist in range(2, reach + 2, 2):
-        evens[dist] = shift_up(own, "seq", dist)
+        evens[dist] = shift_up(own, SEQ, dist)
     odds = list(range(1, reach + 1, 2))
     payload = [jnp.where(core == 0, evens[s - 1], evens[s + 1]) for s in odds]
-    received = swap_partner(payload, "seq")
+    received = swap_partner(payload, SEQ)
     held = []
     for dist in range(reach + 1):
         held.append(evens[dist] if dist % 2 == 0 else received[(dist - 1) // 2])
@@ -61,10 +72,10 @@
     if not paired:
         carried = parts[reach]
         for dist in range(reach - 1, -1, -1):
-            carried = shift_up(carried.astype(jnp.bfloat16), "seq", -1).astype(jnp.float32) + parts[dist]
+            carried = shift_up(carried.astype(jnp.bfloat16), SEQ, -1).astype(jnp.float32) + parts[dist]
         return carried
     odds = list(range(1, reach + 1, 2))
-    received = swap_partner([parts[s] for s in odds], "seq")
+    received = swap_partner([parts[s] for s in odds], SEQ)
     total = None
     for dist in range(0, reach + 2, 2):
         zero = jnp.zeros_like(parts[0])
@@ -75,15 +86,15 @@
         if dist == 0:
             total = summed
         else:
-            total = total + shift_up(summed.astype(jnp.bfloat16), "seq", -dist).astype(jnp.float32)
+            total = total + shift_up(summed.astype(jnp.bfloat16), SEQ, -dist).astype(jnp.float32)
     return total
 
 
 def local(query_rows, key_rows, value_rows, out_grad, lengths, out_weight):
-    seq_count = lax.axis_size("seq")
-    device = lax.axis_index("seq")
-    core = device % 2
-    paired = seq_count % 2 == 0
+    seq_count = axis_count(SEQ)
+    device = lax.axis_index(SEQ)
+    core = lax.axis_index("core")
+    paired = True
     tok_rows = query_rows.shape[1]
     feature_width = query_rows.shape[2]
     total_frames = seq_count * tok_rows
@@ -92,7 +103,7 @@
     utt_lengths = lengths[0]
 
     weight_cols = lax.all_gather(out_weight, "dp", axis=1, tiled=True)
-    weight_full = lax.all_gather(weight_cols, "seq", axis=0, tiled=True)
+    weight_full = lax.all_gather(weight_cols, SEQ, axis=0, tiled=True)
 
     query_heads = head_major(query_rows[0], tok_rows)
     own_kv = jnp.stack([head_major(key_rows[0], tok_rows), head_major(value_rows[0], tok_rows)])
@@ -149,8 +160,16 @@
     partial_weight = lax.dot_general(
         attended, upstream, (((0,), (0,)), ((), ())), preferred_element_type=jnp.float32
     )
+    chip_count = lax.axis_size("chip")
+    halves = partial_weight.reshape(chip_count, 2, -1, partial_weight.shape[1])
+    keep = lax.dynamic_index_in_dim(halves, core, 1, keepdims=False)
+    give = lax.dynamic_index_in_dim(halves, 1 - core, 1, keepdims=False)
+    core_sum = keep + swap_partner(give, SEQ)
     row_share = lax.psum_scatter(
-        partial_weight.astype(jnp.bfloat16), "seq", scatter_dimension=0, tiled=True
+        core_sum.reshape(-1, partial_weight.shape[1]).astype(jnp.bfloat16),
+        "chip",
+        scatter_dimension=0,
+        tiled=True,
     )
     weight_grad = lax.psum_scatter(
         row_share.astype(jnp.float32), "dp", scatter_dimension=1, tiled=True
@@ -202,23 +221,30 @@
 
 
 def solution(mesh):
+    names = list(mesh.axis_names)
+    at = names.index("seq")
+    shape = mesh.devices.shape
+    split_mesh = jax.sharding.Mesh(
+        mesh.devices.reshape(shape[:at] + (shape[at] // 2, 2) + shape[at + 1 :]),
+        tuple(names[:at] + ["chip", "core"] + names[at + 1 :]),
+    )
     return jax.shard_map(
         local,
-        mesh=mesh,
+        mesh=split_mesh,
         in_specs=(
-            P("dp", "seq", None),
-            P("dp", "seq", None),
-            P("dp", "seq", None),
-            P("dp", "seq", None),
+            P("dp", SEQ, None),
+            P("dp", SEQ, None),
+            P("dp", SEQ, None),
+            P("dp", SEQ, None),
             P("dp", None),
-            P("seq", "dp"),
+            P(SEQ, "dp"),
         ),
         out_specs=(
-            P("dp", "seq", None),
-            P("dp", "seq", None),
-            P("dp", "seq", None),
-            P("dp", "seq", None),
-            P("seq", "dp"),
+            P("dp", SEQ, None),
+            P("dp", SEQ, None),
+            P("dp", SEQ, None),
+            P("dp", SEQ, None),
+            P(SEQ, "dp"),
         ),
         check_vma=False,
     )

time: 182 us -> 188 us (1.033)
  waiting for transfers between devices: 86.1 us -> 77.3 us
  other arithmetic: 16.8 us -> 22.1 us
  local copies, waits for them, and re-layouts: 12 us -> 16.5 us
  matrix products: 34.3 us -> 37.5 us
    reduce_scatter x1, waiting for transfers between devices: 50.2 us -> 37.2 us  [local(): lax.psum_scatter(core_sum.reshape(-1, partial_weight.shape[1]).astype(jnp...]
    ppermute x4 -> x5, waiting for transfers between devices: 0.1 us -> 4.88 us  [swap_partner(): return lax.ppermute(block, 'core', [(0, 1), (1, 0)])]
    dot_general x5, matrix products: 3.38 us -> 7.45 us  [local(): jnp.einsum('hqe,hke->hqk', query_heads, held[dist][0], preferred_element_...]
    convert_element_type x0 -> x1, other arithmetic: none -> 3.78 us  [local(): core_sum.reshape(-1, partial_weight.shape[1]).astype(jnp.bfloat16)]
    unnamed x92 -> x90, local copies, waits for them, and re-layouts: 10.8 us -> 14.5 us
  transfers between devices with their start and end apart: 11 -> 12, of which waited for: 5 -> 5; matrix products, arithmetic and copies ran while one was open for 31% -> 35% of each run, Pallas kernels for 0% -> 0%
where the time goes in v5:
time: 188 us; the launch traced here: 186 us
  waiting for transfers between devices  77.3 us (41%)
  matrix products  37.5 us (20%)
  other arithmetic  22.1 us (12%)
  local copies, waits for them, and re-layouts  16.5 us (9%)
  between operations  16.2 us (9%)
  starting transfers between devices  11.3 us (6%)
  blocking collectives  5.14 us (3%)
    reduce_scatter x1, waiting for transfers between devices, local(): lax.psum_scatter(core_sum.reshape(-1, partial_weight.shape[1]).astype(jnp...  37.2 us
    ppermute x4, waiting for transfers between devices, shift_up(): return lax.ppermute(block, axis, route)  28.8 us
    unnamed x90, local copies, waits for them, and re-layouts  14.5 us
    ppermute x4, starting transfers between devices, shift_up(): return lax.ppermute(block, axis, route)  10.1 us
    dot_general x5, matrix products, local(): jnp.einsum('hqe,hke->hqk', query_heads, held[dist][0], preferred_element_...  7.45 us
    dot_general x5, matrix products, local(): jnp.einsum('hqe,hke->hqk', grad_heads, value_block, preferred_element_typ...  6.52 us
    dot_general x5, matrix products, local(): jnp.einsum('hqk,hqe->hke', prob_back, grad_heads, preferred_element_type=...  6.44 us
    reduce_scatter x1, waiting for transfers between devices, local(): lax.psum_scatter(row_share.astype(jnp.float32), 'dp', scatter_dimension=1...  6.42 us
  transfers between devices with their start and end apart: 12, of which 5 were waited for; matrix products, arithmetic and copies ran while one was open for 35% of the time, Pallas kernels for 0%

profile of v5, /device:TPU:4, one launch (start us, length us, event | category | flops | bytes accessed | tf_op | source)
XLA Modules:
  0.0 186.1 jit_solution(12201261286213922624)
XLA Ops:
  8.1 1.2 copy.80
  9.3 1.2 copy.78
  10.5 0.9 pad_maximum_fusion.2
  11.4 3.5 %collective-permute-start.2 = (bf16[2,12,256,64]{2,3,1,0:T(8,128)(2,1)}, bf16[2,12,256,64]{2,3,1,0:T(8,128)(2,1)S(1)}, u32[]{:S(2)}, u32[]{:S(2)}) collective-permute-start(bf16[2,12,256,64]{2,3,1,0:T(8,128)(2,1)} %pad_maximum_fusion.2), channel_id=1, source_target_pairs={{0,8},{2,10},{4,12},{6,14},{8,16},{10,18},{12,20},{14,22},{16,24},... | collective-permute-start | bytes 2359304 | tf_op jit(solution)/shard_map/ppermute | solution.py:30
  15.0 3.4 %collective-permute-start = (bf16[2,12,256,64]{2,3,1,0:T(8,128)(2,1)}, bf16[2,12,256,64]{2,3,1,0:T(8,128)(2,1)S(1)}, u32[]{:S(2)}, u32[]{:S(2)}) collective-permute-start(bf16[2,12,256,64]{2,3,1,0:T(8,128)(2,1)} %pad_maximum_fusion.2), channel_id=1, source_target_pairs={{0,4},{2,6},{4,8},{6,10},{8,12},{10,14},{12,16},{14,18},{16,20},{1... | collective-permute-start | bytes 2359304 | tf_op jit(solution)/shard_map/ppermute | solution.py:30
  18.4 5.1 %all_gather.6 = bf16[48,1536]{1,0:T(8,128)(2,1)} all-gather(bf16[48,768]{1,0:T(8,128)(2,1)S(1)} %copy-done.38), channel_id=1, replica_groups=mesh['chip'=8,'core'=2,'dp'=2] {'dp'}, dimensions={1}, use_global_device_ids=true | all-gather | bytes 221184 | tf_op jit(solution)/shard_map/all_gather | solution.py:105
  25.1 1.2 copy.77
  27.7 1.9 compare_and_fusion.3
  29.5 4.9 %collective-permute-done.2 = bf16[2,12,256,64]{2,3,1,0:T(8,128)(2,1)S(1)} collective-permute-done((bf16[2,12,256,64]{2,3,1,0:T(8,128)(2,1)}, bf16[2,12,256,64]{2,3,1,0:T(8,128)(2,1)S(1)}, u32[]{:S(2)}, u32[]{:S(2)}) %collective-permute-start.2) | collective-permute-done | bytes 786464 | tf_op jit(solution)/shard_map/ppermute | solution.py:30
  34.4 23.9 %collective-permute-done = bf16[2,12,256,64]{2,3,1,0:T(8,128)(2,1)S(1)} collective-permute-done((bf16[2,12,256,64]{2,3,1,0:T(8,128)(2,1)}, bf16[2,12,256,64]{2,3,1,0:T(8,128)(2,1)S(1)}, u32[]{:S(2)}, u32[]{:S(2)}) %collective-permute-start) | collective-permute-done | bytes 786464 | tf_op jit(solution)/shard_map/ppermute | solution.py:30
  58.3 1.4 broadcast_select_fusion.1
  59.7 2.4 %select_reduce_fusion = (f32[12,256]{1,0:T(8,128)S(1)}, f32[12,256,256]{1,2,0:T(8,128)}) fusion(pred[256,256]{0,1:T(8,128)(4,1)S(1)} %get-tuple-element.42, bf16[12,256,64]{1,2,0:T(8,128)(2,1)S(1)} %bitcast.261, bf16[12,256,64]{1,2,0:T(8,128)(2,1)S(1)} %bitcast.273), kind=kOutput, calls=%fused_computation.31 | convolution fusion | flops 103019520 | bytes 4009984 | tf_op jit(solution)/shard_map/hqe,hke->hqk/dot_general | solution.py:126
  62.6 1.6 fusion.11
  65.0 2.1 %fusion.10 = (f32[12,256]{1,0:T(8,128)S(1)}, f32[12,256,256]{2,1,0:T(8,128)S(1)}) fusion(pred[256,256]{0,1:T(8,128)(4,1)S(1)} %copy-done.35, bf16[12,256,64]{1,2,0:T(8,128)(2,1)S(1)} %bitcast.264, bf16[2,12,256,64]{2,3,1,0:T(8,128)(2,1)} %collective-permute-done.3), kind=kOutput, calls=%fused_computation.29 | convolution fusion | flops 103019520 | bytes 4009984 | tf_op jit(solution)/shard_map/hqe,hke->hqk/dot_general | solution.py:126
  67.8 1.6 copy-done.3
  69.5 3.9 %fusion.21 = (f32[12,256]{1,0:T(8,128)S(1)}, f32[12,256]{1,0:T(8,128)S(1)}, f32[12,256]{1,0:T(8,128)S(1)}, f32[12,256]{1,0:T(8,128)S(1)}, f32[12,256]{1,0:T(8,128)S(1)}) fusion(f32[12,256,256]{2,1,0:T(8,128)S(1)} %get-tuple-element.52, f32[12,256]{1,0:T(8,128)S(1)} %maximum_maximum_fusion, pred[256,256]{0,1:T(8,128)(4,1)S(1)} %copy-done.32, ...), kind=kLoop, calls=%fused_computation.44 | loop fusion | flops 19645440 | bytes 16130048 | tf_op jit(solution)/shard_map/reduce_sum | solution.py:139
  74.0 0.9 fusion.59
  74.9 1.9 fusion.61
  76.8 0.9 fusion.63
  77.6 0.9 fusion.67
  78.5 1.0 fusion.119
  79.5 0.8 fusion.116
  80.3 2.1 %copy-done.2 = f32[8,2,48,1536]{3,2,1,0:T(8,128)} copy-done((f32[8,2,48,1536]{3,2,1,0:T(8,128)}, f32[8,2,48,1536]{3,2,1,0:T(8,128)S(1)}, u32[]{:S(2)}) %copy-start.2) | copy-done | bytes 4718616
  82.5 1.7 dynamic-slice_bitcast_fusion
  84.2 4.9 %collective-permute-done.8 = f32[8,48,1536]{2,1,0:T(8,128)} collective-permute-done((f32[8,48,1536]{2,1,0:T(8,128)}, f32[8,48,1536]{2,1,0:T(8,128)}, u32[]{:S(2)}, u32[]{:S(2)}) %collective-permute-start.8) | collective-permute-done | bytes 2359328 | tf_op jit(solution)/shard_map/ppermute | solution.py:34
  89.1 3.8 %fusion.18 = bf16[8,48,1536]{2,1,0:T(8,128)(2,1)} fusion(f32[8,48,1536]{2,1,0:T(8,128)} %collective-permute-done.8, f32[8,2,48,1536]{3,2,1,0:T(8,128)} %copy-done.2, s32[]{:T(128)S(6)} %select_n.193), kind=kLoop, calls=%fused_computation.40 | loop fusion | flops 1179648 | bytes 5898244 | tf_op jit(solution)/shard_map/convert_element_type | solution.py:169
  93.1 2.5 %convolution_convert_fusion.1 = bf16[256,768]{1,0:T(8,128)(2,1)S(1)} fusion(bf16[768,1536]{1,0:T(8,128)(2,1)} %all-gather.2.cloned.1.call-done, bf16[1,256,1536]{2,1,0:T(8,128)(2,1)S(1)} %copy-done), kind=kOutput, calls=%fused_computation.122 | convolution fusion | flops 604176384 | bytes 3538944 | tf_op jit(solution)/shard_map/dot_general | solution.py:156
  95.8 2.8 %fusion.88 = f32[1,12,256,64]{2,3,1,0:T(8,128)S(1)} fusion(bf16[12,256,64]{1,2,0:T(8,128)(2,1)S(1)} %bitcast.282, f32[12,256,256]{2,1,0:T(8,128)} %copy-done.11, f32[12,256]{1,0:T(8,128)S(1)} %copy-done.39, pred[256,256]{0,1:T(8,128)(4,1)S(1)} %copy-done.36), kind=kOutput, calls=%fused_computation.100 | convolution fusion | flops 103809024 | bytes 4403200 | tf_op jit(solution)/shard_map/hqk,hqe->hke/dot_general | solution.py:211
  99.6 1.0 copy-done.4
  100.7 1.1 multiply_convert_fusion
  102.6 2.2 %multiply_convert_fusion.4 = bf16[12,256,256]{1,2,0:T(8,128)(2,1)S(1)} fusion(f32[12,256,256]{2,1,0:T(8,128)S(1)} %copy-done.12, bf16[12,256,64]{1,2,0:T(8,128)(2,1)} %bitcast.286, f32[12,256]{1,0:T(8,128)S(1)} %multiply_reduce_fusion, f32[12,256]{1,0:T(8,128)S(1)} %copy-done.40, pred[256,256]{0,1:T(8,128)(4,1)S(1)} %copy-done.37, ...), kind=kOutput, calls=%fused_computation.21 | convolution fusion | flops 105381888 | bytes 5595136 | tf_op jit(solution)/shard_map/hqe,hke->hqk/dot_general | solution.py:199
  106.0 1.1 multiply_convert_fusion.3
  108.1 0.9 copy-done.8
  109.2 1.1 multiply_convert_fusion.1
  110.5 1.1 multiply_convert_fusion.2
  114.0 1.6 fusion.79
  117.1 2.1 %fusion.42 = (bf16[2,12,256,64]{2,3,1,0:T(8,128)(2,1)}, bf16[2,12,256,64]{2,3,1,0:T(8,128)(2,1)}) fusion(f32[1,12,256,64]{2,3,1,0:T(8,128)S(1)} %fusion.85, f32[1,12,256,64]{2,3,1,0:T(8,128)S(1)} %fusion.97, f32[2,12,256,64]{2,3,1,0:T(8,128)S(1)} %collective-permute-done.5, f32[2,12,256,64]{2,3,1,0:T(8,128)S(1)} %collective-permute-done.4, pred[]{:T(512)S(6)} %eq.89, ...), kind=kLoop, calls=%fused_computation.63 | loop fusion | flops 3145728 | bytes 7864321 | tf_op jit(solution)/shard_map/convert_element_type | solution.py:89
  119.2 1.3 collective-permute-start.7
  120.4 1.9 %collective-permute-start.6 = (bf16[2,12,256,64]{2,3,1,0:T(8,128)(2,1)}, bf16[2,12,256,64]{2,3,1,0:T(8,128)(2,1)}, u32[]{:S(2)}, u32[]{:S(2)}) collective-permute-start(bf16[2,12,256,64]{2,3,1,0:T(8,128)(2,1)} %get-tuple-element.32), channel_id=1, source_target_pairs={{4,0},{6,2},{8,4},{10,6},{12,8},{14,10},{16,12},{18,14},{20,16},{2... | collective-permute-start | bytes 2359304 | tf_op jit(solution)/shard_map/ppermute | solution.py:30
  122.4 1.7 fusion.12
  124.1 2.2 %fusion.115 = bf16[12,256,64]{1,2,0:T(8,128)(2,1)} fusion(f32[12,256,64]{1,2,0:T(8,128)S(1)} %fusion.153, f32[12,256,64]{1,2,0:T(8,128)S(1)} %fusion.122, f32[12,256,64]{1,2,0:T(8,128)S(1)} %fusion.125, f32[12,256,64]{1,2,0:T(8,128)S(1)} %fusion.120, bf16[12,256,256]{1,2,0:T(8,128)(2,1)S(1)} %multiply_convert_fusion.4, ...), kind=kOutput, calls=%fused_computation.121 | convolution fusion | flops 101842944 | bytes 5505024 | tf_op jit(solution)/shard_map/hqk,hke->hqe/dot_general | solution.py:203
  126.2 37.2 %reduce-scatter.3.cloned.1.call-done = bf16[48,1536]{1,0:T(8,128)(2,1)} async-done(((bf16[384,1536]{1,0:T(8,128)(2,1)}), bf16[48,1536]{1,0:T(8,128)(2,1)}) %reduce-scatter.3.cloned.1.call-update) | async-done | bytes 147472 | tf_op jit(solution)/shard_map/reduce_scatter | solution.py:168
  163.4 1.7 convert_element_type.187
  165.7 2.0 %copy.107 = bf16[1,256,768]{2,1,0:T(8,128)(2,1)} copy(bf16[1,256,768]{1,2,0:T(8,128)(2,1)} %bitcast.295) | data formatting | bytes 786432
  167.7 2.6 %fusion.41 = bf16[2,12,256,64]{2,3,1,0:T(8,128)(2,1)S(1)} fusion(f32[1,12,256,64]{2,3,1,0:T(8,128)} %fusion.79, f32[1,12,256,64]{2,3,1,0:T(8,128)S(1)} %fusion.99, bf16[2,12,256,64]{2,3,1,0:T(8,128)(2,1)} %collective-permute-done.7, bf16[2,12,256,64]{2,3,1,0:T(8,128)(2,1)} %collective-permute-done.6, f32[2,12,256,64]{2,3,1,0:T(8,128)} %copy-done.13, pred[]{:T(512)S(6)} %eq.89), kind=kLoop, calls=%fused_computation.60 | loop fusion | flops 3145728 | bytes 5505025 | tf_op jit(solution)/shard_map/convert.1
  170.4 0.9 copy.108
  171.3 0.9 copy.109
  172.2 6.4 %reduce-scatter.5.cloned.1.call-done = f32[48,768]{1,0:T(8,128)} async-done(((f32[48,1536]{1,0:T(8,128)}), f32[48,768]{1,0:T(8,128)}) %reduce-scatter.5.cloned.1.call-update) | async-done | bytes 147472 | tf_op jit(solution)/shard_map/reduce_scatter | solution.py:174
  (131 shorter events, 14.9 us)
Async XLA Ops:
  8.0 71.5 %copy-start = (bf16[1,256,1536]{2,1,0:T(8,128)(2,1)S(1)}, bf16[1,256,1536]{2,1,0:T(8,128)(2,1)}, u32[]{:S(2)}) copy-start(bf16[1,256,1536]{2,1,0:T(8,128)(2,1)} %param.9) | copy-start | bytes 2359300
  8.0 10.3 %copy-start.38 = (bf16[48,768]{1,0:T(8,128)(2,1)S(1)}, bf16[48,768]{1,0:T(8,128)(2,1)}, u32[]{:S(2)}) copy-start(bf16[48,768]{1,0:T(8,128)(2,1)} %param.11) | copy-start | bytes 221188
  8.0 15.6 %copy-start.41 = (s32[1,8]{1,0:T(1,128)S(1)}, s32[1,8]{1,0:T(1,128)}, u32[]{:S(2)}) copy-start(s32[1,8]{1,0:T(1,128)} %param.10) | copy-start | bytes 100
  8.0 85.1 %all-gather.2.cloned.1.call-start = ((), (), s32[]{:S(2)}) async-start(), calls=%async_computation.2 | async-start | bytes 2506752 | tf_op jit(solution)/shard_map/all_gather | solution.py:106
  11.4 23.0 %collective-permute-start.2 = (bf16[2,12,256,64]{2,3,1,0:T(8,128)(2,1)}, bf16[2,12,256,64]{2,3,1,0:T(8,128)(2,1)S(1)}, u32[]{:S(2)}, u32[]{:S(2)}) collective-permute-start(bf16[2,12,256,64]{2,3,1,0:T(8,128)(2,1)} %pad_maximum_fusion.2), channel_id=1, source_target_pairs={{0,8},{2,10},{4,12},{6,14},{8,16},{10,18},{12,20},{14,22},{16,24},... | collective-permute-start | bytes 2359304 | tf_op jit(solution)/shard_map/ppermute | solution.py:30
  15.0 43.3 %collective-permute-start = (bf16[2,12,256,64]{2,3,1,0:T(8,128)(2,1)}, bf16[2,12,256,64]{2,3,1,0:T(8,128)(2,1)S(1)}, u32[]{:S(2)}, u32[]{:S(2)}) collective-permute-start(bf16[2,12,256,64]{2,3,1,0:T(8,128)(2,1)} %pad_maximum_fusion.2), channel_id=1, source_target_pairs={{0,4},{2,6},{4,8},{6,10},{8,12},{10,14},{12,16},{14,18},{16,20},{1... | collective-permute-start | bytes 2359304 | tf_op jit(solution)/shard_map/ppermute | solution.py:30
  23.5 139.9 %reduce-scatter.3.cloned.1.call-start = ((), (), s32[]{:S(2)}) async-start(), calls=%async_computation.3 | async-start | bytes 1327104 | tf_op jit(solution)/shard_map/reduce_scatter | solution.py:168
  29.5 30.2 %copy-start.29 = (pred[256,256]{0,1:T(8,128)(4,1)}, pred[256,256]{0,1:T(8,128)(4,1)S(1)}, u32[]{:S(2)}) copy-start(pred[256,256]{0,1:T(8,128)(4,1)S(1)} %get-tuple-element.42) | copy-start | bytes 196612
  34.4 39.6 %copy-start.14 = (bf16[2,12,256,64]{2,3,1,0:T(8,128)(2,1)}, bf16[2,12,256,64]{2,3,1,0:T(8,128)(2,1)S(1)}, u32[]{:S(2)}) copy-start(bf16[2,12,256,64]{2,3,1,0:T(8,128)(2,1)S(1)} %collective-permute-done.2) | copy-start | bytes 2359300
  58.3 18.5 %copy-start.16 = (bf16[2,12,256,64]{2,3,1,0:T(8,128)(2,1)}, bf16[2,12,256,64]{2,3,1,0:T(8,128)(2,1)S(1)}, u32[]{:S(2)}) copy-start(bf16[2,12,256,64]{2,3,1,0:T(8,128)(2,1)S(1)} %collective-permute-done) | copy-start | bytes 2359300
  59.7 5.2 %collective-permute-start.3 = (bf16[2,12,256,64]{2,3,1,0:T(8,128)(2,1)}, bf16[2,12,256,64]{2,3,1,0:T(8,128)(2,1)}, u32[]{:S(2)}, u32[]{:S(2)}) collective-permute-start(bf16[2,12,256,64]{2,3,1,0:T(8,128)(2,1)} %get-tuple-element.37), channel_id=1, source_target_pairs={{0,2},{2,0},{1,3},{3,1},{4,6},{6,4},{5,7},{7,5},{8,10},{10,8},{9,1... | collective-permute-start | bytes 2359304 | tf_op jit(solution)/shard_map/ppermute | solution.py:34
  62.1 2.1 %copy-start.27 = (pred[256,256]{0,1:T(8,128)(4,1)S(1)}, pred[256,256]{0,1:T(8,128)(4,1)}, u32[]{:S(2)}) copy-start(pred[256,256]{0,1:T(8,128)(4,1)} %get-tuple-element.39) | copy-start | bytes 196612
  62.1 5.0 %collective-permute-start.1 = (bf16[2,12,256,64]{2,3,1,0:T(8,128)(2,1)}, bf16[2,12,256,64]{2,3,1,0:T(8,128)(2,1)S(1)}, u32[]{:S(2)}, u32[]{:S(2)}) collective-permute-start(bf16[2,12,256,64]{2,3,1,0:T(8,128)(2,1)} %get-tuple-element.36), channel_id=1, source_target_pairs={{0,2},{2,0},{1,3},{3,1},{4,6},{6,4},{5,7},{7,5},{8,10},{10,8},{9,1... | collective-permute-start | bytes 2359304 | tf_op jit(solution)/shard_map/ppermute | solution.py:34
  62.6 2.3 %copy-start.35 = (pred[256,256]{0,1:T(8,128)(4,1)S(1)}, pred[256,256]{0,1:T(8,128)(4,1)}, u32[]{:S(2)}) copy-start(pred[256,256]{0,1:T(8,128)(4,1)} %get-tuple-element.40) | copy-start | bytes 196612
  64.2 9.9 %copy-start.5 = (f32[12,256,256]{2,1,0:T(8,128)}, f32[12,256,256]{2,1,0:T(8,128)S(1)}, u32[]{:S(2)}) copy-start(f32[12,256,256]{2,1,0:T(8,128)S(1)} %get-tuple-element.44) | copy-start | bytes 9437188
  64.2 2.9 %copy-start.32 = (pred[256,256]{0,1:T(8,128)(4,1)S(1)}, pred[256,256]{0,1:T(8,128)(4,1)}, u32[]{:S(2)}) copy-start(pred[256,256]{0,1:T(8,128)(4,1)} %get-tuple-element.38) | copy-start | bytes 196612
  64.9 11.9 %copy-start.7 = (f32[12,256,256]{2,1,0:T(8,128)}, f32[12,256,256]{2,1,0:T(8,128)S(1)}, u32[]{:S(2)}) copy-start(f32[12,256,256]{2,1,0:T(8,128)S(1)} %get-tuple-element.48) | copy-start | bytes 9437188
  64.9 4.6 %copy-start.3 = (f32[12,256,256]{1,2,0:T(8,128)S(1)}, f32[12,256,256]{1,2,0:T(8,128)}, u32[]{:S(2)}) copy-start(f32[12,256,256]{1,2,0:T(8,128)} %get-tuple-element.50) | copy-start | bytes 9437188
  64.9 4.5 %copy-start.25 = (pred[256,256]{0,1:T(8,128)(4,1)S(1)}, pred[256,256]{0,1:T(8,128)(4,1)}, u32[]{:S(2)}) copy-start(pred[256,256]{0,1:T(8,128)(4,1)} %get-tuple-element.41) | copy-start | bytes 196612
  65.0 4.5 %copy-start.30 = (pred[256,256]{0,1:T(8,128)(4,1)S(1)}, pred[256,256]{0,1:T(8,128)(4,1)}, u32[]{:S(2)}) copy-start(pred[256,256]{0,1:T(8,128)(4,1)} %copy-done.29) | copy-start | bytes 196612
  67.1 7.8 %copy-start.11 = (f32[12,256,256]{2,1,0:T(8,128)}, f32[12,256,256]{2,1,0:T(8,128)S(1)}, u32[]{:S(2)}) copy-start(f32[12,256,256]{2,1,0:T(8,128)S(1)} %get-tuple-element.46) | copy-start | bytes 9437188
  67.1 11.4 %copy-start.23 = (bf16[2,12,256,64]{2,3,1,0:T(8,128)(2,1)}, bf16[2,12,256,64]{2,3,1,0:T(8,128)(2,1)S(1)}, u32[]{:S(2)}) copy-start(bf16[2,12,256,64]{2,3,1,0:T(8,128)(2,1)S(1)} %collective-permute-done.1) | copy-start | bytes 2359300
  67.8 10.7 %copy-start.9 = (f32[12,256,256]{2,1,0:T(8,128)}, f32[12,256,256]{2,1,0:T(8,128)S(1)}, u32[]{:S(2)}) copy-start(f32[12,256,256]{2,1,0:T(8,128)S(1)} %get-tuple-element.52) | copy-start | bytes 9437188
  80.3 2.1 %copy-start.2 = (f32[8,2,48,1536]{3,2,1,0:T(8,128)}, f32[8,2,48,1536]{3,2,1,0:T(8,128)S(1)}, u32[]{:S(2)}) copy-start(f32[8,2,48,1536]{3,2,1,0:T(8,128)S(1)} %fusion.116) | copy-start | bytes 14155780
  84.2 4.9 %collective-permute-start.8 = (f32[8,48,1536]{2,1,0:T(8,128)}, f32[8,48,1536]{2,1,0:T(8,128)}, u32[]{:S(2)}, u32[]{:S(2)}) collective-permute-start(f32[8,48,1536]{2,1,0:T(8,128)} %dynamic-slice_bitcast_fusion), channel_id=1, source_target_pairs={{0,2},{2,0},{1,3},{3,1},{4,6},{6,4},{5,7},{7,5},{8,10},{10,8},{9,1... | collective-permute-start | bytes 7077896 | tf_op jit(solution)/shard_map/ppermute | solution.py:34
  92.8 3.0 %copy-start.36 = (pred[256,256]{0,1:T(8,128)(4,1)S(1)}, pred[256,256]{0,1:T(8,128)(4,1)}, u32[]{:S(2)}) copy-start(pred[256,256]{0,1:T(8,128)(4,1)} %get-tuple-element.40) | copy-start | bytes 196612
  92.8 3.0 %copy-start.39 = (f32[12,256]{1,0:T(8,128)S(1)}, f32[12,256]{1,0:T(8,128)}, u32[]{:S(2)}) copy-start(f32[12,256]{1,0:T(8,128)} %get-tuple-element.30) | copy-start | bytes 36868
  92.9 85.8 %reduce-scatter.5.cloned.1.call-start = ((), (), s32[]{:S(2)}) async-start(), calls=%async_computation.4 | async-start | bytes 442368 | tf_op jit(solution)/shard_map/reduce_scatter | solution.py:174
  95.6 3.0 %copy-start.33 = (pred[256,256]{0,1:T(8,128)(4,1)S(1)}, pred[256,256]{0,1:T(8,128)(4,1)}, u32[]{:S(2)}) copy-start(pred[256,256]{0,1:T(8,128)(4,1)} %get-tuple-element.38) | copy-start | bytes 196612
  95.8 3.8 %copy-start.21 = (bf16[256,768]{0,1:T(8,128)(2,1)}, bf16[256,768]{0,1:T(8,128)(2,1)S(1)}, u32[]{:S(2)}) copy-start(bf16[256,768]{0,1:T(8,128)(2,1)S(1)} %copy.86) | copy-start | bytes 1179652
  95.8 3.0 %copy-start.10 = (f32[12,256,256]{2,1,0:T(8,128)S(1)}, f32[12,256,256]{2,1,0:T(8,128)}, u32[]{:S(2)}) copy-start(f32[12,256,256]{2,1,0:T(8,128)} %copy-done.9) | copy-start | bytes 9437188
  98.8 1.9 %copy-start.40 = (f32[12,256]{1,0:T(8,128)S(1)}, f32[12,256]{1,0:T(8,128)}, u32[]{:S(2)}) copy-start(f32[12,256]{1,0:T(8,128)} %get-tuple-element.30) | copy-start | bytes 36868
  100.7 1.9 %copy-start.12 = (f32[12,256,256]{2,1,0:T(8,128)S(1)}, f32[12,256,256]{2,1,0:T(8,128)}, u32[]{:S(2)}) copy-start(f32[12,256,256]{2,1,0:T(8,128)} %copy-done.11) | copy-start | bytes 9437188
  100.7 1.9 %copy-start.37 = (pred[256,256]{0,1:T(8,128)(4,1)S(1)}, pred[256,256]{0,1:T(8,128)(4,1)}, u32[]{:S(2)}) copy-start(pred[256,256]{0,1:T(8,128)(4,1)} %get-tuple-element.40) | copy-start | bytes 196612
  105.6 11.5 %collective-permute-start.5 = (f32[2,12,256,64]{2,3,1,0:T(8,128)S(1)}, f32[2,12,256,64]{2,3,1,0:T(8,128)S(1)}, u32[]{:S(2)}, u32[]{:S(2)}) collective-permute-start(f32[2,12,256,64]{2,3,1,0:T(8,128)S(1)} %pad_maximum_fusion.1), channel_id=1, source_target_pairs={{0,2},{2,0},{1,3},{3,1},{4,6},{6,4},{5,7},{7,5},{8,10},{10,8},{9,1... | collective-permute-start | bytes 4718600 | tf_op jit(solution)/shard_map/ppermute | solution.py:34
  107.1 1.9 %copy-start.8 = (f32[12,256,256]{2,1,0:T(8,128)S(1)}, f32[12,256,256]{2,1,0:T(8,128)}, u32[]{:S(2)}) copy-start(f32[12,256,256]{2,1,0:T(8,128)} %copy-done.7) | copy-start | bytes 9437188
  107.1 2.1 %copy-start.17 = (bf16[2,12,256,64]{2,3,1,0:T(8,128)(2,1)S(1)}, bf16[2,12,256,64]{2,3,1,0:T(8,128)(2,1)}, u32[]{:S(2)}) copy-start(bf16[2,12,256,64]{2,3,1,0:T(8,128)(2,1)} %copy-done.16) | copy-start | bytes 2359300
  107.1 2.1 %copy-start.28 = (pred[256,256]{0,1:T(8,128)(4,1)S(1)}, pred[256,256]{0,1:T(8,128)(4,1)}, u32[]{:S(2)}) copy-start(pred[256,256]{0,1:T(8,128)(4,1)} %get-tuple-element.39) | copy-start | bytes 196612
  107.9 2.5 %copy-start.6 = (f32[12,256,256]{2,1,0:T(8,128)S(1)}, f32[12,256,256]{2,1,0:T(8,128)}, u32[]{:S(2)}) copy-start(f32[12,256,256]{2,1,0:T(8,128)} %copy-done.5) | copy-start | bytes 9437188
  107.9 2.6 %copy-start.15 = (bf16[2,12,256,64]{2,3,1,0:T(8,128)(2,1)S(1)}, bf16[2,12,256,64]{2,3,1,0:T(8,128)(2,1)}, u32[]{:S(2)}) copy-start(bf16[2,12,256,64]{2,3,1,0:T(8,128)(2,1)} %copy-done.14) | copy-start | bytes 2359300
  107.9 2.6 %copy-start.26 = (pred[256,256]{0,1:T(8,128)(4,1)S(1)}, pred[256,256]{0,1:T(8,128)(4,1)}, u32[]{:S(2)}) copy-start(pred[256,256]{0,1:T(8,128)(4,1)} %get-tuple-element.41) | copy-start | bytes 196612
  107.9 9.1 %collective-permute-start.4 = (f32[2,12,256,64]{2,3,1,0:T(8,128)S(1)}, f32[2,12,256,64]{2,3,1,0:T(8,128)S(1)}, u32[]{:S(2)}, u32[]{:S(2)}) collective-permute-start(f32[2,12,256,64]{2,3,1,0:T(8,128)S(1)} %pad_maximum_fusion), channel_id=1, source_target_pairs={{0,2},{2,0},{1,3},{3,1},{4,6},{6,4},{5,7},{7,5},{8,10},{10,8},{9,1... | collective-permute-start | bytes 4718600 | tf_op jit(solution)/shard_map/ppermute | solution.py:34
  117.0 5.4 %copy-start.18 = (bf16[768,1536]{1,0:T(8,128)(2,1)S(1)}, bf16[768,1536]{1,0:T(8,128)(2,1)}, u32[]{:S(2)}) copy-start(bf16[768,1536]{1,0:T(8,128)(2,1)} %all-gather.2.cloned.1.call-done) | copy-start | bytes 7077892
  117.0 5.4 %copy-start.20 = (bf16[256,12,64]{0,2,1:T(8,128)(2,1)S(1)}, bf16[256,12,64]{0,2,1:T(8,128)(2,1)}, u32[]{:S(2)}) copy-start(bf16[256,12,64]{0,2,1:T(8,128)(2,1)} %copy-done.19) | copy-start | bytes 1179652
  117.0 2.1 %copy-start.13 = (f32[2,12,256,64]{2,3,1,0:T(8,128)}, f32[2,12,256,64]{2,3,1,0:T(8,128)S(1)}, u32[]{:S(2)}) copy-start(f32[2,12,256,64]{2,3,1,0:T(8,128)S(1)} %collective-permute-done.4) | copy-start | bytes 4718596
  119.2 48.5 %collective-permute-start.7 = (bf16[2,12,256,64]{2,3,1,0:T(8,128)(2,1)}, bf16[2,12,256,64]{2,3,1,0:T(8,128)(2,1)}, u32[]{:S(2)}, u32[]{:S(2)}) collective-permute-start(bf16[2,12,256,64]{2,3,1,0:T(8,128)(2,1)} %get-tuple-element.33), channel_id=1, source_target_pairs={{8,0},{10,2},{12,4},{14,6},{16,8},{18,10},{20,12},{22,14},{24,16},... | collective-permute-start | bytes 2359304 | tf_op jit(solution)/shard_map/ppermute | solution.py:30
  120.4 47.2 %collective-permute-start.6 = (bf16[2,12,256,64]{2,3,1,0:T(8,128)(2,1)}, bf16[2,12,256,64]{2,3,1,0:T(8,128)(2,1)}, u32[]{:S(2)}, u32[]{:S(2)}) collective-permute-start(bf16[2,12,256,64]{2,3,1,0:T(8,128)(2,1)} %get-tuple-element.32), channel_id=1, source_target_pairs={{4,0},{6,2},{8,4},{10,6},{12,8},{14,10},{16,12},{18,14},{20,16},{2... | collective-permute-start | bytes 2359304 | tf_op jit(solution)/shard_map/ppermute | solution.py:30
  165.7 12.9 %copy-start.1 = (bf16[1,256,1536]{2,1,0:T(8,128)(2,1)S(1)}, bf16[1,256,1536]{2,1,0:T(8,128)(2,1)}, u32[]{:S(2)}) copy-start(bf16[1,256,1536]{2,1,0:T(8,128)(2,1)} %param.9) | copy-start | bytes 2359300
  (6 other events, 8.1 us)
Sparse Core Ops, SparseCore 0:
  23.6 43.1 all-gather.1
Sparse Core Ops, SparseCore 1:
  92.9 70.4 reduce-scatter.2
  166.1 12.5 reduce-scatter.4

commit v6 on v4

--- a/solution.py
+++ b/solution.py
@@ -169,10 +169,6 @@
     partial_weight = lax.dot_general(
         attended, upstream, (((0,), (0,)), ((), ())), preferred_element_type=jnp.float32
     )
-    col_share = halving_scatter(partial_weight, "dp", 1, [False] * 8)
-    weight_grad = lax.psum_scatter(
-        col_share.astype(jnp.bfloat16), "seq", scatter_dimension=0, tiled=True
-    ).astype(jnp.float32)
 
     grad_heads = head_major(att_grad, tok_rows)
     delta_rows = jnp.sum(
@@ -212,7 +208,13 @@
         )
         parts[dist] = jnp.stack([key_part, value_part])
 
+    partial_weight, parts = lax.optimization_barrier((partial_weight, parts))
     kv_grad = return_behind(parts, reach, paired, core)
+    seq_bits = max(seq_count.bit_length() - 1, 1)
+    row_share = halving_scatter(
+        partial_weight, "seq", 0, [step > 0 for step in range(seq_bits)]
+    )
+    weight_grad = halving_scatter(row_share, "dp", 1, [False] * 8)
     query_grad = row_major(query_acc * score_scale, tok_rows).astype(jnp.bfloat16)
     key_grad = row_major(kv_grad[0], tok_rows).astype(jnp.bfloat16)
     value_grad = row_major(kv_grad[1], tok_rows).astype(jnp.bfloat16)

time: 247 us -> 215 us (0.87)
  the two profiles are of different devices: /device:TPU:4 before, /device:TPU:0 now
where the time goes in v6:
time: 215 us; the launch traced here: 214 us
  waiting for transfers between devices  59.3 us (28%)
  matrix products  45.4 us (21%)
  starting transfers between devices  44.1 us (21%)
  other arithmetic  25.8 us (12%)
  local copies, waits for them, and re-layouts  19.2 us (9%)
  between operations  14.9 us (7%)
  blocking collectives  5.14 us (2%)
    ppermute x4, waiting for transfers between devices, shift_up(): return lax.ppermute(block, axis, route)  32.2 us
    ppermute x5, starting transfers between devices, halving_scatter(): got = lax.ppermute(give, axis, [(i, i ^ 1 << step) for i in range(count)])  32.1 us
    ppermute x5, waiting for transfers between devices, halving_scatter(): got = lax.ppermute(give, axis, [(i, i ^ 1 << step) for i in range(count)])  20.2 us
    unnamed x109, local copies, waits for them, and re-layouts  13.9 us
    ppermute x4, starting transfers between devices, shift_up(): return lax.ppermute(block, axis, route)  11 us
    dot_general x5, matrix products, local(): jnp.einsum('hqe,hke->hqk', grad_heads, value_block, preferred_element_typ...  7.85 us
    dot_general x5, matrix products, local(): jnp.einsum('hqk,hke->hqe', score_grad, key_block, preferred_element_type=...  7.47 us
    dot_general x5, matrix products, local(): jnp.einsum('hqe,hke->hqk', query_heads, held[dist][0], preferred_element_...  7.39 us
  transfers between devices with their start and end apart: 14, of which 8 were waited for; matrix products, arithmetic and copies ran while one was open for 23% of the time, Pallas kernels for 0%

profile of v6, /device:TPU:0, one launch (start us, length us, event | category | flops | bytes accessed | tf_op | source)
XLA Modules:
  0.0 213.8 jit_solution(10623511565290530999)
XLA Ops:
  7.2 1.2 copy.80
  10.6 5.0 %collective-permute-start.2 = (bf16[2,12,256,64]{2,3,1,0:T(8,128)(2,1)}, bf16[2,12,256,64]{2,3,1,0:T(8,128)(2,1)S(1)}, u32[]{:S(2)}, u32[]{:S(2)}) collective-permute-start(bf16[2,12,256,64]{2,3,1,0:T(8,128)(2,1)} %pad_maximum_fusion.5), channel_id=1, source_target_pairs={{0,8},{2,10},{4,12},{6,14},{8,16},{10,18},{12,20},{14,22},{16,24},... | collective-permute-start | bytes 2359304 | tf_op jit(solution)/shard_map/ppermute | solution.py:18
  15.6 3.5 %collective-permute-start = (bf16[2,12,256,64]{2,3,1,0:T(8,128)(2,1)}, bf16[2,12,256,64]{2,3,1,0:T(8,128)(2,1)S(1)}, u32[]{:S(2)}, u32[]{:S(2)}) collective-permute-start(bf16[2,12,256,64]{2,3,1,0:T(8,128)(2,1)} %pad_maximum_fusion.5), channel_id=1, source_target_pairs={{0,4},{2,6},{4,8},{6,10},{8,12},{10,14},{12,16},{14,18},{16,20},{1... | collective-permute-start | bytes 2359304 | tf_op jit(solution)/shard_map/ppermute | solution.py:18
  19.1 5.1 %all_gather.6 = bf16[48,1536]{1,0:T(8,128)(2,1)} all-gather(bf16[48,768]{1,0:T(8,128)(2,1)S(1)} %copy-done.45), channel_id=1, replica_groups=mesh['seq'=16,'dp'=2] {'dp'}, dimensions={1}, use_global_device_ids=true | all-gather | bytes 221184 | tf_op jit(solution)/shard_map/all_gather | solution.py:114
  28.3 1.9 compare_and_fusion.3
  30.2 3.2 %collective-permute-done.2 = bf16[2,12,256,64]{2,3,1,0:T(8,128)(2,1)S(1)} collective-permute-done((bf16[2,12,256,64]{2,3,1,0:T(8,128)(2,1)}, bf16[2,12,256,64]{2,3,1,0:T(8,128)(2,1)S(1)}, u32[]{:S(2)}, u32[]{:S(2)}) %collective-permute-start.2) | collective-permute-done | bytes 786464 | tf_op jit(solution)/shard_map/ppermute | solution.py:18
  33.3 4.1 %collective-permute-done = bf16[2,12,256,64]{2,3,1,0:T(8,128)(2,1)S(1)} collective-permute-done((bf16[2,12,256,64]{2,3,1,0:T(8,128)(2,1)}, bf16[2,12,256,64]{2,3,1,0:T(8,128)(2,1)S(1)}, u32[]{:S(2)}, u32[]{:S(2)}) %collective-permute-start) | collective-permute-done | bytes 786464 | tf_op jit(solution)/shard_map/ppermute | solution.py:18
  37.4 1.4 broadcast_select_fusion.1
  38.8 2.3 %select_reduce_fusion = (f32[12,256]{1,0:T(8,128)S(1)}, f32[12,256,256]{1,2,0:T(8,128)}) fusion(pred[256,256]{0,1:T(8,128)(4,1)S(1)} %get-tuple-element.58, bf16[12,256,64]{1,2,0:T(8,128)(2,1)S(1)} %bitcast.279, bf16[12,256,64]{1,2,0:T(8,128)(2,1)S(1)} %bitcast.294), kind=kOutput, calls=%fused_computation.31 | convolution fusion | flops 103019520 | bytes 4009984 | tf_op jit(solution)/shard_map/hqe,hke->hqk/dot_general | solution.py:135
  41.6 1.6 fusion.9
  44.0 2.1 fusion.10
  46.9 1.6 copy-done.2
  48.5 4.1 %fusion.20 = (f32[12,256]{1,0:T(8,128)S(1)}, f32[12,256]{1,0:T(8,128)S(1)}, f32[12,256]{1,0:T(8,128)S(1)}, f32[12,256]{1,0:T(8,128)S(1)}, f32[12,256]{1,0:T(8,128)S(1)}) fusion(f32[12,256,256]{2,1,0:T(8,128)S(1)} %get-tuple-element.68, f32[12,256]{1,0:T(8,128)S(1)} %maximum_maximum_fusion, pred[256,256]{0,1:T(8,128)(4,1)S(1)} %copy-done.35, ...), kind=kLoop, calls=%fused_computation.43 | loop fusion | flops 19645440 | bytes 16130048 | tf_op jit(solution)/shard_map/reduce_sum | solution.py:148
  54.9 1.9 fusion.55
  57.7 1.8 fusion.113
  60.3 2.9 %fusion.110 = f32[768,1536]{1,0:T(8,128)} fusion(bf16[256,768]{0,1:T(8,128)(2,1)S(1)} %bitcast.300, bf16[1,256,1536]{2,1,0:T(8,128)(2,1)S(1)} %copy-done), kind=kOutput, calls=%fused_computation.123 | convolution fusion | flops 603979776 | bytes 5898240 | tf_op jit(solution)/shard_map/dot_general | solution.py:169
  63.2 6.9 %all-gather.2.cloned.1.call-done = bf16[768,1536]{1,0:T(8,128)(2,1)} async-done(((bf16[48,1536]{1,0:T(8,128)(2,1)}), bf16[768,1536]{1,0:T(8,128)(2,1)}) %all-gather.2.cloned.1.call-update) | async-done | bytes 2359312 | tf_op jit(solution)/shard_map/all_gather | solution.py:115
  70.1 3.2 %convolution_convert_fusion.1 = bf16[256,768]{1,0:T(8,128)(2,1)} fusion(bf16[768,1536]{1,0:T(8,128)(2,1)} %all-gather.2.cloned.1.call-done, bf16[1,256,1536]{2,1,0:T(8,128)(2,1)S(1)} %copy-done), kind=kOutput, calls=%fused_computation.119 | convolution fusion | flops 604176384 | bytes 3538944 | tf_op jit(solution)/shard_map/dot_general | solution.py:165
  73.3 1.2 copy.88
  74.5 2.8 %fusion.73 = f32[1,12,256,64]{2,3,1,0:T(8,128)S(1)} fusion(bf16[12,256,64]{1,2,0:T(8,128)(2,1)S(1)} %bitcast.302, f32[12,256,256]{1,2,0:T(8,128)} %get-tuple-element.66, f32[12,256]{1,0:T(8,128)} %get-tuple-element.42, pred[256,256]{0,1:T(8,128)(4,1)} %copy-done.42), kind=kOutput, calls=%fused_computation.94 | convolution fusion | flops 103809024 | bytes 4403200 | tf_op jit(solution)/shard_map/hqk,hqe->hke/dot_general | solution.py:206
  88.3 2.2 %multiply_convert_fusion.2 = bf16[12,256,256]{1,2,0:T(8,128)(2,1)S(1)} fusion(f32[12,256,256]{2,1,0:T(8,128)S(1)} %copy-done.7, bf16[12,256,64]{1,2,0:T(8,128)(2,1)} %bitcast.310, f32[12,256]{1,0:T(8,128)S(1)} %multiply_reduce_fusion, f32[12,256]{1,0:T(8,128)S(1)} %copy-done.47, pred[256,256]{0,1:T(8,128)(4,1)S(1)} %copy-done.39, ...), kind=kOutput, calls=%fused_computation.19 | convolution fusion | flops 105381888 | bytes 5603328 | tf_op jit(solution)/shard_map/hqe,hke->hqk/dot_general | solution.py:194
  91.1 1.3 multiply_convert_fusion.3
  93.1 2.1 multiply_convert_fusion.4
  96.4 1.4 pad_maximum_fusion.2
  97.8 1.3 pad_maximum_fusion.4
  99.1 1.3 pad_maximum_fusion.1
  100.6 1.3 pad_maximum_fusion.3
  101.9 1.9 constant_dynamic-slice_fusion.3
  103.8 1.6 copy.145
  106.1 1.8 fusion.152
  107.9 2.1 fusion.117
  110.0 1.8 fusion.120
  111.8 2.2 %bitcast_add_fusion = f32[2,2,2,48,1536]{4,3,0,1,2:T(8,128)S(1)} fusion(f32[2,2,2,48,1536]{4,3,0,1,2:T(8,128)} %collective-permute-done.8, f32[2,2,2,1,48,1536]{5,4,3,2,1,0:T(8,128)S(1)} %copy-done.12), kind=kLoop, calls=%fused_computation.39 | loop fusion | flops 589824 | bytes 7077888 | tf_op jit(solution)/shard_map/add | solution.py:42
  114.1 18.0 %collective-permute-start.9 = (bf16[2,2,48,1536]{3,2,0,1:T(8,128)(2,1)S(1)}, bf16[2,2,48,1536]{3,2,0,1:T(8,128)(2,1)S(1)}, u32[]{:S(2)}, u32[]{:S(2)}) collective-permute-start(bf16[2,2,48,1536]{3,2,0,1:T(8,128)(2,1)S(1)} %fusion.114), channel_id=1, source_target_pairs={{0,4},{2,6},{4,0},{6,2},{8,12},{10,14},{12,8},{14,10},{16,20},{18,... | collective-permute-start | bytes 1769480 | tf_op jit(solution)/shard_map/ppermute | solution.py:41
  132.5 1.4 fusion.109
  133.9 11.8 %collective-permute-done.9 = bf16[2,2,48,1536]{3,2,0,1:T(8,128)(2,1)S(1)} collective-permute-done((bf16[2,2,48,1536]{3,2,0,1:T(8,128)(2,1)S(1)}, bf16[2,2,48,1536]{3,2,0,1:T(8,128)(2,1)S(1)}, u32[]{:S(2)}, u32[]{:S(2)}) %collective-permute-start.9) | collective-permute-done | bytes 589856 | tf_op jit(solution)/shard_map/ppermute | solution.py:41
  145.9 4.6 %collective-permute-start.10 = (bf16[2,48,1536]{2,1,0:T(8,128)(2,1)S(1)}, bf16[2,48,1536]{2,1,0:T(8,128)(2,1)}, u32[]{:S(2)}, u32[]{:S(2)}) collective-permute-start(bf16[2,48,1536]{2,1,0:T(8,128)(2,1)S(1)} %fusion.122), channel_id=1, source_target_pairs={{0,8},{2,10},{4,12},{6,14},{8,0},{10,2},{12,4},{14,6},{16,24},{18,... | collective-permute-start | bytes 884744 | tf_op jit(solution)/shard_map/ppermute | solution.py:41
  150.5 1.9 add_convert_fusion.2
  152.4 1.3 collective-permute-start.6
  153.7 1.3 collective-permute-start.7
  155.0 1.7 fusion.12
  158.7 7.5 %collective-permute-start.11 = (bf16[48,1536]{1,0:T(8,128)(2,1)S(1)}, bf16[48,1536]{1,0:T(8,128)(2,1)S(1)}, u32[]{:S(2)}, u32[]{:S(2)}) collective-permute-start(bf16[48,1536]{1,0:T(8,128)(2,1)S(1)} %fusion.124), channel_id=1, source_target_pairs={{0,16},{2,18},{4,20},{6,22},{8,24},{10,26},{12,28},{14,30},{16,0},... | collective-permute-start | bytes 442376 | tf_op jit(solution)/shard_map/ppermute | solution.py:41
  166.1 7.3 %collective-permute-done.6 = bf16[2,12,256,64]{2,3,1,0:T(8,128)(2,1)} collective-permute-done((bf16[2,12,256,64]{2,3,1,0:T(8,128)(2,1)}, bf16[2,12,256,64]{2,3,1,0:T(8,128)(2,1)}, u32[]{:S(2)}, u32[]{:S(2)}) %collective-permute-start.6) | collective-permute-done | bytes 786464 | tf_op jit(solution)/shard_map/ppermute | solution.py:18
  173.4 17.7 %collective-permute-done.7 = bf16[2,12,256,64]{2,3,1,0:T(8,128)(2,1)} collective-permute-done((bf16[2,12,256,64]{2,3,1,0:T(8,128)(2,1)}, bf16[2,12,256,64]{2,3,1,0:T(8,128)(2,1)}, u32[]{:S(2)}, u32[]{:S(2)}) %collective-permute-start.7) | collective-permute-done | bytes 786464 | tf_op jit(solution)/shard_map/ppermute | solution.py:18
  191.1 2.4 %add_convert_fusion = bf16[2,12,256,64]{2,3,1,0:T(8,128)(2,1)S(1)} fusion(bf16[2,12,256,64]{2,3,1,0:T(8,128)(2,1)} %collective-permute-done.7, bf16[2,12,256,64]{2,3,1,0:T(8,128)(2,1)} %collective-permute-done.6, f32[2,12,256,64]{2,3,1,0:T(8,128)S(1)} %pad_maximum_fusion, f32[2,12,256,64]{2,3,1,0:T(8,128)} %copy-done.22, pred[]{:T(512)S(6)} %eq.96), kind=kLoop, calls=%fused_computation.62 | loop fusion | flops 2752512 | bytes 5505025 | tf_op jit(solution)/shard_map/convert.1
  193.6 7.0 %collective-permute-done.11 = bf16[48,1536]{1,0:T(8,128)(2,1)S(1)} collective-permute-done((bf16[48,1536]{1,0:T(8,128)(2,1)S(1)}, bf16[48,1536]{1,0:T(8,128)(2,1)S(1)}, u32[]{:S(2)}, u32[]{:S(2)}) %collective-permute-start.11) | collective-permute-done | bytes 147488 | tf_op jit(solution)/shard_map/ppermute | solution.py:41
  201.1 1.9 collective-permute-start.12
  204.9 1.4 collective-permute-done.12
  (165 shorter events, 32.0 us)
Async XLA Ops:
  7.2 53.1 %copy-start = (bf16[1,256,1536]{2,1,0:T(8,128)(2,1)S(1)}, bf16[1,256,1536]{2,1,0:T(8,128)(2,1)}, u32[]{:S(2)}) copy-start(bf16[1,256,1536]{2,1,0:T(8,128)(2,1)} %param.9) | copy-start | bytes 2359300
  7.2 11.9 %copy-start.45 = (bf16[48,768]{1,0:T(8,128)(2,1)S(1)}, bf16[48,768]{1,0:T(8,128)(2,1)}, u32[]{:S(2)}) copy-start(bf16[48,768]{1,0:T(8,128)(2,1)} %param.11) | copy-start | bytes 221188
  7.2 17.1 %copy-start.48 = (s32[1,8]{1,0:T(1,128)S(1)}, s32[1,8]{1,0:T(1,128)}, u32[]{:S(2)}) copy-start(s32[1,8]{1,0:T(1,128)} %param.10) | copy-start | bytes 100
  7.2 62.9 %all-gather.2.cloned.1.call-start = ((), (), s32[]{:S(2)}) async-start(), calls=%async_computation | async-start | bytes 2506752 | tf_op jit(solution)/shard_map/all_gather | solution.py:115
  10.6 22.7 %collective-permute-start.2 = (bf16[2,12,256,64]{2,3,1,0:T(8,128)(2,1)}, bf16[2,12,256,64]{2,3,1,0:T(8,128)(2,1)S(1)}, u32[]{:S(2)}, u32[]{:S(2)}) collective-permute-start(bf16[2,12,256,64]{2,3,1,0:T(8,128)(2,1)} %pad_maximum_fusion.5), channel_id=1, source_target_pairs={{0,8},{2,10},{4,12},{6,14},{8,16},{10,18},{12,20},{14,22},{16,24},... | collective-permute-start | bytes 2359304 | tf_op jit(solution)/shard_map/ppermute | solution.py:18
  15.6 21.8 %collective-permute-start = (bf16[2,12,256,64]{2,3,1,0:T(8,128)(2,1)}, bf16[2,12,256,64]{2,3,1,0:T(8,128)(2,1)S(1)}, u32[]{:S(2)}, u32[]{:S(2)}) collective-permute-start(bf16[2,12,256,64]{2,3,1,0:T(8,128)(2,1)} %pad_maximum_fusion.5), channel_id=1, source_target_pairs={{0,4},{2,6},{4,8},{6,10},{8,12},{10,14},{12,16},{14,18},{16,20},{1... | collective-permute-start | bytes 2359304 | tf_op jit(solution)/shard_map/ppermute | solution.py:18
  30.2 8.6 %copy-start.42 = (pred[256,256]{0,1:T(8,128)(4,1)}, pred[256,256]{0,1:T(8,128)(4,1)S(1)}, u32[]{:S(2)}) copy-start(pred[256,256]{0,1:T(8,128)(4,1)S(1)} %get-tuple-element.58) | copy-start | bytes 196612
  37.4 49.1 %copy-start.23 = (bf16[2,12,256,64]{2,3,1,0:T(8,128)(2,1)}, bf16[2,12,256,64]{2,3,1,0:T(8,128)(2,1)S(1)}, u32[]{:S(2)}) copy-start(bf16[2,12,256,64]{2,3,1,0:T(8,128)(2,1)S(1)} %collective-permute-done) | copy-start | bytes 2359300
  38.8 5.1 %collective-permute-start.3 = (bf16[2,12,256,64]{2,3,1,0:T(8,128)(2,1)}, bf16[2,12,256,64]{2,3,1,0:T(8,128)(2,1)}, u32[]{:S(2)}, u32[]{:S(2)}) collective-permute-start(bf16[2,12,256,64]{2,3,1,0:T(8,128)(2,1)} %get-tuple-element.51), channel_id=1, source_target_pairs={{0,2},{2,0},{4,6},{6,4},{8,10},{10,8},{12,14},{14,12},{16,18},{18,... | collective-permute-start | bytes 2359304 | tf_op jit(solution)/shard_map/ppermute | solution.py:23
  41.1 5.0 %collective-permute-start.1 = (bf16[2,12,256,64]{2,3,1,0:T(8,128)(2,1)}, bf16[2,12,256,64]{2,3,1,0:T(8,128)(2,1)S(1)}, u32[]{:S(2)}, u32[]{:S(2)}) collective-permute-start(bf16[2,12,256,64]{2,3,1,0:T(8,128)(2,1)} %get-tuple-element.50), channel_id=1, source_target_pairs={{0,2},{2,0},{4,6},{6,4},{8,10},{10,8},{12,14},{14,12},{16,18},{18,... | collective-permute-start | bytes 2359304 | tf_op jit(solution)/shard_map/ppermute | solution.py:23
  43.2 10.9 %copy-start.8 = (f32[12,256,256]{2,1,0:T(8,128)}, f32[12,256,256]{2,1,0:T(8,128)S(1)}, u32[]{:S(2)}) copy-start(f32[12,256,256]{2,1,0:T(8,128)S(1)} %get-tuple-element.64) | copy-start | bytes 9437188
  43.2 2.9 %copy-start.35 = (pred[256,256]{0,1:T(8,128)(4,1)S(1)}, pred[256,256]{0,1:T(8,128)(4,1)}, u32[]{:S(2)}) copy-start(pred[256,256]{0,1:T(8,128)(4,1)} %get-tuple-element.54) | copy-start | bytes 196612
  43.9 12.9 %copy-start.6 = (f32[12,256,256]{2,1,0:T(8,128)}, f32[12,256,256]{2,1,0:T(8,128)S(1)}, u32[]{:S(2)}) copy-start(f32[12,256,256]{2,1,0:T(8,128)S(1)} %get-tuple-element.60) | copy-start | bytes 9437188
  44.0 4.5 %copy-start.2 = (f32[12,256,256]{1,2,0:T(8,128)S(1)}, f32[12,256,256]{1,2,0:T(8,128)}, u32[]{:S(2)}) copy-start(f32[12,256,256]{1,2,0:T(8,128)} %get-tuple-element.66) | copy-start | bytes 9437188
  44.0 4.5 %copy-start.40 = (pred[256,256]{0,1:T(8,128)(4,1)S(1)}, pred[256,256]{0,1:T(8,128)(4,1)}, u32[]{:S(2)}) copy-start(pred[256,256]{0,1:T(8,128)(4,1)} %get-tuple-element.55) | copy-start | bytes 196612
  44.0 4.5 %copy-start.43 = (pred[256,256]{0,1:T(8,128)(4,1)S(1)}, pred[256,256]{0,1:T(8,128)(4,1)}, u32[]{:S(2)}) copy-start(pred[256,256]{0,1:T(8,128)(4,1)} %copy-done.42) | copy-start | bytes 196612
  46.1 8.8 %copy-start.4 = (f32[12,256,256]{2,1,0:T(8,128)}, f32[12,256,256]{2,1,0:T(8,128)S(1)}, u32[]{:S(2)}) copy-start(f32[12,256,256]{2,1,0:T(8,128)S(1)} %get-tuple-element.62) | copy-start | bytes 9437188
  46.1 11.5 %copy-start.30 = (bf16[2,12,256,64]{2,3,1,0:T(8,128)(2,1)}, bf16[2,12,256,64]{2,3,1,0:T(8,128)(2,1)S(1)}, u32[]{:S(2)}) copy-start(bf16[2,12,256,64]{2,3,1,0:T(8,128)(2,1)S(1)} %collective-permute-done.1) | copy-start | bytes 2359300
  46.9 10.8 %copy-start.10 = (f32[12,256,256]{2,1,0:T(8,128)}, f32[12,256,256]{2,1,0:T(8,128)S(1)}, u32[]{:S(2)}) copy-start(f32[12,256,256]{2,1,0:T(8,128)S(1)} %get-tuple-element.68) | copy-start | bytes 9437188
  73.3 4.0 %copy-start.36 = (pred[256,256]{0,1:T(8,128)(4,1)S(1)}, pred[256,256]{0,1:T(8,128)(4,1)}, u32[]{:S(2)}) copy-start(pred[256,256]{0,1:T(8,128)(4,1)} %get-tuple-element.54) | copy-start | bytes 196612
  73.3 4.0 %copy-start.46 = (f32[12,256]{1,0:T(8,128)S(1)}, f32[12,256]{1,0:T(8,128)}, u32[]{:S(2)}) copy-start(f32[12,256]{1,0:T(8,128)} %get-tuple-element.42) | copy-start | bytes 36868
  74.5 12.0 %copy-start.27 = (bf16[256,768]{0,1:T(8,128)(2,1)}, bf16[256,768]{0,1:T(8,128)(2,1)S(1)}, u32[]{:S(2)}) copy-start(bf16[256,768]{0,1:T(8,128)(2,1)S(1)} %copy.88) | copy-start | bytes 1179652
  74.5 3.0 %copy-start.11 = (f32[12,256,256]{2,1,0:T(8,128)S(1)}, f32[12,256,256]{2,1,0:T(8,128)}, u32[]{:S(2)}) copy-start(f32[12,256,256]{2,1,0:T(8,128)} %copy-done.10) | copy-start | bytes 9437188
  86.5 9.3 %copy-start.17 = (bf16[12,256,256]{1,2,0:T(8,128)(2,1)}, bf16[12,256,256]{1,2,0:T(8,128)(2,1)S(1)}, u32[]{:S(2)}) copy-start(bf16[12,256,256]{1,2,0:T(8,128)(2,1)S(1)} %multiply_convert_fusion) | copy-start | bytes 4718596
  87.6 2.9 %copy-start.18 = (bf16[12,256,256]{1,2,0:T(8,128)(2,1)}, bf16[12,256,256]{1,2,0:T(8,128)(2,1)S(1)}, u32[]{:S(2)}) copy-start(bf16[12,256,256]{1,2,0:T(8,128)(2,1)S(1)} %multiply_convert_fusion.1) | copy-start | bytes 4718596
  88.2 2.9 %copy-start.28 = (bf16[256,768]{0,1:T(8,128)(2,1)S(1)}, bf16[256,768]{0,1:T(8,128)(2,1)}, u32[]{:S(2)}) copy-start(bf16[256,768]{0,1:T(8,128)(2,1)} %copy-done.27) | copy-start | bytes 1179652
  88.3 2.9 %copy-start.31 = (bf16[2,12,256,64]{2,3,1,0:T(8,128)(2,1)S(1)}, bf16[2,12,256,64]{2,3,1,0:T(8,128)(2,1)}, u32[]{:S(2)}) copy-start(bf16[2,12,256,64]{2,3,1,0:T(8,128)(2,1)} %copy-done.30) | copy-start | bytes 2359300
  88.3 2.9 %copy-start.37 = (pred[256,256]{0,1:T(8,128)(4,1)S(1)}, pred[256,256]{0,1:T(8,128)(4,1)}, u32[]{:S(2)}) copy-start(pred[256,256]{0,1:T(8,128)(4,1)} %get-tuple-element.54) | copy-start | bytes 196612
  96.4 5.5 %slice-start = ((s8[4718592]{0:T(1024)(128)(4,1)}), s8[4194304]{0:T(1024)(128)(4,1)S(1)}, s32[]{:S(2)}) async-start(s8[4718592]{0:T(1024)(128)(4,1)} %bitcast.289), calls=%async_computation.1 | async-start | bytes 8388608
  99.1 2.8 %slice-start.1 = ((s8[4718592]{0:T(1024)(128)(4,1)}), s8[524288]{0:T(1024)(128)(4,1)S(1)}, s32[]{:S(2)}) async-start(s8[4718592]{0:T(1024)(128)(4,1)} %bitcast.289), calls=%async_computation.2 | async-start | bytes 1048576
  105.4 6.4 %collective-permute-start.8 = (f32[2,2,2,48,1536]{4,3,0,1,2:T(8,128)}, f32[2,2,2,48,1536]{4,3,0,1,2:T(8,128)}, u32[]{:S(2)}, u32[]{:S(2)}) collective-permute-start(f32[2,2,2,48,1536]{4,3,0,1,2:T(8,128)} %bitcast.277), channel_id=1, source_target_pairs={{0,2},{2,0},{4,6},{6,4},{8,10},{10,8},{12,14},{14,12},{16,18},{18,... | collective-permute-start | bytes 7077896 | tf_op jit(solution)/shard_map/ppermute | solution.py:41
  105.6 44.9 %collective-permute-start.4 = (f32[2,12,256,64]{2,3,1,0:T(8,128)}, f32[2,12,256,64]{2,3,1,0:T(8,128)S(1)}, u32[]{:S(2)}, u32[]{:S(2)}) collective-permute-start(f32[2,12,256,64]{2,3,1,0:T(8,128)} %pad_maximum_fusion.1), channel_id=1, source_target_pairs={{0,2},{2,0},{4,6},{6,4},{8,10},{10,8},{12,14},{14,12},{16,18},{18,... | collective-permute-start | bytes 4718600 | tf_op jit(solution)/shard_map/ppermute | solution.py:23
  105.9 44.6 %collective-permute-start.5 = (f32[2,12,256,64]{2,3,1,0:T(8,128)}, f32[2,12,256,64]{2,3,1,0:T(8,128)S(1)}, u32[]{:S(2)}, u32[]{:S(2)}) collective-permute-start(f32[2,12,256,64]{2,3,1,0:T(8,128)} %pad_maximum_fusion.3), channel_id=1, source_target_pairs={{0,2},{2,0},{4,6},{6,4},{8,10},{10,8},{12,14},{14,12},{16,18},{18,... | collective-permute-start | bytes 4718600 | tf_op jit(solution)/shard_map/ppermute | solution.py:23
  107.9 3.9 %copy-start.12 = (f32[2,2,2,1,48,1536]{5,4,3,2,1,0:T(8,128)S(1)}, f32[2,2,2,1,48,1536]{5,4,3,2,1,0:T(8,128)}, u32[]{:S(2)}) copy-start(f32[2,2,2,1,48,1536]{5,4,3,2,1,0:T(8,128)} %get-tuple-element.44) | copy-start | bytes 7077892
  111.8 20.3 %copy-start.14 = (bf16[12,256,256]{1,2,0:T(8,128)(2,1)S(1)}, bf16[12,256,256]{1,2,0:T(8,128)(2,1)}, u32[]{:S(2)}) copy-start(bf16[12,256,256]{1,2,0:T(8,128)(2,1)} %copy-done.13) | copy-start | bytes 4718596
  111.8 20.3 %copy-start.32 = (bf16[2,12,256,64]{2,3,1,0:T(8,128)(2,1)S(1)}, bf16[2,12,256,64]{2,3,1,0:T(8,128)(2,1)}, u32[]{:S(2)}) copy-start(bf16[2,12,256,64]{2,3,1,0:T(8,128)(2,1)} %copy-done.30) | copy-start | bytes 2359300
  114.0 18.4 %copy-start.16 = (bf16[12,256,256]{1,2,0:T(8,128)(2,1)S(1)}, bf16[12,256,256]{1,2,0:T(8,128)(2,1)}, u32[]{:S(2)}) copy-start(bf16[12,256,256]{1,2,0:T(8,128)(2,1)} %copy-done.15) | copy-start | bytes 4718596
  114.1 31.6 %collective-permute-start.9 = (bf16[2,2,48,1536]{3,2,0,1:T(8,128)(2,1)S(1)}, bf16[2,2,48,1536]{3,2,0,1:T(8,128)(2,1)S(1)}, u32[]{:S(2)}, u32[]{:S(2)}) collective-permute-start(bf16[2,2,48,1536]{3,2,0,1:T(8,128)(2,1)S(1)} %fusion.114), channel_id=1, source_target_pairs={{0,4},{2,6},{4,0},{6,2},{8,12},{10,14},{12,8},{14,10},{16,20},{18,... | collective-permute-start | bytes 1769480 | tf_op jit(solution)/shard_map/ppermute | solution.py:41
  133.9 16.6 %copy-start.20 = (f32[2,12,256,64]{2,3,1,0:T(8,128)S(1)}, f32[2,12,256,64]{2,3,1,0:T(8,128)}, u32[]{:S(2)}) copy-start(f32[2,12,256,64]{2,3,1,0:T(8,128)} %pad_maximum_fusion.2) | copy-start | bytes 4718596
  133.9 16.6 %copy-start.21 = (f32[2,12,256,64]{2,3,1,0:T(8,128)S(1)}, f32[2,12,256,64]{2,3,1,0:T(8,128)}, u32[]{:S(2)}) copy-start(f32[2,12,256,64]{2,3,1,0:T(8,128)} %pad_maximum_fusion.4) | copy-start | bytes 4718596
  145.9 9.1 %copy-start.25 = (bf16[256,12,64]{0,2,1:T(8,128)(2,1)S(1)}, bf16[256,12,64]{0,2,1:T(8,128)(2,1)}, u32[]{:S(2)}) copy-start(bf16[256,12,64]{0,2,1:T(8,128)(2,1)} %copy-done.24) | copy-start | bytes 1179652
  145.9 9.1 %copy-start.26 = (bf16[768,1536]{1,0:T(8,128)(2,1)S(1)}, bf16[768,1536]{1,0:T(8,128)(2,1)}, u32[]{:S(2)}) copy-start(bf16[768,1536]{1,0:T(8,128)(2,1)} %all-gather.2.cloned.1.call-done) | copy-start | bytes 7077892
  145.9 11.7 %collective-permute-start.10 = (bf16[2,48,1536]{2,1,0:T(8,128)(2,1)S(1)}, bf16[2,48,1536]{2,1,0:T(8,128)(2,1)}, u32[]{:S(2)}, u32[]{:S(2)}) collective-permute-start(bf16[2,48,1536]{2,1,0:T(8,128)(2,1)S(1)} %fusion.122), channel_id=1, source_target_pairs={{0,8},{2,10},{4,12},{6,14},{8,0},{10,2},{12,4},{14,6},{16,24},{18,... | collective-permute-start | bytes 884744 | tf_op jit(solution)/shard_map/ppermute | solution.py:41
  152.4 21.0 %collective-permute-start.6 = (bf16[2,12,256,64]{2,3,1,0:T(8,128)(2,1)}, bf16[2,12,256,64]{2,3,1,0:T(8,128)(2,1)}, u32[]{:S(2)}, u32[]{:S(2)}) collective-permute-start(bf16[2,12,256,64]{2,3,1,0:T(8,128)(2,1)} %get-tuple-element.46), channel_id=1, source_target_pairs={{4,0},{6,2},{8,4},{10,6},{12,8},{14,10},{16,12},{18,14},{20,16},{2... | collective-permute-start | bytes 2359304 | tf_op jit(solution)/shard_map/ppermute | solution.py:18
  153.7 37.4 %collective-permute-start.7 = (bf16[2,12,256,64]{2,3,1,0:T(8,128)(2,1)}, bf16[2,12,256,64]{2,3,1,0:T(8,128)(2,1)}, u32[]{:S(2)}, u32[]{:S(2)}) collective-permute-start(bf16[2,12,256,64]{2,3,1,0:T(8,128)(2,1)} %get-tuple-element.47), channel_id=1, source_target_pairs={{8,0},{10,2},{12,4},{14,6},{16,8},{18,10},{20,12},{22,14},{24,16},... | collective-permute-start | bytes 2359304 | tf_op jit(solution)/shard_map/ppermute | solution.py:18
  158.7 41.9 %collective-permute-start.11 = (bf16[48,1536]{1,0:T(8,128)(2,1)S(1)}, bf16[48,1536]{1,0:T(8,128)(2,1)S(1)}, u32[]{:S(2)}, u32[]{:S(2)}) collective-permute-start(bf16[48,1536]{1,0:T(8,128)(2,1)S(1)} %fusion.124), channel_id=1, source_target_pairs={{0,16},{2,18},{4,20},{6,22},{8,24},{10,26},{12,28},{14,30},{16,0},... | collective-permute-start | bytes 442376 | tf_op jit(solution)/shard_map/ppermute | solution.py:41
  191.1 15.9 %copy-start.1 = (bf16[1,256,1536]{2,1,0:T(8,128)(2,1)S(1)}, bf16[1,256,1536]{2,1,0:T(8,128)(2,1)}, u32[]{:S(2)}) copy-start(bf16[1,256,1536]{2,1,0:T(8,128)(2,1)} %param.9) | copy-start | bytes 2359300
  201.1 5.2 %collective-permute-start.12 = (f32[768,48]{0,1:T(8,128)S(1)}, f32[768,48]{0,1:T(8,128)S(1)}, u32[]{:S(2)}, u32[]{:S(2)}) collective-permute-start(f32[768,48]{0,1:T(8,128)S(1)} %bitcast.316), channel_id=1, source_target_pairs={{0,1},{1,0},{2,3},{3,2},{4,5},{5,4},{6,7},{7,6},{8,9},{9,8},{10,11... | collective-permute-start | bytes 442376 | tf_op jit(solution)/shard_map/ppermute | solution.py:41
  (17 other events, 32.9 us)
Sparse Core Ops, SparseCore 0:
  24.3 45.6 all-gather.1

commit v7 on v5

--- a/solution.py
+++ b/solution.py
@@ -12,7 +12,7 @@
 MASKED_SCORE = -1e30
 
 
-SEQ = ("chip", "core")
+SEQ = ("zc", "yc", "core")
 
 
 def axis_count(axis):
@@ -160,14 +160,20 @@
     partial_weight = lax.dot_general(
         attended, upstream, (((0,), (0,)), ((), ())), preferred_element_type=jnp.float32
     )
-    chip_count = lax.axis_size("chip")
-    halves = partial_weight.reshape(chip_count, 2, -1, partial_weight.shape[1])
-    keep = lax.dynamic_index_in_dim(halves, core, 1, keepdims=False)
-    give = lax.dynamic_index_in_dim(halves, 1 - core, 1, keepdims=False)
+    columns = partial_weight.shape[1]
+    quarters = partial_weight.reshape(lax.axis_size("zc"), 2, 2, -1, columns)
+    keep = lax.dynamic_index_in_dim(quarters, core, 2, keepdims=False)
+    give = lax.dynamic_index_in_dim(quarters, 1 - core, 2, keepdims=False)
     core_sum = keep + swap_partner(give, SEQ)
+    row_pair = lax.axis_index("yc")
+    keep = lax.dynamic_index_in_dim(core_sum, row_pair, 1, keepdims=False)
+    give = lax.dynamic_index_in_dim(core_sum, 1 - row_pair, 1, keepdims=False)
+    pair_sum = keep + lax.ppermute(give.astype(jnp.bfloat16), "yc", [(0, 1), (1, 0)]).astype(
+        jnp.float32
+    )
     row_share = lax.psum_scatter(
-        core_sum.reshape(-1, partial_weight.shape[1]).astype(jnp.bfloat16),
-        "chip",
+        pair_sum.reshape(-1, columns).astype(jnp.bfloat16),
+        "zc",
         scatter_dimension=0,
         tiled=True,
     )
@@ -225,8 +231,8 @@
     at = names.index("seq")
     shape = mesh.devices.shape
     split_mesh = jax.sharding.Mesh(
-        mesh.devices.reshape(shape[:at] + (shape[at] // 2, 2) + shape[at + 1 :]),
-        tuple(names[:at] + ["chip", "core"] + names[at + 1 :]),
+        mesh.devices.reshape(shape[:at] + (shape[at] // 4, 2, 2) + shape[at + 1 :]),
+        tuple(names[:at] + ["zc", "yc", "core"] + names[at + 1 :]),
     )
     return jax.shard_map(
         local,

time: 188 us -> 200 us (1.064)
  matrix products: 37.5 us -> 44.6 us
  other arithmetic: 22.1 us -> 26.9 us
  waiting for transfers between devices: 77.3 us -> 73.1 us
  local copies, waits for them, and re-layouts: 16.5 us -> 19.1 us
  starting transfers between devices: 11.3 us -> 13.5 us
    ppermute x4, waiting for transfers between devices: 28.8 us -> 47.6 us  [shift_up(): return lax.ppermute(block, axis, route)]
    reduce_scatter x1, waiting for transfers between devices: 37.2 us -> 20.6 us  [local(): lax.psum_scatter(pair_sum.reshape(-1, columns).astype(jnp.bfloat16), 'zc'...]
    reduce_scatter x1, waiting for transfers between devices: 6.42 us -> 0.01 us  [local(): lax.psum_scatter(row_share.astype(jnp.float32), 'dp', scatter_dimension=1...]
    dot_general x5, matrix products: 3.73 us -> 7.48 us  [local(): jnp.einsum('hqk,hke->hqe', score_grad, key_block, preferred_element_type=...]
    add x0 -> x1, other arithmetic: none -> 2.75 us  [local(): core_sum = keep + swap_partner(give, SEQ)]
    another operation x2, other arithmetic: 0.29 us -> 2.86 us  [local(): parts[dist] = jnp.stack([key_part, value_part])]
    ppermute x4, starting transfers between devices: 10.1 us -> 12.4 us  [shift_up(): return lax.ppermute(block, axis, route)]
    unnamed x90 -> x104, local copies, waits for them, and re-layouts: 14.5 us -> 16.3 us
  transfers between devices with their start and end apart: 12 -> 13, of which waited for: 5 -> 6; matrix products, arithmetic and copies ran while one was open for 35% -> 39% of each run, Pallas kernels for 0% -> 0%
where the time goes in v7:
time: 200 us; the launch traced here: 199 us
  waiting for transfers between devices  73.1 us (37%)
  matrix products  44.6 us (22%)
  other arithmetic  26.9 us (13%)
  local copies, waits for them, and re-layouts  19.1 us (10%)
  between operations  16.2 us (8%)
  starting transfers between devices  13.5 us (7%)
  blocking collectives  5.14 us (3%)
    ppermute x4, waiting for transfers between devices, shift_up(): return lax.ppermute(block, axis, route)  47.6 us
    reduce_scatter x1, waiting for transfers between devices, local(): lax.psum_scatter(pair_sum.reshape(-1, columns).astype(jnp.bfloat16), 'zc'...  20.6 us
    unnamed x104, local copies, waits for them, and re-layouts  16.3 us
    ppermute x4, starting transfers between devices, shift_up(): return lax.ppermute(block, axis, route)  12.4 us
    dot_general x5, matrix products, local(): jnp.einsum('hqk,hqe->hke', prob_back, grad_heads, preferred_element_type=...  8.25 us
    dot_general x5, matrix products, local(): jnp.einsum('hqe,hke->hqk', query_heads, held[dist][0], preferred_element_...  7.48 us
    dot_general x5, matrix products, local(): jnp.einsum('hqk,hke->hqe', score_grad, key_block, preferred_element_type=...  7.48 us
    dot_general x5, matrix products, local(): jnp.einsum('hqe,hke->hqk', grad_heads, value_block, preferred_element_typ...  6.56 us
  transfers between devices with their start and end apart: 13, of which 6 were waited for; matrix products, arithmetic and copies ran while one was open for 39% of the time, Pallas kernels for 0%

profile of v7, /device:TPU:4, one launch (start us, length us, event | category | flops | bytes accessed | tf_op | source)
XLA Modules:
  0.0 198.6 jit_solution(2122614230703928256)
XLA Ops:
  8.1 1.2 copy.80
  9.3 1.2 copy.78
  11.4 3.5 %collective-permute-start.2 = (bf16[2,12,256,64]{2,3,1,0:T(8,128)(2,1)}, bf16[2,12,256,64]{2,3,1,0:T(8,128)(2,1)S(1)}, u32[]{:S(2)}, u32[]{:S(2)}) collective-permute-start(bf16[2,12,256,64]{2,3,1,0:T(8,128)(2,1)} %pad_maximum_fusion.2), channel_id=1, source_target_pairs={{0,8},{2,10},{4,12},{6,14},{8,16},{10,18},{12,20},{14,22},{16,24},... | collective-permute-start | bytes 2359304 | tf_op jit(solution)/shard_map/ppermute | solution.py:30
  15.0 3.4 %collective-permute-start = (bf16[2,12,256,64]{2,3,1,0:T(8,128)(2,1)}, bf16[2,12,256,64]{2,3,1,0:T(8,128)(2,1)S(1)}, u32[]{:S(2)}, u32[]{:S(2)}) collective-permute-start(bf16[2,12,256,64]{2,3,1,0:T(8,128)(2,1)} %pad_maximum_fusion.2), channel_id=1, source_target_pairs={{0,4},{2,6},{4,8},{6,10},{8,12},{10,14},{12,16},{14,18},{16,20},{1... | collective-permute-start | bytes 2359304 | tf_op jit(solution)/shard_map/ppermute | solution.py:30
  18.4 5.1 %all_gather.6 = bf16[48,1536]{1,0:T(8,128)(2,1)} all-gather(bf16[48,768]{1,0:T(8,128)(2,1)S(1)} %copy-done.47), channel_id=1, replica_groups=mesh['zc'=4,'yc'=2,'core'=2,'dp'=2] {'dp'}, dimensions={1}, use_global_device_ids=true | all-gather | bytes 221184 | tf_op jit(solution)/shard_map/all_gather | solution.py:105
  25.1 1.2 copy.77
  27.7 1.9 compare_and_fusion.3
  29.6 4.8 %collective-permute-done.2 = bf16[2,12,256,64]{2,3,1,0:T(8,128)(2,1)S(1)} collective-permute-done((bf16[2,12,256,64]{2,3,1,0:T(8,128)(2,1)}, bf16[2,12,256,64]{2,3,1,0:T(8,128)(2,1)S(1)}, u32[]{:S(2)}, u32[]{:S(2)}) %collective-permute-start.2) | collective-permute-done | bytes 786464 | tf_op jit(solution)/shard_map/ppermute | solution.py:30
  34.4 23.9 %collective-permute-done = bf16[2,12,256,64]{2,3,1,0:T(8,128)(2,1)S(1)} collective-permute-done((bf16[2,12,256,64]{2,3,1,0:T(8,128)(2,1)}, bf16[2,12,256,64]{2,3,1,0:T(8,128)(2,1)S(1)}, u32[]{:S(2)}, u32[]{:S(2)}) %collective-permute-start) | collective-permute-done | bytes 786464 | tf_op jit(solution)/shard_map/ppermute | solution.py:30
  58.3 1.4 broadcast_select_fusion.1
  59.7 2.4 %select_reduce_fusion = (f32[12,256]{1,0:T(8,128)S(1)}, f32[12,256,256]{1,2,0:T(8,128)}) fusion(pred[256,256]{0,1:T(8,128)(4,1)S(1)} %get-tuple-element.42, bf16[12,256,64]{1,2,0:T(8,128)(2,1)S(1)} %bitcast.265, bf16[12,256,64]{1,2,0:T(8,128)(2,1)S(1)} %bitcast.277), kind=kOutput, calls=%fused_computation.31 | convolution fusion | flops 103019520 | bytes 4009984 | tf_op jit(solution)/shard_map/hqe,hke->hqk/dot_general | solution.py:126
  62.6 1.6 fusion.11
  65.0 2.1 %fusion.10 = (f32[12,256]{1,0:T(8,128)S(1)}, f32[12,256,256]{2,1,0:T(8,128)S(1)}) fusion(pred[256,256]{0,1:T(8,128)(4,1)S(1)} %copy-done.41, bf16[12,256,64]{1,2,0:T(8,128)(2,1)S(1)} %bitcast.268, bf16[2,12,256,64]{2,3,1,0:T(8,128)(2,1)} %collective-permute-done.3), kind=kOutput, calls=%fused_computation.29 | convolution fusion | flops 103019520 | bytes 4009984 | tf_op jit(solution)/shard_map/hqe,hke->hqk/dot_general | solution.py:126
  67.9 1.6 copy-done.7
  70.4 4.1 %fusion.20 = (f32[12,256]{1,0:T(8,128)S(1)}, f32[12,256]{1,0:T(8,128)S(1)}, f32[12,256]{1,0:T(8,128)S(1)}, f32[12,256]{1,0:T(8,128)S(1)}, f32[12,256]{1,0:T(8,128)S(1)}) fusion(f32[12,256,256]{2,1,0:T(8,128)S(1)} %get-tuple-element.52, f32[12,256]{1,0:T(8,128)S(1)} %maximum_maximum_fusion, pred[256,256]{0,1:T(8,128)(4,1)S(1)} %copy-done.39, ...), kind=kLoop, calls=%fused_computation.43 | loop fusion | flops 19645440 | bytes 16130048 | tf_op jit(solution)/shard_map/reduce_sum | solution.py:139
  75.4 1.9 fusion.60
  80.0 2.1 %copy-done.2 = f32[4,2,2,48,1536]{4,3,2,1,0:T(8,128)} copy-done((f32[4,2,2,48,1536]{4,3,2,1,0:T(8,128)}, f32[4,2,2,48,1536]{4,3,2,1,0:T(8,128)S(1)}, u32[]{:S(2)}) %copy-start.2) | copy-done | bytes 4718616
  82.1 1.7 dynamic-slice_bitcast_fusion
  83.8 4.8 %collective-permute-done.8 = f32[4,2,48,1536]{3,2,1,0:T(8,128)} collective-permute-done((f32[4,2,48,1536]{3,2,1,0:T(8,128)}, f32[4,2,48,1536]{3,2,1,0:T(8,128)}, u32[]{:S(2)}, u32[]{:S(2)}) %collective-permute-start.8) | collective-permute-done | bytes 2359328 | tf_op jit(solution)/shard_map/ppermute | solution.py:34
  88.7 2.8 %bitcast_add_fusion = f32[4,2,48,1536]{3,2,1,0:T(8,128)S(1)} fusion(f32[4,2,48,1536]{3,2,1,0:T(8,128)} %collective-permute-done.8, f32[4,2,2,48,1536]{4,3,2,1,0:T(8,128)} %copy-done.2, s32[]{:T(128)S(6)} %select_n.200), kind=kLoop, calls=%fused_computation.39 | loop fusion | flops 589824 | bytes 7077892 | tf_op jit(solution)/shard_map/add | solution.py:167
  91.4 1.4 copy-done.13
  93.8 2.5 %convolution_convert_fusion.1 = bf16[256,768]{1,0:T(8,128)(2,1)S(1)} fusion(bf16[768,1536]{1,0:T(8,128)(2,1)} %all-gather.2.cloned.1.call-done, bf16[1,256,1536]{2,1,0:T(8,128)(2,1)S(1)} %copy-done), kind=kOutput, calls=%fused_computation.121 | convolution fusion | flops 604176384 | bytes 3538944 | tf_op jit(solution)/shard_map/dot_general | solution.py:156
  96.5 3.7 %fusion.78 = f32[1,12,256,64]{2,3,1,0:T(8,128)} fusion(bf16[12,256,64]{1,2,0:T(8,128)(2,1)S(1)} %bitcast.286, f32[12,256,256]{1,2,0:T(8,128)} %get-tuple-element.50, f32[12,256]{1,0:T(8,128)S(1)} %get-tuple-element.30, pred[256,256]{0,1:T(8,128)(4,1)S(1)} %copy-done.45), kind=kOutput, calls=%fused_computation.96 | convolution fusion | flops 103809024 | bytes 4403200 | tf_op jit(solution)/shard_map/hqk,hqe->hke/dot_general | solution.py:217
  100.2 1.6 fusion.84
  103.0 1.2 copy-done.10
  107.2 1.3 fusion.154
  108.5 2.1 %multiply_convert_fusion.4 = bf16[12,256,256]{1,2,0:T(8,128)(2,1)S(1)} fusion(f32[12,256,256]{2,1,0:T(8,128)S(1)} %copy-done.12, bf16[12,256,64]{1,2,0:T(8,128)(2,1)S(1)} %bitcast.292, f32[12,256]{1,0:T(8,128)S(1)} %multiply_reduce_fusion, f32[12,256]{1,0:T(8,128)S(1)} %get-tuple-element.30, pred[256,256]{0,1:T(8,128)(4,1)S(1)} %copy-done.42, ...), kind=kOutput, calls=%fused_computation.21 | convolution fusion | flops 105381888 | bytes 5595136 | tf_op jit(solution)/shard_map/hqe,hke->hqk/dot_general | solution.py:205
  111.3 1.3 pad_maximum_fusion.1
  112.8 1.1 multiply_convert_fusion.3
  114.5 1.5 pad_maximum_fusion
  116.4 1.1 multiply_convert_fusion.1
  118.1 1.1 multiply_convert_fusion.2
  119.3 1.4 fusion.121
  120.7 1.3 fusion.123
  122.6 1.3 fusion.126
  123.9 1.6 fusion.90
  125.5 2.0 %fusion.115 = bf16[4,48,1536]{2,1,0:T(8,128)(2,1)} fusion(bf16[4,48,1536]{2,1,0:T(8,128)(2,1)} %collective-permute-done.9, f32[4,2,48,1536]{3,2,1,0:T(8,128)S(1)} %copy-done.14, s32[]{:T(128)S(6)} %select_n.202), kind=kLoop, calls=%fused_computation.123 | loop fusion | flops 884736 | bytes 2359300 | tf_op jit(solution)/shard_map/convert_element_type | solution.py:175
  127.6 2.1 %fusion.94 = f32[1,12,256,64]{2,3,1,0:T(8,128)S(1)} fusion(bf16[12,256,256]{1,2,0:T(8,128)(2,1)} %copy-done.17, bf16[12,256,64]{1,2,0:T(8,128)(2,1)S(1)} %bitcast.273), kind=kOutput, calls=%fused_computation.104 | convolution fusion | flops 100859904 | bytes 2752512 | tf_op jit(solution)/shard_map/hqk,hqe->hke/dot_general | solution.py:214
  129.8 3.7 %fusion.41 = (bf16[2,12,256,64]{2,3,1,0:T(8,128)(2,1)}, bf16[2,12,256,64]{2,3,1,0:T(8,128)(2,1)}) fusion(f32[1,12,256,64]{2,3,1,0:T(8,128)} %fusion.84, f32[1,12,256,64]{2,3,1,0:T(8,128)S(1)} %fusion.96, f32[2,12,256,64]{2,3,1,0:T(8,128)} %collective-permute-done.5, f32[2,12,256,64]{2,3,1,0:T(8,128)} %collective-permute-done.4, pred[]{:T(512)S(6)} %eq.89, ...), kind=kLoop, calls=%fused_computation.62 | loop fusion | flops 3145728 | bytes 7864321 | tf_op jit(solution)/shard_map/convert_element_type | solution.py:89
  133.5 1.6 collective-permute-start.7
  135.0 3.9 %collective-permute-start.6 = (bf16[2,12,256,64]{2,3,1,0:T(8,128)(2,1)}, bf16[2,12,256,64]{2,3,1,0:T(8,128)(2,1)}, u32[]{:S(2)}, u32[]{:S(2)}) collective-permute-start(bf16[2,12,256,64]{2,3,1,0:T(8,128)(2,1)} %get-tuple-element.32), channel_id=1, source_target_pairs={{4,0},{6,2},{8,4},{10,6},{12,8},{14,10},{16,12},{18,14},{20,16},{2... | collective-permute-start | bytes 2359304 | tf_op jit(solution)/shard_map/ppermute | solution.py:30
  139.0 1.7 fusion.12
  140.7 2.2 %fusion.114 = bf16[12,256,64]{1,2,0:T(8,128)(2,1)} fusion(f32[12,256,64]{1,2,0:T(8,128)S(1)} %copy-done.18, f32[12,256,64]{1,2,0:T(8,128)S(1)} %copy-done.20, f32[12,256,64]{1,2,0:T(8,128)S(1)} %copy-done.21, f32[12,256,64]{1,2,0:T(8,128)S(1)} %copy-done.19, bf16[12,256,256]{1,2,0:T(8,128)(2,1)S(1)} %copy-done.16, ...), kind=kOutput, calls=%fused_computation.120 | convolution fusion | flops 101842944 | bytes 5505024 | tf_op jit(solution)/shard_map/hqk,hke->hqe/dot_general | solution.py:209
  142.9 20.6 %reduce-scatter.3.cloned.1.call-done = bf16[48,1536]{1,0:T(8,128)(2,1)} async-done(((bf16[192,1536]{1,0:T(8,128)(2,1)}), bf16[48,1536]{1,0:T(8,128)(2,1)}) %reduce-scatter.3.cloned.1.call-update) | async-done | bytes 147472 | tf_op jit(solution)/shard_map/reduce_scatter | solution.py:174
  163.5 1.7 convert_element_type.199
  165.8 2.0 %copy.107 = bf16[1,256,768]{2,1,0:T(8,128)(2,1)} copy(bf16[1,256,768]{1,2,0:T(8,128)(2,1)} %bitcast.299) | data formatting | bytes 786432
  168.3 18.3 %collective-permute-done.6 = bf16[2,12,256,64]{2,3,1,0:T(8,128)(2,1)} collective-permute-done((bf16[2,12,256,64]{2,3,1,0:T(8,128)(2,1)}, bf16[2,12,256,64]{2,3,1,0:T(8,128)(2,1)}, u32[]{:S(2)}, u32[]{:S(2)}) %collective-permute-start.6) | collective-permute-done | bytes 786464 | tf_op jit(solution)/shard_map/ppermute | solution.py:30
  186.6 2.6 %fusion.40 = bf16[2,12,256,64]{2,3,1,0:T(8,128)(2,1)S(1)} fusion(f32[1,12,256,64]{2,3,1,0:T(8,128)} %fusion.78, f32[1,12,256,64]{2,3,1,0:T(8,128)S(1)} %fusion.98, bf16[2,12,256,64]{2,3,1,0:T(8,128)(2,1)} %collective-permute-done.7, bf16[2,12,256,64]{2,3,1,0:T(8,128)(2,1)} %collective-permute-done.6, f32[2,12,256,64]{2,3,1,0:T(8,128)} %collective-permute-done.4, ...), kind=kLoop, calls=%fused_computation.59 | loop fusion | flops 3145728 | bytes 5505025 | tf_op jit(solution)/shard_map/convert.1
  (149 shorter events, 21.8 us)
Async XLA Ops:
  8.0 71.2 %copy-start = (bf16[1,256,1536]{2,1,0:T(8,128)(2,1)S(1)}, bf16[1,256,1536]{2,1,0:T(8,128)(2,1)}, u32[]{:S(2)}) copy-start(bf16[1,256,1536]{2,1,0:T(8,128)(2,1)} %param.9) | copy-start | bytes 2359300
  8.0 10.3 %copy-start.47 = (bf16[48,768]{1,0:T(8,128)(2,1)S(1)}, bf16[48,768]{1,0:T(8,128)(2,1)}, u32[]{:S(2)}) copy-start(bf16[48,768]{1,0:T(8,128)(2,1)} %param.11) | copy-start | bytes 221188
  8.0 15.6 %copy-start.48 = (s32[1,8]{1,0:T(1,128)S(1)}, s32[1,8]{1,0:T(1,128)}, u32[]{:S(2)}) copy-start(s32[1,8]{1,0:T(1,128)} %param.10) | copy-start | bytes 100
  8.0 85.8 %all-gather.2.cloned.1.call-start = ((), (), s32[]{:S(2)}) async-start(), calls=%async_computation.2 | async-start | bytes 2506752 | tf_op jit(solution)/shard_map/all_gather | solution.py:106
  11.4 23.0 %collective-permute-start.2 = (bf16[2,12,256,64]{2,3,1,0:T(8,128)(2,1)}, bf16[2,12,256,64]{2,3,1,0:T(8,128)(2,1)S(1)}, u32[]{:S(2)}, u32[]{:S(2)}) collective-permute-start(bf16[2,12,256,64]{2,3,1,0:T(8,128)(2,1)} %pad_maximum_fusion.2), channel_id=1, source_target_pairs={{0,8},{2,10},{4,12},{6,14},{8,16},{10,18},{12,20},{14,22},{16,24},... | collective-permute-start | bytes 2359304 | tf_op jit(solution)/shard_map/ppermute | solution.py:30
  15.0 43.3 %collective-permute-start = (bf16[2,12,256,64]{2,3,1,0:T(8,128)(2,1)}, bf16[2,12,256,64]{2,3,1,0:T(8,128)(2,1)S(1)}, u32[]{:S(2)}, u32[]{:S(2)}) collective-permute-start(bf16[2,12,256,64]{2,3,1,0:T(8,128)(2,1)} %pad_maximum_fusion.2), channel_id=1, source_target_pairs={{0,4},{2,6},{4,8},{6,10},{8,12},{10,14},{12,16},{14,18},{16,20},{1... | collective-permute-start | bytes 2359304 | tf_op jit(solution)/shard_map/ppermute | solution.py:30
  23.5 140.0 %reduce-scatter.3.cloned.1.call-start = ((), (), s32[]{:S(2)}) async-start(), calls=%async_computation.3 | async-start | bytes 737280 | tf_op jit(solution)/shard_map/reduce_scatter | solution.py:174
  29.6 30.1 %copy-start.43 = (pred[256,256]{0,1:T(8,128)(4,1)}, pred[256,256]{0,1:T(8,128)(4,1)S(1)}, u32[]{:S(2)}) copy-start(pred[256,256]{0,1:T(8,128)(4,1)S(1)} %get-tuple-element.42) | copy-start | bytes 196612
  34.4 40.1 %copy-start.22 = (bf16[2,12,256,64]{2,3,1,0:T(8,128)(2,1)}, bf16[2,12,256,64]{2,3,1,0:T(8,128)(2,1)S(1)}, u32[]{:S(2)}) copy-start(bf16[2,12,256,64]{2,3,1,0:T(8,128)(2,1)S(1)} %collective-permute-done.2) | copy-start | bytes 2359300
  58.3 18.9 %copy-start.24 = (bf16[2,12,256,64]{2,3,1,0:T(8,128)(2,1)}, bf16[2,12,256,64]{2,3,1,0:T(8,128)(2,1)S(1)}, u32[]{:S(2)}) copy-start(bf16[2,12,256,64]{2,3,1,0:T(8,128)(2,1)S(1)} %collective-permute-done) | copy-start | bytes 2359300
  59.7 5.2 %collective-permute-start.3 = (bf16[2,12,256,64]{2,3,1,0:T(8,128)(2,1)}, bf16[2,12,256,64]{2,3,1,0:T(8,128)(2,1)}, u32[]{:S(2)}, u32[]{:S(2)}) collective-permute-start(bf16[2,12,256,64]{2,3,1,0:T(8,128)(2,1)} %get-tuple-element.37), channel_id=1, source_target_pairs={{0,2},{2,0},{1,3},{3,1},{4,6},{6,4},{5,7},{7,5},{8,10},{10,8},{9,1... | collective-permute-start | bytes 2359304 | tf_op jit(solution)/shard_map/ppermute | solution.py:34
  62.1 5.0 %collective-permute-start.1 = (bf16[2,12,256,64]{2,3,1,0:T(8,128)(2,1)}, bf16[2,12,256,64]{2,3,1,0:T(8,128)(2,1)S(1)}, u32[]{:S(2)}, u32[]{:S(2)}) collective-permute-start(bf16[2,12,256,64]{2,3,1,0:T(8,128)(2,1)} %get-tuple-element.36), channel_id=1, source_target_pairs={{0,2},{2,0},{1,3},{3,1},{4,6},{6,4},{5,7},{7,5},{8,10},{10,8},{9,1... | collective-permute-start | bytes 2359304 | tf_op jit(solution)/shard_map/ppermute | solution.py:34
  62.6 2.3 %copy-start.41 = (pred[256,256]{0,1:T(8,128)(4,1)S(1)}, pred[256,256]{0,1:T(8,128)(4,1)}, u32[]{:S(2)}) copy-start(pred[256,256]{0,1:T(8,128)(4,1)} %get-tuple-element.40) | copy-start | bytes 196612
  64.2 10.3 %copy-start.3 = (f32[12,256,256]{2,1,0:T(8,128)}, f32[12,256,256]{2,1,0:T(8,128)S(1)}, u32[]{:S(2)}) copy-start(f32[12,256,256]{2,1,0:T(8,128)S(1)} %get-tuple-element.44) | copy-start | bytes 9437188
  64.2 2.9 %copy-start.39 = (pred[256,256]{0,1:T(8,128)(4,1)S(1)}, pred[256,256]{0,1:T(8,128)(4,1)}, u32[]{:S(2)}) copy-start(pred[256,256]{0,1:T(8,128)(4,1)} %get-tuple-element.38) | copy-start | bytes 196612
  64.9 12.3 %copy-start.5 = (f32[12,256,256]{2,1,0:T(8,128)}, f32[12,256,256]{2,1,0:T(8,128)S(1)}, u32[]{:S(2)}) copy-start(f32[12,256,256]{2,1,0:T(8,128)S(1)} %get-tuple-element.48) | copy-start | bytes 9437188
  65.0 4.6 %copy-start.7 = (f32[12,256,256]{1,2,0:T(8,128)S(1)}, f32[12,256,256]{1,2,0:T(8,128)}, u32[]{:S(2)}) copy-start(f32[12,256,256]{1,2,0:T(8,128)} %get-tuple-element.50) | copy-start | bytes 9437188
  65.0 4.5 %copy-start.44 = (pred[256,256]{0,1:T(8,128)(4,1)S(1)}, pred[256,256]{0,1:T(8,128)(4,1)}, u32[]{:S(2)}) copy-start(pred[256,256]{0,1:T(8,128)(4,1)} %copy-done.43) | copy-start | bytes 196612
  67.1 8.3 %copy-start.11 = (f32[12,256,256]{2,1,0:T(8,128)}, f32[12,256,256]{2,1,0:T(8,128)S(1)}, u32[]{:S(2)}) copy-start(f32[12,256,256]{2,1,0:T(8,128)S(1)} %get-tuple-element.46) | copy-start | bytes 9437188
  67.1 11.0 %copy-start.31 = (bf16[2,12,256,64]{2,3,1,0:T(8,128)(2,1)}, bf16[2,12,256,64]{2,3,1,0:T(8,128)(2,1)S(1)}, u32[]{:S(2)}) copy-start(bf16[2,12,256,64]{2,3,1,0:T(8,128)(2,1)S(1)} %collective-permute-done.1) | copy-start | bytes 2359300
  67.8 10.3 %copy-start.9 = (f32[12,256,256]{2,1,0:T(8,128)}, f32[12,256,256]{2,1,0:T(8,128)S(1)}, u32[]{:S(2)}) copy-start(f32[12,256,256]{2,1,0:T(8,128)S(1)} %get-tuple-element.52) | copy-start | bytes 9437188
  67.8 2.5 %copy-start.34 = (pred[256,256]{0,1:T(8,128)(4,1)S(1)}, pred[256,256]{0,1:T(8,128)(4,1)}, u32[]{:S(2)}) copy-start(pred[256,256]{0,1:T(8,128)(4,1)} %get-tuple-element.41) | copy-start | bytes 196612
  79.1 4.7 %copy-start.27 = (bf16[256,12,64]{0,2,1:T(8,128)(2,1)}, bf16[256,12,64]{0,2,1:T(8,128)(2,1)S(1)}, u32[]{:S(2)}) copy-start(bf16[256,12,64]{0,2,1:T(8,128)(2,1)S(1)} %get-tuple-element.53) | copy-start | bytes 1179652
  83.8 4.9 %collective-permute-start.8 = (f32[4,2,48,1536]{3,2,1,0:T(8,128)}, f32[4,2,48,1536]{3,2,1,0:T(8,128)}, u32[]{:S(2)}, u32[]{:S(2)}) collective-permute-start(f32[4,2,48,1536]{3,2,1,0:T(8,128)} %dynamic-slice_bitcast_fusion), channel_id=1, source_target_pairs={{0,2},{2,0},{1,3},{3,1},{4,6},{6,4},{5,7},{7,5},{8,10},{10,8},{9,1... | collective-permute-start | bytes 7077896 | tf_op jit(solution)/shard_map/ppermute | solution.py:34
  92.9 3.6 %copy-start.45 = (pred[256,256]{0,1:T(8,128)(4,1)S(1)}, pred[256,256]{0,1:T(8,128)(4,1)}, u32[]{:S(2)}) copy-start(pred[256,256]{0,1:T(8,128)(4,1)} %copy-done.43) | copy-start | bytes 196612
  93.8 31.7 %collective-permute-start.9 = (bf16[4,48,1536]{2,1,0:T(8,128)(2,1)}, bf16[4,48,1536]{2,1,0:T(8,128)(2,1)}, u32[]{:S(2)}, u32[]{:S(2)}) collective-permute-start(bf16[4,48,1536]{2,1,0:T(8,128)(2,1)} %fusion.120), channel_id=1, source_target_pairs={{0,4},{4,0},{1,5},{5,1},{2,6},{6,2},{3,7},{7,3},{8,12},{12,8},{9,1... | collective-permute-start | bytes 1769480 | tf_op jit(solution)/shard_map/ppermute | solution.py:171
  96.3 3.9 %copy-start.37 = (pred[256,256]{0,1:T(8,128)(4,1)S(1)}, pred[256,256]{0,1:T(8,128)(4,1)}, u32[]{:S(2)}) copy-start(pred[256,256]{0,1:T(8,128)(4,1)} %get-tuple-element.39) | copy-start | bytes 196612
  96.5 12.0 %copy-start.29 = (bf16[256,768]{0,1:T(8,128)(2,1)}, bf16[256,768]{0,1:T(8,128)(2,1)S(1)}, u32[]{:S(2)}) copy-start(bf16[256,768]{0,1:T(8,128)(2,1)S(1)} %copy.86) | copy-start | bytes 1179652
  96.5 3.7 %copy-start.6 = (f32[12,256,256]{2,1,0:T(8,128)S(1)}, f32[12,256,256]{2,1,0:T(8,128)}, u32[]{:S(2)}) copy-start(f32[12,256,256]{2,1,0:T(8,128)} %copy-done.5) | copy-start | bytes 9437188
  100.2 2.2 %copy-start.12 = (f32[12,256,256]{2,1,0:T(8,128)S(1)}, f32[12,256,256]{2,1,0:T(8,128)}, u32[]{:S(2)}) copy-start(f32[12,256,256]{2,1,0:T(8,128)} %copy-done.11) | copy-start | bytes 9437188
  100.2 2.2 %copy-start.42 = (pred[256,256]{0,1:T(8,128)(4,1)S(1)}, pred[256,256]{0,1:T(8,128)(4,1)}, u32[]{:S(2)}) copy-start(pred[256,256]{0,1:T(8,128)(4,1)} %get-tuple-element.40) | copy-start | bytes 196612
  110.6 3.3 %copy-start.15 = (bf16[12,256,256]{1,2,0:T(8,128)(2,1)}, bf16[12,256,256]{1,2,0:T(8,128)(2,1)S(1)}, u32[]{:S(2)}) copy-start(bf16[12,256,256]{1,2,0:T(8,128)(2,1)S(1)} %multiply_convert_fusion.4) | copy-start | bytes 4718596
  112.6 17.1 %collective-permute-start.5 = (f32[2,12,256,64]{2,3,1,0:T(8,128)}, f32[2,12,256,64]{2,3,1,0:T(8,128)}, u32[]{:S(2)}, u32[]{:S(2)}) collective-permute-start(f32[2,12,256,64]{2,3,1,0:T(8,128)} %pad_maximum_fusion.1), channel_id=1, source_target_pairs={{0,2},{2,0},{1,3},{3,1},{4,6},{6,4},{5,7},{7,5},{8,10},{10,8},{9,1... | collective-permute-start | bytes 4718600 | tf_op jit(solution)/shard_map/ppermute | solution.py:34
  113.9 2.5 %copy-start.25 = (bf16[2,12,256,64]{2,3,1,0:T(8,128)(2,1)S(1)}, bf16[2,12,256,64]{2,3,1,0:T(8,128)(2,1)}, u32[]{:S(2)}) copy-start(bf16[2,12,256,64]{2,3,1,0:T(8,128)(2,1)} %copy-done.24) | copy-start | bytes 2359300
  113.9 2.5 %copy-start.38 = (pred[256,256]{0,1:T(8,128)(4,1)S(1)}, pred[256,256]{0,1:T(8,128)(4,1)}, u32[]{:S(2)}) copy-start(pred[256,256]{0,1:T(8,128)(4,1)} %get-tuple-element.39) | copy-start | bytes 196612
  116.1 13.7 %collective-permute-start.4 = (f32[2,12,256,64]{2,3,1,0:T(8,128)}, f32[2,12,256,64]{2,3,1,0:T(8,128)}, u32[]{:S(2)}, u32[]{:S(2)}) collective-permute-start(f32[2,12,256,64]{2,3,1,0:T(8,128)} %pad_maximum_fusion), channel_id=1, source_target_pairs={{0,2},{2,0},{1,3},{3,1},{4,6},{6,4},{5,7},{7,5},{8,10},{10,8},{9,1... | collective-permute-start | bytes 4718600 | tf_op jit(solution)/shard_map/ppermute | solution.py:34
  119.3 3.3 %copy-start.17 = (bf16[12,256,256]{1,2,0:T(8,128)(2,1)}, bf16[12,256,256]{1,2,0:T(8,128)(2,1)S(1)}, u32[]{:S(2)}) copy-start(bf16[12,256,256]{1,2,0:T(8,128)(2,1)S(1)} %multiply_convert_fusion.2) | copy-start | bytes 4718596
  127.6 63.6 %reduce-scatter.5.cloned.1.call-start = ((), (), s32[]{:S(2)}) async-start(), calls=%async_computation.4 | async-start | bytes 442368 | tf_op jit(solution)/shard_map/reduce_scatter | solution.py:180
  129.7 9.3 %copy-start.26 = (bf16[768,1536]{1,0:T(8,128)(2,1)S(1)}, bf16[768,1536]{1,0:T(8,128)(2,1)}, u32[]{:S(2)}) copy-start(bf16[768,1536]{1,0:T(8,128)(2,1)} %all-gather.2.cloned.1.call-done) | copy-start | bytes 7077892
  129.7 9.3 %copy-start.28 = (bf16[256,12,64]{0,2,1:T(8,128)(2,1)S(1)}, bf16[256,12,64]{0,2,1:T(8,128)(2,1)}, u32[]{:S(2)}) copy-start(bf16[256,12,64]{0,2,1:T(8,128)(2,1)} %copy-done.27) | copy-start | bytes 1179652
  129.8 10.9 %copy-start.20 = (f32[12,256,64]{1,2,0:T(8,128)S(1)}, f32[12,256,64]{1,2,0:T(8,128)}, u32[]{:S(2)}) copy-start(f32[12,256,64]{1,2,0:T(8,128)} %fusion.123) | copy-start | bytes 2359300
  129.8 10.9 %copy-start.21 = (f32[12,256,64]{1,2,0:T(8,128)S(1)}, f32[12,256,64]{1,2,0:T(8,128)}, u32[]{:S(2)}) copy-start(f32[12,256,64]{1,2,0:T(8,128)} %fusion.126) | copy-start | bytes 2359300
  133.5 7.2 %copy-start.16 = (bf16[12,256,256]{1,2,0:T(8,128)(2,1)S(1)}, bf16[12,256,256]{1,2,0:T(8,128)(2,1)}, u32[]{:S(2)}) copy-start(bf16[12,256,256]{1,2,0:T(8,128)(2,1)} %copy-done.15) | copy-start | bytes 4718596
  133.5 7.2 %copy-start.18 = (f32[12,256,64]{1,2,0:T(8,128)S(1)}, f32[12,256,64]{1,2,0:T(8,128)}, u32[]{:S(2)}) copy-start(f32[12,256,64]{1,2,0:T(8,128)} %fusion.154) | copy-start | bytes 2359300
  133.5 7.2 %copy-start.19 = (f32[12,256,64]{1,2,0:T(8,128)S(1)}, f32[12,256,64]{1,2,0:T(8,128)}, u32[]{:S(2)}) copy-start(f32[12,256,64]{1,2,0:T(8,128)} %fusion.121) | copy-start | bytes 2359300
  133.5 34.8 %collective-permute-start.7 = (bf16[2,12,256,64]{2,3,1,0:T(8,128)(2,1)}, bf16[2,12,256,64]{2,3,1,0:T(8,128)(2,1)}, u32[]{:S(2)}, u32[]{:S(2)}) collective-permute-start(bf16[2,12,256,64]{2,3,1,0:T(8,128)(2,1)} %get-tuple-element.33), channel_id=1, source_target_pairs={{8,0},{10,2},{12,4},{14,6},{16,8},{18,10},{20,12},{22,14},{24,16},... | collective-permute-start | bytes 2359304 | tf_op jit(solution)/shard_map/ppermute | solution.py:30
  135.0 51.6 %collective-permute-start.6 = (bf16[2,12,256,64]{2,3,1,0:T(8,128)(2,1)}, bf16[2,12,256,64]{2,3,1,0:T(8,128)(2,1)}, u32[]{:S(2)}, u32[]{:S(2)}) collective-permute-start(bf16[2,12,256,64]{2,3,1,0:T(8,128)(2,1)} %get-tuple-element.32), channel_id=1, source_target_pairs={{4,0},{6,2},{8,4},{10,6},{12,8},{14,10},{16,12},{18,14},{20,16},{2... | collective-permute-start | bytes 2359304 | tf_op jit(solution)/shard_map/ppermute | solution.py:30
  165.8 25.3 %copy-start.1 = (bf16[1,256,1536]{2,1,0:T(8,128)(2,1)S(1)}, bf16[1,256,1536]{2,1,0:T(8,128)(2,1)}, u32[]{:S(2)}) copy-start(bf16[1,256,1536]{2,1,0:T(8,128)(2,1)} %param.9) | copy-start | bytes 2359300
  (14 other events, 27.3 us)
Sparse Core Ops, SparseCore 0:
  23.6 43.1 all-gather.1
Sparse Core Ops, SparseCore 1:
  127.7 35.8 reduce-scatter.2
  166.2 10.6 reduce-scatter.4

commit v8 on v7

--- a/solution.py
+++ b/solution.py
@@ -171,15 +171,6 @@
     pair_sum = keep + lax.ppermute(give.astype(jnp.bfloat16), "yc", [(0, 1), (1, 0)]).astype(
         jnp.float32
     )
-    row_share = lax.psum_scatter(
-        pair_sum.reshape(-1, columns).astype(jnp.bfloat16),
-        "zc",
-        scatter_dimension=0,
-        tiled=True,
-    )
-    weight_grad = lax.psum_scatter(
-        row_share.astype(jnp.float32), "dp", scatter_dimension=1, tiled=True
-    )
 
     grad_heads = head_major(att_grad, tok_rows)
     delta_rows = jnp.sum(
@@ -191,6 +182,7 @@
     order = [d for d in range(reach, -1, -1) if d % 2 == 1] + [
         d for d in range(reach, -1, -1) if d % 2 == 0
     ]
+    odds_first = [d for d in range(reach, -1, -1) if d % 2 == 1]
     for dist in order:
         key_block = held[dist][0]
         value_block = held[dist][1]
@@ -218,7 +210,22 @@
             "hqk,hqe->hke", prob_back, grad_heads, preferred_element_type=jnp.float32
         )
         parts[dist] = jnp.stack([key_part, value_part])
-
+        if dist == odds_first[-1]:
+            pair_sum, first_parts = lax.optimization_barrier(
+                (pair_sum, [parts[d] for d in odds_first])
+            )
+            for d, p in zip(odds_first, first_parts):
+                parts[d] = p
+
+    row_share = lax.psum_scatter(
+        pair_sum.reshape(-1, columns).astype(jnp.bfloat16),
+        "zc",
+        scatter_dimension=0,
+        tiled=True,
+    )
+    weight_grad = lax.psum_scatter(
+        row_share.astype(jnp.float32), "dp", scatter_dimension=1, tiled=True
+    )
     kv_grad = return_behind(parts, reach, paired, core)
     query_grad = row_major(query_acc * score_scale, tok_rows).astype(jnp.bfloat16)
     key_grad = row_major(kv_grad[0], tok_rows).astype(jnp.bfloat16)

time: 200 us -> 198 us (0.990)
    add x0 -> x1, other arithmetic: none -> 2.03 us  [local(): keep + lax.ppermute(give.astype(jnp.bfloat16), 'yc', [(0, 1), (1, 0)]).as...]
    convert_element_type x1 -> x0, other arithmetic: 2.02 us -> none  [local(): pair_sum.reshape(-1, columns).astype(jnp.bfloat16)]
    unnamed x104 -> x106, local copies, waits for them, and re-layouts: 16.3 us -> 14.9 us
  transfers between devices with their start and end apart: 13 -> 13, of which waited for: 6 -> 5; matrix products, arithmetic and copies ran while one was open for 39% -> 39% of each run, Pallas kernels for 0% -> 0%
where the time goes in v8:
time: 198 us; the launch traced here: 196 us
  waiting for transfers between devices  72.9 us (37%)
  matrix products  46 us (23%)
  other arithmetic  26.5 us (13%)
  local copies, waits for them, and re-layouts  17.8 us (9%)
  between operations  14.5 us (7%)
  starting transfers between devices  13.6 us (7%)
  blocking collectives  5.14 us (3%)
    ppermute x4, waiting for transfers between devices, shift_up(): return lax.ppermute(block, axis, route)  46.5 us
    reduce_scatter x1, waiting for transfers between devices, local(): lax.psum_scatter(pair_sum.reshape(-1, columns).astype(jnp.bfloat16), 'zc'...  21.6 us
    unnamed x106, local copies, waits for them, and re-layouts  14.9 us
    ppermute x4, starting transfers between devices, shift_up(): return lax.ppermute(block, axis, route)  12.4 us
    dot_general x5, matrix products, local(): jnp.einsum('hqk,hqe->hke', prob_back, grad_heads, preferred_element_type=...  8.31 us
    dot_general x5, matrix products, local(): jnp.einsum('hqe,hke->hqk', grad_heads, value_block, preferred_element_typ...  7.79 us
    dot_general x5, matrix products, local(): jnp.einsum('hqk,hke->hqe', score_grad, key_block, preferred_element_type=...  7.56 us
    dot_general x5, matrix products, local(): jnp.einsum('hqe,hke->hqk', query_heads, held[dist][0], preferred_element_...  7.47 us
  transfers between devices with their start and end apart: 13, of which 5 were waited for; matrix products, arithmetic and copies ran while one was open for 39% of the time, Pallas kernels for 0%

profile of v8, /device:TPU:4, one launch (start us, length us, event | category | flops | bytes accessed | tf_op | source)
XLA Modules:
  0.0 196.5 jit_solution(9116553814993287354)
XLA Ops:
  7.2 1.2 copy.80
  8.5 1.2 copy.78
  10.6 3.5 %collective-permute-start.2 = (bf16[2,12,256,64]{2,3,1,0:T(8,128)(2,1)}, bf16[2,12,256,64]{2,3,1,0:T(8,128)(2,1)S(1)}, u32[]{:S(2)}, u32[]{:S(2)}) collective-permute-start(bf16[2,12,256,64]{2,3,1,0:T(8,128)(2,1)} %pad_maximum_fusion.2), channel_id=1, source_target_pairs={{0,8},{2,10},{4,12},{6,14},{8,16},{10,18},{12,20},{14,22},{16,24},... | collective-permute-start | bytes 2359304 | tf_op jit(solution)/shard_map/ppermute | solution.py:30
  14.1 3.4 %collective-permute-start = (bf16[2,12,256,64]{2,3,1,0:T(8,128)(2,1)}, bf16[2,12,256,64]{2,3,1,0:T(8,128)(2,1)S(1)}, u32[]{:S(2)}, u32[]{:S(2)}) collective-permute-start(bf16[2,12,256,64]{2,3,1,0:T(8,128)(2,1)} %pad_maximum_fusion.2), channel_id=1, source_target_pairs={{0,4},{2,6},{4,8},{6,10},{8,12},{10,14},{12,16},{14,18},{16,20},{1... | collective-permute-start | bytes 2359304 | tf_op jit(solution)/shard_map/ppermute | solution.py:30
  17.5 5.1 %all_gather.6 = bf16[48,1536]{1,0:T(8,128)(2,1)} all-gather(bf16[48,768]{1,0:T(8,128)(2,1)S(1)} %copy-done.48), channel_id=1, replica_groups=mesh['zc'=4,'yc'=2,'core'=2,'dp'=2] {'dp'}, dimensions={1}, use_global_device_ids=true | all-gather | bytes 221184 | tf_op jit(solution)/shard_map/all_gather | solution.py:105
  24.3 1.2 copy.77
  26.8 1.9 compare_and_fusion.3
  28.7 4.9 %collective-permute-done.2 = bf16[2,12,256,64]{2,3,1,0:T(8,128)(2,1)S(1)} collective-permute-done((bf16[2,12,256,64]{2,3,1,0:T(8,128)(2,1)}, bf16[2,12,256,64]{2,3,1,0:T(8,128)(2,1)S(1)}, u32[]{:S(2)}, u32[]{:S(2)}) %collective-permute-start.2) | collective-permute-done | bytes 786464 | tf_op jit(solution)/shard_map/ppermute | solution.py:30
  33.6 23.9 %collective-permute-done = bf16[2,12,256,64]{2,3,1,0:T(8,128)(2,1)S(1)} collective-permute-done((bf16[2,12,256,64]{2,3,1,0:T(8,128)(2,1)}, bf16[2,12,256,64]{2,3,1,0:T(8,128)(2,1)S(1)}, u32[]{:S(2)}, u32[]{:S(2)}) %collective-permute-start) | collective-permute-done | bytes 786464 | tf_op jit(solution)/shard_map/ppermute | solution.py:30
  57.5 1.4 broadcast_select_fusion.1
  58.9 2.4 %select_reduce_fusion = (f32[12,256]{1,0:T(8,128)S(1)}, f32[12,256,256]{1,2,0:T(8,128)}) fusion(pred[256,256]{0,1:T(8,128)(4,1)S(1)} %get-tuple-element.48, bf16[12,256,64]{1,2,0:T(8,128)(2,1)S(1)} %bitcast.263, bf16[12,256,64]{1,2,0:T(8,128)(2,1)S(1)} %bitcast.275), kind=kOutput, calls=%fused_computation.31 | convolution fusion | flops 103019520 | bytes 4009984 | tf_op jit(solution)/shard_map/hqe,hke->hqk/dot_general | solution.py:126
  61.8 1.6 fusion.11
  64.1 2.1 %fusion.10 = (f32[12,256]{1,0:T(8,128)S(1)}, f32[12,256,256]{2,1,0:T(8,128)S(1)}) fusion(pred[256,256]{0,1:T(8,128)(4,1)S(1)} %copy-done.45, bf16[12,256,64]{1,2,0:T(8,128)(2,1)S(1)} %bitcast.266, bf16[2,12,256,64]{2,3,1,0:T(8,128)(2,1)} %collective-permute-done.3), kind=kOutput, calls=%fused_computation.29 | convolution fusion | flops 103019520 | bytes 4009984 | tf_op jit(solution)/shard_map/hqe,hke->hqk/dot_general | solution.py:126
  67.0 1.6 copy-done.3
  69.5 4.1 %fusion.20 = (f32[12,256]{1,0:T(8,128)S(1)}, f32[12,256]{1,0:T(8,128)S(1)}, f32[12,256]{1,0:T(8,128)S(1)}, f32[12,256]{1,0:T(8,128)S(1)}, f32[12,256]{1,0:T(8,128)S(1)}) fusion(f32[12,256,256]{2,1,0:T(8,128)S(1)} %get-tuple-element.58, f32[12,256]{1,0:T(8,128)S(1)} %maximum_maximum_fusion, pred[256,256]{0,1:T(8,128)(4,1)S(1)} %copy-done.42, ...), kind=kLoop, calls=%fused_computation.43 | loop fusion | flops 19645440 | bytes 16130048 | tf_op jit(solution)/shard_map/reduce_sum | solution.py:139
  74.5 1.9 fusion.60
  79.1 2.2 %copy-done.2 = f32[4,2,2,48,1536]{4,3,2,1,0:T(8,128)} copy-done((f32[4,2,2,48,1536]{4,3,2,1,0:T(8,128)}, f32[4,2,2,48,1536]{4,3,2,1,0:T(8,128)S(1)}, u32[]{:S(2)}) %copy-start.2) | copy-done | bytes 4718616
  81.3 1.7 dynamic-slice_bitcast_fusion
  83.0 4.8 %collective-permute-done.4 = f32[4,2,48,1536]{3,2,1,0:T(8,128)} collective-permute-done((f32[4,2,48,1536]{3,2,1,0:T(8,128)}, f32[4,2,48,1536]{3,2,1,0:T(8,128)}, u32[]{:S(2)}, u32[]{:S(2)}) %collective-permute-start.4) | collective-permute-done | bytes 2359328 | tf_op jit(solution)/shard_map/ppermute | solution.py:34
  87.9 2.8 %bitcast_add_fusion = f32[4,2,48,1536]{3,2,1,0:T(8,128)S(1)} fusion(f32[4,2,48,1536]{3,2,1,0:T(8,128)} %collective-permute-done.4, f32[4,2,2,48,1536]{4,3,2,1,0:T(8,128)} %copy-done.2, s32[]{:T(128)S(6)} %select_n.197), kind=kLoop, calls=%fused_computation.39 | loop fusion | flops 589824 | bytes 7077892 | tf_op jit(solution)/shard_map/add | solution.py:167
  90.6 1.4 copy-done.13
  93.0 2.5 %convolution_convert_fusion.1 = bf16[256,768]{1,0:T(8,128)(2,1)S(1)} fusion(bf16[768,1536]{1,0:T(8,128)(2,1)} %all-gather.2.cloned.1.call-done, bf16[1,256,1536]{2,1,0:T(8,128)(2,1)S(1)} %copy-done), kind=kOutput, calls=%fused_computation.121 | convolution fusion | flops 604176384 | bytes 3538944 | tf_op jit(solution)/shard_map/dot_general | solution.py:156
  95.7 2.8 %fusion.87 = f32[1,12,256,64]{2,3,1,0:T(8,128)S(1)} fusion(bf16[12,256,64]{1,2,0:T(8,128)(2,1)S(1)} %bitcast.284, f32[12,256,256]{2,1,0:T(8,128)} %copy-done.9, f32[12,256]{1,0:T(8,128)S(1)} %get-tuple-element.36, pred[256,256]{0,1:T(8,128)(4,1)S(1)} %copy-done.46), kind=kOutput, calls=%fused_computation.99 | convolution fusion | flops 103809024 | bytes 4403200 | tf_op jit(solution)/shard_map/hqk,hqe->hke/dot_general | solution.py:209
  101.6 1.3 fusion.153
  102.9 2.2 %multiply_convert_fusion.4 = bf16[12,256,256]{1,2,0:T(8,128)(2,1)S(1)} fusion(f32[12,256,256]{2,1,0:T(8,128)S(1)} %copy-done.10, bf16[12,256,64]{1,2,0:T(8,128)(2,1)S(1)} %bitcast.288, f32[12,256]{1,0:T(8,128)S(1)} %multiply_reduce_fusion, f32[12,256]{1,0:T(8,128)S(1)} %get-tuple-element.36, pred[256,256]{0,1:T(8,128)(4,1)S(1)} %copy-done.47, ...), kind=kOutput, calls=%fused_computation.21 | convolution fusion | flops 105381888 | bytes 5595136 | tf_op jit(solution)/shard_map/hqe,hke->hqk/dot_general | solution.py:197
  105.8 2.3 %multiply_convert_fusion.3 = bf16[12,256,256]{1,2,0:T(8,128)(2,1)S(1)} fusion(f32[12,256,256]{2,1,0:T(8,128)S(1)} %copy-done.12, bf16[12,256,64]{1,2,0:T(8,128)(2,1)} %bitcast.289, f32[12,256]{1,0:T(8,128)S(1)} %multiply_reduce_fusion, f32[12,256]{1,0:T(8,128)S(1)} %get-tuple-element.36, pred[256,256]{0,1:T(8,128)(4,1)S(1)} %copy-done.44, ...), kind=kOutput, calls=%fused_computation.20 | convolution fusion | flops 105381888 | bytes 5603328 | tf_op jit(solution)/shard_map/hqe,hke->hqk/dot_general | solution.py:197
  108.7 1.1 multiply_convert_fusion.1
  109.9 1.3 fusion.120
  111.2 1.5 fusion.122
  112.6 1.4 pad_maximum_fusion
  114.0 1.3 pad_maximum_fusion.1
  115.7 1.1 multiply_convert_fusion.2
  117.4 2.0 %bitcast_add_fusion.1 = bf16[4,48,1536]{2,1,0:T(8,128)(2,1)} fusion(bf16[4,48,1536]{2,1,0:T(8,128)(2,1)} %collective-permute-done.5, f32[4,2,48,1536]{3,2,1,0:T(8,128)S(1)} %copy-done.14, s32[]{:T(128)S(6)} %select_n.199), kind=kLoop, calls=%fused_computation.122 | loop fusion | flops 884736 | bytes 2359300 | tf_op jit(solution)/shard_map/add | solution.py:171
  120.5 1.3 fusion.125
  121.8 1.6 fusion.78
  123.4 1.6 fusion.84
  125.0 1.7 fusion.90
  126.8 2.1 %fusion.94 = f32[1,12,256,64]{2,3,1,0:T(8,128)S(1)} fusion(bf16[12,256,256]{1,2,0:T(8,128)(2,1)} %copy-done.17, bf16[12,256,64]{1,2,0:T(8,128)(2,1)S(1)} %bitcast.271), kind=kOutput, calls=%fused_computation.104 | convolution fusion | flops 100859904 | bytes 2752512 | tf_op jit(solution)/shard_map/hqk,hqe->hke/dot_general | solution.py:206
  129.0 3.5 %fusion.41 = (bf16[2,12,256,64]{2,3,1,0:T(8,128)(2,1)}, bf16[2,12,256,64]{2,3,1,0:T(8,128)(2,1)}) fusion(f32[1,12,256,64]{2,3,1,0:T(8,128)S(1)} %copy-done.33, f32[1,12,256,64]{2,3,1,0:T(8,128)S(1)} %fusion.95, f32[2,12,256,64]{2,3,1,0:T(8,128)} %collective-permute-done.7, f32[2,12,256,64]{2,3,1,0:T(8,128)} %collective-permute-done.6, pred[]{:T(512)S(6)} %eq.89, ...), kind=kLoop, calls=%fused_computation.63 | loop fusion | flops 3145728 | bytes 7864321 | tf_op jit(solution)/shard_map/convert_element_type | solution.py:89
  132.4 1.6 collective-permute-start.9
  134.0 3.9 %collective-permute-start.8 = (bf16[2,12,256,64]{2,3,1,0:T(8,128)(2,1)}, bf16[2,12,256,64]{2,3,1,0:T(8,128)(2,1)}, u32[]{:S(2)}, u32[]{:S(2)}) collective-permute-start(bf16[2,12,256,64]{2,3,1,0:T(8,128)(2,1)} %get-tuple-element.38), channel_id=1, source_target_pairs={{4,0},{6,2},{8,4},{10,6},{12,8},{14,10},{16,12},{18,14},{20,16},{2... | collective-permute-start | bytes 2359304 | tf_op jit(solution)/shard_map/ppermute | solution.py:30
  137.9 1.7 fusion.12
  139.6 2.2 %fusion.114 = bf16[12,256,64]{1,2,0:T(8,128)(2,1)} fusion(f32[12,256,64]{1,2,0:T(8,128)S(1)} %copy-done.18, f32[12,256,64]{1,2,0:T(8,128)S(1)} %copy-done.20, f32[12,256,64]{1,2,0:T(8,128)S(1)} %copy-done.21, f32[12,256,64]{1,2,0:T(8,128)S(1)} %copy-done.19, bf16[12,256,256]{1,2,0:T(8,128)(2,1)S(1)} %copy-done.16, ...), kind=kOutput, calls=%fused_computation.120 | convolution fusion | flops 101842944 | bytes 5505024 | tf_op jit(solution)/shard_map/hqk,hke->hqe/dot_general | solution.py:201
  141.9 21.6 %reduce-scatter.3.cloned.1.call-done = bf16[48,1536]{1,0:T(8,128)(2,1)} async-done(((bf16[192,1536]{1,0:T(8,128)(2,1)}), bf16[48,1536]{1,0:T(8,128)(2,1)}) %reduce-scatter.3.cloned.1.call-update) | async-done | bytes 147472 | tf_op jit(solution)/shard_map/reduce_scatter | solution.py:220
  163.4 1.7 convert_element_type.199
  165.7 2.0 %copy.107 = bf16[1,256,768]{2,1,0:T(8,128)(2,1)} copy(bf16[1,256,768]{1,2,0:T(8,128)(2,1)} %bitcast.297) | data formatting | bytes 786432
  167.7 17.7 %collective-permute-done.8 = bf16[2,12,256,64]{2,3,1,0:T(8,128)(2,1)} collective-permute-done((bf16[2,12,256,64]{2,3,1,0:T(8,128)(2,1)}, bf16[2,12,256,64]{2,3,1,0:T(8,128)(2,1)}, u32[]{:S(2)}, u32[]{:S(2)}) %collective-permute-start.8) | collective-permute-done | bytes 786464 | tf_op jit(solution)/shard_map/ppermute | solution.py:30
  185.4 2.6 %fusion.40 = bf16[2,12,256,64]{2,3,1,0:T(8,128)(2,1)S(1)} fusion(f32[1,12,256,64]{2,3,1,0:T(8,128)} %fusion.78, f32[1,12,256,64]{2,3,1,0:T(8,128)S(1)} %fusion.98, bf16[2,12,256,64]{2,3,1,0:T(8,128)(2,1)} %collective-permute-done.9, bf16[2,12,256,64]{2,3,1,0:T(8,128)(2,1)} %collective-permute-done.8, f32[2,12,256,64]{2,3,1,0:T(8,128)} %collective-permute-done.6, ...), kind=kLoop, calls=%fused_computation.59 | loop fusion | flops 3145728 | bytes 5505025 | tf_op jit(solution)/shard_map/convert.1
  (151 shorter events, 20.5 us)
Async XLA Ops:
  7.2 71.2 %copy-start = (bf16[1,256,1536]{2,1,0:T(8,128)(2,1)S(1)}, bf16[1,256,1536]{2,1,0:T(8,128)(2,1)}, u32[]{:S(2)}) copy-start(bf16[1,256,1536]{2,1,0:T(8,128)(2,1)} %param.9) | copy-start | bytes 2359300
  7.2 10.3 %copy-start.48 = (bf16[48,768]{1,0:T(8,128)(2,1)S(1)}, bf16[48,768]{1,0:T(8,128)(2,1)}, u32[]{:S(2)}) copy-start(bf16[48,768]{1,0:T(8,128)(2,1)} %param.11) | copy-start | bytes 221188
  7.2 15.6 %copy-start.49 = (s32[1,8]{1,0:T(1,128)S(1)}, s32[1,8]{1,0:T(1,128)}, u32[]{:S(2)}) copy-start(s32[1,8]{1,0:T(1,128)} %param.10) | copy-start | bytes 100
  7.2 85.8 %all-gather.2.cloned.1.call-start = ((), (), s32[]{:S(2)}) async-start(), calls=%async_computation.2 | async-start | bytes 2506752 | tf_op jit(solution)/shard_map/all_gather | solution.py:106
  10.6 23.0 %collective-permute-start.2 = (bf16[2,12,256,64]{2,3,1,0:T(8,128)(2,1)}, bf16[2,12,256,64]{2,3,1,0:T(8,128)(2,1)S(1)}, u32[]{:S(2)}, u32[]{:S(2)}) collective-permute-start(bf16[2,12,256,64]{2,3,1,0:T(8,128)(2,1)} %pad_maximum_fusion.2), channel_id=1, source_target_pairs={{0,8},{2,10},{4,12},{6,14},{8,16},{10,18},{12,20},{14,22},{16,24},... | collective-permute-start | bytes 2359304 | tf_op jit(solution)/shard_map/ppermute | solution.py:30
  14.1 43.3 %collective-permute-start = (bf16[2,12,256,64]{2,3,1,0:T(8,128)(2,1)}, bf16[2,12,256,64]{2,3,1,0:T(8,128)(2,1)S(1)}, u32[]{:S(2)}, u32[]{:S(2)}) collective-permute-start(bf16[2,12,256,64]{2,3,1,0:T(8,128)(2,1)} %pad_maximum_fusion.2), channel_id=1, source_target_pairs={{0,4},{2,6},{4,8},{6,10},{8,12},{10,14},{12,16},{14,18},{16,20},{1... | collective-permute-start | bytes 2359304 | tf_op jit(solution)/shard_map/ppermute | solution.py:30
  22.7 140.7 %reduce-scatter.3.cloned.1.call-start = ((), (), s32[]{:S(2)}) async-start(), calls=%async_computation.3 | async-start | bytes 737280 | tf_op jit(solution)/shard_map/reduce_scatter | solution.py:220
  28.7 30.2 %copy-start.39 = (pred[256,256]{0,1:T(8,128)(4,1)}, pred[256,256]{0,1:T(8,128)(4,1)S(1)}, u32[]{:S(2)}) copy-start(pred[256,256]{0,1:T(8,128)(4,1)S(1)} %get-tuple-element.48) | copy-start | bytes 196612
  33.6 40.1 %copy-start.22 = (bf16[2,12,256,64]{2,3,1,0:T(8,128)(2,1)}, bf16[2,12,256,64]{2,3,1,0:T(8,128)(2,1)S(1)}, u32[]{:S(2)}) copy-start(bf16[2,12,256,64]{2,3,1,0:T(8,128)(2,1)S(1)} %collective-permute-done.2) | copy-start | bytes 2359300
  57.5 18.9 %copy-start.24 = (bf16[2,12,256,64]{2,3,1,0:T(8,128)(2,1)}, bf16[2,12,256,64]{2,3,1,0:T(8,128)(2,1)S(1)}, u32[]{:S(2)}) copy-start(bf16[2,12,256,64]{2,3,1,0:T(8,128)(2,1)S(1)} %collective-permute-done) | copy-start | bytes 2359300
  58.9 5.2 %collective-permute-start.3 = (bf16[2,12,256,64]{2,3,1,0:T(8,128)(2,1)}, bf16[2,12,256,64]{2,3,1,0:T(8,128)(2,1)}, u32[]{:S(2)}, u32[]{:S(2)}) collective-permute-start(bf16[2,12,256,64]{2,3,1,0:T(8,128)(2,1)} %get-tuple-element.43), channel_id=1, source_target_pairs={{0,2},{2,0},{1,3},{3,1},{4,6},{6,4},{5,7},{7,5},{8,10},{10,8},{9,1... | collective-permute-start | bytes 2359304 | tf_op jit(solution)/shard_map/ppermute | solution.py:34
  61.3 5.0 %collective-permute-start.1 = (bf16[2,12,256,64]{2,3,1,0:T(8,128)(2,1)}, bf16[2,12,256,64]{2,3,1,0:T(8,128)(2,1)S(1)}, u32[]{:S(2)}, u32[]{:S(2)}) collective-permute-start(bf16[2,12,256,64]{2,3,1,0:T(8,128)(2,1)} %get-tuple-element.42), channel_id=1, source_target_pairs={{0,2},{2,0},{1,3},{3,1},{4,6},{6,4},{5,7},{7,5},{8,10},{10,8},{9,1... | collective-permute-start | bytes 2359304 | tf_op jit(solution)/shard_map/ppermute | solution.py:34
  63.4 10.3 %copy-start.5 = (f32[12,256,256]{2,1,0:T(8,128)}, f32[12,256,256]{2,1,0:T(8,128)S(1)}, u32[]{:S(2)}) copy-start(f32[12,256,256]{2,1,0:T(8,128)S(1)} %get-tuple-element.50) | copy-start | bytes 9437188
  63.4 2.9 %copy-start.42 = (pred[256,256]{0,1:T(8,128)(4,1)S(1)}, pred[256,256]{0,1:T(8,128)(4,1)}, u32[]{:S(2)}) copy-start(pred[256,256]{0,1:T(8,128)(4,1)} %get-tuple-element.44) | copy-start | bytes 196612
  64.1 12.3 %copy-start.7 = (f32[12,256,256]{2,1,0:T(8,128)}, f32[12,256,256]{2,1,0:T(8,128)S(1)}, u32[]{:S(2)}) copy-start(f32[12,256,256]{2,1,0:T(8,128)S(1)} %get-tuple-element.54) | copy-start | bytes 9437188
  64.1 4.6 %copy-start.3 = (f32[12,256,256]{1,2,0:T(8,128)S(1)}, f32[12,256,256]{1,2,0:T(8,128)}, u32[]{:S(2)}) copy-start(f32[12,256,256]{1,2,0:T(8,128)} %get-tuple-element.56) | copy-start | bytes 9437188
  64.1 4.5 %copy-start.40 = (pred[256,256]{0,1:T(8,128)(4,1)S(1)}, pred[256,256]{0,1:T(8,128)(4,1)}, u32[]{:S(2)}) copy-start(pred[256,256]{0,1:T(8,128)(4,1)} %copy-done.39) | copy-start | bytes 196612
  66.3 8.3 %copy-start.9 = (f32[12,256,256]{2,1,0:T(8,128)}, f32[12,256,256]{2,1,0:T(8,128)S(1)}, u32[]{:S(2)}) copy-start(f32[12,256,256]{2,1,0:T(8,128)S(1)} %get-tuple-element.52) | copy-start | bytes 9437188
  66.3 11.0 %copy-start.31 = (bf16[2,12,256,64]{2,3,1,0:T(8,128)(2,1)}, bf16[2,12,256,64]{2,3,1,0:T(8,128)(2,1)S(1)}, u32[]{:S(2)}) copy-start(bf16[2,12,256,64]{2,3,1,0:T(8,128)(2,1)S(1)} %collective-permute-done.1) | copy-start | bytes 2359300
  67.0 10.3 %copy-start.11 = (f32[12,256,256]{2,1,0:T(8,128)}, f32[12,256,256]{2,1,0:T(8,128)S(1)}, u32[]{:S(2)}) copy-start(f32[12,256,256]{2,1,0:T(8,128)S(1)} %get-tuple-element.58) | copy-start | bytes 9437188
  78.3 4.7 %copy-start.27 = (bf16[256,12,64]{0,2,1:T(8,128)(2,1)}, bf16[256,12,64]{0,2,1:T(8,128)(2,1)S(1)}, u32[]{:S(2)}) copy-start(bf16[256,12,64]{0,2,1:T(8,128)(2,1)S(1)} %get-tuple-element.59) | copy-start | bytes 1179652
  83.0 4.9 %collective-permute-start.4 = (f32[4,2,48,1536]{3,2,1,0:T(8,128)}, f32[4,2,48,1536]{3,2,1,0:T(8,128)}, u32[]{:S(2)}, u32[]{:S(2)}) collective-permute-start(f32[4,2,48,1536]{3,2,1,0:T(8,128)} %dynamic-slice_bitcast_fusion), channel_id=1, source_target_pairs={{0,2},{2,0},{1,3},{3,1},{4,6},{6,4},{5,7},{7,5},{8,10},{10,8},{9,1... | collective-permute-start | bytes 7077896 | tf_op jit(solution)/shard_map/ppermute | solution.py:34
  92.0 3.6 %copy-start.46 = (pred[256,256]{0,1:T(8,128)(4,1)S(1)}, pred[256,256]{0,1:T(8,128)(4,1)}, u32[]{:S(2)}) copy-start(pred[256,256]{0,1:T(8,128)(4,1)} %get-tuple-element.46) | copy-start | bytes 196612
  93.0 23.9 %collective-permute-start.5 = (bf16[4,48,1536]{2,1,0:T(8,128)(2,1)}, bf16[4,48,1536]{2,1,0:T(8,128)(2,1)}, u32[]{:S(2)}, u32[]{:S(2)}) collective-permute-start(bf16[4,48,1536]{2,1,0:T(8,128)(2,1)} %fusion.119), channel_id=1, source_target_pairs={{0,4},{4,0},{1,5},{5,1},{2,6},{6,2},{3,7},{7,3},{8,12},{12,8},{9,1... | collective-permute-start | bytes 1769480 | tf_op jit(solution)/shard_map/ppermute | solution.py:171
  95.4 3.0 %copy-start.43 = (pred[256,256]{0,1:T(8,128)(4,1)S(1)}, pred[256,256]{0,1:T(8,128)(4,1)}, u32[]{:S(2)}) copy-start(pred[256,256]{0,1:T(8,128)(4,1)} %get-tuple-element.44) | copy-start | bytes 196612
  95.6 7.3 %copy-start.29 = (bf16[256,768]{0,1:T(8,128)(2,1)}, bf16[256,768]{0,1:T(8,128)(2,1)S(1)}, u32[]{:S(2)}) copy-start(bf16[256,768]{0,1:T(8,128)(2,1)S(1)} %copy.86) | copy-start | bytes 1179652
  95.6 3.0 %copy-start.12 = (f32[12,256,256]{2,1,0:T(8,128)S(1)}, f32[12,256,256]{2,1,0:T(8,128)}, u32[]{:S(2)}) copy-start(f32[12,256,256]{2,1,0:T(8,128)} %copy-done.11) | copy-start | bytes 9437188
  105.1 2.9 %copy-start.15 = (bf16[12,256,256]{1,2,0:T(8,128)(2,1)}, bf16[12,256,256]{1,2,0:T(8,128)(2,1)S(1)}, u32[]{:S(2)}) copy-start(bf16[12,256,256]{1,2,0:T(8,128)(2,1)S(1)} %multiply_convert_fusion.4) | copy-start | bytes 4718596
  105.8 2.9 %copy-start.8 = (f32[12,256,256]{2,1,0:T(8,128)S(1)}, f32[12,256,256]{2,1,0:T(8,128)}, u32[]{:S(2)}) copy-start(f32[12,256,256]{2,1,0:T(8,128)} %copy-done.7) | copy-start | bytes 9437188
  105.8 2.9 %copy-start.25 = (bf16[2,12,256,64]{2,3,1,0:T(8,128)(2,1)S(1)}, bf16[2,12,256,64]{2,3,1,0:T(8,128)(2,1)}, u32[]{:S(2)}) copy-start(bf16[2,12,256,64]{2,3,1,0:T(8,128)(2,1)} %copy-done.24) | copy-start | bytes 2359300
  105.8 2.9 %copy-start.30 = (bf16[256,768]{0,1:T(8,128)(2,1)S(1)}, bf16[256,768]{0,1:T(8,128)(2,1)}, u32[]{:S(2)}) copy-start(bf16[256,768]{0,1:T(8,128)(2,1)} %copy-done.29) | copy-start | bytes 1179652
  105.8 2.9 %copy-start.38 = (pred[256,256]{0,1:T(8,128)(4,1)S(1)}, pred[256,256]{0,1:T(8,128)(4,1)}, u32[]{:S(2)}) copy-start(pred[256,256]{0,1:T(8,128)(4,1)} %get-tuple-element.45) | copy-start | bytes 196612
  112.6 3.1 %copy-start.23 = (bf16[2,12,256,64]{2,3,1,0:T(8,128)(2,1)S(1)}, bf16[2,12,256,64]{2,3,1,0:T(8,128)(2,1)}, u32[]{:S(2)}) copy-start(bf16[2,12,256,64]{2,3,1,0:T(8,128)(2,1)} %copy-done.22) | copy-start | bytes 2359300
  112.6 3.1 %copy-start.36 = (pred[256,256]{0,1:T(8,128)(4,1)S(1)}, pred[256,256]{0,1:T(8,128)(4,1)}, u32[]{:S(2)}) copy-start(pred[256,256]{0,1:T(8,128)(4,1)} %get-tuple-element.47) | copy-start | bytes 196612
  116.9 5.0 %copy-start.17 = (bf16[12,256,256]{1,2,0:T(8,128)(2,1)}, bf16[12,256,256]{1,2,0:T(8,128)(2,1)S(1)}, u32[]{:S(2)}) copy-start(bf16[12,256,256]{1,2,0:T(8,128)(2,1)S(1)} %multiply_convert_fusion.2) | copy-start | bytes 4718596
  119.4 9.5 %collective-permute-start.7 = (f32[2,12,256,64]{2,3,1,0:T(8,128)}, f32[2,12,256,64]{2,3,1,0:T(8,128)}, u32[]{:S(2)}, u32[]{:S(2)}) collective-permute-start(f32[2,12,256,64]{2,3,1,0:T(8,128)} %pad_maximum_fusion), channel_id=1, source_target_pairs={{0,2},{2,0},{1,3},{3,1},{4,6},{6,4},{5,7},{7,5},{8,10},{10,8},{9,1... | collective-permute-start | bytes 4718600 | tf_op jit(solution)/shard_map/ppermute | solution.py:34
  119.6 9.4 %collective-permute-start.6 = (f32[2,12,256,64]{2,3,1,0:T(8,128)}, f32[2,12,256,64]{2,3,1,0:T(8,128)}, u32[]{:S(2)}, u32[]{:S(2)}) collective-permute-start(f32[2,12,256,64]{2,3,1,0:T(8,128)} %pad_maximum_fusion.1), channel_id=1, source_target_pairs={{0,2},{2,0},{1,3},{3,1},{4,6},{6,4},{5,7},{7,5},{8,10},{10,8},{9,1... | collective-permute-start | bytes 4718600 | tf_op jit(solution)/shard_map/ppermute | solution.py:34
  126.7 63.3 %reduce-scatter.5.cloned.1.call-start = ((), (), s32[]{:S(2)}) async-start(), calls=%async_computation.4 | async-start | bytes 442368 | tf_op jit(solution)/shard_map/reduce_scatter | solution.py:226
  128.9 9.0 %copy-start.26 = (bf16[768,1536]{1,0:T(8,128)(2,1)S(1)}, bf16[768,1536]{1,0:T(8,128)(2,1)}, u32[]{:S(2)}) copy-start(bf16[768,1536]{1,0:T(8,128)(2,1)} %all-gather.2.cloned.1.call-done) | copy-start | bytes 7077892
  128.9 9.0 %copy-start.28 = (bf16[256,12,64]{0,2,1:T(8,128)(2,1)S(1)}, bf16[256,12,64]{0,2,1:T(8,128)(2,1)}, u32[]{:S(2)}) copy-start(bf16[256,12,64]{0,2,1:T(8,128)(2,1)} %copy-done.27) | copy-start | bytes 1179652
  128.9 10.7 %copy-start.20 = (f32[12,256,64]{1,2,0:T(8,128)S(1)}, f32[12,256,64]{1,2,0:T(8,128)}, u32[]{:S(2)}) copy-start(f32[12,256,64]{1,2,0:T(8,128)} %fusion.122) | copy-start | bytes 2359300
  129.0 10.7 %copy-start.21 = (f32[12,256,64]{1,2,0:T(8,128)S(1)}, f32[12,256,64]{1,2,0:T(8,128)}, u32[]{:S(2)}) copy-start(f32[12,256,64]{1,2,0:T(8,128)} %fusion.125) | copy-start | bytes 2359300
  132.4 7.2 %copy-start.16 = (bf16[12,256,256]{1,2,0:T(8,128)(2,1)S(1)}, bf16[12,256,256]{1,2,0:T(8,128)(2,1)}, u32[]{:S(2)}) copy-start(bf16[12,256,256]{1,2,0:T(8,128)(2,1)} %copy-done.15) | copy-start | bytes 4718596
  132.4 7.2 %copy-start.18 = (f32[12,256,64]{1,2,0:T(8,128)S(1)}, f32[12,256,64]{1,2,0:T(8,128)}, u32[]{:S(2)}) copy-start(f32[12,256,64]{1,2,0:T(8,128)} %fusion.153) | copy-start | bytes 2359300
  132.4 7.2 %copy-start.19 = (f32[12,256,64]{1,2,0:T(8,128)S(1)}, f32[12,256,64]{1,2,0:T(8,128)}, u32[]{:S(2)}) copy-start(f32[12,256,64]{1,2,0:T(8,128)} %fusion.120) | copy-start | bytes 2359300
  132.4 35.3 %collective-permute-start.9 = (bf16[2,12,256,64]{2,3,1,0:T(8,128)(2,1)}, bf16[2,12,256,64]{2,3,1,0:T(8,128)(2,1)}, u32[]{:S(2)}, u32[]{:S(2)}) collective-permute-start(bf16[2,12,256,64]{2,3,1,0:T(8,128)(2,1)} %get-tuple-element.39), channel_id=1, source_target_pairs={{8,0},{10,2},{12,4},{14,6},{16,8},{18,10},{20,12},{22,14},{24,16},... | collective-permute-start | bytes 2359304 | tf_op jit(solution)/shard_map/ppermute | solution.py:30
  134.0 51.4 %collective-permute-start.8 = (bf16[2,12,256,64]{2,3,1,0:T(8,128)(2,1)}, bf16[2,12,256,64]{2,3,1,0:T(8,128)(2,1)}, u32[]{:S(2)}, u32[]{:S(2)}) collective-permute-start(bf16[2,12,256,64]{2,3,1,0:T(8,128)(2,1)} %get-tuple-element.38), channel_id=1, source_target_pairs={{4,0},{6,2},{8,4},{10,6},{12,8},{14,10},{16,12},{18,14},{20,16},{2... | collective-permute-start | bytes 2359304 | tf_op jit(solution)/shard_map/ppermute | solution.py:30
  165.7 24.2 %copy-start.1 = (bf16[1,256,1536]{2,1,0:T(8,128)(2,1)S(1)}, bf16[1,256,1536]{2,1,0:T(8,128)(2,1)}, u32[]{:S(2)}) copy-start(bf16[1,256,1536]{2,1,0:T(8,128)(2,1)} %param.9) | copy-start | bytes 2359300
  (15 other events, 33.5 us)
Sparse Core Ops, SparseCore 0:
  22.8 43.1 all-gather.1
  126.8 36.5 reduce-scatter.2
  166.2 10.6 reduce-scatter.4

commit v9 on v2

--- a/solution.py
+++ b/solution.py
@@ -46,8 +46,22 @@
             held.append(shift_up(held[-1], "seq", 1))
         return held
     evens = {0: own}
-    for dist in range(2, reach + 2, 2):
-        evens[dist] = shift_up(own, "seq", dist)
+    count = lax.axis_size("seq")
+    if reach == 4 and count % 4 == 0:
+        row = (lax.axis_index("seq") // 2) % 2
+        later = [i for i in range(count) if (i // 2) % 2 == 1]
+        earlier = [i for i in range(count) if (i // 2) % 2 == 0 and i + 2 < count]
+        far = [shift_up(own[k], "seq", 4) for k in range(2)]
+        near = []
+        for k in range(2):
+            direct = lax.ppermute(own[k], "seq", [(i - 2, i) for i in later])
+            relayed = lax.ppermute(far[k], "seq", [(i + 2, i) for i in earlier])
+            near.append(jnp.where(row == 1, direct, relayed))
+        evens[2] = jnp.stack(near)
+        evens[4] = jnp.stack(far)
+    else:
+        for dist in range(2, reach + 2, 2):
+            evens[dist] = shift_up(own, "seq", dist)
     odds = list(range(1, reach + 1, 2))
     payload = [jnp.where(core == 0, evens[s - 1], evens[s + 1]) for s in odds]
     received = swap_partner(payload, "seq")
@@ -65,17 +79,27 @@
         return carried
     odds = list(range(1, reach + 1, 2))
     received = swap_partner([parts[s] for s in odds], "seq")
-    total = None
+    summed = {}
     for dist in range(0, reach + 2, 2):
         zero = jnp.zeros_like(parts[0])
         from_core1 = received[dist // 2] if dist // 2 < len(odds) else zero
         from_core0 = received[dist // 2 - 1] if dist >= 2 and dist // 2 - 1 < len(odds) else zero
         own = parts[dist] if dist <= reach else zero
-        summed = own + jnp.where(core == 0, from_core1, from_core0)
-        if dist == 0:
-            total = summed
-        else:
-            total = total + shift_up(summed.astype(jnp.bfloat16), "seq", -dist).astype(jnp.float32)
+        summed[dist] = own + jnp.where(core == 0, from_core1, from_core0)
+    count = lax.axis_size("seq")
+    if reach == 4 and count % 4 == 0:
+        row = (lax.axis_index("seq") // 2) % 2
+        later = [i for i in range(count) if (i // 2) % 2 == 1]
+        earlier = [i for i in range(count) if (i // 2) % 2 == 0 and i + 2 < count]
+        near = summed[2].astype(jnp.bfloat16)
+        direct = lax.ppermute(near, "seq", [(i, i - 2) for i in later])
+        relayed = lax.ppermute(near, "seq", [(i, i + 2) for i in earlier])
+        far = summed[4] + jnp.where(row == 1, relayed.astype(jnp.float32), 0.0)
+        total = summed[0] + jnp.where(row == 0, direct.astype(jnp.float32), 0.0)
+        return total + shift_up(far.astype(jnp.bfloat16), "seq", -4).astype(jnp.float32)
+    total = summed[0]
+    for dist in range(2, reach + 2, 2):
+        total = total + shift_up(summed[dist].astype(jnp.bfloat16), "seq", -dist).astype(jnp.float32)
     return total
 
 

time: 182 us -> 177 us (0.973)
  waiting for transfers between devices: 86.1 us -> 45.8 us
  starting transfers between devices: 11.5 us -> 27.4 us
  local copies, waits for them, and re-layouts: 12 us -> 19.9 us
  matrix products: 34.3 us -> 42.1 us
  other arithmetic: 16.8 us -> 18.9 us
    reduce_scatter x1, waiting for transfers between devices: 50.2 us -> 13.9 us  [local(): lax.psum_scatter(partial_weight.astype(jnp.bfloat16), 'seq', scatter_dime...]
    ppermute x0 -> x6, waiting for transfers between devices: none -> 27.2 us  [the longest x1 19.3 us: return_behind(): relayed = lax.ppermute(near, 'seq', [(i, i + 2) for i in earlier])]
    ppermute x4 -> x3, waiting for transfers between devices: 29.1 us -> 2.12 us  [shift_up(): return lax.ppermute(block, axis, route)]
    ppermute x0 -> x6, starting transfers between devices: none -> 18 us  [the longest x2 8.14 us: gather_behind(): relayed = lax.ppermute(far[k], 'seq', [(i + 2, i) for i in earlier])]
    unnamed x92 -> x72, local copies, waits for them, and re-layouts: 10.8 us -> 16.1 us
    dot_general x5, matrix products: 3.38 us -> 8.13 us  [local(): jnp.einsum('hqe,hke->hqk', query_heads, held[dist][0], preferred_element_...]
    reduce_scatter x1, waiting for transfers between devices: 6.6 us -> 2.56 us  [local(): lax.psum_scatter(row_share.astype(jnp.float32), 'dp', scatter_dimension=1...]
    mul x0 -> x1, local copies, waits for them, and re-layouts: none -> 3.56 us  [local(): jnp.einsum('hqe,hke->hqk', query_heads, held[dist][0], preferred_element_...]
  transfers between devices with their start and end apart: 11 -> 16, of which waited for: 5 -> 6; matrix products, arithmetic and copies ran while one was open for 31% -> 41% of each run, Pallas kernels for 0% -> 0%
where the time goes in v9:
time: 177 us; the launch traced here: 175 us
  waiting for transfers between devices  45.8 us (26%)
  matrix products  42.1 us (24%)
  starting transfers between devices  27.4 us (15%)
  local copies, waits for them, and re-layouts  19.9 us (11%)
  other arithmetic  18.9 us (11%)
  between operations  14.4 us (8%)
  blocking collectives  6.31 us (4%)
    ppermute x1, waiting for transfers between devices, return_behind(): relayed = lax.ppermute(near, 'seq', [(i, i + 2) for i in earlier])  19.3 us
    unnamed x72, local copies, waits for them, and re-layouts  16.1 us
    reduce_scatter x1, waiting for transfers between devices, local(): lax.psum_scatter(partial_weight.astype(jnp.bfloat16), 'seq', scatter_dime...  13.9 us
    ppermute x3, starting transfers between devices, shift_up(): return lax.ppermute(block, axis, route)  8.27 us
    ppermute x2, starting transfers between devices, gather_behind(): relayed = lax.ppermute(far[k], 'seq', [(i + 2, i) for i in earlier])  8.14 us
    dot_general x5, matrix products, local(): jnp.einsum('hqe,hke->hqk', query_heads, held[dist][0], preferred_element_...  8.13 us
    ppermute x2, waiting for transfers between devices, gather_behind(): relayed = lax.ppermute(far[k], 'seq', [(i + 2, i) for i in earlier])  7.86 us
    dot_general x5, matrix products, local(): jnp.einsum('hqe,hke->hqk', grad_heads, value_block, preferred_element_typ...  6.77 us
  transfers between devices with their start and end apart: 16, of which 6 were waited for; matrix products, arithmetic and copies ran while one was open for 41% of the time, Pallas kernels for 0%

profile of v9, /device:TPU:4, one launch (start us, length us, event | category | flops | bytes accessed | tf_op | source)
XLA Modules:
  0.0 174.9 jit_solution(3458776337497082358)
XLA Ops:
  7.2 1.2 copy.84
  8.5 3.5 %collective-permute-start.1 = (bf16[12,256,64]{1,2,0:T(8,128)(2,1)S(1)}, bf16[12,256,64]{1,2,0:T(8,128)(2,1)S(1)}, u32[]{:S(2)}, u32[]{:S(2)}) collective-permute-start(bf16[12,256,64]{1,2,0:T(8,128)(2,1)S(1)} %bitcast.223), channel_id=1, source_target_pairs={{0,8},{2,10},{4,12},{6,14},{8,16},{10,18},{12,20},{14,22},{16,24},... | collective-permute-start | bytes 1179656 | tf_op jit(solution)/shard_map/ppermute | solution.py:18
  12.0 1.3 collective-permute-start
  13.3 1.2 copy.86
  14.4 3.5 %collective-permute-start.4 = (bf16[12,256,64]{1,2,0:T(8,128)(2,1)S(1)}, bf16[12,256,64]{1,2,0:T(8,128)(2,1)S(1)}, u32[]{:S(2)}, u32[]{:S(2)}) collective-permute-start(bf16[12,256,64]{1,2,0:T(8,128)(2,1)S(1)} %bitcast.243), channel_id=1, source_target_pairs={{0,8},{2,10},{4,12},{6,14},{8,16},{10,18},{12,20},{14,22},{16,24},... | collective-permute-start | bytes 1179656 | tf_op jit(solution)/shard_map/ppermute | solution.py:18
  17.9 1.3 collective-permute-start.3
  19.2 6.3 %all_gather.6 = bf16[48,1536]{1,0:T(8,128)(2,1)} all-gather(bf16[48,768]{1,0:T(8,128)(2,1)} %param.11), channel_id=1, replica_groups=mesh['seq'=16,'dp'=2] {'dp'}, dimensions={1}, use_global_device_ids=true | all-gather | bytes 221184 | tf_op jit(solution)/shard_map/all_gather | solution.py:118
  26.7 6.1 %collective-permute-start.2 = (bf16[12,256,64]{1,2,0:T(8,128)(2,1)S(1)}, bf16[12,256,64]{1,2,0:T(8,128)(2,1)}, u32[]{:S(2)}, u32[]{:S(2)}) collective-permute-start(bf16[12,256,64]{1,2,0:T(8,128)(2,1)S(1)} %collective-permute-done.1), channel_id=1, source_target_pairs={{4,0},{6,2},{12,8},{14,10},{20,16},{22,18},{28,24},{30,26},{5,1},{... | collective-permute-start | bytes 1179656 | tf_op jit(solution)/shard_map/ppermute | solution.py:58
  33.4 1.2 copy.83
  34.7 2.1 %collective-permute-start.5 = (bf16[12,256,64]{1,2,0:T(8,128)(2,1)S(1)}, bf16[12,256,64]{1,2,0:T(8,128)(2,1)}, u32[]{:S(2)}, u32[]{:S(2)}) collective-permute-start(bf16[12,256,64]{1,2,0:T(8,128)(2,1)S(1)} %collective-permute-done.4), channel_id=1, source_target_pairs={{4,0},{6,2},{12,8},{14,10},{20,16},{22,18},{28,24},{30,26},{5,1},{... | collective-permute-start | bytes 1179656 | tf_op jit(solution)/shard_map/ppermute | solution.py:58
  36.7 2.3 %select_reduce_fusion.1 = (f32[12,256]{1,0:T(8,128)S(1)}, f32[12,256,256]{1,2,0:T(8,128)}) fusion(pred[256,256]{0,1:T(8,128)(4,1)S(1)} %get-tuple-element.40, bf16[12,256,64]{1,2,0:T(8,128)(2,1)S(1)} %bitcast.213, bf16[12,256,64]{1,2,0:T(8,128)(2,1)S(1)} %bitcast.225), kind=kOutput, calls=%fused_computation.29 | convolution fusion | flops 103019520 | bytes 4009984 | tf_op jit(solution)/shard_map/hqe,hke->hqk/dot_general | solution.py:139
  39.8 3.4 %collective-permute-done.2 = bf16[12,256,64]{1,2,0:T(8,128)(2,1)} collective-permute-done((bf16[12,256,64]{1,2,0:T(8,128)(2,1)S(1)}, bf16[12,256,64]{1,2,0:T(8,128)(2,1)}, u32[]{:S(2)}, u32[]{:S(2)}) %collective-permute-start.2) | collective-permute-done | bytes 393248 | tf_op jit(solution)/shard_map/ppermute | solution.py:58
  43.2 1.0 broadcast_select_fusion.1
  44.2 4.4 %collective-permute-done.5 = bf16[12,256,64]{1,2,0:T(8,128)(2,1)} collective-permute-done((bf16[12,256,64]{1,2,0:T(8,128)(2,1)S(1)}, bf16[12,256,64]{1,2,0:T(8,128)(2,1)}, u32[]{:S(2)}, u32[]{:S(2)}) %collective-permute-start.5) | collective-permute-done | bytes 393248 | tf_op jit(solution)/shard_map/ppermute | solution.py:58
  48.7 1.0 broadcast_select_fusion
  49.7 2.3 %maximum_select_fusion = (bf16[2,12,256,64]{2,3,1,0:T(8,128)(2,1)}, bf16[2,12,256,64]{2,3,1,0:T(8,128)(2,1)}) fusion(bf16[1,12,256,64]{2,3,1,0:T(8,128)(2,1)S(1)} %bitcast.245, bf16[1,12,256,64]{2,3,1,0:T(8,128)(2,1)S(1)} %bitcast.226, pred[]{:T(512)S(6)} %eq.101, bf16[1,12,256,64]{2,3,1,0:T(8,128)(2,1)S(1)} %bitcast.248, ...), kind=kLoop, calls=%fused_computation.122 | loop fusion | flops 1966080 | bytes 3932161 | tf_op jit(solution)/shard_map/jit(_where)/select_n | solution.py:66
  52.1 2.3 %convolution_multiply_fusion = f32[12,256,256]{2,1,0:T(8,128)} fusion(bf16[12,256,64]{1,2,0:T(8,128)(2,1)S(1)} %bitcast.214, bf16[12,256,64]{1,2,0:T(8,128)(2,1)S(1)} %collective-permute-done.1), kind=kOutput, calls=%fused_computation.47 | convolution fusion | flops 101449728 | bytes 3932160 | tf_op jit(solution)/shard_map/hqe,hke->hqk/dot_general | solution.py:139
  54.4 3.6 %copy.88 = f32[12,256,256]{1,2,0:T(8,128)} copy(f32[12,256,256]{2,1,0:T(8,128)} %convolution_multiply_fusion) | data formatting | bytes 6291456 | tf_op jit(solution)/shard_map/mul | solution.py:139
  58.5 2.2 %select_reduce_fusion = f32[12,256]{1,0:T(8,128)S(1)} fusion(f32[12,256,256]{1,2,0:T(8,128)} %copy.88, pred[256,256]{0,1:T(8,128)(4,1)S(1)} %get-tuple-element.39), kind=kLoop, calls=%fused_computation.28 | loop fusion | flops 1569792 | bytes 3223552 | tf_op jit(solution)/shard_map/reduce_max | solution.py:144
  61.4 2.1 %fusion.6 = (f32[12,256]{1,0:T(8,128)S(1)}, f32[12,256,256]{2,1,0:T(8,128)S(1)}) fusion(pred[256,256]{0,1:T(8,128)(4,1)S(1)} %get-tuple-element.36, bf16[12,256,64]{1,2,0:T(8,128)(2,1)S(1)} %bitcast.216, bf16[2,12,256,64]{2,3,1,0:T(8,128)(2,1)} %collective-permute-done.6), kind=kOutput, calls=%fused_computation.25 | convolution fusion | flops 103019520 | bytes 4009984 | tf_op jit(solution)/shard_map/hqe,hke->hqk/dot_general | solution.py:139
  64.6 3.2 %copy-done.4 = f32[12,256,256]{1,2,0:T(8,128)S(1)} copy-done((f32[12,256,256]{1,2,0:T(8,128)S(1)}, f32[12,256,256]{1,2,0:T(8,128)}, u32[]{:S(2)}) %copy-start.4) | copy-done | bytes 3145752
  67.8 3.9 %fusion.19 = (f32[12,256]{1,0:T(8,128)S(1)}, f32[12,256]{1,0:T(8,128)S(1)}, f32[12,256]{1,0:T(8,128)S(1)}, f32[12,256]{1,0:T(8,128)S(1)}, f32[12,256]{1,0:T(8,128)S(1)}) fusion(f32[12,256,256]{2,1,0:T(8,128)S(1)} %get-tuple-element.48, f32[12,256]{1,0:T(8,128)S(1)} %maximum_maximum_fusion, pred[256,256]{0,1:T(8,128)(4,1)S(1)} %get-tuple-element.36, ...), kind=kLoop, calls=%fused_computation.41 | loop fusion | flops 18859008 | bytes 16130048 | tf_op jit(solution)/shard_map/reduce_sum | solution.py:152
  74.2 1.9 %fusion.101 = f32[12,256,64]{1,2,0:T(8,128)S(1)} fusion(f32[12,256,64]{1,2,0:T(8,128)S(1)} %fusion.66, f32[12,256,256]{2,1,0:T(8,128)S(1)} %get-tuple-element.48, f32[12,256]{1,0:T(8,128)S(1)} %maximum_maximum_fusion, pred[256,256]{0,1:T(8,128)(4,1)S(1)} %get-tuple-element.36, bf16[2,12,256,64]{2,3,1,0:T(8,128)(2,1)} %collective-permute-done.6), kind=kOutput, calls=%fused_computation.116 | convolution fusion | flops 104792064 | bytes 5189632 | tf_op jit(solution)/shard_map/hqk,hke->hqe/dot_general | solution.py:153
  76.1 1.8 %fusion.116 = (bf16[256,12,64]{0,2,1:T(8,128)(2,1)S(1)}, f32[12,256,64]{1,2,0:T(8,128)}) fusion(f32[256,12]{0,1:T(8,128)S(1)} %bitcast.253, f32[12,256,64]{1,2,0:T(8,128)S(1)} %fusion.33, f32[12,256,64]{1,2,0:T(8,128)S(1)} %fusion.60, f32[12,256,64]{1,2,0:T(8,128)S(1)} %fusion.101, bf16[12,256,64]{1,2,0:T(8,128)(2,1)S(1)} %broadcast_select_fusion, ...), kind=kOutput, calls=%fused_computation.128 | convolution fusion | flops 105578496 | bytes 7168000 | tf_op jit(solution)/shard_map/hqk,hke->hqe/dot_general | solution.py:153
  78.7 2.2 %convolution_convert_fusion = bf16[768,1536]{1,0:T(8,128)(2,1)} fusion(bf16[256,768]{0,1:T(8,128)(2,1)S(1)} %bitcast.241, bf16[1,256,1536]{2,1,0:T(8,128)(2,1)S(1)} %copy-done), kind=kOutput, calls=%fused_computation | convolution fusion | flops 605159424 | bytes 3538944 | tf_op jit(solution)/shard_map/dot_general | solution.py:173
  81.1 2.5 %convolution_convert_fusion.2 = bf16[256,768]{1,0:T(8,128)(2,1)S(1)} fusion(bf16[768,1536]{1,0:T(8,128)(2,1)} %all-gather.2.cloned.1.call-done, bf16[1,256,1536]{2,1,0:T(8,128)(2,1)S(1)} %copy-done), kind=kOutput, calls=%fused_computation.121 | convolution fusion | flops 604176384 | bytes 3538944 | tf_op jit(solution)/shard_map/dot_general | solution.py:169
  83.8 2.7 %fusion.84 = f32[1,12,256,64]{2,3,1,0:T(8,128)S(1)} fusion(bf16[12,256,64]{1,2,0:T(8,128)(2,1)S(1)} %bitcast.228, f32[12,256,256]{2,1,0:T(8,128)} %copy-done.10, f32[12,256]{1,0:T(8,128)S(1)} %get-tuple-element.30, pred[256,256]{0,1:T(8,128)(4,1)S(1)} %get-tuple-element.36), kind=kOutput, calls=%fused_computation.98 | convolution fusion | flops 103809024 | bytes 4403200 | tf_op jit(solution)/shard_map/hqk,hqe->hke/dot_general | solution.py:216
  88.9 1.1 multiply_convert_fusion.1
  90.9 1.1 multiply_convert_fusion
  92.8 2.4 %multiply_convert_fusion.3 = bf16[12,256,256]{1,2,0:T(8,128)(2,1)S(1)} fusion(f32[12,256,256]{2,1,0:T(8,128)S(1)} %copy-done.11, bf16[12,256,64]{1,2,0:T(8,128)(2,1)S(1)} %bitcast.233, f32[12,256]{1,0:T(8,128)S(1)} %multiply_reduce_fusion, f32[12,256]{1,0:T(8,128)S(1)} %get-tuple-element.30, pred[256,256]{0,1:T(8,128)(4,1)S(1)} %get-tuple-element.36, ...), kind=kOutput, calls=%fused_computation.18 | convolution fusion | flops 105381888 | bytes 5595136 | tf_op jit(solution)/shard_map/hqe,hke->hqk/dot_general | solution.py:204
  96.4 1.1 multiply_convert_fusion.4
  99.0 1.5 fusion.117
  104.0 1.3 fusion.40
  105.3 1.3 collective-permute-start.11
  107.6 1.1 fusion.113
  108.7 6.0 %collective-permute-start.10 = (bf16[2,12,256,64]{2,3,1,0:T(8,128)(2,1)}, bf16[2,12,256,64]{2,3,1,0:T(8,128)(2,1)}, u32[]{:S(2)}, u32[]{:S(2)}) collective-permute-start(bf16[2,12,256,64]{2,3,1,0:T(8,128)(2,1)} %fusion.40), channel_id=1, source_target_pairs={{4,0},{6,2},{12,8},{14,10},{20,16},{22,18},{28,24},{30,26},{5,1},{... | collective-permute-start | bytes 2359304 | tf_op jit(solution)/shard_map/ppermute | solution.py:95
  114.7 19.3 %collective-permute-done.11 = bf16[2,12,256,64]{2,3,1,0:T(8,128)(2,1)S(1)} collective-permute-done((bf16[2,12,256,64]{2,3,1,0:T(8,128)(2,1)}, bf16[2,12,256,64]{2,3,1,0:T(8,128)(2,1)S(1)}, u32[]{:S(2)}, u32[]{:S(2)}) %collective-permute-start.11) | collective-permute-done | bytes 786464 | tf_op jit(solution)/shard_map/ppermute | solution.py:96
  134.0 1.3 fusion.42
  135.3 1.3 collective-permute-start.12
  136.6 1.7 fusion.10
  138.3 1.6 fusion.81
  139.9 13.9 %reduce-scatter.3.cloned.1.call-done = bf16[48,1536]{1,0:T(8,128)(2,1)} async-done(((bf16[768,1536]{1,0:T(8,128)(2,1)}), bf16[48,1536]{1,0:T(8,128)(2,1)}) %reduce-scatter.3.cloned.1.call-update) | async-done | bytes 147472 | tf_op jit(solution)/shard_map/reduce_scatter | solution.py:176
  153.9 1.7 convert_element_type.187
  155.6 2.0 %fusion.99 = f32[1,12,256,64]{2,3,1,0:T(8,128)S(1)} fusion(bf16[12,256,256]{1,2,0:T(8,128)(2,1)} %copy-done.12, bf16[12,256,64]{1,2,0:T(8,128)(2,1)S(1)} %bitcast.222), kind=kOutput, calls=%fused_computation.114 | convolution fusion | flops 100859904 | bytes 2752512 | tf_op jit(solution)/shard_map/hqk,hqe->hke/dot_general | solution.py:213
  157.6 2.0 %copy.116 = bf16[1,256,768]{2,1,0:T(8,128)(2,1)} copy(bf16[1,256,768]{1,2,0:T(8,128)(2,1)} %bitcast.252) | data formatting | bytes 786432
  159.6 2.1 %collective-permute-done.12 = bf16[2,12,256,64]{2,3,1,0:T(8,128)(2,1)} collective-permute-done((bf16[2,12,256,64]{2,3,1,0:T(8,128)(2,1)}, bf16[2,12,256,64]{2,3,1,0:T(8,128)(2,1)}, u32[]{:S(2)}, u32[]{:S(2)}) %collective-permute-start.12) | collective-permute-done | bytes 786464 | tf_op jit(solution)/shard_map/ppermute | solution.py:18
  161.7 2.2 %fusion.39 = bf16[2,12,256,64]{2,3,1,0:T(8,128)(2,1)S(1)} fusion(f32[1,12,256,64]{2,3,1,0:T(8,128)} %fusion.81, f32[1,12,256,64]{2,3,1,0:T(8,128)S(1)} %fusion.99, bf16[2,12,256,64]{2,3,1,0:T(8,128)(2,1)} %collective-permute-done.12, bf16[2,12,256,64]{2,3,1,0:T(8,128)(2,1)} %collective-permute-done.10, f32[2,12,256,64]{2,3,1,0:T(8,128)S(1)} %collective-permute-done.8, ...), kind=kLoop, calls=%fused_computation.57 | loop fusion | flops 3538944 | bytes 5505026 | tf_op jit(solution)/shard_map/convert.1
  165.8 2.6 %reduce-scatter.5.cloned.1.call-done = f32[48,768]{1,0:T(8,128)} async-done(((f32[48,1536]{1,0:T(8,128)}), f32[48,768]{1,0:T(8,128)}) %reduce-scatter.5.cloned.1.call-update) | async-done | bytes 147472 | tf_op jit(solution)/shard_map/reduce_scatter | solution.py:179
  (123 shorter events, 21.2 us)
Async XLA Ops:
  7.2 71.5 %copy-start = (bf16[1,256,1536]{2,1,0:T(8,128)(2,1)S(1)}, bf16[1,256,1536]{2,1,0:T(8,128)(2,1)}, u32[]{:S(2)}) copy-start(bf16[1,256,1536]{2,1,0:T(8,128)(2,1)} %param.9) | copy-start | bytes 2359300
  7.2 73.9 %all-gather.2.cloned.1.call-start = ((), (), s32[]{:S(2)}) async-start(), calls=%async_computation.2 | async-start | bytes 2506752 | tf_op jit(solution)/shard_map/all_gather | solution.py:119
  8.5 18.3 %collective-permute-start.1 = (bf16[12,256,64]{1,2,0:T(8,128)(2,1)S(1)}, bf16[12,256,64]{1,2,0:T(8,128)(2,1)S(1)}, u32[]{:S(2)}, u32[]{:S(2)}) collective-permute-start(bf16[12,256,64]{1,2,0:T(8,128)(2,1)S(1)} %bitcast.223), channel_id=1, source_target_pairs={{0,8},{2,10},{4,12},{6,14},{8,16},{10,18},{12,20},{14,22},{16,24},... | collective-permute-start | bytes 1179656 | tf_op jit(solution)/shard_map/ppermute | solution.py:18
  12.0 27.0 %collective-permute-start = (bf16[12,256,64]{1,2,0:T(8,128)(2,1)S(1)}, bf16[12,256,64]{1,2,0:T(8,128)(2,1)S(1)}, u32[]{:S(2)}, u32[]{:S(2)}) collective-permute-start(bf16[12,256,64]{1,2,0:T(8,128)(2,1)S(1)} %bitcast.224), channel_id=1, source_target_pairs={{0,4},{2,6},{8,12},{10,14},{16,20},{18,22},{24,28},{26,30},{1,5},{... | collective-permute-start | bytes 1179656 | tf_op jit(solution)/shard_map/ppermute | solution.py:57
  14.4 20.2 %collective-permute-start.4 = (bf16[12,256,64]{1,2,0:T(8,128)(2,1)S(1)}, bf16[12,256,64]{1,2,0:T(8,128)(2,1)S(1)}, u32[]{:S(2)}, u32[]{:S(2)}) collective-permute-start(bf16[12,256,64]{1,2,0:T(8,128)(2,1)S(1)} %bitcast.243), channel_id=1, source_target_pairs={{0,8},{2,10},{4,12},{6,14},{8,16},{10,18},{12,20},{14,22},{16,24},... | collective-permute-start | bytes 1179656 | tf_op jit(solution)/shard_map/ppermute | solution.py:18
  17.9 26.3 %collective-permute-start.3 = (bf16[12,256,64]{1,2,0:T(8,128)(2,1)S(1)}, bf16[12,256,64]{1,2,0:T(8,128)(2,1)}, u32[]{:S(2)}, u32[]{:S(2)}) collective-permute-start(bf16[12,256,64]{1,2,0:T(8,128)(2,1)S(1)} %bitcast.244), channel_id=1, source_target_pairs={{0,4},{2,6},{8,12},{10,14},{16,20},{18,22},{24,28},{26,30},{1,5},{... | collective-permute-start | bytes 1179656 | tf_op jit(solution)/shard_map/ppermute | solution.py:57
  25.6 128.3 %reduce-scatter.3.cloned.1.call-start = ((), (), s32[]{:S(2)}) async-start(), calls=%async_computation.3 | async-start | bytes 2506752 | tf_op jit(solution)/shard_map/reduce_scatter | solution.py:176
  26.7 25.4 %copy-start.13 = (bf16[12,256,64]{1,2,0:T(8,128)(2,1)}, bf16[12,256,64]{1,2,0:T(8,128)(2,1)S(1)}, u32[]{:S(2)}) copy-start(bf16[12,256,64]{1,2,0:T(8,128)(2,1)S(1)} %collective-permute-done.1) | copy-start | bytes 1179652
  26.7 16.4 %collective-permute-start.2 = (bf16[12,256,64]{1,2,0:T(8,128)(2,1)S(1)}, bf16[12,256,64]{1,2,0:T(8,128)(2,1)}, u32[]{:S(2)}, u32[]{:S(2)}) collective-permute-start(bf16[12,256,64]{1,2,0:T(8,128)(2,1)S(1)} %collective-permute-done.1), channel_id=1, source_target_pairs={{4,0},{6,2},{12,8},{14,10},{20,16},{22,18},{28,24},{30,26},{5,1},{... | collective-permute-start | bytes 1179656 | tf_op jit(solution)/shard_map/ppermute | solution.py:58
  33.3 38.4 %copy-start.16 = (pred[256,256]{0,1:T(8,128)(4,1)}, pred[256,256]{0,1:T(8,128)(4,1)S(1)}, u32[]{:S(2)}) copy-start(pred[256,256]{0,1:T(8,128)(4,1)S(1)} %get-tuple-element.39) | copy-start | bytes 196612
  33.4 53.2 %copy-start.30 = (pred[256,256]{0,1:T(8,128)(4,1)}, pred[256,256]{0,1:T(8,128)(4,1)S(1)}, u32[]{:S(2)}) copy-start(pred[256,256]{0,1:T(8,128)(4,1)S(1)} %get-tuple-element.38) | copy-start | bytes 196612
  33.4 54.6 %copy-start.28 = (pred[256,256]{0,1:T(8,128)(4,1)}, pred[256,256]{0,1:T(8,128)(4,1)S(1)}, u32[]{:S(2)}) copy-start(pred[256,256]{0,1:T(8,128)(4,1)S(1)} %get-tuple-element.37) | copy-start | bytes 196612
  33.4 56.6 %copy-start.26 = (pred[256,256]{0,1:T(8,128)(4,1)}, pred[256,256]{0,1:T(8,128)(4,1)S(1)}, u32[]{:S(2)}) copy-start(pred[256,256]{0,1:T(8,128)(4,1)S(1)} %get-tuple-element.40) | copy-start | bytes 196612
  34.6 9.6 %copy-start.20 = (bf16[12,256,64]{1,2,0:T(8,128)(2,1)}, bf16[12,256,64]{1,2,0:T(8,128)(2,1)S(1)}, u32[]{:S(2)}) copy-start(bf16[12,256,64]{1,2,0:T(8,128)(2,1)S(1)} %collective-permute-done.4) | copy-start | bytes 1179652
  34.7 14.0 %collective-permute-start.5 = (bf16[12,256,64]{1,2,0:T(8,128)(2,1)S(1)}, bf16[12,256,64]{1,2,0:T(8,128)(2,1)}, u32[]{:S(2)}, u32[]{:S(2)}) collective-permute-start(bf16[12,256,64]{1,2,0:T(8,128)(2,1)S(1)} %collective-permute-done.4), channel_id=1, source_target_pairs={{4,0},{6,2},{12,8},{14,10},{20,16},{22,18},{28,24},{30,26},{5,1},{... | collective-permute-start | bytes 1179656 | tf_op jit(solution)/shard_map/ppermute | solution.py:58
  39.0 0.7 copy-start.32
  52.1 9.3 %collective-permute-start.6 = (bf16[2,12,256,64]{2,3,1,0:T(8,128)(2,1)}, bf16[2,12,256,64]{2,3,1,0:T(8,128)(2,1)}, u32[]{:S(2)}, u32[]{:S(2)}) collective-permute-start(bf16[2,12,256,64]{2,3,1,0:T(8,128)(2,1)} %get-tuple-element.34), channel_id=1, source_target_pairs={{0,2},{2,0},{4,6},{6,4},{8,10},{10,8},{12,14},{14,12},{16,18},{18,... | collective-permute-start | bytes 2359304 | tf_op jit(solution)/shard_map/ppermute | solution.py:23
  58.0 5.6 %collective-permute-start.7 = (bf16[2,12,256,64]{2,3,1,0:T(8,128)(2,1)}, bf16[2,12,256,64]{2,3,1,0:T(8,128)(2,1)S(1)}, u32[]{:S(2)}, u32[]{:S(2)}) collective-permute-start(bf16[2,12,256,64]{2,3,1,0:T(8,128)(2,1)} %get-tuple-element.35), channel_id=1, source_target_pairs={{0,2},{2,0},{4,6},{6,4},{8,10},{10,8},{12,14},{14,12},{16,18},{18,... | collective-permute-start | bytes 2359304 | tf_op jit(solution)/shard_map/ppermute | solution.py:23
  61.3 14.8 %copy-start.6 = (f32[12,256,256]{2,1,0:T(8,128)}, f32[12,256,256]{2,1,0:T(8,128)S(1)}, u32[]{:S(2)}) copy-start(f32[12,256,256]{2,1,0:T(8,128)S(1)} %get-tuple-element.44) | copy-start | bytes 9437188
  61.4 3.2 %copy-start.2 = (f32[12,256,256]{1,2,0:T(8,128)S(1)}, f32[12,256,256]{1,2,0:T(8,128)}, u32[]{:S(2)}) copy-start(f32[12,256,256]{1,2,0:T(8,128)} %copy.88) | copy-start | bytes 9437188
  61.4 6.5 %copy-start.4 = (f32[12,256,256]{1,2,0:T(8,128)S(1)}, f32[12,256,256]{1,2,0:T(8,128)}, u32[]{:S(2)}) copy-start(f32[12,256,256]{1,2,0:T(8,128)} %get-tuple-element.46) | copy-start | bytes 9437188
  63.5 10.7 %copy-start.10 = (f32[12,256,256]{2,1,0:T(8,128)}, f32[12,256,256]{2,1,0:T(8,128)S(1)}, u32[]{:S(2)}) copy-start(f32[12,256,256]{2,1,0:T(8,128)S(1)} %get-tuple-element.48) | copy-start | bytes 9437188
  63.5 9.8 %copy-start.24 = (bf16[2,12,256,64]{2,3,1,0:T(8,128)(2,1)}, bf16[2,12,256,64]{2,3,1,0:T(8,128)(2,1)S(1)}, u32[]{:S(2)}) copy-start(bf16[2,12,256,64]{2,3,1,0:T(8,128)(2,1)S(1)} %collective-permute-done.7) | copy-start | bytes 2359300
  64.2 9.1 %copy-start.8 = (f32[12,256,256]{2,1,0:T(8,128)}, f32[12,256,256]{2,1,0:T(8,128)S(1)}, u32[]{:S(2)}) copy-start(f32[12,256,256]{2,1,0:T(8,128)S(1)} %get-tuple-element.42) | copy-start | bytes 9437188
  67.8 3.9 %copy-start.21 = (bf16[12,256,64]{1,2,0:T(8,128)(2,1)S(1)}, bf16[12,256,64]{1,2,0:T(8,128)(2,1)}, u32[]{:S(2)}) copy-start(bf16[12,256,64]{1,2,0:T(8,128)(2,1)} %copy-done.20) | copy-start | bytes 1179652
  80.9 87.4 %reduce-scatter.5.cloned.1.call-start = ((), (), s32[]{:S(2)}) async-start(), calls=%async_computation.4 | async-start | bytes 442368 | tf_op jit(solution)/shard_map/reduce_scatter | solution.py:179
  83.8 2.8 %copy-start.9 = (f32[12,256,256]{2,1,0:T(8,128)S(1)}, f32[12,256,256]{2,1,0:T(8,128)}, u32[]{:S(2)}) copy-start(f32[12,256,256]{2,1,0:T(8,128)} %copy-done.8) | copy-start | bytes 9437188
  86.6 1.1 copy-start.23
  86.6 2.2 %copy-start.7 = (f32[12,256,256]{2,1,0:T(8,128)S(1)}, f32[12,256,256]{2,1,0:T(8,128)}, u32[]{:S(2)}) copy-start(f32[12,256,256]{2,1,0:T(8,128)} %copy-done.6) | copy-start | bytes 9437188
  88.9 2.0 %copy-start.5 = (f32[12,256,256]{1,2,0:T(8,128)S(1)}, f32[12,256,256]{1,2,0:T(8,128)}, u32[]{:S(2)}) copy-start(f32[12,256,256]{1,2,0:T(8,128)} %get-tuple-element.46) | copy-start | bytes 9437188
  90.9 2.0 %copy-start.11 = (f32[12,256,256]{2,1,0:T(8,128)S(1)}, f32[12,256,256]{2,1,0:T(8,128)}, u32[]{:S(2)}) copy-start(f32[12,256,256]{2,1,0:T(8,128)} %copy-done.10) | copy-start | bytes 9437188
  92.8 5.7 %copy-start.12 = (bf16[12,256,256]{1,2,0:T(8,128)(2,1)}, bf16[12,256,256]{1,2,0:T(8,128)(2,1)S(1)}, u32[]{:S(2)}) copy-start(bf16[12,256,256]{1,2,0:T(8,128)(2,1)S(1)} %multiply_convert_fusion) | copy-start | bytes 4718596
  95.2 1.1 copy-start.25
  95.3 1.1 copy-start.31
  96.0 8.0 %collective-permute-start.8 = (f32[2,12,256,64]{2,3,1,0:T(8,128)S(1)}, f32[2,12,256,64]{2,3,1,0:T(8,128)S(1)}, u32[]{:S(2)}, u32[]{:S(2)}) collective-permute-start(f32[2,12,256,64]{2,3,1,0:T(8,128)S(1)} %pad_maximum_fusion), channel_id=1, source_target_pairs={{0,2},{2,0},{4,6},{6,4},{8,10},{10,8},{12,14},{14,12},{16,18},{18,... | collective-permute-start | bytes 4718600 | tf_op jit(solution)/shard_map/ppermute | solution.py:23
  98.3 5.7 %collective-permute-start.9 = (f32[2,12,256,64]{2,3,1,0:T(8,128)S(1)}, f32[2,12,256,64]{2,3,1,0:T(8,128)S(1)}, u32[]{:S(2)}, u32[]{:S(2)}) collective-permute-start(f32[2,12,256,64]{2,3,1,0:T(8,128)S(1)} %pad_maximum_fusion.1), channel_id=1, source_target_pairs={{0,2},{2,0},{4,6},{6,4},{8,10},{10,8},{12,14},{14,12},{16,18},{18,... | collective-permute-start | bytes 4718600 | tf_op jit(solution)/shard_map/ppermute | solution.py:23
  98.9 2.2 %copy-start.3 = (f32[12,256,256]{1,2,0:T(8,128)S(1)}, f32[12,256,256]{1,2,0:T(8,128)}, u32[]{:S(2)}) copy-start(f32[12,256,256]{1,2,0:T(8,128)} %copy.88) | copy-start | bytes 9437188
  99.0 2.2 %copy-start.17 = (pred[256,256]{0,1:T(8,128)(4,1)S(1)}, pred[256,256]{0,1:T(8,128)(4,1)}, u32[]{:S(2)}) copy-start(pred[256,256]{0,1:T(8,128)(4,1)} %copy-done.16) | copy-start | bytes 196612
  99.0 2.2 %copy-start.22 = (bf16[12,256,64]{1,2,0:T(8,128)(2,1)S(1)}, bf16[12,256,64]{1,2,0:T(8,128)(2,1)}, u32[]{:S(2)}) copy-start(bf16[12,256,64]{1,2,0:T(8,128)(2,1)} %copy-done.20) | copy-start | bytes 1179652
  101.2 1.1 copy-start.14
  102.2 1.1 copy-start.29
  105.3 28.7 %collective-permute-start.11 = (bf16[2,12,256,64]{2,3,1,0:T(8,128)(2,1)}, bf16[2,12,256,64]{2,3,1,0:T(8,128)(2,1)S(1)}, u32[]{:S(2)}, u32[]{:S(2)}) collective-permute-start(bf16[2,12,256,64]{2,3,1,0:T(8,128)(2,1)} %fusion.40), channel_id=1, source_target_pairs={{0,4},{2,6},{8,12},{10,14},{16,20},{18,22},{24,28},{26,30},{1,5},{... | collective-permute-start | bytes 2359304 | tf_op jit(solution)/shard_map/ppermute | solution.py:96
  108.7 27.9 %copy-start.15 = (bf16[768,1536]{1,0:T(8,128)(2,1)S(1)}, bf16[768,1536]{1,0:T(8,128)(2,1)}, u32[]{:S(2)}) copy-start(bf16[768,1536]{1,0:T(8,128)(2,1)} %all-gather.2.cloned.1.call-done) | copy-start | bytes 7077892
  108.7 27.9 %copy-start.19 = (bf16[256,12,64]{0,2,1:T(8,128)(2,1)S(1)}, bf16[256,12,64]{0,2,1:T(8,128)(2,1)}, u32[]{:S(2)}) copy-start(bf16[256,12,64]{0,2,1:T(8,128)(2,1)} %copy-done.18) | copy-start | bytes 1179652
  108.7 29.6 %copy-start.27 = (pred[256,256]{0,1:T(8,128)(4,1)S(1)}, pred[256,256]{0,1:T(8,128)(4,1)}, u32[]{:S(2)}) copy-start(pred[256,256]{0,1:T(8,128)(4,1)} %copy-done.26) | copy-start | bytes 196612
  108.7 50.8 %collective-permute-start.10 = (bf16[2,12,256,64]{2,3,1,0:T(8,128)(2,1)}, bf16[2,12,256,64]{2,3,1,0:T(8,128)(2,1)}, u32[]{:S(2)}, u32[]{:S(2)}) collective-permute-start(bf16[2,12,256,64]{2,3,1,0:T(8,128)(2,1)} %fusion.40), channel_id=1, source_target_pairs={{4,0},{6,2},{12,8},{14,10},{20,16},{22,18},{28,24},{30,26},{5,1},{... | collective-permute-start | bytes 2359304 | tf_op jit(solution)/shard_map/ppermute | solution.py:95
  135.3 26.3 %collective-permute-start.12 = (bf16[2,12,256,64]{2,3,1,0:T(8,128)(2,1)}, bf16[2,12,256,64]{2,3,1,0:T(8,128)(2,1)}, u32[]{:S(2)}, u32[]{:S(2)}) collective-permute-start(bf16[2,12,256,64]{2,3,1,0:T(8,128)(2,1)} %fusion.42), channel_id=1, source_target_pairs={{8,0},{10,2},{12,4},{14,6},{16,8},{18,10},{20,12},{22,14},{24,16},... | collective-permute-start | bytes 2359304 | tf_op jit(solution)/shard_map/ppermute | solution.py:18
  157.6 10.8 %copy-start.1 = (bf16[1,256,1536]{2,1,0:T(8,128)(2,1)S(1)}, bf16[1,256,1536]{2,1,0:T(8,128)(2,1)}, u32[]{:S(2)}) copy-start(bf16[1,256,1536]{2,1,0:T(8,128)(2,1)} %param.9) | copy-start | bytes 2359300
  (1 other events, 0.7 us)
Sparse Core Ops, SparseCore 0:
  25.7 42.9 all-gather.1
  81.0 72.8 reduce-scatter.2
  156.8 11.5 reduce-scatter.4

commit v10 on v9

--- a/solution.py
+++ b/solution.py
@@ -115,8 +115,8 @@
     score_scale = HEAD_DIM ** (-0.5)
     utt_lengths = lengths[0]
 
-    weight_cols = lax.all_gather(out_weight, "dp", axis=1, tiled=True)
-    weight_full = lax.all_gather(weight_cols, "seq", axis=0, tiled=True)
+    weight_rows = lax.all_gather(out_weight, "seq", axis=0, tiled=True)
+    weight_full = lax.all_gather(weight_rows, "dp", axis=1, tiled=True)
 
     query_heads = head_major(query_rows[0], tok_rows)
     own_kv = jnp.stack([head_major(key_rows[0], tok_rows), head_major(value_rows[0], tok_rows)])

time: 177 us -> 203 us (1.15)
  waiting for transfers between devices: 45.8 us -> 72 us
  blocking collectives: 6.31 us -> 0 us
  local copies, waits for them, and re-layouts: 19.9 us -> 22.3 us
  matrix products: 42.1 us -> 44.2 us
    all_gather x1 -> x2, waiting for transfers between devices: 0.02 us -> 21.2 us  [the longest x1 21.2 us: local(): weight_full = lax.all_gather(weight_rows, 'dp', axis=1, tiled=True)]
    all_gather x1 -> x0, blocking collectives: 6.31 us -> none  [local(): weight_cols = lax.all_gather(out_weight, 'dp', axis=1, tiled=True)]
    reduce_scatter x1, waiting for transfers between devices: 13.9 us -> 19.1 us  [local(): lax.psum_scatter(partial_weight.astype(jnp.bfloat16), 'seq', scatter_dime...]
    unnamed x72 -> x82, local copies, waits for them, and re-layouts: 16.1 us -> 18.5 us
    dot_general x5, matrix products: 6.16 us -> 8.39 us  [local(): jnp.einsum('hqk,hke->hqe', expo_full.astype(jnp.bfloat16), held[dist][1],...]
    reduce_scatter x1, waiting for transfers between devices: 2.56 us -> 4.66 us  [local(): lax.psum_scatter(row_share.astype(jnp.float32), 'dp', scatter_dimension=1...]
  transfers between devices with their start and end apart: 16 -> 17, of which waited for: 6 -> 8; matrix products, arithmetic and copies ran while one was open for 41% -> 37% of each run, Pallas kernels for 0% -> 0%
where the time goes in v10:
time: 203 us; the launch traced here: 201 us
  waiting for transfers between devices  72 us (35%)
  matrix products  44.2 us (22%)
  starting transfers between devices  27.2 us (13%)
  local copies, waits for them, and re-layouts  22.3 us (11%)
  other arithmetic  20.4 us (10%)
  between operations  14.4 us (7%)
    all_gather x1, waiting for transfers between devices, local(): weight_full = lax.all_gather(weight_rows, 'dp', axis=1, tiled=True)  21.2 us
    reduce_scatter x1, waiting for transfers between devices, local(): lax.psum_scatter(partial_weight.astype(jnp.bfloat16), 'seq', scatter_dime...  19.1 us
    ppermute x1, waiting for transfers between devices, return_behind(): relayed = lax.ppermute(near, 'seq', [(i, i + 2) for i in earlier])  19 us
    unnamed x82, local copies, waits for them, and re-layouts  18.5 us
    dot_general x5, matrix products, local(): jnp.einsum('hqk,hke->hqe', expo_full.astype(jnp.bfloat16), held[dist][1],...  8.39 us
    ppermute x3, starting transfers between devices, shift_up(): return lax.ppermute(block, axis, route)  8.27 us
    ppermute x2, starting transfers between devices, gather_behind(): relayed = lax.ppermute(far[k], 'seq', [(i + 2, i) for i in earlier])  8.22 us
    dot_general x5, matrix products, local(): jnp.einsum('hqe,hke->hqk', query_heads, held[dist][0], preferred_element_...  8.14 us
  transfers between devices with their start and end apart: 17, of which 8 were waited for; matrix products, arithmetic and copies ran while one was open for 37% of the time, Pallas kernels for 0%

profile of v10, /device:TPU:4, one launch (start us, length us, event | category | flops | bytes accessed | tf_op | source)
XLA Modules:
  0.0 200.6 jit_solution(7682936424300401785)
XLA Ops:
  7.2 1.2 copy.84
  8.5 3.5 %collective-permute-start.1 = (bf16[12,256,64]{1,2,0:T(8,128)(2,1)S(1)}, bf16[12,256,64]{1,2,0:T(8,128)(2,1)S(1)}, u32[]{:S(2)}, u32[]{:S(2)}) collective-permute-start(bf16[12,256,64]{1,2,0:T(8,128)(2,1)S(1)} %bitcast.223), channel_id=1, source_target_pairs={{0,8},{2,10},{4,12},{6,14},{8,16},{10,18},{12,20},{14,22},{16,24},... | collective-permute-start | bytes 1179656 | tf_op jit(solution)/shard_map/ppermute | solution.py:18
  12.0 1.3 collective-permute-start
  13.3 1.2 copy.86
  14.4 3.5 %collective-permute-start.4 = (bf16[12,256,64]{1,2,0:T(8,128)(2,1)S(1)}, bf16[12,256,64]{1,2,0:T(8,128)(2,1)S(1)}, u32[]{:S(2)}, u32[]{:S(2)}) collective-permute-start(bf16[12,256,64]{1,2,0:T(8,128)(2,1)S(1)} %bitcast.243), channel_id=1, source_target_pairs={{0,8},{2,10},{4,12},{6,14},{8,16},{10,18},{12,20},{14,22},{16,24},... | collective-permute-start | bytes 1179656 | tf_op jit(solution)/shard_map/ppermute | solution.py:18
  17.9 1.3 collective-permute-start.3
  20.4 1.0 collective-permute-done.1
  21.5 5.1 %collective-permute-start.2 = (bf16[12,256,64]{1,2,0:T(8,128)(2,1)S(1)}, bf16[12,256,64]{1,2,0:T(8,128)(2,1)}, u32[]{:S(2)}, u32[]{:S(2)}) collective-permute-start(bf16[12,256,64]{1,2,0:T(8,128)(2,1)S(1)} %collective-permute-done.1), channel_id=1, source_target_pairs={{4,0},{6,2},{12,8},{14,10},{20,16},{22,18},{28,24},{30,26},{5,1},{... | collective-permute-start | bytes 1179656 | tf_op jit(solution)/shard_map/ppermute | solution.py:58
  27.1 1.2 copy.83
  28.7 3.2 %collective-permute-start.5 = (bf16[12,256,64]{1,2,0:T(8,128)(2,1)S(1)}, bf16[12,256,64]{1,2,0:T(8,128)(2,1)}, u32[]{:S(2)}, u32[]{:S(2)}) collective-permute-start(bf16[12,256,64]{1,2,0:T(8,128)(2,1)S(1)} %collective-permute-done.4), channel_id=1, source_target_pairs={{4,0},{6,2},{12,8},{14,10},{20,16},{22,18},{28,24},{30,26},{5,1},{... | collective-permute-start | bytes 1179656 | tf_op jit(solution)/shard_map/ppermute | solution.py:58
  31.9 2.3 %select_reduce_fusion.1 = (f32[12,256]{1,0:T(8,128)S(1)}, f32[12,256,256]{1,2,0:T(8,128)}) fusion(pred[256,256]{0,1:T(8,128)(4,1)S(1)} %get-tuple-element.40, bf16[12,256,64]{1,2,0:T(8,128)(2,1)S(1)} %bitcast.213, bf16[12,256,64]{1,2,0:T(8,128)(2,1)S(1)} %bitcast.225), kind=kOutput, calls=%fused_computation.29 | convolution fusion | flops 103019520 | bytes 4009984 | tf_op jit(solution)/shard_map/hqe,hke->hqk/dot_general | solution.py:139
  35.0 1.1 collective-permute-done.2
  37.2 5.3 %collective-permute-done.5 = bf16[12,256,64]{1,2,0:T(8,128)(2,1)} collective-permute-done((bf16[12,256,64]{1,2,0:T(8,128)(2,1)S(1)}, bf16[12,256,64]{1,2,0:T(8,128)(2,1)}, u32[]{:S(2)}, u32[]{:S(2)}) %collective-permute-start.5) | collective-permute-done | bytes 393248 | tf_op jit(solution)/shard_map/ppermute | solution.py:58
  43.5 2.4 %maximum_select_fusion = (bf16[2,12,256,64]{2,3,1,0:T(8,128)(2,1)}, bf16[2,12,256,64]{2,3,1,0:T(8,128)(2,1)}) fusion(bf16[1,12,256,64]{2,3,1,0:T(8,128)(2,1)S(1)} %bitcast.245, bf16[1,12,256,64]{2,3,1,0:T(8,128)(2,1)S(1)} %bitcast.226, pred[]{:T(512)S(6)} %eq.101, bf16[1,12,256,64]{2,3,1,0:T(8,128)(2,1)S(1)} %bitcast.248, ...), kind=kLoop, calls=%fused_computation.122 | loop fusion | flops 1966080 | bytes 3932161 | tf_op jit(solution)/shard_map/jit(_where)/select_n | solution.py:66
  45.9 2.3 %convolution_multiply_fusion = f32[12,256,256]{2,1,0:T(8,128)} fusion(bf16[12,256,64]{1,2,0:T(8,128)(2,1)S(1)} %bitcast.214, bf16[12,256,64]{1,2,0:T(8,128)(2,1)S(1)} %collective-permute-done.1), kind=kOutput, calls=%fused_computation.47 | convolution fusion | flops 101449728 | bytes 3932160 | tf_op jit(solution)/shard_map/hqe,hke->hqk/dot_general | solution.py:139
  48.3 3.6 %copy.88 = f32[12,256,256]{1,2,0:T(8,128)} copy(f32[12,256,256]{2,1,0:T(8,128)} %convolution_multiply_fusion) | data formatting | bytes 6291456 | tf_op jit(solution)/shard_map/mul | solution.py:139
  52.3 2.2 %select_reduce_fusion = f32[12,256]{1,0:T(8,128)S(1)} fusion(f32[12,256,256]{1,2,0:T(8,128)} %copy.88, pred[256,256]{0,1:T(8,128)(4,1)S(1)} %get-tuple-element.39), kind=kLoop, calls=%fused_computation.28 | loop fusion | flops 1569792 | bytes 3223552 | tf_op jit(solution)/shard_map/reduce_max | solution.py:144
  55.2 2.1 %fusion.6 = (f32[12,256]{1,0:T(8,128)S(1)}, f32[12,256,256]{2,1,0:T(8,128)S(1)}) fusion(pred[256,256]{0,1:T(8,128)(4,1)S(1)} %get-tuple-element.36, bf16[12,256,64]{1,2,0:T(8,128)(2,1)S(1)} %bitcast.216, bf16[2,12,256,64]{2,3,1,0:T(8,128)(2,1)} %collective-permute-done.6), kind=kOutput, calls=%fused_computation.25 | convolution fusion | flops 103019520 | bytes 4009984 | tf_op jit(solution)/shard_map/hqe,hke->hqk/dot_general | solution.py:139
  59.4 1.5 copy-done.10
  61.7 4.5 %fusion.19 = (f32[12,256]{1,0:T(8,128)S(1)}, f32[12,256]{1,0:T(8,128)S(1)}, f32[12,256]{1,0:T(8,128)}, f32[12,256]{1,0:T(8,128)}, f32[12,256]{1,0:T(8,128)}) fusion(f32[12,256,256]{2,1,0:T(8,128)S(1)} %get-tuple-element.48, f32[12,256]{1,0:T(8,128)S(1)} %maximum_maximum_fusion, pred[256,256]{0,1:T(8,128)(4,1)S(1)} %get-tuple-element.36, ...), kind=kLoop, calls=%fused_computation.41 | loop fusion | flops 18859008 | bytes 16130048 | tf_op jit(solution)/shard_map/reduce_sum | solution.py:152
  67.4 2.7 %fusion.33 = f32[12,256,64]{1,2,0:T(8,128)S(1)} fusion(bf16[12,256,64]{1,2,0:T(8,128)(2,1)S(1)} %copy-done.25, f32[12,256,256]{1,2,0:T(8,128)} %copy.88, f32[12,256]{1,0:T(8,128)S(1)} %maximum_maximum_fusion, pred[256,256]{0,1:T(8,128)(4,1)S(1)} %get-tuple-element.39), kind=kOutput, calls=%fused_computation.52 | convolution fusion | flops 103809024 | bytes 4403200 | tf_op jit(solution)/shard_map/hqk,hke->hqe/dot_general | solution.py:153
  73.1 1.3 copy-done.14
  74.4 2.1 %fusion.101 = f32[12,256,64]{1,2,0:T(8,128)S(1)} fusion(f32[12,256,64]{1,2,0:T(8,128)S(1)} %fusion.66, f32[12,256,256]{2,1,0:T(8,128)S(1)} %copy-done.14, f32[12,256]{1,0:T(8,128)S(1)} %maximum_maximum_fusion, pred[256,256]{0,1:T(8,128)(4,1)S(1)} %get-tuple-element.36, bf16[2,12,256,64]{2,3,1,0:T(8,128)(2,1)} %collective-permute-done.6), kind=kOutput, calls=%fused_computation.116 | convolution fusion | flops 104792064 | bytes 5189632 | tf_op jit(solution)/shard_map/hqk,hke->hqe/dot_general | solution.py:153
  76.6 1.9 fusion.116
  79.2 2.2 %convolution_convert_fusion = bf16[768,1536]{1,0:T(8,128)(2,1)} fusion(bf16[256,768]{0,1:T(8,128)(2,1)S(1)} %bitcast.241, bf16[1,256,1536]{2,1,0:T(8,128)(2,1)S(1)} %copy-done), kind=kOutput, calls=%fused_computation | convolution fusion | flops 605159424 | bytes 3538944 | tf_op jit(solution)/shard_map/dot_general | solution.py:173
  81.4 21.2 %all-gather.5.cloned.1.call-done = bf16[768,1536]{1,0:T(8,128)(2,1)} async-done(((bf16[768,768]{1,0:T(8,128)(2,1)}), bf16[768,1536]{1,0:T(8,128)(2,1)}) %all-gather.5.cloned.1.call-update) | async-done | bytes 2359312 | tf_op jit(solution)/shard_map/all_gather | solution.py:119
  102.6 2.5 %convolution_convert_fusion.2 = bf16[256,768]{1,0:T(8,128)(2,1)S(1)} fusion(bf16[768,1536]{1,0:T(8,128)(2,1)} %all-gather.5.cloned.1.call-done, bf16[1,256,1536]{2,1,0:T(8,128)(2,1)S(1)} %copy-done), kind=kOutput, calls=%fused_computation.121 | convolution fusion | flops 604176384 | bytes 3538944 | tf_op jit(solution)/shard_map/dot_general | solution.py:169
  105.3 2.7 %fusion.84 = f32[1,12,256,64]{2,3,1,0:T(8,128)S(1)} fusion(bf16[12,256,64]{1,2,0:T(8,128)(2,1)S(1)} %bitcast.228, f32[12,256,256]{2,1,0:T(8,128)} %copy-done.13, f32[12,256]{1,0:T(8,128)S(1)} %get-tuple-element.30, pred[256,256]{0,1:T(8,128)(4,1)S(1)} %get-tuple-element.36), kind=kOutput, calls=%fused_computation.98 | convolution fusion | flops 103809024 | bytes 4403200 | tf_op jit(solution)/shard_map/hqk,hqe->hke/dot_general | solution.py:216
  110.3 1.1 multiply_convert_fusion.1
  112.2 1.1 multiply_convert_fusion
  114.1 2.4 %multiply_convert_fusion.3 = bf16[12,256,256]{1,2,0:T(8,128)(2,1)S(1)} fusion(f32[12,256,256]{2,1,0:T(8,128)S(1)} %copy-done.15, bf16[12,256,64]{1,2,0:T(8,128)(2,1)S(1)} %bitcast.233, f32[12,256]{1,0:T(8,128)S(1)} %multiply_reduce_fusion, f32[12,256]{1,0:T(8,128)S(1)} %get-tuple-element.30, pred[256,256]{0,1:T(8,128)(4,1)S(1)} %get-tuple-element.36, ...), kind=kOutput, calls=%fused_computation.18 | convolution fusion | flops 105381888 | bytes 5595136 | tf_op jit(solution)/shard_map/hqe,hke->hqk/dot_general | solution.py:204
  117.7 1.1 multiply_convert_fusion.4
  120.2 1.5 fusion.117
  125.3 1.3 fusion.40
  126.6 1.3 collective-permute-start.11
  128.9 1.1 fusion.113
  130.0 5.7 %collective-permute-start.10 = (bf16[2,12,256,64]{2,3,1,0:T(8,128)(2,1)}, bf16[2,12,256,64]{2,3,1,0:T(8,128)(2,1)}, u32[]{:S(2)}, u32[]{:S(2)}) collective-permute-start(bf16[2,12,256,64]{2,3,1,0:T(8,128)(2,1)} %fusion.40), channel_id=1, source_target_pairs={{4,0},{6,2},{12,8},{14,10},{20,16},{22,18},{28,24},{30,26},{5,1},{... | collective-permute-start | bytes 2359304 | tf_op jit(solution)/shard_map/ppermute | solution.py:95
  135.7 19.0 %collective-permute-done.11 = bf16[2,12,256,64]{2,3,1,0:T(8,128)(2,1)S(1)} collective-permute-done((bf16[2,12,256,64]{2,3,1,0:T(8,128)(2,1)}, bf16[2,12,256,64]{2,3,1,0:T(8,128)(2,1)S(1)}, u32[]{:S(2)}, u32[]{:S(2)}) %collective-permute-start.11) | collective-permute-done | bytes 786464 | tf_op jit(solution)/shard_map/ppermute | solution.py:96
  154.7 1.3 fusion.42
  156.1 1.3 collective-permute-start.12
  157.4 1.7 fusion.10
  159.0 1.6 fusion.81
  160.7 19.1 %reduce-scatter.3.cloned.1.call-done = bf16[48,1536]{1,0:T(8,128)(2,1)} async-done(((bf16[768,1536]{1,0:T(8,128)(2,1)}), bf16[48,1536]{1,0:T(8,128)(2,1)}) %reduce-scatter.3.cloned.1.call-update) | async-done | bytes 147472 | tf_op jit(solution)/shard_map/reduce_scatter | solution.py:176
  179.7 1.6 convert_element_type.187
  181.4 2.0 fusion.99
  183.4 2.0 copy.116
  185.4 2.1 %fusion.39 = bf16[2,12,256,64]{2,3,1,0:T(8,128)(2,1)S(1)} fusion(f32[1,12,256,64]{2,3,1,0:T(8,128)} %fusion.81, f32[1,12,256,64]{2,3,1,0:T(8,128)S(1)} %fusion.99, bf16[2,12,256,64]{2,3,1,0:T(8,128)(2,1)} %collective-permute-done.12, bf16[2,12,256,64]{2,3,1,0:T(8,128)(2,1)} %collective-permute-done.10, f32[2,12,256,64]{2,3,1,0:T(8,128)S(1)} %collective-permute-done.8, ...), kind=kLoop, calls=%fused_computation.57 | loop fusion | flops 3538944 | bytes 5505026 | tf_op jit(solution)/shard_map/convert.1
  189.4 4.7 %reduce-scatter.5.cloned.1.call-done = f32[48,768]{1,0:T(8,128)} async-done(((f32[48,1536]{1,0:T(8,128)}), f32[48,768]{1,0:T(8,128)}) %reduce-scatter.5.cloned.1.call-update) | async-done | bytes 147472 | tf_op jit(solution)/shard_map/reduce_scatter | solution.py:179
  (135 shorter events, 26.7 us)
Async XLA Ops:
  7.2 72.0 %copy-start = (bf16[1,256,1536]{2,1,0:T(8,128)(2,1)S(1)}, bf16[1,256,1536]{2,1,0:T(8,128)(2,1)}, u32[]{:S(2)}) copy-start(bf16[1,256,1536]{2,1,0:T(8,128)(2,1)} %param.9) | copy-start | bytes 2359300
  7.2 59.0 %all-gather.3.cloned.1.call-start = ((), (), s32[]{:S(2)}) async-start(), calls=%async_computation.2 | async-start | bytes 1253376 | tf_op jit(solution)/shard_map/all_gather | solution.py:118
  8.5 13.0 %collective-permute-start.1 = (bf16[12,256,64]{1,2,0:T(8,128)(2,1)S(1)}, bf16[12,256,64]{1,2,0:T(8,128)(2,1)S(1)}, u32[]{:S(2)}, u32[]{:S(2)}) collective-permute-start(bf16[12,256,64]{1,2,0:T(8,128)(2,1)S(1)} %bitcast.223), channel_id=1, source_target_pairs={{0,8},{2,10},{4,12},{6,14},{8,16},{10,18},{12,20},{14,22},{16,24},... | collective-permute-start | bytes 1179656 | tf_op jit(solution)/shard_map/ppermute | solution.py:18
  12.0 22.2 %collective-permute-start = (bf16[12,256,64]{1,2,0:T(8,128)(2,1)S(1)}, bf16[12,256,64]{1,2,0:T(8,128)(2,1)S(1)}, u32[]{:S(2)}, u32[]{:S(2)}) collective-permute-start(bf16[12,256,64]{1,2,0:T(8,128)(2,1)S(1)} %bitcast.224), channel_id=1, source_target_pairs={{0,4},{2,6},{8,12},{10,14},{16,20},{18,22},{24,28},{26,30},{1,5},{... | collective-permute-start | bytes 1179656 | tf_op jit(solution)/shard_map/ppermute | solution.py:57
  14.4 14.3 %collective-permute-start.4 = (bf16[12,256,64]{1,2,0:T(8,128)(2,1)S(1)}, bf16[12,256,64]{1,2,0:T(8,128)(2,1)S(1)}, u32[]{:S(2)}, u32[]{:S(2)}) collective-permute-start(bf16[12,256,64]{1,2,0:T(8,128)(2,1)S(1)} %bitcast.243), channel_id=1, source_target_pairs={{0,8},{2,10},{4,12},{6,14},{8,16},{10,18},{12,20},{14,22},{16,24},... | collective-permute-start | bytes 1179656 | tf_op jit(solution)/shard_map/ppermute | solution.py:18
  17.9 19.2 %collective-permute-start.3 = (bf16[12,256,64]{1,2,0:T(8,128)(2,1)S(1)}, bf16[12,256,64]{1,2,0:T(8,128)(2,1)}, u32[]{:S(2)}, u32[]{:S(2)}) collective-permute-start(bf16[12,256,64]{1,2,0:T(8,128)(2,1)S(1)} %bitcast.244), channel_id=1, source_target_pairs={{0,4},{2,6},{8,12},{10,14},{16,20},{18,22},{24,28},{26,30},{1,5},{... | collective-permute-start | bytes 1179656 | tf_op jit(solution)/shard_map/ppermute | solution.py:57
  19.3 83.4 %all-gather.5.cloned.1.call-start = ((), (), s32[]{:S(2)}) async-start(), calls=%async_computation.3 | async-start | bytes 3538944 | tf_op jit(solution)/shard_map/all_gather | solution.py:119
  21.5 24.5 %copy-start.17 = (bf16[12,256,64]{1,2,0:T(8,128)(2,1)}, bf16[12,256,64]{1,2,0:T(8,128)(2,1)S(1)}, u32[]{:S(2)}) copy-start(bf16[12,256,64]{1,2,0:T(8,128)(2,1)S(1)} %collective-permute-done.1) | copy-start | bytes 1179652
  21.5 14.6 %collective-permute-start.2 = (bf16[12,256,64]{1,2,0:T(8,128)(2,1)S(1)}, bf16[12,256,64]{1,2,0:T(8,128)(2,1)}, u32[]{:S(2)}, u32[]{:S(2)}) collective-permute-start(bf16[12,256,64]{1,2,0:T(8,128)(2,1)S(1)} %collective-permute-done.1), channel_id=1, source_target_pairs={{4,0},{6,2},{12,8},{14,10},{20,16},{22,18},{28,24},{30,26},{5,1},{... | collective-permute-start | bytes 1179656 | tf_op jit(solution)/shard_map/ppermute | solution.py:58
  27.0 40.4 %copy-start.20 = (pred[256,256]{0,1:T(8,128)(4,1)}, pred[256,256]{0,1:T(8,128)(4,1)S(1)}, u32[]{:S(2)}) copy-start(pred[256,256]{0,1:T(8,128)(4,1)S(1)} %get-tuple-element.39) | copy-start | bytes 196612
  27.0 81.0 %copy-start.35 = (pred[256,256]{0,1:T(8,128)(4,1)}, pred[256,256]{0,1:T(8,128)(4,1)S(1)}, u32[]{:S(2)}) copy-start(pred[256,256]{0,1:T(8,128)(4,1)S(1)} %get-tuple-element.38) | copy-start | bytes 196612
  27.0 82.4 %copy-start.33 = (pred[256,256]{0,1:T(8,128)(4,1)}, pred[256,256]{0,1:T(8,128)(4,1)S(1)}, u32[]{:S(2)}) copy-start(pred[256,256]{0,1:T(8,128)(4,1)S(1)} %get-tuple-element.37) | copy-start | bytes 196612
  27.1 84.3 %copy-start.31 = (pred[256,256]{0,1:T(8,128)(4,1)}, pred[256,256]{0,1:T(8,128)(4,1)S(1)}, u32[]{:S(2)}) copy-start(pred[256,256]{0,1:T(8,128)(4,1)S(1)} %get-tuple-element.40) | copy-start | bytes 196612
  28.7 8.4 %copy-start.24 = (bf16[12,256,64]{1,2,0:T(8,128)(2,1)}, bf16[12,256,64]{1,2,0:T(8,128)(2,1)S(1)}, u32[]{:S(2)}) copy-start(bf16[12,256,64]{1,2,0:T(8,128)(2,1)S(1)} %collective-permute-done.4) | copy-start | bytes 1179652
  28.7 13.8 %collective-permute-start.5 = (bf16[12,256,64]{1,2,0:T(8,128)(2,1)S(1)}, bf16[12,256,64]{1,2,0:T(8,128)(2,1)}, u32[]{:S(2)}, u32[]{:S(2)}) collective-permute-start(bf16[12,256,64]{1,2,0:T(8,128)(2,1)S(1)} %collective-permute-done.4), channel_id=1, source_target_pairs={{4,0},{6,2},{12,8},{14,10},{20,16},{22,18},{28,24},{30,26},{5,1},{... | collective-permute-start | bytes 1179656 | tf_op jit(solution)/shard_map/ppermute | solution.py:58
  45.9 9.3 %collective-permute-start.6 = (bf16[2,12,256,64]{2,3,1,0:T(8,128)(2,1)}, bf16[2,12,256,64]{2,3,1,0:T(8,128)(2,1)}, u32[]{:S(2)}, u32[]{:S(2)}) collective-permute-start(bf16[2,12,256,64]{2,3,1,0:T(8,128)(2,1)} %get-tuple-element.34), channel_id=1, source_target_pairs={{0,2},{2,0},{4,6},{6,4},{8,10},{10,8},{12,14},{14,12},{16,18},{18,... | collective-permute-start | bytes 2359304 | tf_op jit(solution)/shard_map/ppermute | solution.py:23
  51.9 5.5 %collective-permute-start.7 = (bf16[2,12,256,64]{2,3,1,0:T(8,128)(2,1)}, bf16[2,12,256,64]{2,3,1,0:T(8,128)(2,1)S(1)}, u32[]{:S(2)}, u32[]{:S(2)}) collective-permute-start(bf16[2,12,256,64]{2,3,1,0:T(8,128)(2,1)} %get-tuple-element.35), channel_id=1, source_target_pairs={{0,2},{2,0},{4,6},{6,4},{8,10},{10,8},{12,14},{14,12},{16,18},{18,... | collective-permute-start | bytes 2359304 | tf_op jit(solution)/shard_map/ppermute | solution.py:23
  55.2 3.3 %copy-start.7 = (f32[12,256,256]{2,1,0:T(8,128)}, f32[12,256,256]{2,1,0:T(8,128)S(1)}, u32[]{:S(2)}) copy-start(f32[12,256,256]{2,1,0:T(8,128)S(1)} %get-tuple-element.44) | copy-start | bytes 9437188
  55.2 5.7 %copy-start.2 = (f32[12,256,256]{1,2,0:T(8,128)S(1)}, f32[12,256,256]{1,2,0:T(8,128)}, u32[]{:S(2)}) copy-start(f32[12,256,256]{1,2,0:T(8,128)} %copy.88) | copy-start | bytes 9437188
  55.2 6.5 %copy-start.4 = (f32[12,256,256]{1,2,0:T(8,128)S(1)}, f32[12,256,256]{1,2,0:T(8,128)}, u32[]{:S(2)}) copy-start(f32[12,256,256]{1,2,0:T(8,128)} %get-tuple-element.46) | copy-start | bytes 9437188
  57.4 2.0 copy-start.13
  57.4 1.2 copy-start.28
  58.1 2.8 %copy-start.10 = (f32[12,256,256]{2,1,0:T(8,128)}, f32[12,256,256]{2,1,0:T(8,128)S(1)}, u32[]{:S(2)}) copy-start(f32[12,256,256]{2,1,0:T(8,128)S(1)} %get-tuple-element.42) | copy-start | bytes 9437188
  61.7 5.7 %copy-start.25 = (bf16[12,256,64]{1,2,0:T(8,128)(2,1)S(1)}, bf16[12,256,64]{1,2,0:T(8,128)(2,1)}, u32[]{:S(2)}) copy-start(bf16[12,256,64]{1,2,0:T(8,128)(2,1)} %copy-done.24) | copy-start | bytes 1179652
  66.2 113.5 %reduce-scatter.3.cloned.1.call-start = ((), (), s32[]{:S(2)}) async-start(), calls=%async_computation.4 | async-start | bytes 2506752 | tf_op jit(solution)/shard_map/reduce_scatter | solution.py:176
  66.4 3.6 %copy-start.5 = (f32[12,256,256]{1,2,0:T(8,128)S(1)}, f32[12,256,256]{1,2,0:T(8,128)}, u32[]{:S(2)}) copy-start(f32[12,256,256]{1,2,0:T(8,128)} %get-tuple-element.46) | copy-start | bytes 9437188
  70.1 1.9 copy-start.11
  70.1 2.1 %copy-start.29 = (bf16[2,12,256,64]{2,3,1,0:T(8,128)(2,1)S(1)}, bf16[2,12,256,64]{2,3,1,0:T(8,128)(2,1)}, u32[]{:S(2)}) copy-start(bf16[2,12,256,64]{2,3,1,0:T(8,128)(2,1)} %copy-done.28) | copy-start | bytes 2359300
  72.2 2.2 %copy-start.14 = (f32[12,256,256]{2,1,0:T(8,128)S(1)}, f32[12,256,256]{2,1,0:T(8,128)}, u32[]{:S(2)}) copy-start(f32[12,256,256]{2,1,0:T(8,128)} %copy-done.13) | copy-start | bytes 9437188
  74.4 2.2 %copy-start.8 = (f32[12,256,256]{2,1,0:T(8,128)S(1)}, f32[12,256,256]{2,1,0:T(8,128)}, u32[]{:S(2)}) copy-start(f32[12,256,256]{2,1,0:T(8,128)} %copy-done.7) | copy-start | bytes 9437188
  81.4 112.7 %reduce-scatter.5.cloned.1.call-start = ((), (), s32[]{:S(2)}) async-start(), calls=%async_computation.5 | async-start | bytes 442368 | tf_op jit(solution)/shard_map/reduce_scatter | solution.py:179
  105.3 2.8 %copy-start.12 = (f32[12,256,256]{2,1,0:T(8,128)S(1)}, f32[12,256,256]{2,1,0:T(8,128)}, u32[]{:S(2)}) copy-start(f32[12,256,256]{2,1,0:T(8,128)} %copy-done.10) | copy-start | bytes 9437188
  108.1 2.1 %copy-start.9 = (f32[12,256,256]{2,1,0:T(8,128)S(1)}, f32[12,256,256]{2,1,0:T(8,128)}, u32[]{:S(2)}) copy-start(f32[12,256,256]{2,1,0:T(8,128)} %copy-done.7) | copy-start | bytes 9437188
  110.3 1.9 copy-start.6
  112.2 1.9 copy-start.15
  114.1 5.7 %copy-start.16 = (bf16[12,256,256]{1,2,0:T(8,128)(2,1)}, bf16[12,256,256]{1,2,0:T(8,128)(2,1)S(1)}, u32[]{:S(2)}) copy-start(bf16[12,256,256]{1,2,0:T(8,128)(2,1)S(1)} %multiply_convert_fusion) | copy-start | bytes 4718596
  117.3 8.0 %collective-permute-start.8 = (f32[2,12,256,64]{2,3,1,0:T(8,128)S(1)}, f32[2,12,256,64]{2,3,1,0:T(8,128)S(1)}, u32[]{:S(2)}, u32[]{:S(2)}) collective-permute-start(f32[2,12,256,64]{2,3,1,0:T(8,128)S(1)} %pad_maximum_fusion), channel_id=1, source_target_pairs={{0,2},{2,0},{4,6},{6,4},{8,10},{10,8},{12,14},{14,12},{16,18},{18,... | collective-permute-start | bytes 4718600 | tf_op jit(solution)/shard_map/ppermute | solution.py:23
  119.5 5.7 %collective-permute-start.9 = (f32[2,12,256,64]{2,3,1,0:T(8,128)S(1)}, f32[2,12,256,64]{2,3,1,0:T(8,128)S(1)}, u32[]{:S(2)}, u32[]{:S(2)}) collective-permute-start(f32[2,12,256,64]{2,3,1,0:T(8,128)S(1)} %pad_maximum_fusion.1), channel_id=1, source_target_pairs={{0,2},{2,0},{4,6},{6,4},{8,10},{10,8},{12,14},{14,12},{16,18},{18,... | collective-permute-start | bytes 4718600 | tf_op jit(solution)/shard_map/ppermute | solution.py:23
  120.2 2.2 %copy-start.3 = (f32[12,256,256]{1,2,0:T(8,128)S(1)}, f32[12,256,256]{1,2,0:T(8,128)}, u32[]{:S(2)}) copy-start(f32[12,256,256]{1,2,0:T(8,128)} %copy.88) | copy-start | bytes 9437188
  120.2 2.2 %copy-start.21 = (pred[256,256]{0,1:T(8,128)(4,1)S(1)}, pred[256,256]{0,1:T(8,128)(4,1)}, u32[]{:S(2)}) copy-start(pred[256,256]{0,1:T(8,128)(4,1)} %copy-done.20) | copy-start | bytes 196612
  120.2 2.2 %copy-start.26 = (bf16[12,256,64]{1,2,0:T(8,128)(2,1)S(1)}, bf16[12,256,64]{1,2,0:T(8,128)(2,1)}, u32[]{:S(2)}) copy-start(bf16[12,256,64]{1,2,0:T(8,128)(2,1)} %copy-done.24) | copy-start | bytes 1179652
  126.6 28.2 %collective-permute-start.11 = (bf16[2,12,256,64]{2,3,1,0:T(8,128)(2,1)}, bf16[2,12,256,64]{2,3,1,0:T(8,128)(2,1)S(1)}, u32[]{:S(2)}, u32[]{:S(2)}) collective-permute-start(bf16[2,12,256,64]{2,3,1,0:T(8,128)(2,1)} %fusion.40), channel_id=1, source_target_pairs={{0,4},{2,6},{8,12},{10,14},{16,20},{18,22},{24,28},{26,30},{1,5},{... | collective-permute-start | bytes 2359304 | tf_op jit(solution)/shard_map/ppermute | solution.py:96
  130.0 27.3 %copy-start.19 = (bf16[768,1536]{1,0:T(8,128)(2,1)S(1)}, bf16[768,1536]{1,0:T(8,128)(2,1)}, u32[]{:S(2)}) copy-start(bf16[768,1536]{1,0:T(8,128)(2,1)} %all-gather.5.cloned.1.call-done) | copy-start | bytes 7077892
  130.0 27.4 %copy-start.23 = (bf16[256,12,64]{0,2,1:T(8,128)(2,1)S(1)}, bf16[256,12,64]{0,2,1:T(8,128)(2,1)}, u32[]{:S(2)}) copy-start(bf16[256,12,64]{0,2,1:T(8,128)(2,1)} %copy-done.22) | copy-start | bytes 1179652
  130.0 29.0 %copy-start.32 = (pred[256,256]{0,1:T(8,128)(4,1)S(1)}, pred[256,256]{0,1:T(8,128)(4,1)}, u32[]{:S(2)}) copy-start(pred[256,256]{0,1:T(8,128)(4,1)} %copy-done.31) | copy-start | bytes 196612
  130.0 55.4 %collective-permute-start.10 = (bf16[2,12,256,64]{2,3,1,0:T(8,128)(2,1)}, bf16[2,12,256,64]{2,3,1,0:T(8,128)(2,1)}, u32[]{:S(2)}, u32[]{:S(2)}) collective-permute-start(bf16[2,12,256,64]{2,3,1,0:T(8,128)(2,1)} %fusion.40), channel_id=1, source_target_pairs={{4,0},{6,2},{12,8},{14,10},{20,16},{22,18},{28,24},{30,26},{5,1},{... | collective-permute-start | bytes 2359304 | tf_op jit(solution)/shard_map/ppermute | solution.py:95
  156.1 29.3 %collective-permute-start.12 = (bf16[2,12,256,64]{2,3,1,0:T(8,128)(2,1)}, bf16[2,12,256,64]{2,3,1,0:T(8,128)(2,1)}, u32[]{:S(2)}, u32[]{:S(2)}) collective-permute-start(bf16[2,12,256,64]{2,3,1,0:T(8,128)(2,1)} %fusion.42), channel_id=1, source_target_pairs={{8,0},{10,2},{12,4},{14,6},{16,8},{18,10},{20,12},{22,14},{24,16},... | collective-permute-start | bytes 2359304 | tf_op jit(solution)/shard_map/ppermute | solution.py:18
  183.4 10.7 %copy-start.1 = (bf16[1,256,1536]{2,1,0:T(8,128)(2,1)S(1)}, bf16[1,256,1536]{2,1,0:T(8,128)(2,1)}, u32[]{:S(2)}) copy-start(bf16[1,256,1536]{2,1,0:T(8,128)(2,1)} %param.9) | copy-start | bytes 2359300
  (7 other events, 7.0 us)
Sparse Core Ops, SparseCore 0:
  19.4 38.7 all-gather.2
  66.3 36.2 all-gather.4
  106.4 73.2 reduce-scatter.2
  182.5 11.5 reduce-scatter.4

commit v11 on v9

--- a/solution.py
+++ b/solution.py
@@ -21,6 +21,26 @@
 def swap_partner(block, axis):
     count = lax.axis_size(axis)
     return lax.ppermute(block, axis, [(i, i ^ 1) for i in range(count)])
+
+
+def halving_scatter(total, axis, dim, sends_narrow):
+    count = lax.axis_size(axis)
+    if count & (count - 1):
+        return lax.psum_scatter(total, axis, scatter_dimension=dim, tiled=True)
+    me = lax.axis_index(axis)
+    bits = count.bit_length() - 1
+    moved = jnp.moveaxis(total, dim, 0)
+    rest = moved.shape[1:]
+    blocks = moved.reshape((2,) * bits + (moved.shape[0] // count,) + rest)
+    for step in range(bits):
+        own_bit = (me >> step) % 2
+        keep = lax.dynamic_index_in_dim(blocks, own_bit, blocks.ndim - len(rest) - 2, keepdims=False)
+        give = lax.dynamic_index_in_dim(blocks, 1 - own_bit, blocks.ndim - len(rest) - 2, keepdims=False)
+        if sends_narrow[step]:
+            give = give.astype(jnp.bfloat16)
+        got = lax.ppermute(give, axis, [(i, i ^ (1 << step)) for i in range(count)])
+        blocks = keep + got.astype(keep.dtype)
+    return jnp.moveaxis(blocks, 0, dim)
 
 
 def frame_labels(utt_lengths, first_frame, frame_count, total_frames):
@@ -176,9 +196,7 @@
     row_share = lax.psum_scatter(
         partial_weight.astype(jnp.bfloat16), "seq", scatter_dimension=0, tiled=True
     )
-    weight_grad = lax.psum_scatter(
-        row_share.astype(jnp.float32), "dp", scatter_dimension=1, tiled=True
-    )
+    weight_grad = halving_scatter(row_share.astype(jnp.float32), "dp", 1, [False] * 8)
 
     grad_heads = head_major(att_grad, tok_rows)
     delta_rows = jnp.sum(

time: 177 us -> 178 us (level)
  waiting for transfers between devices: 45.8 us -> 39.1 us
  other arithmetic: 18.9 us -> 22.5 us
  starting transfers between devices: 27.4 us -> 29.4 us
    reduce_scatter x1, waiting for transfers between devices: 13.9 us -> 6.92 us  [local(): lax.psum_scatter(partial_weight.astype(jnp.bfloat16), 'seq', scatter_dime...]
    ppermute x1, waiting for transfers between devices: 19.3 us -> 14 us  [return_behind(): relayed = lax.ppermute(near, 'seq', [(i, i + 2) for i in earlier])]
    ppermute x3, waiting for transfers between devices: 2.12 us -> 7.35 us  [shift_up(): return lax.ppermute(block, axis, route)]
    ppermute x0 -> x1, waiting for transfers between devices: none -> 2.89 us  [halving_scatter(): got = lax.ppermute(give, axis, [(i, i ^ 1 << step) for i in range(count)])]
    reduce_scatter x1 -> x0, waiting for transfers between devices: 2.56 us -> none  [local(): lax.psum_scatter(row_share.astype(jnp.float32), 'dp', scatter_dimension=1...]
    another operation x2, other arithmetic: 0.29 us -> 2.59 us  [local(): parts[dist] = jnp.stack([key_part, value_part])]
    unnamed x72 -> x87, local copies, waits for them, and re-layouts: 16.1 us -> 16.1 us
  transfers between devices with their start and end apart: 16 -> 16, of which waited for: 6 -> 6; matrix products, arithmetic and copies ran while one was open for 41% -> 40% of each run, Pallas kernels for 0% -> 0%
where the time goes in v11:
time: 178 us; the launch traced here: 176 us
  matrix products  43.2 us (24%)
  waiting for transfers between devices  39.1 us (22%)
  starting transfers between devices  29.4 us (17%)
  other arithmetic  22.5 us (13%)
  local copies, waits for them, and re-layouts  20.4 us (11%)
  between operations  14.8 us (8%)
  blocking collectives  6.31 us (4%)
    unnamed x87, local copies, waits for them, and re-layouts  16.1 us
    ppermute x1, waiting for transfers between devices, return_behind(): relayed = lax.ppermute(near, 'seq', [(i, i + 2) for i in earlier])  14 us
    ppermute x3, starting transfers between devices, shift_up(): return lax.ppermute(block, axis, route)  8.28 us
    dot_general x5, matrix products, local(): jnp.einsum('hqe,hke->hqk', query_heads, held[dist][0], preferred_element_...  8.14 us
    ppermute x2, starting transfers between devices, gather_behind(): relayed = lax.ppermute(far[k], 'seq', [(i + 2, i) for i in earlier])  8.09 us
    ppermute x2, waiting for transfers between devices, gather_behind(): relayed = lax.ppermute(far[k], 'seq', [(i + 2, i) for i in earlier])  7.92 us
    ppermute x3, waiting for transfers between devices, shift_up(): return lax.ppermute(block, axis, route)  7.35 us
    reduce_scatter x1, waiting for transfers between devices, local(): lax.psum_scatter(partial_weight.astype(jnp.bfloat16), 'seq', scatter_dime...  6.92 us
  transfers between devices with their start and end apart: 16, of which 6 were waited for; matrix products, arithmetic and copies ran while one was open for 40% of the time, Pallas kernels for 0%

profile of v11, /device:TPU:4, one launch (start us, length us, event | category | flops | bytes accessed | tf_op | source)
XLA Modules:
  0.0 175.7 jit_solution(16113176874692322786)
XLA Ops:
  7.2 1.2 copy.84
  8.5 3.5 %collective-permute-start.1 = (bf16[12,256,64]{1,2,0:T(8,128)(2,1)S(1)}, bf16[12,256,64]{1,2,0:T(8,128)(2,1)S(1)}, u32[]{:S(2)}, u32[]{:S(2)}) collective-permute-start(bf16[12,256,64]{1,2,0:T(8,128)(2,1)S(1)} %bitcast.236), channel_id=1, source_target_pairs={{0,8},{2,10},{4,12},{6,14},{8,16},{10,18},{12,20},{14,22},{16,24},... | collective-permute-start | bytes 1179656 | tf_op jit(solution)/shard_map/ppermute | solution.py:18
  12.0 1.3 collective-permute-start
  13.3 1.2 copy.86
  14.4 3.5 %collective-permute-start.4 = (bf16[12,256,64]{1,2,0:T(8,128)(2,1)S(1)}, bf16[12,256,64]{1,2,0:T(8,128)(2,1)S(1)}, u32[]{:S(2)}, u32[]{:S(2)}) collective-permute-start(bf16[12,256,64]{1,2,0:T(8,128)(2,1)S(1)} %bitcast.256), channel_id=1, source_target_pairs={{0,8},{2,10},{4,12},{6,14},{8,16},{10,18},{12,20},{14,22},{16,24},... | collective-permute-start | bytes 1179656 | tf_op jit(solution)/shard_map/ppermute | solution.py:18
  17.9 1.3 collective-permute-start.3
  19.2 6.3 %all_gather.6 = bf16[48,1536]{1,0:T(8,128)(2,1)} all-gather(bf16[48,768]{1,0:T(8,128)(2,1)} %param.11), channel_id=1, replica_groups=mesh['seq'=16,'dp'=2] {'dp'}, dimensions={1}, use_global_device_ids=true | all-gather | bytes 221184 | tf_op jit(solution)/shard_map/all_gather | solution.py:138
  26.7 6.0 %collective-permute-start.2 = (bf16[12,256,64]{1,2,0:T(8,128)(2,1)S(1)}, bf16[12,256,64]{1,2,0:T(8,128)(2,1)}, u32[]{:S(2)}, u32[]{:S(2)}) collective-permute-start(bf16[12,256,64]{1,2,0:T(8,128)(2,1)S(1)} %collective-permute-done.1), channel_id=1, source_target_pairs={{4,0},{6,2},{12,8},{14,10},{20,16},{22,18},{28,24},{30,26},{5,1},{... | collective-permute-start | bytes 1179656 | tf_op jit(solution)/shard_map/ppermute | solution.py:78
  33.3 1.2 copy.83
  34.6 2.0 %collective-permute-start.5 = (bf16[12,256,64]{1,2,0:T(8,128)(2,1)S(1)}, bf16[12,256,64]{1,2,0:T(8,128)(2,1)}, u32[]{:S(2)}, u32[]{:S(2)}) collective-permute-start(bf16[12,256,64]{1,2,0:T(8,128)(2,1)S(1)} %collective-permute-done.4), channel_id=1, source_target_pairs={{4,0},{6,2},{12,8},{14,10},{20,16},{22,18},{28,24},{30,26},{5,1},{... | collective-permute-start | bytes 1179656 | tf_op jit(solution)/shard_map/ppermute | solution.py:78
  36.6 2.3 %select_reduce_fusion.1 = (f32[12,256]{1,0:T(8,128)S(1)}, f32[12,256,256]{1,2,0:T(8,128)}) fusion(pred[256,256]{0,1:T(8,128)(4,1)S(1)} %get-tuple-element.42, bf16[12,256,64]{1,2,0:T(8,128)(2,1)S(1)} %bitcast.226, bf16[12,256,64]{1,2,0:T(8,128)(2,1)S(1)} %bitcast.238), kind=kOutput, calls=%fused_computation.29 | convolution fusion | flops 103019520 | bytes 4009984 | tf_op jit(solution)/shard_map/hqe,hke->hqk/dot_general | solution.py:159
  39.7 3.5 %collective-permute-done.2 = bf16[12,256,64]{1,2,0:T(8,128)(2,1)} collective-permute-done((bf16[12,256,64]{1,2,0:T(8,128)(2,1)S(1)}, bf16[12,256,64]{1,2,0:T(8,128)(2,1)}, u32[]{:S(2)}, u32[]{:S(2)}) %collective-permute-start.2) | collective-permute-done | bytes 393248 | tf_op jit(solution)/shard_map/ppermute | solution.py:78
  43.2 1.0 broadcast_select_fusion.1
  44.2 4.4 %collective-permute-done.5 = bf16[12,256,64]{1,2,0:T(8,128)(2,1)} collective-permute-done((bf16[12,256,64]{1,2,0:T(8,128)(2,1)S(1)}, bf16[12,256,64]{1,2,0:T(8,128)(2,1)}, u32[]{:S(2)}, u32[]{:S(2)}) %collective-permute-start.5) | collective-permute-done | bytes 393248 | tf_op jit(solution)/shard_map/ppermute | solution.py:78
  48.7 1.0 broadcast_select_fusion
  49.7 2.5 %maximum_select_fusion = (bf16[2,12,256,64]{2,3,1,0:T(8,128)(2,1)}, bf16[2,12,256,64]{2,3,1,0:T(8,128)(2,1)}) fusion(bf16[1,12,256,64]{2,3,1,0:T(8,128)(2,1)S(1)} %bitcast.258, bf16[1,12,256,64]{2,3,1,0:T(8,128)(2,1)S(1)} %bitcast.239, pred[]{:T(512)S(6)} %eq.102, bf16[1,12,256,64]{2,3,1,0:T(8,128)(2,1)S(1)} %bitcast.261, ...), kind=kLoop, calls=%fused_computation.122 | loop fusion | flops 1966080 | bytes 3932161 | tf_op jit(solution)/shard_map/jit(_where)/select_n | solution.py:86
  52.3 2.3 %convolution_multiply_fusion = f32[12,256,256]{2,1,0:T(8,128)} fusion(bf16[12,256,64]{1,2,0:T(8,128)(2,1)S(1)} %bitcast.227, bf16[12,256,64]{1,2,0:T(8,128)(2,1)S(1)} %collective-permute-done.1), kind=kOutput, calls=%fused_computation.47 | convolution fusion | flops 101449728 | bytes 3932160 | tf_op jit(solution)/shard_map/hqe,hke->hqk/dot_general | solution.py:159
  54.6 3.6 %copy.88 = f32[12,256,256]{1,2,0:T(8,128)} copy(f32[12,256,256]{2,1,0:T(8,128)} %convolution_multiply_fusion) | data formatting | bytes 6291456 | tf_op jit(solution)/shard_map/mul | solution.py:159
  58.7 2.1 %select_reduce_fusion = f32[12,256]{1,0:T(8,128)S(1)} fusion(f32[12,256,256]{1,2,0:T(8,128)} %copy.88, pred[256,256]{0,1:T(8,128)(4,1)S(1)} %get-tuple-element.41), kind=kLoop, calls=%fused_computation.28 | loop fusion | flops 1569792 | bytes 3223552 | tf_op jit(solution)/shard_map/reduce_max | solution.py:164
  61.6 2.1 %fusion.6 = (f32[12,256]{1,0:T(8,128)S(1)}, f32[12,256,256]{2,1,0:T(8,128)S(1)}) fusion(pred[256,256]{0,1:T(8,128)(4,1)S(1)} %get-tuple-element.38, bf16[12,256,64]{1,2,0:T(8,128)(2,1)S(1)} %bitcast.229, bf16[2,12,256,64]{2,3,1,0:T(8,128)(2,1)} %collective-permute-done.6), kind=kOutput, calls=%fused_computation.25 | convolution fusion | flops 103019520 | bytes 4009984 | tf_op jit(solution)/shard_map/hqe,hke->hqk/dot_general | solution.py:159
  64.8 3.2 %copy-done.5 = f32[12,256,256]{1,2,0:T(8,128)S(1)} copy-done((f32[12,256,256]{1,2,0:T(8,128)S(1)}, f32[12,256,256]{1,2,0:T(8,128)}, u32[]{:S(2)}) %copy-start.5) | copy-done | bytes 3145752
  68.0 4.0 %fusion.19 = (f32[12,256]{1,0:T(8,128)S(1)}, f32[12,256]{1,0:T(8,128)S(1)}, f32[12,256]{1,0:T(8,128)S(1)}, f32[12,256]{1,0:T(8,128)S(1)}, f32[12,256]{1,0:T(8,128)S(1)}) fusion(f32[12,256,256]{2,1,0:T(8,128)S(1)} %get-tuple-element.50, f32[12,256]{1,0:T(8,128)S(1)} %maximum_maximum_fusion, pred[256,256]{0,1:T(8,128)(4,1)S(1)} %get-tuple-element.38, ...), kind=kLoop, calls=%fused_computation.41 | loop fusion | flops 18859008 | bytes 16130048 | tf_op jit(solution)/shard_map/reduce_sum | solution.py:172
  74.6 1.9 %fusion.101 = f32[12,256,64]{1,2,0:T(8,128)S(1)} fusion(f32[12,256,64]{1,2,0:T(8,128)S(1)} %fusion.66, f32[12,256,256]{2,1,0:T(8,128)S(1)} %get-tuple-element.50, f32[12,256]{1,0:T(8,128)S(1)} %maximum_maximum_fusion, pred[256,256]{0,1:T(8,128)(4,1)S(1)} %get-tuple-element.38, bf16[2,12,256,64]{2,3,1,0:T(8,128)(2,1)} %collective-permute-done.6), kind=kOutput, calls=%fused_computation.116 | convolution fusion | flops 104792064 | bytes 5189632 | tf_op jit(solution)/shard_map/hqk,hke->hqe/dot_general | solution.py:173
  76.5 1.8 %fusion.116 = (bf16[256,12,64]{0,2,1:T(8,128)(2,1)S(1)}, f32[12,256,64]{1,2,0:T(8,128)}) fusion(f32[256,12]{0,1:T(8,128)S(1)} %bitcast.267, f32[12,256,64]{1,2,0:T(8,128)S(1)} %fusion.33, f32[12,256,64]{1,2,0:T(8,128)S(1)} %fusion.60, f32[12,256,64]{1,2,0:T(8,128)S(1)} %fusion.101, bf16[12,256,64]{1,2,0:T(8,128)(2,1)S(1)} %broadcast_select_fusion, ...), kind=kOutput, calls=%fused_computation.128 | convolution fusion | flops 105578496 | bytes 7168000 | tf_op jit(solution)/shard_map/hqk,hke->hqe/dot_general | solution.py:173
  79.1 2.2 %convolution_convert_fusion = bf16[768,1536]{1,0:T(8,128)(2,1)} fusion(bf16[256,768]{0,1:T(8,128)(2,1)S(1)} %bitcast.254, bf16[1,256,1536]{2,1,0:T(8,128)(2,1)S(1)} %copy-done), kind=kOutput, calls=%fused_computation | convolution fusion | flops 605159424 | bytes 3538944 | tf_op jit(solution)/shard_map/dot_general | solution.py:193
  81.3 2.5 %convolution_convert_fusion.2 = bf16[256,768]{1,0:T(8,128)(2,1)S(1)} fusion(bf16[768,1536]{1,0:T(8,128)(2,1)} %all-gather.2.cloned.1.call-done, bf16[1,256,1536]{2,1,0:T(8,128)(2,1)S(1)} %copy-done), kind=kOutput, calls=%fused_computation.121 | convolution fusion | flops 604176384 | bytes 3538944 | tf_op jit(solution)/shard_map/dot_general | solution.py:189
  83.9 2.7 %fusion.84 = f32[1,12,256,64]{2,3,1,0:T(8,128)S(1)} fusion(bf16[12,256,64]{1,2,0:T(8,128)(2,1)S(1)} %bitcast.241, f32[12,256,256]{2,1,0:T(8,128)} %copy-done.13, f32[12,256]{1,0:T(8,128)S(1)} %get-tuple-element.30, pred[256,256]{0,1:T(8,128)(4,1)S(1)} %get-tuple-element.38), kind=kOutput, calls=%fused_computation.98 | convolution fusion | flops 103809024 | bytes 4403200 | tf_op jit(solution)/shard_map/hqk,hqe->hke/dot_general | solution.py:234
  89.0 1.1 multiply_convert_fusion
  91.0 2.4 %multiply_convert_fusion.3 = bf16[12,256,256]{1,2,0:T(8,128)(2,1)S(1)} fusion(f32[12,256,256]{2,1,0:T(8,128)S(1)} %copy-done.14, bf16[12,256,64]{1,2,0:T(8,128)(2,1)S(1)} %bitcast.245, f32[12,256]{1,0:T(8,128)S(1)} %multiply_reduce_fusion, f32[12,256]{1,0:T(8,128)S(1)} %get-tuple-element.30, pred[256,256]{0,1:T(8,128)(4,1)S(1)} %get-tuple-element.38, ...), kind=kOutput, calls=%fused_computation.18 | convolution fusion | flops 105381888 | bytes 5595136 | tf_op jit(solution)/shard_map/hqe,hke->hqk/dot_general | solution.py:222
  94.0 1.3 pad_maximum_fusion
  95.3 1.1 multiply_convert_fusion.4
  97.0 1.3 pad_maximum_fusion.1
  100.0 1.4 fusion.117
  103.8 1.1 multiply_convert_fusion.1
  105.0 1.1 copy-done.17
  107.4 2.2 %fusion.97 = f32[1,12,256,64]{2,3,1,0:T(8,128)S(1)} fusion(bf16[12,256,256]{1,2,0:T(8,128)(2,1)} %copy-done.17, bf16[12,256,64]{1,2,0:T(8,128)(2,1)S(1)} %bitcast.233), kind=kOutput, calls=%fused_computation.110 | convolution fusion | flops 100859904 | bytes 2752512 | tf_op jit(solution)/shard_map/hqk,hqe->hke/dot_general | solution.py:231
  109.6 3.3 %fusion.10 = bf16[1,256,1536]{2,1,0:T(8,128)(2,1)} fusion(bf16[256,768]{0,1:T(8,128)(2,1)S(1)} %bitcast.255, bf16[768,1536]{1,0:T(8,128)(2,1)} %all-gather.2.cloned.1.call-done), kind=kOutput, calls=%fused_computation.32 | convolution fusion | flops 604372992 | bytes 3538944 | tf_op jit(solution)/shard_map/dot_general | solution.py:185
  113.7 2.9 %fusion.40 = bf16[2,12,256,64]{2,3,1,0:T(8,128)(2,1)} fusion(f32[1,12,256,64]{2,3,1,0:T(8,128)S(1)} %fusion.87, f32[1,12,256,64]{2,3,1,0:T(8,128)S(1)} %fusion.97, f32[2,12,256,64]{2,3,1,0:T(8,128)} %collective-permute-done.9, f32[2,12,256,64]{2,3,1,0:T(8,128)} %collective-permute-done.8, pred[]{:T(512)S(6)} %eq.102), kind=kLoop, calls=%fused_computation.60 | loop fusion | flops 1572864 | bytes 5505025 | tf_op jit(solution)/shard_map/convert_element_type | solution.py:114
  116.6 1.5 collective-permute-start.11
  119.4 1.7 fusion.81
  121.1 6.1 %collective-permute-start.10 = (bf16[2,12,256,64]{2,3,1,0:T(8,128)(2,1)}, bf16[2,12,256,64]{2,3,1,0:T(8,128)(2,1)}, u32[]{:S(2)}, u32[]{:S(2)}) collective-permute-start(bf16[2,12,256,64]{2,3,1,0:T(8,128)(2,1)} %fusion.40), channel_id=1, source_target_pairs={{4,0},{6,2},{12,8},{14,10},{20,16},{22,18},{28,24},{30,26},{5,1},{... | collective-permute-start | bytes 2359304 | tf_op jit(solution)/shard_map/ppermute | solution.py:115
  127.2 14.0 %collective-permute-done.11 = bf16[2,12,256,64]{2,3,1,0:T(8,128)(2,1)S(1)} collective-permute-done((bf16[2,12,256,64]{2,3,1,0:T(8,128)(2,1)}, bf16[2,12,256,64]{2,3,1,0:T(8,128)(2,1)S(1)}, u32[]{:S(2)}, u32[]{:S(2)}) %collective-permute-start.11) | collective-permute-done | bytes 786464 | tf_op jit(solution)/shard_map/ppermute | solution.py:116
  141.6 1.3 collective-permute-start.12
  142.9 6.9 %reduce-scatter.2.cloned.1.call-done = bf16[48,1536]{1,0:T(8,128)(2,1)} async-done(((bf16[768,1536]{1,0:T(8,128)(2,1)}), bf16[48,1536]{1,0:T(8,128)(2,1)}) %reduce-scatter.2.cloned.1.call-update) | async-done | bytes 147472 | tf_op jit(solution)/shard_map/reduce_scatter | solution.py:196
  151.2 1.7 collective-permute-start.13
  153.6 2.9 %collective-permute-done.13 = f32[768,48]{0,1:T(8,128)S(1)} collective-permute-done((f32[768,48]{0,1:T(8,128)S(1)}, f32[768,48]{0,1:T(8,128)S(1)}, u32[]{:S(2)}, u32[]{:S(2)}) %collective-permute-start.13) | collective-permute-done | bytes 147488 | tf_op jit(solution)/shard_map/ppermute | solution.py:41
  157.1 7.3 %collective-permute-done.12 = bf16[2,12,256,64]{2,3,1,0:T(8,128)(2,1)} collective-permute-done((bf16[2,12,256,64]{2,3,1,0:T(8,128)(2,1)S(1)}, bf16[2,12,256,64]{2,3,1,0:T(8,128)(2,1)}, u32[]{:S(2)}, u32[]{:S(2)}) %collective-permute-start.12) | collective-permute-done | bytes 786464 | tf_op jit(solution)/shard_map/ppermute | solution.py:18
  164.5 2.5 %fusion.39 = bf16[2,12,256,64]{2,3,1,0:T(8,128)(2,1)S(1)} fusion(f32[1,12,256,64]{2,3,1,0:T(8,128)S(1)} %copy-done.33, f32[1,12,256,64]{2,3,1,0:T(8,128)S(1)} %fusion.99, bf16[2,12,256,64]{2,3,1,0:T(8,128)(2,1)} %collective-permute-done.12, bf16[2,12,256,64]{2,3,1,0:T(8,128)(2,1)} %collective-permute-done.10, f32[2,12,256,64]{2,3,1,0:T(8,128)} %collective-permute-done.8, ...), kind=kLoop, calls=%fused_computation.57 | loop fusion | flops 3538944 | bytes 5505026 | tf_op jit(solution)/shard_map/convert.3
  (140 shorter events, 24.9 us)
Async XLA Ops:
  7.2 71.9 %copy-start = (bf16[1,256,1536]{2,1,0:T(8,128)(2,1)S(1)}, bf16[1,256,1536]{2,1,0:T(8,128)(2,1)}, u32[]{:S(2)}) copy-start(bf16[1,256,1536]{2,1,0:T(8,128)(2,1)} %param.9) | copy-start | bytes 2359300
  7.2 74.1 %all-gather.2.cloned.1.call-start = ((), (), s32[]{:S(2)}) async-start(), calls=%async_computation.1 | async-start | bytes 2506752 | tf_op jit(solution)/shard_map/all_gather | solution.py:139
  8.5 18.3 %collective-permute-start.1 = (bf16[12,256,64]{1,2,0:T(8,128)(2,1)S(1)}, bf16[12,256,64]{1,2,0:T(8,128)(2,1)S(1)}, u32[]{:S(2)}, u32[]{:S(2)}) collective-permute-start(bf16[12,256,64]{1,2,0:T(8,128)(2,1)S(1)} %bitcast.236), channel_id=1, source_target_pairs={{0,8},{2,10},{4,12},{6,14},{8,16},{10,18},{12,20},{14,22},{16,24},... | collective-permute-start | bytes 1179656 | tf_op jit(solution)/shard_map/ppermute | solution.py:18
  12.0 27.0 %collective-permute-start = (bf16[12,256,64]{1,2,0:T(8,128)(2,1)S(1)}, bf16[12,256,64]{1,2,0:T(8,128)(2,1)S(1)}, u32[]{:S(2)}, u32[]{:S(2)}) collective-permute-start(bf16[12,256,64]{1,2,0:T(8,128)(2,1)S(1)} %bitcast.237), channel_id=1, source_target_pairs={{0,4},{2,6},{8,12},{10,14},{16,20},{18,22},{24,28},{26,30},{1,5},{... | collective-permute-start | bytes 1179656 | tf_op jit(solution)/shard_map/ppermute | solution.py:77
  14.4 20.1 %collective-permute-start.4 = (bf16[12,256,64]{1,2,0:T(8,128)(2,1)S(1)}, bf16[12,256,64]{1,2,0:T(8,128)(2,1)S(1)}, u32[]{:S(2)}, u32[]{:S(2)}) collective-permute-start(bf16[12,256,64]{1,2,0:T(8,128)(2,1)S(1)} %bitcast.256), channel_id=1, source_target_pairs={{0,8},{2,10},{4,12},{6,14},{8,16},{10,18},{12,20},{14,22},{16,24},... | collective-permute-start | bytes 1179656 | tf_op jit(solution)/shard_map/ppermute | solution.py:18
  17.9 26.3 %collective-permute-start.3 = (bf16[12,256,64]{1,2,0:T(8,128)(2,1)S(1)}, bf16[12,256,64]{1,2,0:T(8,128)(2,1)}, u32[]{:S(2)}, u32[]{:S(2)}) collective-permute-start(bf16[12,256,64]{1,2,0:T(8,128)(2,1)S(1)} %bitcast.257), channel_id=1, source_target_pairs={{0,4},{2,6},{8,12},{10,14},{16,20},{18,22},{24,28},{26,30},{1,5},{... | collective-permute-start | bytes 1179656 | tf_op jit(solution)/shard_map/ppermute | solution.py:77
  25.6 124.2 %reduce-scatter.2.cloned.1.call-start = ((), (), s32[]{:S(2)}) async-start(), calls=%async_computation.2 | async-start | bytes 2506752 | tf_op jit(solution)/shard_map/reduce_scatter | solution.py:196
  26.7 25.6 %copy-start.18 = (bf16[12,256,64]{1,2,0:T(8,128)(2,1)}, bf16[12,256,64]{1,2,0:T(8,128)(2,1)S(1)}, u32[]{:S(2)}) copy-start(bf16[12,256,64]{1,2,0:T(8,128)(2,1)S(1)} %collective-permute-done.1) | copy-start | bytes 1179652
  26.7 16.4 %collective-permute-start.2 = (bf16[12,256,64]{1,2,0:T(8,128)(2,1)S(1)}, bf16[12,256,64]{1,2,0:T(8,128)(2,1)}, u32[]{:S(2)}, u32[]{:S(2)}) collective-permute-start(bf16[12,256,64]{1,2,0:T(8,128)(2,1)S(1)} %collective-permute-done.1), channel_id=1, source_target_pairs={{4,0},{6,2},{12,8},{14,10},{20,16},{22,18},{28,24},{30,26},{5,1},{... | collective-permute-start | bytes 1179656 | tf_op jit(solution)/shard_map/ppermute | solution.py:78
  33.3 38.8 %copy-start.20 = (pred[256,256]{0,1:T(8,128)(4,1)}, pred[256,256]{0,1:T(8,128)(4,1)S(1)}, u32[]{:S(2)}) copy-start(pred[256,256]{0,1:T(8,128)(4,1)S(1)} %get-tuple-element.41) | copy-start | bytes 196612
  33.3 43.2 %copy-start.36 = (pred[256,256]{0,1:T(8,128)(4,1)}, pred[256,256]{0,1:T(8,128)(4,1)S(1)}, u32[]{:S(2)}) copy-start(pred[256,256]{0,1:T(8,128)(4,1)S(1)} %get-tuple-element.39) | copy-start | bytes 196612
  33.3 54.8 %copy-start.34 = (pred[256,256]{0,1:T(8,128)(4,1)}, pred[256,256]{0,1:T(8,128)(4,1)S(1)}, u32[]{:S(2)}) copy-start(pred[256,256]{0,1:T(8,128)(4,1)S(1)} %get-tuple-element.42) | copy-start | bytes 196612
  34.6 9.7 %copy-start.27 = (bf16[12,256,64]{1,2,0:T(8,128)(2,1)}, bf16[12,256,64]{1,2,0:T(8,128)(2,1)S(1)}, u32[]{:S(2)}) copy-start(bf16[12,256,64]{1,2,0:T(8,128)(2,1)S(1)} %collective-permute-done.4) | copy-start | bytes 1179652
  34.6 14.1 %collective-permute-start.5 = (bf16[12,256,64]{1,2,0:T(8,128)(2,1)S(1)}, bf16[12,256,64]{1,2,0:T(8,128)(2,1)}, u32[]{:S(2)}, u32[]{:S(2)}) collective-permute-start(bf16[12,256,64]{1,2,0:T(8,128)(2,1)S(1)} %collective-permute-done.4), channel_id=1, source_target_pairs={{4,0},{6,2},{12,8},{14,10},{20,16},{22,18},{28,24},{30,26},{5,1},{... | collective-permute-start | bytes 1179656 | tf_op jit(solution)/shard_map/ppermute | solution.py:78
  49.7 26.8 %copy-start.25 = (bf16[12,256,64]{1,2,0:T(8,128)(2,1)}, bf16[12,256,64]{1,2,0:T(8,128)(2,1)S(1)}, u32[]{:S(2)}) copy-start(bf16[12,256,64]{1,2,0:T(8,128)(2,1)S(1)} %broadcast_select_fusion) | copy-start | bytes 1179652
  52.3 9.3 %collective-permute-start.6 = (bf16[2,12,256,64]{2,3,1,0:T(8,128)(2,1)}, bf16[2,12,256,64]{2,3,1,0:T(8,128)(2,1)}, u32[]{:S(2)}, u32[]{:S(2)}) collective-permute-start(bf16[2,12,256,64]{2,3,1,0:T(8,128)(2,1)} %get-tuple-element.34), channel_id=1, source_target_pairs={{0,2},{2,0},{4,6},{6,4},{8,10},{10,8},{12,14},{14,12},{16,18},{18,... | collective-permute-start | bytes 2359304 | tf_op jit(solution)/shard_map/ppermute | solution.py:23
  58.2 5.6 %collective-permute-start.7 = (bf16[2,12,256,64]{2,3,1,0:T(8,128)(2,1)}, bf16[2,12,256,64]{2,3,1,0:T(8,128)(2,1)S(1)}, u32[]{:S(2)}, u32[]{:S(2)}) collective-permute-start(bf16[2,12,256,64]{2,3,1,0:T(8,128)(2,1)} %get-tuple-element.35), channel_id=1, source_target_pairs={{0,2},{2,0},{4,6},{6,4},{8,10},{10,8},{12,14},{14,12},{16,18},{18,... | collective-permute-start | bytes 2359304 | tf_op jit(solution)/shard_map/ppermute | solution.py:23
  61.5 15.0 %copy-start.8 = (f32[12,256,256]{2,1,0:T(8,128)}, f32[12,256,256]{2,1,0:T(8,128)S(1)}, u32[]{:S(2)}) copy-start(f32[12,256,256]{2,1,0:T(8,128)S(1)} %get-tuple-element.46) | copy-start | bytes 9437188
  61.5 3.2 %copy-start.2 = (f32[12,256,256]{1,2,0:T(8,128)S(1)}, f32[12,256,256]{1,2,0:T(8,128)}, u32[]{:S(2)}) copy-start(f32[12,256,256]{1,2,0:T(8,128)} %copy.88) | copy-start | bytes 9437188
  61.6 6.5 %copy-start.5 = (f32[12,256,256]{1,2,0:T(8,128)S(1)}, f32[12,256,256]{1,2,0:T(8,128)}, u32[]{:S(2)}) copy-start(f32[12,256,256]{1,2,0:T(8,128)} %get-tuple-element.48) | copy-start | bytes 9437188
  63.7 10.9 %copy-start.13 = (f32[12,256,256]{2,1,0:T(8,128)}, f32[12,256,256]{2,1,0:T(8,128)S(1)}, u32[]{:S(2)}) copy-start(f32[12,256,256]{2,1,0:T(8,128)S(1)} %get-tuple-element.50) | copy-start | bytes 9437188
  63.7 10.0 %copy-start.31 = (bf16[2,12,256,64]{2,3,1,0:T(8,128)(2,1)}, bf16[2,12,256,64]{2,3,1,0:T(8,128)(2,1)S(1)}, u32[]{:S(2)}) copy-start(bf16[2,12,256,64]{2,3,1,0:T(8,128)(2,1)S(1)} %collective-permute-done.7) | copy-start | bytes 2359300
  64.4 9.3 %copy-start.11 = (f32[12,256,256]{2,1,0:T(8,128)}, f32[12,256,256]{2,1,0:T(8,128)S(1)}, u32[]{:S(2)}) copy-start(f32[12,256,256]{2,1,0:T(8,128)S(1)} %get-tuple-element.44) | copy-start | bytes 9437188
  68.0 4.1 %copy-start.28 = (bf16[12,256,64]{1,2,0:T(8,128)(2,1)S(1)}, bf16[12,256,64]{1,2,0:T(8,128)(2,1)}, u32[]{:S(2)}) copy-start(bf16[12,256,64]{1,2,0:T(8,128)(2,1)} %copy-done.27) | copy-start | bytes 1179652
  83.9 2.8 %copy-start.12 = (f32[12,256,256]{2,1,0:T(8,128)S(1)}, f32[12,256,256]{2,1,0:T(8,128)}, u32[]{:S(2)}) copy-start(f32[12,256,256]{2,1,0:T(8,128)} %copy-done.11) | copy-start | bytes 9437188
  86.8 2.2 %copy-start.6 = (f32[12,256,256]{1,2,0:T(8,128)S(1)}, f32[12,256,256]{1,2,0:T(8,128)}, u32[]{:S(2)}) copy-start(f32[12,256,256]{1,2,0:T(8,128)} %get-tuple-element.48) | copy-start | bytes 9437188
  91.0 11.5 %copy-start.15 = (bf16[12,256,256]{1,2,0:T(8,128)(2,1)}, bf16[12,256,256]{1,2,0:T(8,128)(2,1)S(1)}, u32[]{:S(2)}) copy-start(bf16[12,256,256]{1,2,0:T(8,128)(2,1)S(1)} %multiply_convert_fusion) | copy-start | bytes 4718596
  95.3 18.4 %collective-permute-start.8 = (f32[2,12,256,64]{2,3,1,0:T(8,128)}, f32[2,12,256,64]{2,3,1,0:T(8,128)}, u32[]{:S(2)}, u32[]{:S(2)}) collective-permute-start(f32[2,12,256,64]{2,3,1,0:T(8,128)} %pad_maximum_fusion), channel_id=1, source_target_pairs={{0,2},{2,0},{4,6},{6,4},{8,10},{10,8},{12,14},{14,12},{16,18},{18,... | collective-permute-start | bytes 4718600 | tf_op jit(solution)/shard_map/ppermute | solution.py:23
  96.4 2.5 %copy-start.3 = (f32[12,256,256]{1,2,0:T(8,128)S(1)}, f32[12,256,256]{1,2,0:T(8,128)}, u32[]{:S(2)}) copy-start(f32[12,256,256]{1,2,0:T(8,128)} %copy.88) | copy-start | bytes 9437188
  96.4 2.5 %copy-start.21 = (pred[256,256]{0,1:T(8,128)(4,1)S(1)}, pred[256,256]{0,1:T(8,128)(4,1)}, u32[]{:S(2)}) copy-start(pred[256,256]{0,1:T(8,128)(4,1)} %copy-done.20) | copy-start | bytes 196612
  96.4 2.6 %copy-start.29 = (bf16[12,256,64]{1,2,0:T(8,128)(2,1)S(1)}, bf16[12,256,64]{1,2,0:T(8,128)(2,1)}, u32[]{:S(2)}) copy-start(bf16[12,256,64]{1,2,0:T(8,128)(2,1)} %copy-done.27) | copy-start | bytes 1179652
  98.3 3.1 %copy-start.19 = (bf16[12,256,64]{1,2,0:T(8,128)(2,1)S(1)}, bf16[12,256,64]{1,2,0:T(8,128)(2,1)}, u32[]{:S(2)}) copy-start(bf16[12,256,64]{1,2,0:T(8,128)(2,1)} %copy-done.18) | copy-start | bytes 1179652
  98.3 15.4 %collective-permute-start.9 = (f32[2,12,256,64]{2,3,1,0:T(8,128)}, f32[2,12,256,64]{2,3,1,0:T(8,128)}, u32[]{:S(2)}, u32[]{:S(2)}) collective-permute-start(f32[2,12,256,64]{2,3,1,0:T(8,128)} %pad_maximum_fusion.1), channel_id=1, source_target_pairs={{0,2},{2,0},{4,6},{6,4},{8,10},{10,8},{12,14},{14,12},{16,18},{18,... | collective-permute-start | bytes 4718600 | tf_op jit(solution)/shard_map/ppermute | solution.py:23
  101.8 2.0 %copy-start.26 = (bf16[12,256,64]{1,2,0:T(8,128)(2,1)S(1)}, bf16[12,256,64]{1,2,0:T(8,128)(2,1)}, u32[]{:S(2)}) copy-start(bf16[12,256,64]{1,2,0:T(8,128)(2,1)} %copy-done.25) | copy-start | bytes 1179652
  106.1 3.5 %copy-start.24 = (bf16[256,12,64]{0,2,1:T(8,128)(2,1)S(1)}, bf16[256,12,64]{0,2,1:T(8,128)(2,1)}, u32[]{:S(2)}) copy-start(bf16[256,12,64]{0,2,1:T(8,128)(2,1)} %copy-done.23) | copy-start | bytes 1179652
  107.4 5.5 %copy-start.10 = (f32[12,256,256]{2,1,0:T(8,128)S(1)}, f32[12,256,256]{2,1,0:T(8,128)}, u32[]{:S(2)}) copy-start(f32[12,256,256]{2,1,0:T(8,128)} %copy-done.8) | copy-start | bytes 9437188
  107.4 5.5 %copy-start.38 = (pred[256,256]{0,1:T(8,128)(4,1)S(1)}, pred[256,256]{0,1:T(8,128)(4,1)}, u32[]{:S(2)}) copy-start(pred[256,256]{0,1:T(8,128)(4,1)} %copy-done.36) | copy-start | bytes 196612
  113.6 5.1 %copy-start.4 = (f32[12,256,256]{1,2,0:T(8,128)S(1)}, f32[12,256,256]{1,2,0:T(8,128)}, u32[]{:S(2)}) copy-start(f32[12,256,256]{1,2,0:T(8,128)} %copy.88) | copy-start | bytes 9437188
  113.7 5.1 %copy-start.22 = (pred[256,256]{0,1:T(8,128)(4,1)S(1)}, pred[256,256]{0,1:T(8,128)(4,1)}, u32[]{:S(2)}) copy-start(pred[256,256]{0,1:T(8,128)(4,1)} %copy-done.20) | copy-start | bytes 196612
  116.6 2.8 %copy-start.7 = (f32[12,256,256]{1,2,0:T(8,128)S(1)}, f32[12,256,256]{1,2,0:T(8,128)}, u32[]{:S(2)}) copy-start(f32[12,256,256]{1,2,0:T(8,128)} %get-tuple-element.48) | copy-start | bytes 9437188
  116.6 2.8 %copy-start.35 = (pred[256,256]{0,1:T(8,128)(4,1)S(1)}, pred[256,256]{0,1:T(8,128)(4,1)}, u32[]{:S(2)}) copy-start(pred[256,256]{0,1:T(8,128)(4,1)} %copy-done.34) | copy-start | bytes 196612
  116.6 24.6 %collective-permute-start.11 = (bf16[2,12,256,64]{2,3,1,0:T(8,128)(2,1)}, bf16[2,12,256,64]{2,3,1,0:T(8,128)(2,1)S(1)}, u32[]{:S(2)}, u32[]{:S(2)}) collective-permute-start(bf16[2,12,256,64]{2,3,1,0:T(8,128)(2,1)} %fusion.40), channel_id=1, source_target_pairs={{0,4},{2,6},{8,12},{10,14},{16,20},{18,22},{24,28},{26,30},{1,5},{... | collective-permute-start | bytes 2359304 | tf_op jit(solution)/shard_map/ppermute | solution.py:116
  121.1 31.9 %copy-start.16 = (bf16[12,256,256]{1,2,0:T(8,128)(2,1)S(1)}, bf16[12,256,256]{1,2,0:T(8,128)(2,1)}, u32[]{:S(2)}) copy-start(bf16[12,256,256]{1,2,0:T(8,128)(2,1)} %copy-done.15) | copy-start | bytes 4718596
  121.1 36.1 %collective-permute-start.10 = (bf16[2,12,256,64]{2,3,1,0:T(8,128)(2,1)}, bf16[2,12,256,64]{2,3,1,0:T(8,128)(2,1)}, u32[]{:S(2)}, u32[]{:S(2)}) collective-permute-start(bf16[2,12,256,64]{2,3,1,0:T(8,128)(2,1)} %fusion.40), channel_id=1, source_target_pairs={{4,0},{6,2},{12,8},{14,10},{20,16},{22,18},{28,24},{30,26},{5,1},{... | collective-permute-start | bytes 2359304 | tf_op jit(solution)/shard_map/ppermute | solution.py:115
  141.6 22.9 %collective-permute-start.12 = (bf16[2,12,256,64]{2,3,1,0:T(8,128)(2,1)S(1)}, bf16[2,12,256,64]{2,3,1,0:T(8,128)(2,1)}, u32[]{:S(2)}, u32[]{:S(2)}) collective-permute-start(bf16[2,12,256,64]{2,3,1,0:T(8,128)(2,1)S(1)} %fusion.42), channel_id=1, source_target_pairs={{8,0},{10,2},{12,4},{14,6},{16,8},{18,10},{20,12},{22,14},{24,16},... | collective-permute-start | bytes 2359304 | tf_op jit(solution)/shard_map/ppermute | solution.py:18
  150.9 13.5 %copy-start.33 = (f32[1,12,256,64]{2,3,1,0:T(8,128)S(1)}, f32[1,12,256,64]{2,3,1,0:T(8,128)}, u32[]{:S(2)}) copy-start(f32[1,12,256,64]{2,3,1,0:T(8,128)} %fusion.81) | copy-start | bytes 2359300
  151.2 5.2 %collective-permute-start.13 = (f32[768,48]{0,1:T(8,128)S(1)}, f32[768,48]{0,1:T(8,128)S(1)}, u32[]{:S(2)}, u32[]{:S(2)}) collective-permute-start(f32[768,48]{0,1:T(8,128)S(1)} %bitcast.266), channel_id=1, source_target_pairs={{0,1},{1,0},{2,3},{3,2},{4,5},{5,4},{6,7},{7,6},{8,9},{9,8},{10,11... | collective-permute-start | bytes 442376 | tf_op jit(solution)/shard_map/ppermute | solution.py:41
  156.5 12.4 %copy-start.1 = (bf16[1,256,1536]{2,1,0:T(8,128)(2,1)S(1)}, bf16[1,256,1536]{2,1,0:T(8,128)(2,1)}, u32[]{:S(2)}) copy-start(bf16[1,256,1536]{2,1,0:T(8,128)(2,1)} %param.9) | copy-start | bytes 2359300
  (8 other events, 11.6 us)
Sparse Core Ops, SparseCore 0:
  25.7 42.9 all-gather.1
  81.4 68.3 reduce-scatter.1

commit v12 on v10

--- a/solution.py
+++ b/solution.py
@@ -115,8 +115,11 @@
     score_scale = HEAD_DIM ** (-0.5)
     utt_lengths = lengths[0]
 
-    weight_rows = lax.all_gather(out_weight, "seq", axis=0, tiled=True)
-    weight_full = lax.all_gather(weight_rows, "dp", axis=1, tiled=True)
+    row_blocks, col_blocks = lax.axis_size("seq"), lax.axis_size("dp")
+    pieces = lax.all_gather(out_weight, ("seq", "dp"), axis=0, tiled=False)
+    weight_full = jnp.transpose(
+        pieces.reshape((row_blocks, col_blocks) + out_weight.shape), (0, 2, 1, 3)
+    ).reshape(row_blocks * out_weight.shape[0], col_blocks * out_weight.shape[1])
 
     query_heads = head_major(query_rows[0], tok_rows)
     own_kv = jnp.stack([head_major(key_rows[0], tok_rows), head_major(value_rows[0], tok_rows)])
@@ -162,17 +165,18 @@
     attended = row_major(attended_heads, tok_rows)
     log_sum = top_score + jnp.log(row_sum)
 
+    upstream = out_grad[0]
+    partial_weight = lax.dot_general(
+        attended, upstream, (((0,), (0,)), ((), ())), preferred_element_type=jnp.float32
+    )
+    partial_weight, attended = lax.optimization_barrier((partial_weight, attended))
     mixed_out = jnp.dot(attended, weight_full, preferred_element_type=jnp.float32).astype(
         jnp.bfloat16
     )
-    upstream = out_grad[0]
     att_grad = lax.dot_general(
         upstream, weight_full, (((1,), (1,)), ((), ())), preferred_element_type=jnp.float32
     ).astype(jnp.bfloat16)
 
-    partial_weight = lax.dot_general(
-        attended, upstream, (((0,), (0,)), ((), ())), preferred_element_type=jnp.float32
-    )
     row_share = lax.psum_scatter(
         partial_weight.astype(jnp.bfloat16), "seq", scatter_dimension=0, tiled=True
     )

time: 203 us -> 168 us (0.83)
  waiting for transfers between devices: 72 us -> 36.5 us
  local copies, waits for them, and re-layouts: 22.3 us -> 25.4 us
  matrix products: 44.2 us -> 41.3 us
    all_gather x2 -> x1, waiting for transfers between devices: 21.2 us -> 3.03 us  [local(): pieces = lax.all_gather(out_weight, ('seq', 'dp'), axis=0, tiled=False)]
    reduce_scatter x1, waiting for transfers between devices: 19.1 us -> 1.62 us  [local(): lax.psum_scatter(partial_weight.astype(jnp.bfloat16), 'seq', scatter_dime...]
    ppermute x3, waiting for transfers between devices: 1.47 us -> 11.2 us  [shift_up(): return lax.ppermute(block, axis, route)]
    reduce_scatter x1, waiting for transfers between devices: 4.66 us -> 0.01 us  [local(): lax.psum_scatter(row_share.astype(jnp.float32), 'dp', scatter_dimension=1...]
    ppermute x1, waiting for transfers between devices: 19 us -> 14.4 us  [return_behind(): relayed = lax.ppermute(near, 'seq', [(i, i + 2) for i in earlier])]
    reshape x0 -> x1, local copies, waits for them, and re-layouts: none -> 3.93 us  [local(): pieces.reshape((row_blocks, col_blocks) + out_weight.shape)]
    dot_general x5, matrix products: 8.39 us -> 6.16 us  [local(): jnp.einsum('hqk,hke->hqe', expo_full.astype(jnp.bfloat16), held[dist][1],...]
    unnamed x82 -> x101, local copies, waits for them, and re-layouts: 18.5 us -> 16.6 us
  transfers between devices with their start and end apart: 17 -> 16, of which waited for: 8 -> 8; matrix products, arithmetic and copies ran while one was open for 37% -> 46% of each run, Pallas kernels for 0% -> 0%
where the time goes in v12:
time: 168 us; the launch traced here: 166 us
  matrix products  41.3 us (25%)
  waiting for transfers between devices  36.5 us (22%)
  starting transfers between devices  27.5 us (16%)
  local copies, waits for them, and re-layouts  25.4 us (15%)
  other arithmetic  19.1 us (11%)
  between operations  16.3 us (10%)
    unnamed x101, local copies, waits for them, and re-layouts  16.6 us
    ppermute x1, waiting for transfers between devices, return_behind(): relayed = lax.ppermute(near, 'seq', [(i, i + 2) for i in earlier])  14.4 us
    ppermute x3, waiting for transfers between devices, shift_up(): return lax.ppermute(block, axis, route)  11.2 us
    ppermute x3, starting transfers between devices, shift_up(): return lax.ppermute(block, axis, route)  8.27 us
    ppermute x2, starting transfers between devices, gather_behind(): relayed = lax.ppermute(far[k], 'seq', [(i + 2, i) for i in earlier])  8.22 us
    dot_general x5, matrix products, local(): jnp.einsum('hqe,hke->hqk', query_heads, held[dist][0], preferred_element_...  8.13 us
    dot_general x5, matrix products, local(): jnp.einsum('hqe,hke->hqk', grad_heads, value_block, preferred_element_typ...  6.75 us
    dot_general x5, matrix products, local(): jnp.einsum('hqk,hqe->hke', prob_back, grad_heads, preferred_element_type=...  6.62 us
  transfers between devices with their start and end apart: 16, of which 8 were waited for; matrix products, arithmetic and copies ran while one was open for 46% of the time, Pallas kernels for 0%

profile of v12, /device:TPU:4, one launch (start us, length us, event | category | flops | bytes accessed | tf_op | source)
XLA Modules:
  0.0 166.1 jit_solution(3909329471458463762)
XLA Ops:
  8.1 1.2 copy.85
  9.3 3.5 %collective-permute-start.1 = (bf16[12,256,64]{1,2,0:T(8,128)(2,1)S(1)}, bf16[12,256,64]{1,2,0:T(8,128)(2,1)S(1)}, u32[]{:S(2)}, u32[]{:S(2)}) collective-permute-start(bf16[12,256,64]{1,2,0:T(8,128)(2,1)S(1)} %bitcast.231), channel_id=1, source_target_pairs={{0,8},{2,10},{4,12},{6,14},{8,16},{10,18},{12,20},{14,22},{16,24},... | collective-permute-start | bytes 1179656 | tf_op jit(solution)/shard_map/ppermute | solution.py:18
  12.8 1.3 collective-permute-start
  14.1 1.2 copy.87
  15.3 3.5 %collective-permute-start.4 = (bf16[12,256,64]{1,2,0:T(8,128)(2,1)S(1)}, bf16[12,256,64]{1,2,0:T(8,128)(2,1)S(1)}, u32[]{:S(2)}, u32[]{:S(2)}) collective-permute-start(bf16[12,256,64]{1,2,0:T(8,128)(2,1)S(1)} %bitcast.252), channel_id=1, source_target_pairs={{0,8},{2,10},{4,12},{6,14},{8,16},{10,18},{12,20},{14,22},{16,24},... | collective-permute-start | bytes 1179656 | tf_op jit(solution)/shard_map/ppermute | solution.py:18
  18.8 1.3 collective-permute-start.3
  22.3 5.0 %collective-permute-start.2 = (bf16[12,256,64]{1,2,0:T(8,128)(2,1)S(1)}, bf16[12,256,64]{1,2,0:T(8,128)(2,1)}, u32[]{:S(2)}, u32[]{:S(2)}) collective-permute-start(bf16[12,256,64]{1,2,0:T(8,128)(2,1)S(1)} %collective-permute-done.1), channel_id=1, source_target_pairs={{4,0},{6,2},{12,8},{14,10},{20,16},{22,18},{28,24},{30,26},{5,1},{... | collective-permute-start | bytes 1179656 | tf_op jit(solution)/shard_map/ppermute | solution.py:58
  27.9 1.2 copy.84
  29.6 3.2 %collective-permute-start.5 = (bf16[12,256,64]{1,2,0:T(8,128)(2,1)S(1)}, bf16[12,256,64]{1,2,0:T(8,128)(2,1)}, u32[]{:S(2)}, u32[]{:S(2)}) collective-permute-start(bf16[12,256,64]{1,2,0:T(8,128)(2,1)S(1)} %collective-permute-done.4), channel_id=1, source_target_pairs={{4,0},{6,2},{12,8},{14,10},{20,16},{22,18},{28,24},{30,26},{5,1},{... | collective-permute-start | bytes 1179656 | tf_op jit(solution)/shard_map/ppermute | solution.py:58
  32.7 2.3 %select_reduce_fusion.1 = (f32[12,256]{1,0:T(8,128)S(1)}, f32[12,256,256]{1,2,0:T(8,128)}) fusion(pred[256,256]{0,1:T(8,128)(4,1)S(1)} %get-tuple-element.44, bf16[12,256,64]{1,2,0:T(8,128)(2,1)S(1)} %bitcast.218, bf16[12,256,64]{1,2,0:T(8,128)(2,1)S(1)} %bitcast.233), kind=kOutput, calls=%fused_computation.28 | convolution fusion | flops 103019520 | bytes 4009984 | tf_op jit(solution)/shard_map/hqe,hke->hqk/dot_general | solution.py:142
  36.7 1.0 broadcast_select_fusion.1
  37.8 5.3 %collective-permute-done.5 = bf16[12,256,64]{1,2,0:T(8,128)(2,1)} collective-permute-done((bf16[12,256,64]{1,2,0:T(8,128)(2,1)S(1)}, bf16[12,256,64]{1,2,0:T(8,128)(2,1)}, u32[]{:S(2)}, u32[]{:S(2)}) %collective-permute-start.5) | collective-permute-done | bytes 393248 | tf_op jit(solution)/shard_map/ppermute | solution.py:58
  43.1 1.0 broadcast_select_fusion
  44.1 2.5 %maximum_select_fusion = (bf16[2,12,256,64]{2,3,1,0:T(8,128)(2,1)}, bf16[2,12,256,64]{2,3,1,0:T(8,128)(2,1)}) fusion(bf16[1,12,256,64]{2,3,1,0:T(8,128)(2,1)S(1)} %bitcast.254, bf16[1,12,256,64]{2,3,1,0:T(8,128)(2,1)S(1)} %bitcast.234, pred[]{:T(512)S(6)} %eq.101, bf16[1,12,256,64]{2,3,1,0:T(8,128)(2,1)S(1)} %bitcast.257, ...), kind=kLoop, calls=%fused_computation.121 | loop fusion | flops 1966080 | bytes 3932161 | tf_op jit(solution)/shard_map/jit(_where)/select_n | solution.py:66
  46.7 2.3 %convolution_multiply_fusion = f32[12,256,256]{2,1,0:T(8,128)} fusion(bf16[12,256,64]{1,2,0:T(8,128)(2,1)S(1)} %bitcast.219, bf16[12,256,64]{1,2,0:T(8,128)(2,1)S(1)} %collective-permute-done.1), kind=kOutput, calls=%fused_computation.46 | convolution fusion | flops 101449728 | bytes 3932160 | tf_op jit(solution)/shard_map/hqe,hke->hqk/dot_general | solution.py:142
  49.0 3.6 %copy.89 = f32[12,256,256]{1,2,0:T(8,128)} copy(f32[12,256,256]{2,1,0:T(8,128)} %convolution_multiply_fusion) | data formatting | bytes 6291456 | tf_op jit(solution)/shard_map/mul | solution.py:142
  53.1 2.1 %select_reduce_fusion = f32[12,256]{1,0:T(8,128)S(1)} fusion(f32[12,256,256]{1,2,0:T(8,128)} %copy.89, pred[256,256]{0,1:T(8,128)(4,1)S(1)} %get-tuple-element.43), kind=kLoop, calls=%fused_computation.27 | loop fusion | flops 1569792 | bytes 3223552 | tf_op jit(solution)/shard_map/reduce_max | solution.py:147
  56.0 2.1 %fusion.6 = (f32[12,256]{1,0:T(8,128)S(1)}, f32[12,256,256]{2,1,0:T(8,128)S(1)}) fusion(pred[256,256]{0,1:T(8,128)(4,1)S(1)} %get-tuple-element.40, bf16[12,256,64]{1,2,0:T(8,128)(2,1)S(1)} %bitcast.221, bf16[2,12,256,64]{2,3,1,0:T(8,128)(2,1)} %collective-permute-done.6), kind=kOutput, calls=%fused_computation.24 | convolution fusion | flops 103019520 | bytes 4009984 | tf_op jit(solution)/shard_map/hqe,hke->hqk/dot_general | solution.py:142
  59.2 3.2 %copy-done.4 = f32[12,256,256]{1,2,0:T(8,128)S(1)} copy-done((f32[12,256,256]{1,2,0:T(8,128)S(1)}, f32[12,256,256]{1,2,0:T(8,128)}, u32[]{:S(2)}) %copy-start.4) | copy-done | bytes 3145752
  62.4 3.9 %fusion.19 = (f32[12,256]{1,0:T(8,128)S(1)}, f32[12,256]{1,0:T(8,128)S(1)}, f32[12,256]{1,0:T(8,128)S(1)}, f32[12,256]{1,0:T(8,128)S(1)}, f32[12,256]{1,0:T(8,128)S(1)}) fusion(f32[12,256,256]{2,1,0:T(8,128)S(1)} %get-tuple-element.52, f32[12,256]{1,0:T(8,128)S(1)} %maximum_maximum_fusion, pred[256,256]{0,1:T(8,128)(4,1)S(1)} %get-tuple-element.40, ...), kind=kLoop, calls=%fused_computation.40 | loop fusion | flops 18859008 | bytes 16130048 | tf_op jit(solution)/shard_map/reduce_sum | solution.py:155
  68.8 1.9 %fusion.101 = f32[12,256,64]{1,2,0:T(8,128)S(1)} fusion(f32[12,256,64]{1,2,0:T(8,128)S(1)} %fusion.66, f32[12,256,256]{2,1,0:T(8,128)S(1)} %get-tuple-element.52, f32[12,256]{1,0:T(8,128)S(1)} %maximum_maximum_fusion, pred[256,256]{0,1:T(8,128)(4,1)S(1)} %get-tuple-element.40, bf16[2,12,256,64]{2,3,1,0:T(8,128)(2,1)} %collective-permute-done.6), kind=kOutput, calls=%fused_computation.115 | convolution fusion | flops 104792064 | bytes 5189632 | tf_op jit(solution)/shard_map/hqk,hke->hqe/dot_general | solution.py:156
  70.7 1.8 %fusion.117 = (bf16[256,12,64]{0,2,1:T(8,128)(2,1)S(1)}, f32[12,256,64]{1,2,0:T(8,128)}) fusion(f32[256,12]{0,1:T(8,128)S(1)} %bitcast.262, f32[12,256,64]{1,2,0:T(8,128)S(1)} %fusion.33, f32[12,256,64]{1,2,0:T(8,128)S(1)} %fusion.60, f32[12,256,64]{1,2,0:T(8,128)S(1)} %fusion.101, bf16[12,256,64]{1,2,0:T(8,128)(2,1)S(1)} %broadcast_select_fusion, ...), kind=kOutput, calls=%fused_computation.128 | convolution fusion | flops 105578496 | bytes 7168000 | tf_op jit(solution)/shard_map/hqk,hke->hqe/dot_general | solution.py:156
  73.3 2.2 %fusion.115 = bf16[768,1536]{1,0:T(8,128)(2,1)} fusion(bf16[256,768]{0,1:T(8,128)(2,1)S(1)} %bitcast.250, bf16[1,256,1536]{2,1,0:T(8,128)(2,1)S(1)} %copy-done), kind=kOutput, calls=%fused_computation.125 | convolution fusion | flops 603979776 | bytes 3538944 | tf_op jit(solution)/shard_map/dot_general | solution.py:169
  75.8 3.0 %all-gather.3.cloned.1.call-done = bf16[1536,768]{1,0:T(8,128)(2,1)} async-done(((bf16[48,768]{1,0:T(8,128)(2,1)}), bf16[1536,768]{1,0:T(8,128)(2,1)}) %all-gather.3.cloned.1.call-update) | async-done | bytes 2359312 | tf_op jit(solution)/shard_map/all_gather | solution.py:119
  78.8 3.9 %copy.95 = bf16[16,2,48,768]{3,1,2,0:T(2,128)(2,1)S(1)} copy(bf16[16,2,48,768]{3,2,1,0:T(8,128)(2,1)} %bitcast.249) | data formatting | bytes 4718592 | tf_op jit(solution)/shard_map/reshape | solution.py:121
  83.2 1.6 convolution_convert_fusion.1
  84.7 1.2 copy.96
  85.9 2.8 %fusion.84 = f32[1,12,256,64]{2,3,1,0:T(8,128)S(1)} fusion(bf16[12,256,64]{1,2,0:T(8,128)(2,1)S(1)} %bitcast.236, f32[12,256,256]{2,1,0:T(8,128)} %copy-done.10, f32[12,256]{1,0:T(8,128)S(1)} %get-tuple-element.34, pred[256,256]{0,1:T(8,128)(4,1)} %copy-done.42), kind=kOutput, calls=%fused_computation.97 | convolution fusion | flops 103809024 | bytes 4403200 | tf_op jit(solution)/shard_map/hqk,hqe->hke/dot_general | solution.py:220
  91.4 1.1 multiply_convert_fusion.1
  93.4 1.1 multiply_convert_fusion
  95.4 2.4 %multiply_convert_fusion.3 = bf16[12,256,256]{1,2,0:T(8,128)(2,1)S(1)} fusion(f32[12,256,256]{2,1,0:T(8,128)S(1)} %copy-done.11, bf16[12,256,64]{1,2,0:T(8,128)(2,1)S(1)} %bitcast.241, f32[12,256]{1,0:T(8,128)S(1)} %multiply_reduce_fusion, f32[12,256]{1,0:T(8,128)S(1)} %get-tuple-element.34, pred[256,256]{0,1:T(8,128)(4,1)S(1)} %copy-done.43, ...), kind=kOutput, calls=%fused_computation.17 | convolution fusion | flops 105381888 | bytes 5595136 | tf_op jit(solution)/shard_map/hqe,hke->hqk/dot_general | solution.py:208
  99.0 1.1 multiply_convert_fusion.4
  101.6 1.5 fusion.118
  106.7 1.4 fusion.40
  108.1 1.4 collective-permute-start.11
  110.6 1.1 fusion.113
  111.7 5.6 %collective-permute-start.10 = (bf16[2,12,256,64]{2,3,1,0:T(8,128)(2,1)}, bf16[2,12,256,64]{2,3,1,0:T(8,128)(2,1)}, u32[]{:S(2)}, u32[]{:S(2)}) collective-permute-start(bf16[2,12,256,64]{2,3,1,0:T(8,128)(2,1)} %fusion.40), channel_id=1, source_target_pairs={{4,0},{6,2},{12,8},{14,10},{20,16},{22,18},{28,24},{30,26},{5,1},{... | collective-permute-start | bytes 2359304 | tf_op jit(solution)/shard_map/ppermute | solution.py:95
  117.3 14.4 %collective-permute-done.11 = bf16[2,12,256,64]{2,3,1,0:T(8,128)(2,1)S(1)} collective-permute-done((bf16[2,12,256,64]{2,3,1,0:T(8,128)(2,1)}, bf16[2,12,256,64]{2,3,1,0:T(8,128)(2,1)S(1)}, u32[]{:S(2)}, u32[]{:S(2)}) %collective-permute-start.11) | collective-permute-done | bytes 786464 | tf_op jit(solution)/shard_map/ppermute | solution.py:96
  131.7 1.3 fusion.42
  133.0 1.3 collective-permute-start.12
  134.3 1.7 %fusion.10 = bf16[1,256,1536]{2,1,0:T(8,128)(2,1)} fusion(bf16[256,768]{0,1:T(8,128)(2,1)S(1)} %bitcast.251, bf16[768,1536]{1,0:T(8,128)(2,1)S(1)} %bitcast.229), kind=kOutput, calls=%fused_computation.31 | convolution fusion | flops 604372992 | bytes 3538944 | tf_op jit(solution)/shard_map/dot_general | solution.py:173
  136.0 1.6 fusion.81
  137.6 1.6 reduce-scatter.3.cloned.1.call-done
  139.2 1.6 convert_element_type.187
  140.9 2.0 %fusion.99 = f32[1,12,256,64]{2,3,1,0:T(8,128)S(1)} fusion(bf16[12,256,256]{1,2,0:T(8,128)(2,1)} %copy-done.14, bf16[12,256,64]{1,2,0:T(8,128)(2,1)S(1)} %bitcast.227), kind=kOutput, calls=%fused_computation.113 | convolution fusion | flops 100859904 | bytes 2752512 | tf_op jit(solution)/shard_map/hqk,hqe->hke/dot_general | solution.py:217
  142.9 2.0 %copy.118 = bf16[1,256,768]{2,1,0:T(8,128)(2,1)} copy(bf16[1,256,768]{1,2,0:T(8,128)(2,1)} %bitcast.261) | data formatting | bytes 786432
  144.9 9.7 %collective-permute-done.12 = bf16[2,12,256,64]{2,3,1,0:T(8,128)(2,1)} collective-permute-done((bf16[2,12,256,64]{2,3,1,0:T(8,128)(2,1)}, bf16[2,12,256,64]{2,3,1,0:T(8,128)(2,1)}, u32[]{:S(2)}, u32[]{:S(2)}) %collective-permute-start.12) | collective-permute-done | bytes 786464 | tf_op jit(solution)/shard_map/ppermute | solution.py:18
  154.6 2.1 %fusion.39 = bf16[2,12,256,64]{2,3,1,0:T(8,128)(2,1)S(1)} fusion(f32[1,12,256,64]{2,3,1,0:T(8,128)} %fusion.81, f32[1,12,256,64]{2,3,1,0:T(8,128)S(1)} %fusion.99, bf16[2,12,256,64]{2,3,1,0:T(8,128)(2,1)} %collective-permute-done.12, bf16[2,12,256,64]{2,3,1,0:T(8,128)(2,1)} %collective-permute-done.10, f32[2,12,256,64]{2,3,1,0:T(8,128)S(1)} %copy-done.13, ...), kind=kLoop, calls=%fused_computation.56 | loop fusion | flops 3538944 | bytes 5505026 | tf_op jit(solution)/shard_map/convert.1
  (152 shorter events, 24.3 us)
Async XLA Ops:
  8.0 65.3 %copy-start = (bf16[1,256,1536]{2,1,0:T(8,128)(2,1)S(1)}, bf16[1,256,1536]{2,1,0:T(8,128)(2,1)}, u32[]{:S(2)}) copy-start(bf16[1,256,1536]{2,1,0:T(8,128)(2,1)} %param.9) | copy-start | bytes 2359300
  8.0 70.8 %all-gather.3.cloned.1.call-start = ((), (), s32[]{:S(2)}) async-start(), calls=%async_computation.4 | async-start | bytes 2433024 | tf_op jit(solution)/shard_map/all_gather | solution.py:119
  9.3 34.8 %copy-start.15 = (bf16[1,256,768]{1,2,0:T(8,128)(2,1)}, bf16[1,256,768]{1,2,0:T(8,128)(2,1)S(1)}, u32[]{:S(2)}) copy-start(bf16[1,256,768]{1,2,0:T(8,128)(2,1)S(1)} %copy.85) | copy-start | bytes 1179652
  9.3 13.0 %collective-permute-start.1 = (bf16[12,256,64]{1,2,0:T(8,128)(2,1)S(1)}, bf16[12,256,64]{1,2,0:T(8,128)(2,1)S(1)}, u32[]{:S(2)}, u32[]{:S(2)}) collective-permute-start(bf16[12,256,64]{1,2,0:T(8,128)(2,1)S(1)} %bitcast.231), channel_id=1, source_target_pairs={{0,8},{2,10},{4,12},{6,14},{8,16},{10,18},{12,20},{14,22},{16,24},... | collective-permute-start | bytes 1179656 | tf_op jit(solution)/shard_map/ppermute | solution.py:18
  12.8 22.2 %collective-permute-start = (bf16[12,256,64]{1,2,0:T(8,128)(2,1)S(1)}, bf16[12,256,64]{1,2,0:T(8,128)(2,1)S(1)}, u32[]{:S(2)}, u32[]{:S(2)}) collective-permute-start(bf16[12,256,64]{1,2,0:T(8,128)(2,1)S(1)} %bitcast.232), channel_id=1, source_target_pairs={{0,4},{2,6},{8,12},{10,14},{16,20},{18,22},{24,28},{26,30},{1,5},{... | collective-permute-start | bytes 1179656 | tf_op jit(solution)/shard_map/ppermute | solution.py:57
  15.3 51.8 %copy-start.25 = (bf16[1,256,768]{1,2,0:T(8,128)(2,1)}, bf16[1,256,768]{1,2,0:T(8,128)(2,1)S(1)}, u32[]{:S(2)}) copy-start(bf16[1,256,768]{1,2,0:T(8,128)(2,1)S(1)} %copy.87) | copy-start | bytes 1179652
  15.3 14.3 %collective-permute-start.4 = (bf16[12,256,64]{1,2,0:T(8,128)(2,1)S(1)}, bf16[12,256,64]{1,2,0:T(8,128)(2,1)S(1)}, u32[]{:S(2)}, u32[]{:S(2)}) collective-permute-start(bf16[12,256,64]{1,2,0:T(8,128)(2,1)S(1)} %bitcast.252), channel_id=1, source_target_pairs={{0,8},{2,10},{4,12},{6,14},{8,16},{10,18},{12,20},{14,22},{16,24},... | collective-permute-start | bytes 1179656 | tf_op jit(solution)/shard_map/ppermute | solution.py:18
  18.8 19.0 %collective-permute-start.3 = (bf16[12,256,64]{1,2,0:T(8,128)(2,1)S(1)}, bf16[12,256,64]{1,2,0:T(8,128)(2,1)}, u32[]{:S(2)}, u32[]{:S(2)}) collective-permute-start(bf16[12,256,64]{1,2,0:T(8,128)(2,1)S(1)} %bitcast.253), channel_id=1, source_target_pairs={{0,4},{2,6},{8,12},{10,14},{16,20},{18,22},{24,28},{26,30},{1,5},{... | collective-permute-start | bytes 1179656 | tf_op jit(solution)/shard_map/ppermute | solution.py:57
  20.1 119.1 %reduce-scatter.3.cloned.1.call-start = ((), (), s32[]{:S(2)}) async-start(), calls=%async_computation.2 | async-start | bytes 2506752 | tf_op jit(solution)/shard_map/reduce_scatter | solution.py:180
  22.3 24.4 %copy-start.19 = (bf16[12,256,64]{1,2,0:T(8,128)(2,1)}, bf16[12,256,64]{1,2,0:T(8,128)(2,1)S(1)}, u32[]{:S(2)}) copy-start(bf16[12,256,64]{1,2,0:T(8,128)(2,1)S(1)} %collective-permute-done.1) | copy-start | bytes 1179652
  22.3 14.4 %collective-permute-start.2 = (bf16[12,256,64]{1,2,0:T(8,128)(2,1)S(1)}, bf16[12,256,64]{1,2,0:T(8,128)(2,1)}, u32[]{:S(2)}, u32[]{:S(2)}) collective-permute-start(bf16[12,256,64]{1,2,0:T(8,128)(2,1)S(1)} %collective-permute-done.1), channel_id=1, source_target_pairs={{4,0},{6,2},{12,8},{14,10},{20,16},{22,18},{28,24},{30,26},{5,1},{... | collective-permute-start | bytes 1179656 | tf_op jit(solution)/shard_map/ppermute | solution.py:58
  27.9 38.4 %copy-start.21 = (pred[256,256]{0,1:T(8,128)(4,1)}, pred[256,256]{0,1:T(8,128)(4,1)S(1)}, u32[]{:S(2)}) copy-start(pred[256,256]{0,1:T(8,128)(4,1)S(1)} %get-tuple-element.43) | copy-start | bytes 196612
  27.9 39.2 %copy-start.35 = (pred[256,256]{0,1:T(8,128)(4,1)}, pred[256,256]{0,1:T(8,128)(4,1)S(1)}, u32[]{:S(2)}) copy-start(pred[256,256]{0,1:T(8,128)(4,1)S(1)} %get-tuple-element.44) | copy-start | bytes 196612
  27.9 40.0 %copy-start.39 = (pred[256,256]{0,1:T(8,128)(4,1)}, pred[256,256]{0,1:T(8,128)(4,1)S(1)}, u32[]{:S(2)}) copy-start(pred[256,256]{0,1:T(8,128)(4,1)S(1)} %get-tuple-element.42) | copy-start | bytes 196612
  27.9 40.9 %copy-start.42 = (pred[256,256]{0,1:T(8,128)(4,1)}, pred[256,256]{0,1:T(8,128)(4,1)S(1)}, u32[]{:S(2)}) copy-start(pred[256,256]{0,1:T(8,128)(4,1)S(1)} %get-tuple-element.40) | copy-start | bytes 196612
  27.9 42.8 %copy-start.37 = (pred[256,256]{0,1:T(8,128)(4,1)}, pred[256,256]{0,1:T(8,128)(4,1)S(1)}, u32[]{:S(2)}) copy-start(pred[256,256]{0,1:T(8,128)(4,1)S(1)} %get-tuple-element.41) | copy-start | bytes 196612
  29.6 8.2 %copy-start.29 = (bf16[12,256,64]{1,2,0:T(8,128)(2,1)}, bf16[12,256,64]{1,2,0:T(8,128)(2,1)S(1)}, u32[]{:S(2)}) copy-start(bf16[12,256,64]{1,2,0:T(8,128)(2,1)S(1)} %collective-permute-done.4) | copy-start | bytes 1179652
  29.6 13.5 %collective-permute-start.5 = (bf16[12,256,64]{1,2,0:T(8,128)(2,1)S(1)}, bf16[12,256,64]{1,2,0:T(8,128)(2,1)}, u32[]{:S(2)}, u32[]{:S(2)}) collective-permute-start(bf16[12,256,64]{1,2,0:T(8,128)(2,1)S(1)} %collective-permute-done.4), channel_id=1, source_target_pairs={{4,0},{6,2},{12,8},{14,10},{20,16},{22,18},{28,24},{30,26},{5,1},{... | collective-permute-start | bytes 1179656 | tf_op jit(solution)/shard_map/ppermute | solution.py:58
  37.7 17.5 %copy-start.17 = (bf16[12,256,64]{1,2,0:T(8,128)(2,1)}, bf16[12,256,64]{1,2,0:T(8,128)(2,1)S(1)}, u32[]{:S(2)}) copy-start(bf16[12,256,64]{1,2,0:T(8,128)(2,1)S(1)} %broadcast_select_fusion.1) | copy-start | bytes 1179652
  44.1 26.6 %copy-start.27 = (bf16[12,256,64]{1,2,0:T(8,128)(2,1)}, bf16[12,256,64]{1,2,0:T(8,128)(2,1)S(1)}, u32[]{:S(2)}) copy-start(bf16[12,256,64]{1,2,0:T(8,128)(2,1)S(1)} %broadcast_select_fusion) | copy-start | bytes 1179652
  46.7 9.3 %collective-permute-start.6 = (bf16[2,12,256,64]{2,3,1,0:T(8,128)(2,1)}, bf16[2,12,256,64]{2,3,1,0:T(8,128)(2,1)}, u32[]{:S(2)}, u32[]{:S(2)}) collective-permute-start(bf16[2,12,256,64]{2,3,1,0:T(8,128)(2,1)} %get-tuple-element.38), channel_id=1, source_target_pairs={{0,2},{2,0},{4,6},{6,4},{8,10},{10,8},{12,14},{14,12},{16,18},{18,... | collective-permute-start | bytes 2359304 | tf_op jit(solution)/shard_map/ppermute | solution.py:23
  52.6 5.6 %collective-permute-start.7 = (bf16[2,12,256,64]{2,3,1,0:T(8,128)(2,1)}, bf16[2,12,256,64]{2,3,1,0:T(8,128)(2,1)S(1)}, u32[]{:S(2)}, u32[]{:S(2)}) collective-permute-start(bf16[2,12,256,64]{2,3,1,0:T(8,128)(2,1)} %get-tuple-element.39), channel_id=1, source_target_pairs={{0,2},{2,0},{4,6},{6,4},{8,10},{10,8},{12,14},{14,12},{16,18},{18,... | collective-permute-start | bytes 2359304 | tf_op jit(solution)/shard_map/ppermute | solution.py:23
  56.0 14.8 %copy-start.6 = (f32[12,256,256]{2,1,0:T(8,128)}, f32[12,256,256]{2,1,0:T(8,128)S(1)}, u32[]{:S(2)}) copy-start(f32[12,256,256]{2,1,0:T(8,128)S(1)} %get-tuple-element.48) | copy-start | bytes 9437188
  56.0 3.2 %copy-start.2 = (f32[12,256,256]{1,2,0:T(8,128)S(1)}, f32[12,256,256]{1,2,0:T(8,128)}, u32[]{:S(2)}) copy-start(f32[12,256,256]{1,2,0:T(8,128)} %copy.89) | copy-start | bytes 9437188
  56.0 6.4 %copy-start.4 = (f32[12,256,256]{1,2,0:T(8,128)S(1)}, f32[12,256,256]{1,2,0:T(8,128)}, u32[]{:S(2)}) copy-start(f32[12,256,256]{1,2,0:T(8,128)} %get-tuple-element.50) | copy-start | bytes 9437188
  58.1 10.7 %copy-start.10 = (f32[12,256,256]{2,1,0:T(8,128)}, f32[12,256,256]{2,1,0:T(8,128)S(1)}, u32[]{:S(2)}) copy-start(f32[12,256,256]{2,1,0:T(8,128)S(1)} %get-tuple-element.52) | copy-start | bytes 9437188
  58.2 9.8 %copy-start.33 = (bf16[2,12,256,64]{2,3,1,0:T(8,128)(2,1)}, bf16[2,12,256,64]{2,3,1,0:T(8,128)(2,1)S(1)}, u32[]{:S(2)}) copy-start(bf16[2,12,256,64]{2,3,1,0:T(8,128)(2,1)S(1)} %collective-permute-done.7) | copy-start | bytes 2359300
  58.9 9.1 %copy-start.8 = (f32[12,256,256]{2,1,0:T(8,128)}, f32[12,256,256]{2,1,0:T(8,128)S(1)}, u32[]{:S(2)}) copy-start(f32[12,256,256]{2,1,0:T(8,128)S(1)} %get-tuple-element.46) | copy-start | bytes 9437188
  62.4 3.9 %copy-start.30 = (bf16[12,256,64]{1,2,0:T(8,128)(2,1)S(1)}, bf16[12,256,64]{1,2,0:T(8,128)(2,1)}, u32[]{:S(2)}) copy-start(bf16[12,256,64]{1,2,0:T(8,128)(2,1)} %copy-done.29) | copy-start | bytes 1179652
  66.3 4.4 %copy-start.45 = (f32[12,256]{1,0:T(8,128)}, f32[12,256]{1,0:T(8,128)S(1)}, u32[]{:S(2)}) copy-start(f32[12,256]{1,0:T(8,128)S(1)} %get-tuple-element.35) | copy-start | bytes 36868
  75.5 83.1 %reduce-scatter.5.cloned.1.call-start = ((), (), s32[]{:S(2)}) async-start(), calls=%async_computation.3 | async-start | bytes 442368 | tf_op jit(solution)/shard_map/reduce_scatter | solution.py:183
  84.7 4.1 %copy-start.40 = (pred[256,256]{0,1:T(8,128)(4,1)S(1)}, pred[256,256]{0,1:T(8,128)(4,1)}, u32[]{:S(2)}) copy-start(pred[256,256]{0,1:T(8,128)(4,1)} %copy-done.39) | copy-start | bytes 196612
  85.9 3.1 %copy-start.9 = (f32[12,256,256]{2,1,0:T(8,128)S(1)}, f32[12,256,256]{2,1,0:T(8,128)}, u32[]{:S(2)}) copy-start(f32[12,256,256]{2,1,0:T(8,128)} %copy-done.8) | copy-start | bytes 9437188
  89.0 2.3 %copy-start.7 = (f32[12,256,256]{2,1,0:T(8,128)S(1)}, f32[12,256,256]{2,1,0:T(8,128)}, u32[]{:S(2)}) copy-start(f32[12,256,256]{2,1,0:T(8,128)} %copy-done.6) | copy-start | bytes 9437188
  89.0 2.3 %copy-start.28 = (bf16[12,256,64]{1,2,0:T(8,128)(2,1)S(1)}, bf16[12,256,64]{1,2,0:T(8,128)(2,1)}, u32[]{:S(2)}) copy-start(bf16[12,256,64]{1,2,0:T(8,128)(2,1)} %copy-done.27) | copy-start | bytes 1179652
  89.0 2.3 %copy-start.38 = (pred[256,256]{0,1:T(8,128)(4,1)S(1)}, pred[256,256]{0,1:T(8,128)(4,1)}, u32[]{:S(2)}) copy-start(pred[256,256]{0,1:T(8,128)(4,1)} %copy-done.37) | copy-start | bytes 196612
  95.4 5.7 %copy-start.14 = (bf16[12,256,256]{1,2,0:T(8,128)(2,1)}, bf16[12,256,256]{1,2,0:T(8,128)(2,1)S(1)}, u32[]{:S(2)}) copy-start(bf16[12,256,256]{1,2,0:T(8,128)(2,1)S(1)} %multiply_convert_fusion) | copy-start | bytes 4718596
  98.6 8.1 %collective-permute-start.8 = (f32[2,12,256,64]{2,3,1,0:T(8,128)S(1)}, f32[2,12,256,64]{2,3,1,0:T(8,128)S(1)}, u32[]{:S(2)}, u32[]{:S(2)}) collective-permute-start(f32[2,12,256,64]{2,3,1,0:T(8,128)S(1)} %pad_maximum_fusion), channel_id=1, source_target_pairs={{0,2},{2,0},{4,6},{6,4},{8,10},{10,8},{12,14},{14,12},{16,18},{18,... | collective-permute-start | bytes 4718600 | tf_op jit(solution)/shard_map/ppermute | solution.py:23
  100.8 5.9 %collective-permute-start.9 = (f32[2,12,256,64]{2,3,1,0:T(8,128)S(1)}, f32[2,12,256,64]{2,3,1,0:T(8,128)S(1)}, u32[]{:S(2)}, u32[]{:S(2)}) collective-permute-start(f32[2,12,256,64]{2,3,1,0:T(8,128)S(1)} %pad_maximum_fusion.1), channel_id=1, source_target_pairs={{0,2},{2,0},{4,6},{6,4},{8,10},{10,8},{12,14},{14,12},{16,18},{18,... | collective-permute-start | bytes 4718600 | tf_op jit(solution)/shard_map/ppermute | solution.py:23
  101.5 2.2 %copy-start.3 = (f32[12,256,256]{1,2,0:T(8,128)S(1)}, f32[12,256,256]{1,2,0:T(8,128)}, u32[]{:S(2)}) copy-start(f32[12,256,256]{1,2,0:T(8,128)} %copy.89) | copy-start | bytes 9437188
  106.7 3.4 %copy-start.12 = (f32[2,12,256,64]{2,3,1,0:T(8,128)}, f32[2,12,256,64]{2,3,1,0:T(8,128)S(1)}, u32[]{:S(2)}) copy-start(f32[2,12,256,64]{2,3,1,0:T(8,128)S(1)} %collective-permute-done.8) | copy-start | bytes 4718596
  108.1 2.4 %copy-start.18 = (bf16[12,256,64]{1,2,0:T(8,128)(2,1)S(1)}, bf16[12,256,64]{1,2,0:T(8,128)(2,1)}, u32[]{:S(2)}) copy-start(bf16[12,256,64]{1,2,0:T(8,128)(2,1)} %copy-done.17) | copy-start | bytes 1179652
  108.1 23.6 %collective-permute-start.11 = (bf16[2,12,256,64]{2,3,1,0:T(8,128)(2,1)}, bf16[2,12,256,64]{2,3,1,0:T(8,128)(2,1)S(1)}, u32[]{:S(2)}, u32[]{:S(2)}) collective-permute-start(bf16[2,12,256,64]{2,3,1,0:T(8,128)(2,1)} %fusion.40), channel_id=1, source_target_pairs={{0,4},{2,6},{8,12},{10,14},{16,20},{18,22},{24,28},{26,30},{1,5},{... | collective-permute-start | bytes 2359304 | tf_op jit(solution)/shard_map/ppermute | solution.py:96
  111.7 22.6 %copy-start.24 = (bf16[256,12,64]{0,2,1:T(8,128)(2,1)S(1)}, bf16[256,12,64]{0,2,1:T(8,128)(2,1)}, u32[]{:S(2)}) copy-start(bf16[256,12,64]{0,2,1:T(8,128)(2,1)} %copy-done.23) | copy-start | bytes 1179652
  111.7 33.2 %collective-permute-start.10 = (bf16[2,12,256,64]{2,3,1,0:T(8,128)(2,1)}, bf16[2,12,256,64]{2,3,1,0:T(8,128)(2,1)}, u32[]{:S(2)}, u32[]{:S(2)}) collective-permute-start(bf16[2,12,256,64]{2,3,1,0:T(8,128)(2,1)} %fusion.40), channel_id=1, source_target_pairs={{4,0},{6,2},{12,8},{14,10},{20,16},{22,18},{28,24},{30,26},{5,1},{... | collective-permute-start | bytes 2359304 | tf_op jit(solution)/shard_map/ppermute | solution.py:95
  133.0 21.6 %collective-permute-start.12 = (bf16[2,12,256,64]{2,3,1,0:T(8,128)(2,1)}, bf16[2,12,256,64]{2,3,1,0:T(8,128)(2,1)}, u32[]{:S(2)}, u32[]{:S(2)}) collective-permute-start(bf16[2,12,256,64]{2,3,1,0:T(8,128)(2,1)} %fusion.42), channel_id=1, source_target_pairs={{8,0},{10,2},{12,4},{14,6},{16,8},{18,10},{20,12},{22,14},{24,16},... | collective-permute-start | bytes 2359304 | tf_op jit(solution)/shard_map/ppermute | solution.py:18
  137.6 17.0 %copy-start.13 = (f32[2,12,256,64]{2,3,1,0:T(8,128)S(1)}, f32[2,12,256,64]{2,3,1,0:T(8,128)}, u32[]{:S(2)}) copy-start(f32[2,12,256,64]{2,3,1,0:T(8,128)} %copy-done.12) | copy-start | bytes 4718596
  142.9 15.8 %copy-start.1 = (bf16[1,256,1536]{2,1,0:T(8,128)(2,1)S(1)}, bf16[1,256,1536]{2,1,0:T(8,128)(2,1)}, u32[]{:S(2)}) copy-start(bf16[1,256,1536]{2,1,0:T(8,128)(2,1)} %param.9) | copy-start | bytes 2359300
  (15 other events, 22.7 us)
Sparse Core Ops, SparseCore 0:
  20.2 58.5 all-gather.2
Sparse Core Ops, SparseCore 1:
  75.6 63.5 reduce-scatter.2
  142.0 12.0 reduce-scatter.4

commit v13 on v12

--- a/solution.py
+++ b/solution.py
@@ -192,8 +192,8 @@
     query_acc = None
     parts = [None] * (reach + 1)
     order = [d for d in range(reach, -1, -1) if d % 2 == 1] + [
-        d for d in range(reach, -1, -1) if d % 2 == 0
-    ]
+        d for d in range(2, reach + 1, 2)
+    ] + [0]
     for dist in order:
         key_block = held[dist][0]
         value_block = held[dist][1]

time: 168 us -> 167 us (level)
  waiting for transfers between devices: 36.5 us -> 44.5 us
  local copies, waits for them, and re-layouts: 25.4 us -> 18.9 us
    all_gather x1, waiting for transfers between devices: 3.03 us -> 8 us  [local(): pieces = lax.all_gather(out_weight, ('seq', 'dp'), axis=0, tiled=False)]
    mul x1 -> x0, local copies, waits for them, and re-layouts: 3.56 us -> none  [local(): jnp.einsum('hqe,hke->hqk', query_heads, held[dist][0], preferred_element_...]
    ppermute x2, waiting for transfers between devices: 6.2 us -> 9.74 us  [gather_behind(): relayed = lax.ppermute(far[k], 'seq', [(i + 2, i) for i in earlier])]
    unnamed x101, local copies, waits for them, and re-layouts: 16.6 us -> 13.6 us
    reduce_max x1 -> x0, other arithmetic: 2.15 us -> none  [local(): block_top = jnp.max(scores, axis=2)]
    ppermute x3, waiting for transfers between devices: 11.2 us -> 13 us  [shift_up(): return lax.ppermute(block, axis, route)]
  transfers between devices with their start and end apart: 16 -> 16, of which waited for: 8 -> 6; matrix products, arithmetic and copies ran while one was open for 46% -> 43% of each run, Pallas kernels for 0% -> 0%
where the time goes in v13:
time: 167 us; the launch traced here: 166 us
  waiting for transfers between devices  44.5 us (27%)
  matrix products  41.2 us (25%)
  starting transfers between devices  26.9 us (16%)
  local copies, waits for them, and re-layouts  18.9 us (11%)
  other arithmetic  17.7 us (11%)
  between operations  16.4 us (10%)
    unnamed x101, local copies, waits for them, and re-layouts  13.6 us
    ppermute x1, waiting for transfers between devices, return_behind(): relayed = lax.ppermute(near, 'seq', [(i, i + 2) for i in earlier])  13.6 us
    ppermute x3, waiting for transfers between devices, shift_up(): return lax.ppermute(block, axis, route)  13 us
    ppermute x2, waiting for transfers between devices, gather_behind(): relayed = lax.ppermute(far[k], 'seq', [(i + 2, i) for i in earlier])  9.74 us
    ppermute x3, starting transfers between devices, shift_up(): return lax.ppermute(block, axis, route)  8.27 us
    all_gather x1, waiting for transfers between devices, local(): pieces = lax.all_gather(out_weight, ('seq', 'dp'), axis=0, tiled=False)  8 us
    dot_general x5, matrix products, local(): jnp.einsum('hqe,hke->hqk', grad_heads, value_block, preferred_element_typ...  7.97 us
    ppermute x2, starting transfers between devices, gather_behind(): relayed = lax.ppermute(far[k], 'seq', [(i + 2, i) for i in earlier])  7.75 us
  transfers between devices with their start and end apart: 16, of which 6 were waited for; matrix products, arithmetic and copies ran while one was open for 43% of the time, Pallas kernels for 0%

profile of v13, /device:TPU:4, one launch (start us, length us, event | category | flops | bytes accessed | tf_op | source)
XLA Modules:
  0.0 165.6 jit_solution(15675922540475198615)
XLA Ops:
  8.1 1.2 copy.81
  9.3 3.5 %collective-permute-start.1 = (bf16[12,256,64]{1,2,0:T(8,128)(2,1)S(1)}, bf16[12,256,64]{1,2,0:T(8,128)(2,1)S(1)}, u32[]{:S(2)}, u32[]{:S(2)}) collective-permute-start(bf16[12,256,64]{1,2,0:T(8,128)(2,1)S(1)} %bitcast.232), channel_id=1, source_target_pairs={{0,8},{2,10},{4,12},{6,14},{8,16},{10,18},{12,20},{14,22},{16,24},... | collective-permute-start | bytes 1179656 | tf_op jit(solution)/shard_map/ppermute | solution.py:18
  12.8 1.3 collective-permute-start
  14.1 1.2 copy.83
  15.3 3.5 %collective-permute-start.4 = (bf16[12,256,64]{1,2,0:T(8,128)(2,1)S(1)}, bf16[12,256,64]{1,2,0:T(8,128)(2,1)S(1)}, u32[]{:S(2)}, u32[]{:S(2)}) collective-permute-start(bf16[12,256,64]{1,2,0:T(8,128)(2,1)S(1)} %bitcast.241), channel_id=1, source_target_pairs={{0,8},{2,10},{4,12},{6,14},{8,16},{10,18},{12,20},{14,22},{16,24},... | collective-permute-start | bytes 1179656 | tf_op jit(solution)/shard_map/ppermute | solution.py:18
  18.8 1.3 collective-permute-start.3
  21.2 1.2 copy.80
  22.5 5.3 %collective-permute-start.2 = (bf16[12,256,64]{1,2,0:T(8,128)(2,1)S(1)}, bf16[12,256,64]{1,2,0:T(8,128)(2,1)S(1)}, u32[]{:S(2)}, u32[]{:S(2)}) collective-permute-start(bf16[12,256,64]{1,2,0:T(8,128)(2,1)S(1)} %collective-permute-done.1), channel_id=1, source_target_pairs={{4,0},{6,2},{12,8},{14,10},{20,16},{22,18},{28,24},{30,26},{5,1},{... | collective-permute-start | bytes 1179656 | tf_op jit(solution)/shard_map/ppermute | solution.py:58
  27.8 1.8 %collective-permute-done.4 = bf16[12,256,64]{1,2,0:T(8,128)(2,1)S(1)} collective-permute-done((bf16[12,256,64]{1,2,0:T(8,128)(2,1)S(1)}, bf16[12,256,64]{1,2,0:T(8,128)(2,1)S(1)}, u32[]{:S(2)}, u32[]{:S(2)}) %collective-permute-start.4) | collective-permute-done | bytes 393248 | tf_op jit(solution)/shard_map/ppermute | solution.py:18
  29.6 2.4 %collective-permute-start.5 = (bf16[12,256,64]{1,2,0:T(8,128)(2,1)S(1)}, bf16[12,256,64]{1,2,0:T(8,128)(2,1)S(1)}, u32[]{:S(2)}, u32[]{:S(2)}) collective-permute-start(bf16[12,256,64]{1,2,0:T(8,128)(2,1)S(1)} %collective-permute-done.4), channel_id=1, source_target_pairs={{4,0},{6,2},{12,8},{14,10},{20,16},{22,18},{28,24},{30,26},{5,1},{... | collective-permute-start | bytes 1179656 | tf_op jit(solution)/shard_map/ppermute | solution.py:58
  33.4 4.4 %collective-permute-done.2 = bf16[12,256,64]{1,2,0:T(8,128)(2,1)S(1)} collective-permute-done((bf16[12,256,64]{1,2,0:T(8,128)(2,1)S(1)}, bf16[12,256,64]{1,2,0:T(8,128)(2,1)S(1)}, u32[]{:S(2)}, u32[]{:S(2)}) %collective-permute-start.2) | collective-permute-done | bytes 393248 | tf_op jit(solution)/shard_map/ppermute | solution.py:58
  37.9 1.1 broadcast_select_fusion.1
  38.9 5.3 %collective-permute-done.5 = bf16[12,256,64]{1,2,0:T(8,128)(2,1)S(1)} collective-permute-done((bf16[12,256,64]{1,2,0:T(8,128)(2,1)S(1)}, bf16[12,256,64]{1,2,0:T(8,128)(2,1)S(1)}, u32[]{:S(2)}, u32[]{:S(2)}) %collective-permute-start.5) | collective-permute-done | bytes 393248 | tf_op jit(solution)/shard_map/ppermute | solution.py:58
  44.2 1.1 broadcast_select_fusion
  45.3 2.5 %maximum_select_fusion = (bf16[2,12,256,64]{2,3,1,0:T(8,128)(2,1)}, bf16[2,12,256,64]{2,3,1,0:T(8,128)(2,1)}) fusion(bf16[1,12,256,64]{2,3,1,0:T(8,128)(2,1)S(1)} %bitcast.243, bf16[1,12,256,64]{2,3,1,0:T(8,128)(2,1)S(1)} %bitcast.234, pred[]{:T(512)S(6)} %eq.101, bf16[1,12,256,64]{2,3,1,0:T(8,128)(2,1)S(1)} %bitcast.246, ...), kind=kLoop, calls=%fused_computation.118 | loop fusion | flops 1966080 | bytes 3932161 | tf_op jit(solution)/shard_map/jit(_where)/select_n | solution.py:66
  47.9 2.3 %select_reduce_fusion.1 = (f32[12,256]{1,0:T(8,128)S(1)}, f32[12,256,256]{1,2,0:T(8,128)}) fusion(pred[256,256]{0,1:T(8,128)(4,1)S(1)} %get-tuple-element.44, bf16[12,256,64]{1,2,0:T(8,128)(2,1)S(1)} %bitcast.218, bf16[12,256,64]{1,2,0:T(8,128)(2,1)S(1)} %bitcast.235), kind=kOutput, calls=%fused_computation.28 | convolution fusion | flops 103019520 | bytes 4009984 | tf_op jit(solution)/shard_map/hqe,hke->hqk/dot_general | solution.py:142
  52.1 2.1 %fusion.6 = (f32[12,256]{1,0:T(8,128)S(1)}, f32[12,256,256]{2,1,0:T(8,128)S(1)}) fusion(pred[256,256]{0,1:T(8,128)(4,1)S(1)} %get-tuple-element.40, bf16[12,256,64]{1,2,0:T(8,128)(2,1)S(1)} %bitcast.221, bf16[2,12,256,64]{2,3,1,0:T(8,128)(2,1)} %collective-permute-done.6), kind=kOutput, calls=%fused_computation.24 | convolution fusion | flops 103019520 | bytes 4009984 | tf_op jit(solution)/shard_map/hqe,hke->hqk/dot_general | solution.py:142
  55.0 1.6 copy-done.2
  56.7 3.9 %fusion.17 = (f32[12,256]{1,0:T(8,128)S(1)}, f32[12,256]{1,0:T(8,128)S(1)}, f32[12,256]{1,0:T(8,128)S(1)}, f32[12,256]{1,0:T(8,128)S(1)}, f32[12,256]{1,0:T(8,128)S(1)}) fusion(f32[12,256,256]{2,1,0:T(8,128)S(1)} %get-tuple-element.54, f32[12,256]{1,0:T(8,128)S(1)} %maximum_maximum_fusion, pred[256,256]{0,1:T(8,128)(4,1)S(1)} %get-tuple-element.40, ...), kind=kLoop, calls=%fused_computation.38 | loop fusion | flops 19645440 | bytes 16130048 | tf_op jit(solution)/shard_map/reduce_sum | solution.py:155
  63.9 1.9 %fusion.99 = f32[12,256,64]{1,2,0:T(8,128)S(1)} fusion(f32[12,256,64]{1,2,0:T(8,128)S(1)} %fusion.64, f32[12,256,256]{2,1,0:T(8,128)S(1)} %get-tuple-element.54, f32[12,256]{1,0:T(8,128)S(1)} %maximum_maximum_fusion, pred[256,256]{0,1:T(8,128)(4,1)S(1)} %get-tuple-element.40, bf16[2,12,256,64]{2,3,1,0:T(8,128)(2,1)} %collective-permute-done.6), kind=kOutput, calls=%fused_computation.112 | convolution fusion | flops 104792064 | bytes 5189632 | tf_op jit(solution)/shard_map/hqk,hke->hqe/dot_general | solution.py:156
  65.8 1.8 %fusion.115 = (bf16[256,12,64]{0,2,1:T(8,128)(2,1)S(1)}, f32[12,256,64]{1,2,0:T(8,128)}) fusion(f32[256,12]{0,1:T(8,128)S(1)} %bitcast.262, f32[12,256,64]{1,2,0:T(8,128)S(1)} %fusion.56, f32[12,256,64]{1,2,0:T(8,128)S(1)} %fusion.58, f32[12,256,64]{1,2,0:T(8,128)S(1)} %fusion.99, bf16[12,256,64]{1,2,0:T(8,128)(2,1)S(1)} %broadcast_select_fusion, ...), kind=kOutput, calls=%fused_computation.125 | convolution fusion | flops 105578496 | bytes 7168000 | tf_op jit(solution)/shard_map/hqk,hke->hqe/dot_general | solution.py:156
  68.3 2.2 %fusion.113 = bf16[768,1536]{1,0:T(8,128)(2,1)} fusion(bf16[256,768]{0,1:T(8,128)(2,1)S(1)} %bitcast.239, bf16[1,256,1536]{2,1,0:T(8,128)(2,1)S(1)} %copy-done), kind=kOutput, calls=%fused_computation.122 | convolution fusion | flops 603979776 | bytes 3538944 | tf_op jit(solution)/shard_map/dot_general | solution.py:169
  70.8 8.0 %all-gather.3.cloned.1.call-done = bf16[1536,768]{1,0:T(8,128)(2,1)} async-done(((bf16[48,768]{1,0:T(8,128)(2,1)}), bf16[1536,768]{1,0:T(8,128)(2,1)}) %all-gather.3.cloned.1.call-update) | async-done | bytes 2359312 | tf_op jit(solution)/shard_map/all_gather | solution.py:119
  78.8 4.0 %copy.90 = bf16[16,2,48,768]{3,1,2,0:T(2,128)(2,1)S(1)} copy(bf16[16,2,48,768]{3,2,1,0:T(8,128)(2,1)} %bitcast.238) | data formatting | bytes 4718592 | tf_op jit(solution)/shard_map/reshape | solution.py:121
  83.2 1.6 convolution_convert_fusion.1
  84.8 1.2 copy.91
  86.0 2.9 %fusion.82 = f32[1,12,256,64]{2,3,1,0:T(8,128)S(1)} fusion(bf16[12,256,64]{1,2,0:T(8,128)(2,1)S(1)} %bitcast.248, f32[12,256,256]{2,1,0:T(8,128)} %copy-done.10, f32[12,256]{1,0:T(8,128)} %get-tuple-element.34, pred[256,256]{0,1:T(8,128)(4,1)} %copy-done.40), kind=kOutput, calls=%fused_computation.94 | convolution fusion | flops 103809024 | bytes 4403200 | tf_op jit(solution)/shard_map/hqk,hqe->hke/dot_general | solution.py:220
  91.4 2.3 %multiply_convert_fusion.2 = bf16[12,256,256]{1,2,0:T(8,128)(2,1)S(1)} fusion(f32[12,256,256]{2,1,0:T(8,128)S(1)} %copy-done.7, bf16[12,256,64]{1,2,0:T(8,128)(2,1)} %bitcast.251, bf16[12,256,64]{1,2,0:T(8,128)(2,1)S(1)} %copy-done.26, f32[12,256]{1,0:T(8,128)S(1)} %multiply_reduce_fusion, f32[12,256]{1,0:T(8,128)S(1)} %copy-done.46, ...), kind=kOutput, calls=%fused_computation.16 | convolution fusion | flops 105381888 | bytes 5595136 | tf_op jit(solution)/shard_map/hqe,hke->hqk/dot_general | solution.py:208
  93.8 1.1 multiply_convert_fusion
  95.6 2.4 %multiply_convert_fusion.3 = bf16[12,256,256]{1,2,0:T(8,128)(2,1)S(1)} fusion(f32[12,256,256]{2,1,0:T(8,128)S(1)} %copy-done.11, bf16[12,256,64]{1,2,0:T(8,128)(2,1)S(1)} %bitcast.253, f32[12,256]{1,0:T(8,128)S(1)} %multiply_reduce_fusion, f32[12,256]{1,0:T(8,128)S(1)} %copy-done.46, pred[256,256]{0,1:T(8,128)(4,1)S(1)} %copy-done.41, ...), kind=kOutput, calls=%fused_computation.17 | convolution fusion | flops 105381888 | bytes 5595136 | tf_op jit(solution)/shard_map/hqe,hke->hqk/dot_general | solution.py:208
  99.2 1.1 multiply_convert_fusion.4
  101.8 1.5 fusion.116
  104.0 1.1 multiply_convert_fusion.1
  106.8 1.4 fusion.38
  108.2 1.3 collective-permute-start.11
  110.8 1.6 fusion.79
  112.4 5.6 %collective-permute-start.10 = (bf16[2,12,256,64]{2,3,1,0:T(8,128)(2,1)}, bf16[2,12,256,64]{2,3,1,0:T(8,128)(2,1)}, u32[]{:S(2)}, u32[]{:S(2)}) collective-permute-start(bf16[2,12,256,64]{2,3,1,0:T(8,128)(2,1)} %fusion.38), channel_id=1, source_target_pairs={{4,0},{6,2},{12,8},{14,10},{20,16},{22,18},{28,24},{30,26},{5,1},{... | collective-permute-start | bytes 2359304 | tf_op jit(solution)/shard_map/ppermute | solution.py:95
  118.0 13.6 %collective-permute-done.11 = bf16[2,12,256,64]{2,3,1,0:T(8,128)(2,1)S(1)} collective-permute-done((bf16[2,12,256,64]{2,3,1,0:T(8,128)(2,1)}, bf16[2,12,256,64]{2,3,1,0:T(8,128)(2,1)S(1)}, u32[]{:S(2)}, u32[]{:S(2)}) %collective-permute-start.11) | collective-permute-done | bytes 786464 | tf_op jit(solution)/shard_map/ppermute | solution.py:96
  131.6 1.3 fusion.40
  132.9 1.3 collective-permute-start.12
  134.2 1.7 %fusion.9 = bf16[1,256,1536]{2,1,0:T(8,128)(2,1)} fusion(bf16[256,768]{0,1:T(8,128)(2,1)S(1)} %bitcast.240, bf16[768,1536]{1,0:T(8,128)(2,1)S(1)} %bitcast.229), kind=kOutput, calls=%fused_computation.30 | convolution fusion | flops 604372992 | bytes 3538944 | tf_op jit(solution)/shard_map/dot_general | solution.py:173
  135.9 1.2 fusion.111
  137.1 1.8 %convert_element_type.187 = f32[48,1536]{1,0:T(8,128)} convert(bf16[48,1536]{1,0:T(8,128)(2,1)} %reduce-scatter.3.cloned.1.call-done) | non-fusion elementwise | flops 73728 | bytes 442368 | tf_op jit(solution)/shard_map/convert_element_type | solution.py:184
  138.9 2.0 %fusion.96 = f32[1,12,256,64]{2,3,1,0:T(8,128)S(1)} fusion(bf16[12,256,256]{1,2,0:T(8,128)(2,1)} %copy-done.14, bf16[12,256,64]{1,2,0:T(8,128)(2,1)S(1)} %bitcast.227), kind=kOutput, calls=%fused_computation.109 | convolution fusion | flops 100859904 | bytes 2752512 | tf_op jit(solution)/shard_map/hqk,hqe->hke/dot_general | solution.py:217
  140.9 2.0 %copy.112 = bf16[1,256,768]{2,1,0:T(8,128)(2,1)} copy(bf16[1,256,768]{1,2,0:T(8,128)(2,1)} %bitcast.247) | data formatting | bytes 786432
  142.9 11.3 %collective-permute-done.12 = bf16[2,12,256,64]{2,3,1,0:T(8,128)(2,1)} collective-permute-done((bf16[2,12,256,64]{2,3,1,0:T(8,128)(2,1)}, bf16[2,12,256,64]{2,3,1,0:T(8,128)(2,1)}, u32[]{:S(2)}, u32[]{:S(2)}) %collective-permute-start.12) | collective-permute-done | bytes 786464 | tf_op jit(solution)/shard_map/ppermute | solution.py:18
  154.2 2.1 %fusion.37 = bf16[2,12,256,64]{2,3,1,0:T(8,128)(2,1)S(1)} fusion(f32[1,12,256,64]{2,3,1,0:T(8,128)} %fusion.79, f32[1,12,256,64]{2,3,1,0:T(8,128)S(1)} %fusion.96, bf16[2,12,256,64]{2,3,1,0:T(8,128)(2,1)} %collective-permute-done.12, bf16[2,12,256,64]{2,3,1,0:T(8,128)(2,1)} %collective-permute-done.10, f32[2,12,256,64]{2,3,1,0:T(8,128)S(1)} %copy-done.13, ...), kind=kLoop, calls=%fused_computation.54 | loop fusion | flops 3538944 | bytes 5505026 | tf_op jit(solution)/shard_map/convert.1
  156.3 0.9 copy.113
  (150 shorter events, 20.2 us)
Async XLA Ops:
  8.0 60.3 %copy-start = (bf16[1,256,1536]{2,1,0:T(8,128)(2,1)S(1)}, bf16[1,256,1536]{2,1,0:T(8,128)(2,1)}, u32[]{:S(2)}) copy-start(bf16[1,256,1536]{2,1,0:T(8,128)(2,1)} %param.9) | copy-start | bytes 2359300
  8.0 70.7 %all-gather.3.cloned.1.call-start = ((), (), s32[]{:S(2)}) async-start(), calls=%async_computation.4 | async-start | bytes 2433024 | tf_op jit(solution)/shard_map/all_gather | solution.py:119
  9.3 38.6 %copy-start.17 = (bf16[1,256,768]{1,2,0:T(8,128)(2,1)}, bf16[1,256,768]{1,2,0:T(8,128)(2,1)S(1)}, u32[]{:S(2)}) copy-start(bf16[1,256,768]{1,2,0:T(8,128)(2,1)S(1)} %copy.81) | copy-start | bytes 1179652
  9.3 13.1 %collective-permute-start.1 = (bf16[12,256,64]{1,2,0:T(8,128)(2,1)S(1)}, bf16[12,256,64]{1,2,0:T(8,128)(2,1)S(1)}, u32[]{:S(2)}, u32[]{:S(2)}) collective-permute-start(bf16[12,256,64]{1,2,0:T(8,128)(2,1)S(1)} %bitcast.232), channel_id=1, source_target_pairs={{0,8},{2,10},{4,12},{6,14},{8,16},{10,18},{12,20},{14,22},{16,24},... | collective-permute-start | bytes 1179656 | tf_op jit(solution)/shard_map/ppermute | solution.py:18
  12.8 19.8 %collective-permute-start = (bf16[12,256,64]{1,2,0:T(8,128)(2,1)S(1)}, bf16[12,256,64]{1,2,0:T(8,128)(2,1)S(1)}, u32[]{:S(2)}, u32[]{:S(2)}) collective-permute-start(bf16[12,256,64]{1,2,0:T(8,128)(2,1)S(1)} %bitcast.233), channel_id=1, source_target_pairs={{0,4},{2,6},{8,12},{10,14},{16,20},{18,22},{24,28},{26,30},{1,5},{... | collective-permute-start | bytes 1179656 | tf_op jit(solution)/shard_map/ppermute | solution.py:57
  15.3 45.9 %copy-start.23 = (bf16[1,256,768]{1,2,0:T(8,128)(2,1)}, bf16[1,256,768]{1,2,0:T(8,128)(2,1)S(1)}, u32[]{:S(2)}) copy-start(bf16[1,256,768]{1,2,0:T(8,128)(2,1)S(1)} %copy.83) | copy-start | bytes 1179652
  15.3 14.3 %collective-permute-start.4 = (bf16[12,256,64]{1,2,0:T(8,128)(2,1)S(1)}, bf16[12,256,64]{1,2,0:T(8,128)(2,1)S(1)}, u32[]{:S(2)}, u32[]{:S(2)}) collective-permute-start(bf16[12,256,64]{1,2,0:T(8,128)(2,1)S(1)} %bitcast.241), channel_id=1, source_target_pairs={{0,8},{2,10},{4,12},{6,14},{8,16},{10,18},{12,20},{14,22},{16,24},... | collective-permute-start | bytes 1179656 | tf_op jit(solution)/shard_map/ppermute | solution.py:18
  18.8 20.1 %collective-permute-start.3 = (bf16[12,256,64]{1,2,0:T(8,128)(2,1)S(1)}, bf16[12,256,64]{1,2,0:T(8,128)(2,1)}, u32[]{:S(2)}, u32[]{:S(2)}) collective-permute-start(bf16[12,256,64]{1,2,0:T(8,128)(2,1)S(1)} %bitcast.242), channel_id=1, source_target_pairs={{0,4},{2,6},{8,12},{10,14},{16,20},{18,22},{24,28},{26,30},{1,5},{... | collective-permute-start | bytes 1179656 | tf_op jit(solution)/shard_map/ppermute | solution.py:57
  20.1 117.0 %reduce-scatter.3.cloned.1.call-start = ((), (), s32[]{:S(2)}) async-start(), calls=%async_computation.2 | async-start | bytes 2506752 | tf_op jit(solution)/shard_map/reduce_scatter | solution.py:180
  22.5 28.3 %copy-start.19 = (bf16[12,256,64]{1,2,0:T(8,128)(2,1)}, bf16[12,256,64]{1,2,0:T(8,128)(2,1)S(1)}, u32[]{:S(2)}) copy-start(bf16[12,256,64]{1,2,0:T(8,128)(2,1)S(1)} %collective-permute-done.1) | copy-start | bytes 1179652
  22.5 15.4 %collective-permute-start.2 = (bf16[12,256,64]{1,2,0:T(8,128)(2,1)S(1)}, bf16[12,256,64]{1,2,0:T(8,128)(2,1)S(1)}, u32[]{:S(2)}, u32[]{:S(2)}) collective-permute-start(bf16[12,256,64]{1,2,0:T(8,128)(2,1)S(1)} %collective-permute-done.1), channel_id=1, source_target_pairs={{4,0},{6,2},{12,8},{14,10},{20,16},{22,18},{28,24},{30,26},{5,1},{... | collective-permute-start | bytes 1179656 | tf_op jit(solution)/shard_map/ppermute | solution.py:58
  29.6 9.4 %copy-start.42 = (bf16[12,256,64]{1,2,0:T(8,128)(2,1)}, bf16[12,256,64]{1,2,0:T(8,128)(2,1)S(1)}, u32[]{:S(2)}) copy-start(bf16[12,256,64]{1,2,0:T(8,128)(2,1)S(1)} %collective-permute-done.4) | copy-start | bytes 1179652
  29.6 14.7 %collective-permute-start.5 = (bf16[12,256,64]{1,2,0:T(8,128)(2,1)S(1)}, bf16[12,256,64]{1,2,0:T(8,128)(2,1)S(1)}, u32[]{:S(2)}, u32[]{:S(2)}) collective-permute-start(bf16[12,256,64]{1,2,0:T(8,128)(2,1)S(1)} %collective-permute-done.4), channel_id=1, source_target_pairs={{4,0},{6,2},{12,8},{14,10},{20,16},{22,18},{28,24},{30,26},{5,1},{... | collective-permute-start | bytes 1179656 | tf_op jit(solution)/shard_map/ppermute | solution.py:58
  32.6 28.6 %copy-start.32 = (pred[256,256]{0,1:T(8,128)(4,1)}, pred[256,256]{0,1:T(8,128)(4,1)S(1)}, u32[]{:S(2)}) copy-start(pred[256,256]{0,1:T(8,128)(4,1)S(1)} %get-tuple-element.44) | copy-start | bytes 196612
  32.6 29.5 %copy-start.34 = (pred[256,256]{0,1:T(8,128)(4,1)}, pred[256,256]{0,1:T(8,128)(4,1)S(1)}, u32[]{:S(2)}) copy-start(pred[256,256]{0,1:T(8,128)(4,1)S(1)} %get-tuple-element.43) | copy-start | bytes 196612
  32.6 30.4 %copy-start.38 = (pred[256,256]{0,1:T(8,128)(4,1)}, pred[256,256]{0,1:T(8,128)(4,1)S(1)}, u32[]{:S(2)}) copy-start(pred[256,256]{0,1:T(8,128)(4,1)S(1)} %get-tuple-element.42) | copy-start | bytes 196612
  32.6 31.3 %copy-start.40 = (pred[256,256]{0,1:T(8,128)(4,1)}, pred[256,256]{0,1:T(8,128)(4,1)S(1)}, u32[]{:S(2)}) copy-start(pred[256,256]{0,1:T(8,128)(4,1)S(1)} %get-tuple-element.40) | copy-start | bytes 196612
  32.6 33.1 %copy-start.36 = (pred[256,256]{0,1:T(8,128)(4,1)}, pred[256,256]{0,1:T(8,128)(4,1)S(1)}, u32[]{:S(2)}) copy-start(pred[256,256]{0,1:T(8,128)(4,1)S(1)} %get-tuple-element.41) | copy-start | bytes 196612
  38.9 12.5 %copy-start.15 = (bf16[12,256,64]{1,2,0:T(8,128)(2,1)}, bf16[12,256,64]{1,2,0:T(8,128)(2,1)S(1)}, u32[]{:S(2)}) copy-start(bf16[12,256,64]{1,2,0:T(8,128)(2,1)S(1)} %broadcast_select_fusion.1) | copy-start | bytes 1179652
  45.3 20.5 %copy-start.25 = (bf16[12,256,64]{1,2,0:T(8,128)(2,1)}, bf16[12,256,64]{1,2,0:T(8,128)(2,1)S(1)}, u32[]{:S(2)}) copy-start(bf16[12,256,64]{1,2,0:T(8,128)(2,1)S(1)} %broadcast_select_fusion) | copy-start | bytes 1179652
  47.9 4.3 %collective-permute-start.6 = (bf16[2,12,256,64]{2,3,1,0:T(8,128)(2,1)}, bf16[2,12,256,64]{2,3,1,0:T(8,128)(2,1)}, u32[]{:S(2)}, u32[]{:S(2)}) collective-permute-start(bf16[2,12,256,64]{2,3,1,0:T(8,128)(2,1)} %get-tuple-element.38), channel_id=1, source_target_pairs={{0,2},{2,0},{4,6},{6,4},{8,10},{10,8},{12,14},{14,12},{16,18},{18,... | collective-permute-start | bytes 2359304 | tf_op jit(solution)/shard_map/ppermute | solution.py:23
  50.2 4.1 %collective-permute-start.7 = (bf16[2,12,256,64]{2,3,1,0:T(8,128)(2,1)}, bf16[2,12,256,64]{2,3,1,0:T(8,128)(2,1)S(1)}, u32[]{:S(2)}, u32[]{:S(2)}) collective-permute-start(bf16[2,12,256,64]{2,3,1,0:T(8,128)(2,1)} %get-tuple-element.39), channel_id=1, source_target_pairs={{0,2},{2,0},{4,6},{6,4},{8,10},{10,8},{12,14},{14,12},{16,18},{18,... | collective-permute-start | bytes 2359304 | tf_op jit(solution)/shard_map/ppermute | solution.py:23
  51.4 10.7 %copy-start.4 = (f32[12,256,256]{1,2,0:T(8,128)}, f32[12,256,256]{1,2,0:T(8,128)S(1)}, u32[]{:S(2)}) copy-start(f32[12,256,256]{1,2,0:T(8,128)S(1)} %get-tuple-element.46) | copy-start | bytes 9437188
  52.1 13.7 %copy-start.6 = (f32[12,256,256]{2,1,0:T(8,128)}, f32[12,256,256]{2,1,0:T(8,128)S(1)}, u32[]{:S(2)}) copy-start(f32[12,256,256]{2,1,0:T(8,128)S(1)} %get-tuple-element.50) | copy-start | bytes 9437188
  52.1 4.5 %copy-start.2 = (f32[12,256,256]{1,2,0:T(8,128)S(1)}, f32[12,256,256]{1,2,0:T(8,128)}, u32[]{:S(2)}) copy-start(f32[12,256,256]{1,2,0:T(8,128)} %get-tuple-element.52) | copy-start | bytes 9437188
  54.3 9.6 %copy-start.10 = (f32[12,256,256]{2,1,0:T(8,128)}, f32[12,256,256]{2,1,0:T(8,128)S(1)}, u32[]{:S(2)}) copy-start(f32[12,256,256]{2,1,0:T(8,128)S(1)} %get-tuple-element.54) | copy-start | bytes 9437188
  54.3 8.7 %copy-start.30 = (bf16[2,12,256,64]{2,3,1,0:T(8,128)(2,1)}, bf16[2,12,256,64]{2,3,1,0:T(8,128)(2,1)S(1)}, u32[]{:S(2)}) copy-start(bf16[2,12,256,64]{2,3,1,0:T(8,128)(2,1)S(1)} %collective-permute-done.7) | copy-start | bytes 2359300
  55.0 8.0 %copy-start.8 = (f32[12,256,256]{2,1,0:T(8,128)}, f32[12,256,256]{2,1,0:T(8,128)S(1)}, u32[]{:S(2)}) copy-start(f32[12,256,256]{2,1,0:T(8,128)S(1)} %get-tuple-element.48) | copy-start | bytes 9437188
  70.5 87.7 %reduce-scatter.5.cloned.1.call-start = ((), (), s32[]{:S(2)}) async-start(), calls=%async_computation.3 | async-start | bytes 442368 | tf_op jit(solution)/shard_map/reduce_scatter | solution.py:183
  86.0 4.0 %copy-start.27 = (bf16[256,768]{0,1:T(8,128)(2,1)}, bf16[256,768]{0,1:T(8,128)(2,1)S(1)}, u32[]{:S(2)}) copy-start(bf16[256,768]{0,1:T(8,128)(2,1)S(1)} %copy.91) | copy-start | bytes 1179652
  86.0 3.2 %copy-start.9 = (f32[12,256,256]{2,1,0:T(8,128)S(1)}, f32[12,256,256]{2,1,0:T(8,128)}, u32[]{:S(2)}) copy-start(f32[12,256,256]{2,1,0:T(8,128)} %copy-done.8) | copy-start | bytes 9437188
  86.0 3.2 %copy-start.39 = (pred[256,256]{0,1:T(8,128)(4,1)S(1)}, pred[256,256]{0,1:T(8,128)(4,1)}, u32[]{:S(2)}) copy-start(pred[256,256]{0,1:T(8,128)(4,1)} %copy-done.38) | copy-start | bytes 196612
  86.0 3.2 %copy-start.46 = (f32[12,256]{1,0:T(8,128)S(1)}, f32[12,256]{1,0:T(8,128)}, u32[]{:S(2)}) copy-start(f32[12,256]{1,0:T(8,128)} %get-tuple-element.34) | copy-start | bytes 36868
  91.4 2.3 %copy-start.3 = (f32[12,256,256]{1,2,0:T(8,128)S(1)}, f32[12,256,256]{1,2,0:T(8,128)}, u32[]{:S(2)}) copy-start(f32[12,256,256]{1,2,0:T(8,128)} %get-tuple-element.52) | copy-start | bytes 9437188
  91.4 2.3 %copy-start.24 = (bf16[1,256,768]{1,2,0:T(8,128)(2,1)S(1)}, bf16[1,256,768]{1,2,0:T(8,128)(2,1)}, u32[]{:S(2)}) copy-start(bf16[1,256,768]{1,2,0:T(8,128)(2,1)} %copy-done.23) | copy-start | bytes 1179652
  91.4 2.3 %copy-start.28 = (bf16[256,768]{0,1:T(8,128)(2,1)S(1)}, bf16[256,768]{0,1:T(8,128)(2,1)}, u32[]{:S(2)}) copy-start(bf16[256,768]{0,1:T(8,128)(2,1)} %copy-done.27) | copy-start | bytes 1179652
  91.4 2.3 %copy-start.33 = (pred[256,256]{0,1:T(8,128)(4,1)S(1)}, pred[256,256]{0,1:T(8,128)(4,1)}, u32[]{:S(2)}) copy-start(pred[256,256]{0,1:T(8,128)(4,1)} %copy-done.32) | copy-start | bytes 196612
  95.6 5.7 %copy-start.14 = (bf16[12,256,256]{1,2,0:T(8,128)(2,1)}, bf16[12,256,256]{1,2,0:T(8,128)(2,1)S(1)}, u32[]{:S(2)}) copy-start(bf16[12,256,256]{1,2,0:T(8,128)(2,1)S(1)} %multiply_convert_fusion) | copy-start | bytes 4718596
  98.8 8.1 %collective-permute-start.8 = (f32[2,12,256,64]{2,3,1,0:T(8,128)S(1)}, f32[2,12,256,64]{2,3,1,0:T(8,128)S(1)}, u32[]{:S(2)}, u32[]{:S(2)}) collective-permute-start(f32[2,12,256,64]{2,3,1,0:T(8,128)S(1)} %pad_maximum_fusion), channel_id=1, source_target_pairs={{0,2},{2,0},{4,6},{6,4},{8,10},{10,8},{12,14},{14,12},{16,18},{18,... | collective-permute-start | bytes 4718600 | tf_op jit(solution)/shard_map/ppermute | solution.py:23
  101.1 5.8 %collective-permute-start.9 = (f32[2,12,256,64]{2,3,1,0:T(8,128)S(1)}, f32[2,12,256,64]{2,3,1,0:T(8,128)S(1)}, u32[]{:S(2)}, u32[]{:S(2)}) collective-permute-start(f32[2,12,256,64]{2,3,1,0:T(8,128)S(1)} %pad_maximum_fusion.1), channel_id=1, source_target_pairs={{0,2},{2,0},{4,6},{6,4},{8,10},{10,8},{12,14},{14,12},{16,18},{18,... | collective-permute-start | bytes 4718600 | tf_op jit(solution)/shard_map/ppermute | solution.py:23
  106.8 3.3 %copy-start.12 = (f32[2,12,256,64]{2,3,1,0:T(8,128)}, f32[2,12,256,64]{2,3,1,0:T(8,128)S(1)}, u32[]{:S(2)}) copy-start(f32[2,12,256,64]{2,3,1,0:T(8,128)S(1)} %collective-permute-done.8) | copy-start | bytes 4718596
  108.2 23.4 %collective-permute-start.11 = (bf16[2,12,256,64]{2,3,1,0:T(8,128)(2,1)}, bf16[2,12,256,64]{2,3,1,0:T(8,128)(2,1)S(1)}, u32[]{:S(2)}, u32[]{:S(2)}) collective-permute-start(bf16[2,12,256,64]{2,3,1,0:T(8,128)(2,1)} %fusion.38), channel_id=1, source_target_pairs={{0,4},{2,6},{8,12},{10,14},{16,20},{18,22},{24,28},{26,30},{1,5},{... | collective-permute-start | bytes 2359304 | tf_op jit(solution)/shard_map/ppermute | solution.py:96
  112.4 21.8 %copy-start.22 = (bf16[256,12,64]{0,2,1:T(8,128)(2,1)S(1)}, bf16[256,12,64]{0,2,1:T(8,128)(2,1)}, u32[]{:S(2)}) copy-start(bf16[256,12,64]{0,2,1:T(8,128)(2,1)} %copy-done.21) | copy-start | bytes 1179652
  112.4 23.5 %copy-start.16 = (bf16[12,256,64]{1,2,0:T(8,128)(2,1)S(1)}, bf16[12,256,64]{1,2,0:T(8,128)(2,1)}, u32[]{:S(2)}) copy-start(bf16[12,256,64]{1,2,0:T(8,128)(2,1)} %copy-done.15) | copy-start | bytes 1179652
  112.4 30.5 %collective-permute-start.10 = (bf16[2,12,256,64]{2,3,1,0:T(8,128)(2,1)}, bf16[2,12,256,64]{2,3,1,0:T(8,128)(2,1)}, u32[]{:S(2)}, u32[]{:S(2)}) collective-permute-start(bf16[2,12,256,64]{2,3,1,0:T(8,128)(2,1)} %fusion.38), channel_id=1, source_target_pairs={{4,0},{6,2},{12,8},{14,10},{20,16},{22,18},{28,24},{30,26},{5,1},{... | collective-permute-start | bytes 2359304 | tf_op jit(solution)/shard_map/ppermute | solution.py:95
  132.9 21.2 %collective-permute-start.12 = (bf16[2,12,256,64]{2,3,1,0:T(8,128)(2,1)}, bf16[2,12,256,64]{2,3,1,0:T(8,128)(2,1)}, u32[]{:S(2)}, u32[]{:S(2)}) collective-permute-start(bf16[2,12,256,64]{2,3,1,0:T(8,128)(2,1)} %fusion.40), channel_id=1, source_target_pairs={{8,0},{10,2},{12,4},{14,6},{16,8},{18,10},{20,12},{22,14},{24,16},... | collective-permute-start | bytes 2359304 | tf_op jit(solution)/shard_map/ppermute | solution.py:18
  137.1 17.1 %copy-start.13 = (f32[2,12,256,64]{2,3,1,0:T(8,128)S(1)}, f32[2,12,256,64]{2,3,1,0:T(8,128)}, u32[]{:S(2)}) copy-start(f32[2,12,256,64]{2,3,1,0:T(8,128)} %copy-done.12) | copy-start | bytes 4718596
  140.9 17.3 %copy-start.1 = (bf16[1,256,1536]{2,1,0:T(8,128)(2,1)S(1)}, bf16[1,256,1536]{2,1,0:T(8,128)(2,1)}, u32[]{:S(2)}) copy-start(bf16[1,256,1536]{2,1,0:T(8,128)(2,1)} %param.9) | copy-start | bytes 2359300
  (15 other events, 24.4 us)
Sparse Core Ops, SparseCore 0:
  20.2 58.4 all-gather.2
Sparse Core Ops, SparseCore 1:
  70.6 62.1 reduce-scatter.2
  139.0 12.5 reduce-scatter.4

commit v14 on v13

--- a/solution.py
+++ b/solution.py
@@ -86,17 +86,6 @@
         from_core0 = received[dist // 2 - 1] if dist >= 2 and dist // 2 - 1 < len(odds) else zero
         own = parts[dist] if dist <= reach else zero
         summed[dist] = own + jnp.where(core == 0, from_core1, from_core0)
-    count = lax.axis_size("seq")
-    if reach == 4 and count % 4 == 0:
-        row = (lax.axis_index("seq") // 2) % 2
-        later = [i for i in range(count) if (i // 2) % 2 == 1]
-        earlier = [i for i in range(count) if (i // 2) % 2 == 0 and i + 2 < count]
-        near = summed[2].astype(jnp.bfloat16)
-        direct = lax.ppermute(near, "seq", [(i, i - 2) for i in later])
-        relayed = lax.ppermute(near, "seq", [(i, i + 2) for i in earlier])
-        far = summed[4] + jnp.where(row == 1, relayed.astype(jnp.float32), 0.0)
-        total = summed[0] + jnp.where(row == 0, direct.astype(jnp.float32), 0.0)
-        return total + shift_up(far.astype(jnp.bfloat16), "seq", -4).astype(jnp.float32)
     total = summed[0]
     for dist in range(2, reach + 2, 2):
         total = total + shift_up(summed[dist].astype(jnp.bfloat16), "seq", -dist).astype(jnp.float32)

time: 167 us -> 168 us (level)
  the two profiles are of different devices: /device:TPU:4 before, /device:TPU:0 now
where the time goes in v14:
time: 168 us; the launch traced here: 167 us
  waiting for transfers between devices  64.8 us (39%)
  matrix products  31.9 us (19%)
  starting transfers between devices  20.1 us (12%)
  local copies, waits for them, and re-layouts  18.5 us (11%)
  between operations  16.3 us (10%)
  other arithmetic  15.6 us (9%)
    ppermute x4, waiting for transfers between devices, shift_up(): return lax.ppermute(block, axis, route)  22.3 us
    ppermute x2, waiting for transfers between devices, gather_behind(): relayed = lax.ppermute(far[k], 'seq', [(i + 2, i) for i in earlier])  15.8 us
    reduce_scatter x1, waiting for transfers between devices, local(): lax.psum_scatter(partial_weight.astype(jnp.bfloat16), 'seq', scatter_dime...  13.5 us
    unnamed x101, local copies, waits for them, and re-layouts  13.3 us
    all_gather x1, waiting for transfers between devices, local(): pieces = lax.all_gather(out_weight, ('seq', 'dp'), axis=0, tiled=False)  13.1 us
    ppermute x4, starting transfers between devices, shift_up(): return lax.ppermute(block, axis, route)  11.1 us
    dot_general x5, matrix products, local(): jnp.einsum('hqk,hqe->hke', prob_back, grad_heads, preferred_element_type=...  6.47 us
    dot_general x5, matrix products, local(): jnp.einsum('hqe,hke->hqk', grad_heads, value_block, preferred_element_typ...  5.4 us
  transfers between devices with their start and end apart: 15, of which 7 were waited for; matrix products, arithmetic and copies ran while one was open for 35% of the time, Pallas kernels for 0%

profile of v14, /device:TPU:0, one launch (start us, length us, event | category | flops | bytes accessed | tf_op | source)
XLA Modules:
  0.0 167.2 jit_solution(13890311045485938838)
XLA Ops:
  8.1 1.2 copy.81
  9.3 5.0 %collective-permute-start.1 = (bf16[12,256,64]{1,2,0:T(8,128)(2,1)S(1)}, bf16[12,256,64]{1,2,0:T(8,128)(2,1)S(1)}, u32[]{:S(2)}, u32[]{:S(2)}) collective-permute-start(bf16[12,256,64]{1,2,0:T(8,128)(2,1)S(1)} %bitcast.232), channel_id=1, source_target_pairs={{0,8},{2,10},{4,12},{6,14},{8,16},{10,18},{12,20},{14,22},{16,24},... | collective-permute-start | bytes 1179656 | tf_op jit(solution)/shard_map/ppermute | solution.py:18
  14.3 3.4 %collective-permute-start = (bf16[12,256,64]{1,2,0:T(8,128)(2,1)S(1)}, bf16[12,256,64]{1,2,0:T(8,128)(2,1)S(1)}, u32[]{:S(2)}, u32[]{:S(2)}) collective-permute-start(bf16[12,256,64]{1,2,0:T(8,128)(2,1)S(1)} %bitcast.233), channel_id=1, source_target_pairs={{0,4},{2,6},{8,12},{10,14},{16,20},{18,22},{24,28},{26,30},{1,5},{... | collective-permute-start | bytes 1179656 | tf_op jit(solution)/shard_map/ppermute | solution.py:57
  17.7 1.2 copy.83
  18.9 3.5 %collective-permute-start.4 = (bf16[12,256,64]{1,2,0:T(8,128)(2,1)S(1)}, bf16[12,256,64]{1,2,0:T(8,128)(2,1)S(1)}, u32[]{:S(2)}, u32[]{:S(2)}) collective-permute-start(bf16[12,256,64]{1,2,0:T(8,128)(2,1)S(1)} %bitcast.241), channel_id=1, source_target_pairs={{0,8},{2,10},{4,12},{6,14},{8,16},{10,18},{12,20},{14,22},{16,24},... | collective-permute-start | bytes 1179656 | tf_op jit(solution)/shard_map/ppermute | solution.py:18
  22.4 1.3 collective-permute-start.3
  23.9 0.8 reduce-window.8
  25.4 1.2 copy.80
  28.0 1.3 collective-permute-start.2
  30.0 1.0 collective-permute-done.4
  31.0 1.3 collective-permute-start.5
  32.9 9.4 %collective-permute-done.2 = bf16[12,256,64]{1,2,0:T(8,128)(2,1)S(1)} collective-permute-done((bf16[12,256,64]{1,2,0:T(8,128)(2,1)S(1)}, bf16[12,256,64]{1,2,0:T(8,128)(2,1)S(1)}, u32[]{:S(2)}, u32[]{:S(2)}) %collective-permute-start.2) | collective-permute-done | bytes 393248 | tf_op jit(solution)/shard_map/ppermute | solution.py:58
  42.4 6.4 %collective-permute-done.5 = bf16[12,256,64]{1,2,0:T(8,128)(2,1)S(1)} collective-permute-done((bf16[12,256,64]{1,2,0:T(8,128)(2,1)S(1)}, bf16[12,256,64]{1,2,0:T(8,128)(2,1)S(1)}, u32[]{:S(2)}, u32[]{:S(2)}) %collective-permute-start.5) | collective-permute-done | bytes 393248 | tf_op jit(solution)/shard_map/ppermute | solution.py:58
  53.3 3.9 %fusion.17 = (f32[12,256]{1,0:T(8,128)S(1)}, f32[12,256]{1,0:T(8,128)S(1)}, f32[12,256]{1,0:T(8,128)S(1)}, f32[12,256]{1,0:T(8,128)S(1)}, f32[12,256]{1,0:T(8,128)S(1)}) fusion(f32[12,256,256]{2,1,0:T(8,128)S(1)} %get-tuple-element.56, f32[12,256]{1,0:T(8,128)S(1)} %maximum_maximum_fusion, pred[256,256]{0,1:T(8,128)(4,1)S(1)} %get-tuple-element.42, ...), kind=kLoop, calls=%fused_computation.38 | loop fusion | flops 19645440 | bytes 16130048 | tf_op jit(solution)/shard_map/reduce_sum | solution.py:144
  57.9 0.9 fusion.63
  58.8 0.9 fusion.55
  59.7 0.9 fusion.57
  60.6 0.9 fusion.98
  61.5 1.8 %fusion.114 = (bf16[256,12,64]{0,2,1:T(8,128)(2,1)S(1)}, f32[12,256,64]{1,2,0:T(8,128)}) fusion(f32[256,12]{0,1:T(8,128)S(1)} %bitcast.262, f32[12,256,64]{1,2,0:T(8,128)S(1)} %fusion.55, f32[12,256,64]{1,2,0:T(8,128)S(1)} %fusion.57, f32[12,256,64]{1,2,0:T(8,128)S(1)} %fusion.98, bf16[12,256,64]{1,2,0:T(8,128)(2,1)S(1)} %broadcast_select_fusion, ...), kind=kOutput, calls=%fused_computation.124 | convolution fusion | flops 105578496 | bytes 7168000 | tf_op jit(solution)/shard_map/hqk,hke->hqe/dot_general | solution.py:145
  63.2 0.7 copy-done.21
  64.0 2.2 %fusion.112 = bf16[768,1536]{1,0:T(8,128)(2,1)} fusion(bf16[256,768]{0,1:T(8,128)(2,1)S(1)} %bitcast.239, bf16[1,256,1536]{2,1,0:T(8,128)(2,1)S(1)} %copy-done), kind=kOutput, calls=%fused_computation.121 | convolution fusion | flops 603979776 | bytes 3538944 | tf_op jit(solution)/shard_map/dot_general | solution.py:158
  66.4 13.1 %all-gather.3.cloned.1.call-done = bf16[1536,768]{1,0:T(8,128)(2,1)} async-done(((bf16[48,768]{1,0:T(8,128)(2,1)}), bf16[1536,768]{1,0:T(8,128)(2,1)}) %all-gather.3.cloned.1.call-update) | async-done | bytes 2359312 | tf_op jit(solution)/shard_map/all_gather | solution.py:108
  79.5 4.0 %copy.90 = bf16[16,2,48,768]{3,1,2,0:T(2,128)(2,1)S(1)} copy(bf16[16,2,48,768]{3,2,1,0:T(8,128)(2,1)} %bitcast.238) | data formatting | bytes 4718592 | tf_op jit(solution)/shard_map/reshape | solution.py:110
  84.0 1.6 convolution_convert_fusion.1
  85.5 1.2 copy.91
  86.8 2.8 %fusion.81 = f32[1,12,256,64]{2,3,1,0:T(8,128)S(1)} fusion(bf16[12,256,64]{1,2,0:T(8,128)(2,1)S(1)} %bitcast.248, f32[12,256,256]{2,1,0:T(8,128)} %copy-done.10, f32[12,256]{1,0:T(8,128)} %get-tuple-element.34, pred[256,256]{0,1:T(8,128)(4,1)} %copy-done.42), kind=kOutput, calls=%fused_computation.93 | convolution fusion | flops 103809024 | bytes 4403200 | tf_op jit(solution)/shard_map/hqk,hqe->hke/dot_general | solution.py:209
  91.0 0.9 copy-done.7
  91.9 1.1 multiply_convert_fusion.2
  93.1 1.0 copy-done.11
  94.3 1.1 multiply_convert_fusion.3
  96.6 1.1 multiply_convert_fusion.4
  99.4 0.8 copy-done.5
  100.3 1.1 multiply_convert_fusion.1
  102.3 1.1 multiply_convert_fusion
  105.7 0.7 fusion.84
  107.1 1.6 fusion.78
  108.7 1.9 %fusion.38 = (bf16[2,12,256,64]{2,3,1,0:T(8,128)(2,1)}, bf16[2,12,256,64]{2,3,1,0:T(8,128)(2,1)}) fusion(f32[1,12,256,64]{2,3,1,0:T(8,128)S(1)} %fusion.84, f32[1,12,256,64]{2,3,1,0:T(8,128)S(1)} %fusion.93, f32[2,12,256,64]{2,3,1,0:T(8,128)S(1)} %collective-permute-done.9, f32[2,12,256,64]{2,3,1,0:T(8,128)S(1)} %collective-permute-done.8, pred[]{:T(512)S(6)} %eq.96, ...), kind=kLoop, calls=%fused_computation.57 | loop fusion | flops 3145728 | bytes 7864321 | tf_op jit(solution)/shard_map/convert_element_type | solution.py:91
  110.6 1.4 collective-permute-start.10
  112.0 1.3 collective-permute-start.11
  113.3 1.7 %fusion.9 = bf16[1,256,1536]{2,1,0:T(8,128)(2,1)} fusion(bf16[256,768]{0,1:T(8,128)(2,1)S(1)} %bitcast.240, bf16[768,1536]{1,0:T(8,128)(2,1)S(1)} %bitcast.229), kind=kOutput, calls=%fused_computation.30 | convolution fusion | flops 604372992 | bytes 3538944 | tf_op jit(solution)/shard_map/dot_general | solution.py:162
  115.0 1.2 fusion.110
  116.2 13.5 %reduce-scatter.3.cloned.1.call-done = bf16[48,1536]{1,0:T(8,128)(2,1)} async-done(((bf16[768,1536]{1,0:T(8,128)(2,1)}), bf16[48,1536]{1,0:T(8,128)(2,1)}) %reduce-scatter.3.cloned.1.call-update) | async-done | bytes 147472 | tf_op jit(solution)/shard_map/reduce_scatter | solution.py:169
  129.6 1.6 convert_element_type.183
  131.9 2.0 %copy.112 = bf16[1,256,768]{2,1,0:T(8,128)(2,1)} copy(bf16[1,256,768]{1,2,0:T(8,128)(2,1)} %bitcast.247) | data formatting | bytes 786432
  134.2 21.0 %collective-permute-done.11 = bf16[2,12,256,64]{2,3,1,0:T(8,128)(2,1)} collective-permute-done((bf16[2,12,256,64]{2,3,1,0:T(8,128)(2,1)}, bf16[2,12,256,64]{2,3,1,0:T(8,128)(2,1)}, u32[]{:S(2)}, u32[]{:S(2)}) %collective-permute-start.11) | collective-permute-done | bytes 786464 | tf_op jit(solution)/shard_map/ppermute | solution.py:18
  155.2 2.6 %fusion.37 = bf16[2,12,256,64]{2,3,1,0:T(8,128)(2,1)S(1)} fusion(f32[1,12,256,64]{2,3,1,0:T(8,128)} %fusion.78, f32[1,12,256,64]{2,3,1,0:T(8,128)S(1)} %fusion.95, bf16[2,12,256,64]{2,3,1,0:T(8,128)(2,1)} %collective-permute-done.11, bf16[2,12,256,64]{2,3,1,0:T(8,128)(2,1)} %collective-permute-done.10, f32[2,12,256,64]{2,3,1,0:T(8,128)} %copy-done.16, ...), kind=kLoop, calls=%fused_computation.54 | loop fusion | flops 3145728 | bytes 5505025 | tf_op jit(solution)/shard_map/convert.1
  157.9 0.9 copy.113
  158.8 0.9 copy.114
  (147 shorter events, 18.8 us)
Async XLA Ops:
  8.0 56.0 %copy-start = (bf16[1,256,1536]{2,1,0:T(8,128)(2,1)S(1)}, bf16[1,256,1536]{2,1,0:T(8,128)(2,1)}, u32[]{:S(2)}) copy-start(bf16[1,256,1536]{2,1,0:T(8,128)(2,1)} %param.9) | copy-start | bytes 2359300
  8.0 71.5 %all-gather.3.cloned.1.call-start = ((), (), s32[]{:S(2)}) async-start(), calls=%async_computation.4 | async-start | bytes 2433024 | tf_op jit(solution)/shard_map/all_gather | solution.py:108
  9.3 39.9 %copy-start.17 = (bf16[1,256,768]{1,2,0:T(8,128)(2,1)}, bf16[1,256,768]{1,2,0:T(8,128)(2,1)S(1)}, u32[]{:S(2)}) copy-start(bf16[1,256,768]{1,2,0:T(8,128)(2,1)S(1)} %copy.81) | copy-start | bytes 1179652
  9.3 18.7 %collective-permute-start.1 = (bf16[12,256,64]{1,2,0:T(8,128)(2,1)S(1)}, bf16[12,256,64]{1,2,0:T(8,128)(2,1)S(1)}, u32[]{:S(2)}, u32[]{:S(2)}) collective-permute-start(bf16[12,256,64]{1,2,0:T(8,128)(2,1)S(1)} %bitcast.232), channel_id=1, source_target_pairs={{0,8},{2,10},{4,12},{6,14},{8,16},{10,18},{12,20},{14,22},{16,24},... | collective-permute-start | bytes 1179656 | tf_op jit(solution)/shard_map/ppermute | solution.py:18
  14.3 18.7 %collective-permute-start = (bf16[12,256,64]{1,2,0:T(8,128)(2,1)S(1)}, bf16[12,256,64]{1,2,0:T(8,128)(2,1)S(1)}, u32[]{:S(2)}, u32[]{:S(2)}) collective-permute-start(bf16[12,256,64]{1,2,0:T(8,128)(2,1)S(1)} %bitcast.233), channel_id=1, source_target_pairs={{0,4},{2,6},{8,12},{10,14},{16,20},{18,22},{24,28},{26,30},{1,5},{... | collective-permute-start | bytes 1179656 | tf_op jit(solution)/shard_map/ppermute | solution.py:57
  18.9 39.0 %copy-start.23 = (bf16[1,256,768]{1,2,0:T(8,128)(2,1)}, bf16[1,256,768]{1,2,0:T(8,128)(2,1)S(1)}, u32[]{:S(2)}) copy-start(bf16[1,256,768]{1,2,0:T(8,128)(2,1)S(1)} %copy.83) | copy-start | bytes 1179652
  18.9 12.1 %collective-permute-start.4 = (bf16[12,256,64]{1,2,0:T(8,128)(2,1)S(1)}, bf16[12,256,64]{1,2,0:T(8,128)(2,1)S(1)}, u32[]{:S(2)}, u32[]{:S(2)}) collective-permute-start(bf16[12,256,64]{1,2,0:T(8,128)(2,1)S(1)} %bitcast.241), channel_id=1, source_target_pairs={{0,8},{2,10},{4,12},{6,14},{8,16},{10,18},{12,20},{14,22},{16,24},... | collective-permute-start | bytes 1179656 | tf_op jit(solution)/shard_map/ppermute | solution.py:18
  22.4 20.0 %collective-permute-start.3 = (bf16[12,256,64]{1,2,0:T(8,128)(2,1)S(1)}, bf16[12,256,64]{1,2,0:T(8,128)(2,1)S(1)}, u32[]{:S(2)}, u32[]{:S(2)}) collective-permute-start(bf16[12,256,64]{1,2,0:T(8,128)(2,1)S(1)} %bitcast.242), channel_id=1, source_target_pairs={{0,4},{2,6},{8,12},{10,14},{16,20},{18,22},{24,28},{26,30},{1,5},{... | collective-permute-start | bytes 1179656 | tf_op jit(solution)/shard_map/ppermute | solution.py:57
  23.7 105.9 %reduce-scatter.3.cloned.1.call-start = ((), (), s32[]{:S(2)}) async-start(), calls=%async_computation.2 | async-start | bytes 2506752 | tf_op jit(solution)/shard_map/reduce_scatter | solution.py:169
  28.0 22.5 %copy-start.19 = (bf16[12,256,64]{1,2,0:T(8,128)(2,1)}, bf16[12,256,64]{1,2,0:T(8,128)(2,1)S(1)}, u32[]{:S(2)}) copy-start(bf16[12,256,64]{1,2,0:T(8,128)(2,1)S(1)} %collective-permute-done.1) | copy-start | bytes 1179652
  28.0 14.3 %collective-permute-start.2 = (bf16[12,256,64]{1,2,0:T(8,128)(2,1)S(1)}, bf16[12,256,64]{1,2,0:T(8,128)(2,1)S(1)}, u32[]{:S(2)}, u32[]{:S(2)}) collective-permute-start(bf16[12,256,64]{1,2,0:T(8,128)(2,1)S(1)} %collective-permute-done.1), channel_id=1, source_target_pairs={{4,0},{6,2},{12,8},{14,10},{20,16},{22,18},{28,24},{30,26},{5,1},{... | collective-permute-start | bytes 1179656 | tf_op jit(solution)/shard_map/ppermute | solution.py:58
  31.0 27.7 %copy-start.44 = (bf16[12,256,64]{1,2,0:T(8,128)(2,1)}, bf16[12,256,64]{1,2,0:T(8,128)(2,1)S(1)}, u32[]{:S(2)}) copy-start(bf16[12,256,64]{1,2,0:T(8,128)(2,1)S(1)} %collective-permute-done.4) | copy-start | bytes 1179652
  31.0 17.8 %collective-permute-start.5 = (bf16[12,256,64]{1,2,0:T(8,128)(2,1)S(1)}, bf16[12,256,64]{1,2,0:T(8,128)(2,1)S(1)}, u32[]{:S(2)}, u32[]{:S(2)}) collective-permute-start(bf16[12,256,64]{1,2,0:T(8,128)(2,1)S(1)} %collective-permute-done.4), channel_id=1, source_target_pairs={{4,0},{6,2},{12,8},{14,10},{20,16},{22,18},{28,24},{30,26},{5,1},{... | collective-permute-start | bytes 1179656 | tf_op jit(solution)/shard_map/ppermute | solution.py:58
  32.9 25.0 %copy-start.34 = (pred[256,256]{0,1:T(8,128)(4,1)}, pred[256,256]{0,1:T(8,128)(4,1)S(1)}, u32[]{:S(2)}) copy-start(pred[256,256]{0,1:T(8,128)(4,1)S(1)} %get-tuple-element.46) | copy-start | bytes 196612
  32.9 25.9 %copy-start.36 = (pred[256,256]{0,1:T(8,128)(4,1)}, pred[256,256]{0,1:T(8,128)(4,1)S(1)}, u32[]{:S(2)}) copy-start(pred[256,256]{0,1:T(8,128)(4,1)S(1)} %get-tuple-element.45) | copy-start | bytes 196612
  32.9 26.8 %copy-start.40 = (pred[256,256]{0,1:T(8,128)(4,1)}, pred[256,256]{0,1:T(8,128)(4,1)S(1)}, u32[]{:S(2)}) copy-start(pred[256,256]{0,1:T(8,128)(4,1)S(1)} %get-tuple-element.44) | copy-start | bytes 196612
  32.9 27.6 %copy-start.42 = (pred[256,256]{0,1:T(8,128)(4,1)}, pred[256,256]{0,1:T(8,128)(4,1)S(1)}, u32[]{:S(2)}) copy-start(pred[256,256]{0,1:T(8,128)(4,1)S(1)} %get-tuple-element.42) | copy-start | bytes 196612
  32.9 28.5 %copy-start.38 = (pred[256,256]{0,1:T(8,128)(4,1)}, pred[256,256]{0,1:T(8,128)(4,1)S(1)}, u32[]{:S(2)}) copy-start(pred[256,256]{0,1:T(8,128)(4,1)S(1)} %get-tuple-element.43) | copy-start | bytes 196612
  42.4 8.8 %copy-start.14 = (bf16[12,256,64]{1,2,0:T(8,128)(2,1)}, bf16[12,256,64]{1,2,0:T(8,128)(2,1)S(1)}, u32[]{:S(2)}) copy-start(bf16[12,256,64]{1,2,0:T(8,128)(2,1)S(1)} %broadcast_select_fusion.1) | copy-start | bytes 1179652
  48.9 12.5 %copy-start.25 = (bf16[12,256,64]{1,2,0:T(8,128)(2,1)}, bf16[12,256,64]{1,2,0:T(8,128)(2,1)S(1)}, u32[]{:S(2)}) copy-start(bf16[12,256,64]{1,2,0:T(8,128)(2,1)S(1)} %broadcast_select_fusion) | copy-start | bytes 1179652
  49.1 2.8 %collective-permute-start.6 = (bf16[2,12,256,64]{2,3,1,0:T(8,128)(2,1)S(1)}, bf16[2,12,256,64]{2,3,1,0:T(8,128)(2,1)S(1)}, u32[]{:S(2)}, u32[]{:S(2)}) collective-permute-start(bf16[2,12,256,64]{2,3,1,0:T(8,128)(2,1)S(1)} %get-tuple-element.40), channel_id=1, source_target_pairs={{0,2},{2,0},{4,6},{6,4},{8,10},{10,8},{12,14},{14,12},{16,18},{18,... | collective-permute-start | bytes 2359304 | tf_op jit(solution)/shard_map/ppermute | solution.py:23
  49.9 8.0 %copy-start.2 = (f32[12,256,256]{1,2,0:T(8,128)}, f32[12,256,256]{1,2,0:T(8,128)S(1)}, u32[]{:S(2)}) copy-start(f32[12,256,256]{1,2,0:T(8,128)S(1)} %get-tuple-element.54) | copy-start | bytes 9437188
  49.9 2.7 %collective-permute-start.7 = (bf16[2,12,256,64]{2,3,1,0:T(8,128)(2,1)S(1)}, bf16[2,12,256,64]{2,3,1,0:T(8,128)(2,1)S(1)}, u32[]{:S(2)}, u32[]{:S(2)}) collective-permute-start(bf16[2,12,256,64]{2,3,1,0:T(8,128)(2,1)S(1)} %get-tuple-element.41), channel_id=1, source_target_pairs={{0,2},{2,0},{4,6},{6,4},{8,10},{10,8},{12,14},{14,12},{16,18},{18,... | collective-permute-start | bytes 2359304 | tf_op jit(solution)/shard_map/ppermute | solution.py:23
  51.2 7.6 %copy-start.4 = (f32[12,256,256]{1,2,0:T(8,128)}, f32[12,256,256]{1,2,0:T(8,128)S(1)}, u32[]{:S(2)}) copy-start(f32[12,256,256]{1,2,0:T(8,128)S(1)} %get-tuple-element.48) | copy-start | bytes 9437188
  51.9 9.6 %copy-start.6 = (f32[12,256,256]{2,1,0:T(8,128)}, f32[12,256,256]{2,1,0:T(8,128)S(1)}, u32[]{:S(2)}) copy-start(f32[12,256,256]{2,1,0:T(8,128)S(1)} %get-tuple-element.52) | copy-start | bytes 9437188
  51.9 8.6 %copy-start.32 = (bf16[2,12,256,64]{2,3,1,0:T(8,128)(2,1)}, bf16[2,12,256,64]{2,3,1,0:T(8,128)(2,1)S(1)}, u32[]{:S(2)}) copy-start(bf16[2,12,256,64]{2,3,1,0:T(8,128)(2,1)S(1)} %collective-permute-done.6) | copy-start | bytes 2359300
  52.6 7.9 %copy-start.10 = (f32[12,256,256]{2,1,0:T(8,128)}, f32[12,256,256]{2,1,0:T(8,128)S(1)}, u32[]{:S(2)}) copy-start(f32[12,256,256]{2,1,0:T(8,128)S(1)} %get-tuple-element.56) | copy-start | bytes 9437188
  52.6 7.0 %copy-start.30 = (bf16[2,12,256,64]{2,3,1,0:T(8,128)(2,1)}, bf16[2,12,256,64]{2,3,1,0:T(8,128)(2,1)S(1)}, u32[]{:S(2)}) copy-start(bf16[2,12,256,64]{2,3,1,0:T(8,128)(2,1)S(1)} %collective-permute-done.7) | copy-start | bytes 2359300
  53.3 6.3 %copy-start.8 = (f32[12,256,256]{2,1,0:T(8,128)}, f32[12,256,256]{2,1,0:T(8,128)S(1)}, u32[]{:S(2)}) copy-start(f32[12,256,256]{2,1,0:T(8,128)S(1)} %get-tuple-element.50) | copy-start | bytes 9437188
  66.2 93.5 %reduce-scatter.5.cloned.1.call-start = ((), (), s32[]{:S(2)}) async-start(), calls=%async_computation.3 | async-start | bytes 442368 | tf_op jit(solution)/shard_map/reduce_scatter | solution.py:172
  86.7 6.3 %copy-start.27 = (bf16[256,768]{0,1:T(8,128)(2,1)}, bf16[256,768]{0,1:T(8,128)(2,1)S(1)}, u32[]{:S(2)}) copy-start(bf16[256,768]{0,1:T(8,128)(2,1)S(1)} %copy.91) | copy-start | bytes 1179652
  86.7 3.0 %copy-start.9 = (f32[12,256,256]{2,1,0:T(8,128)S(1)}, f32[12,256,256]{2,1,0:T(8,128)}, u32[]{:S(2)}) copy-start(f32[12,256,256]{2,1,0:T(8,128)} %copy-done.8) | copy-start | bytes 9437188
  86.7 3.0 %copy-start.41 = (pred[256,256]{0,1:T(8,128)(4,1)S(1)}, pred[256,256]{0,1:T(8,128)(4,1)}, u32[]{:S(2)}) copy-start(pred[256,256]{0,1:T(8,128)(4,1)} %copy-done.40) | copy-start | bytes 196612
  86.7 3.0 %copy-start.46 = (f32[12,256]{1,0:T(8,128)S(1)}, f32[12,256]{1,0:T(8,128)}, u32[]{:S(2)}) copy-start(f32[12,256]{1,0:T(8,128)} %get-tuple-element.34) | copy-start | bytes 36868
  89.7 2.1 %copy-start.7 = (f32[12,256,256]{2,1,0:T(8,128)S(1)}, f32[12,256,256]{2,1,0:T(8,128)}, u32[]{:S(2)}) copy-start(f32[12,256,256]{2,1,0:T(8,128)} %copy-done.6) | copy-start | bytes 9437188
  89.8 2.2 %copy-start.26 = (bf16[12,256,64]{1,2,0:T(8,128)(2,1)S(1)}, bf16[12,256,64]{1,2,0:T(8,128)(2,1)}, u32[]{:S(2)}) copy-start(bf16[12,256,64]{1,2,0:T(8,128)(2,1)} %copy-done.25) | copy-start | bytes 1179652
  89.8 2.2 %copy-start.39 = (pred[256,256]{0,1:T(8,128)(4,1)S(1)}, pred[256,256]{0,1:T(8,128)(4,1)}, u32[]{:S(2)}) copy-start(pred[256,256]{0,1:T(8,128)(4,1)} %copy-done.38) | copy-start | bytes 196612
  91.9 2.2 %copy-start.11 = (f32[12,256,256]{2,1,0:T(8,128)S(1)}, f32[12,256,256]{2,1,0:T(8,128)}, u32[]{:S(2)}) copy-start(f32[12,256,256]{2,1,0:T(8,128)} %copy-done.10) | copy-start | bytes 9437188
  91.9 2.4 %copy-start.33 = (bf16[2,12,256,64]{2,3,1,0:T(8,128)(2,1)S(1)}, bf16[2,12,256,64]{2,3,1,0:T(8,128)(2,1)}, u32[]{:S(2)}) copy-start(bf16[2,12,256,64]{2,3,1,0:T(8,128)(2,1)} %copy-done.32) | copy-start | bytes 2359300
  91.9 2.4 %copy-start.43 = (pred[256,256]{0,1:T(8,128)(4,1)S(1)}, pred[256,256]{0,1:T(8,128)(4,1)}, u32[]{:S(2)}) copy-start(pred[256,256]{0,1:T(8,128)(4,1)} %copy-done.42) | copy-start | bytes 196612
  96.2 12.5 %collective-permute-start.8 = (f32[2,12,256,64]{2,3,1,0:T(8,128)S(1)}, f32[2,12,256,64]{2,3,1,0:T(8,128)S(1)}, u32[]{:S(2)}, u32[]{:S(2)}) collective-permute-start(f32[2,12,256,64]{2,3,1,0:T(8,128)S(1)} %pad_maximum_fusion), channel_id=1, source_target_pairs={{0,2},{2,0},{4,6},{6,4},{8,10},{10,8},{12,14},{14,12},{16,18},{18,... | collective-permute-start | bytes 4718600 | tf_op jit(solution)/shard_map/ppermute | solution.py:23
  98.5 10.2 %collective-permute-start.9 = (f32[2,12,256,64]{2,3,1,0:T(8,128)S(1)}, f32[2,12,256,64]{2,3,1,0:T(8,128)S(1)}, u32[]{:S(2)}, u32[]{:S(2)}) collective-permute-start(f32[2,12,256,64]{2,3,1,0:T(8,128)S(1)} %pad_maximum_fusion.1), channel_id=1, source_target_pairs={{0,2},{2,0},{4,6},{6,4},{8,10},{10,8},{12,14},{14,12},{16,18},{18,... | collective-permute-start | bytes 4718600 | tf_op jit(solution)/shard_map/ppermute | solution.py:23
  108.7 4.7 %copy-start.22 = (bf16[256,12,64]{0,2,1:T(8,128)(2,1)S(1)}, bf16[256,12,64]{0,2,1:T(8,128)(2,1)}, u32[]{:S(2)}) copy-start(bf16[256,12,64]{0,2,1:T(8,128)(2,1)} %copy-done.21) | copy-start | bytes 1179652
  110.6 4.4 %copy-start.15 = (bf16[12,256,64]{1,2,0:T(8,128)(2,1)S(1)}, bf16[12,256,64]{1,2,0:T(8,128)(2,1)}, u32[]{:S(2)}) copy-start(bf16[12,256,64]{1,2,0:T(8,128)(2,1)} %copy-done.14) | copy-start | bytes 1179652
  110.6 23.6 %collective-permute-start.10 = (bf16[2,12,256,64]{2,3,1,0:T(8,128)(2,1)}, bf16[2,12,256,64]{2,3,1,0:T(8,128)(2,1)}, u32[]{:S(2)}, u32[]{:S(2)}) collective-permute-start(bf16[2,12,256,64]{2,3,1,0:T(8,128)(2,1)} %get-tuple-element.36), channel_id=1, source_target_pairs={{4,0},{6,2},{8,4},{10,6},{12,8},{14,10},{16,12},{18,14},{20,16},{2... | collective-permute-start | bytes 2359304 | tf_op jit(solution)/shard_map/ppermute | solution.py:18
  112.0 43.2 %collective-permute-start.11 = (bf16[2,12,256,64]{2,3,1,0:T(8,128)(2,1)}, bf16[2,12,256,64]{2,3,1,0:T(8,128)(2,1)}, u32[]{:S(2)}, u32[]{:S(2)}) collective-permute-start(bf16[2,12,256,64]{2,3,1,0:T(8,128)(2,1)} %get-tuple-element.37), channel_id=1, source_target_pairs={{8,0},{10,2},{12,4},{14,6},{16,8},{18,10},{20,12},{22,14},{24,16},... | collective-permute-start | bytes 2359304 | tf_op jit(solution)/shard_map/ppermute | solution.py:18
  115.0 16.3 %copy-start.13 = (bf16[12,256,256]{1,2,0:T(8,128)(2,1)S(1)}, bf16[12,256,256]{1,2,0:T(8,128)(2,1)}, u32[]{:S(2)}) copy-start(bf16[12,256,256]{1,2,0:T(8,128)(2,1)} %copy-done.12) | copy-start | bytes 4718596
  131.9 27.8 %copy-start.1 = (bf16[1,256,1536]{2,1,0:T(8,128)(2,1)S(1)}, bf16[1,256,1536]{2,1,0:T(8,128)(2,1)}, u32[]{:S(2)}) copy-start(bf16[1,256,1536]{2,1,0:T(8,128)(2,1)} %param.9) | copy-start | bytes 2359300
  (14 other events, 21.9 us)
Sparse Core Ops, SparseCore 0:
  23.9 55.6 all-gather.2
Sparse Core Ops, SparseCore 1:
  66.3 63.3 reduce-scatter.2
  132.4 10.2 reduce-scatter.4

commit v15 on v5

--- a/solution.py
+++ b/solution.py
@@ -57,8 +57,22 @@
             held.append(shift_up(held[-1], SEQ, 1))
         return held
     evens = {0: own}
-    for dist in range(2, reach + 2, 2):
-        evens[dist] = shift_up(own, SEQ, dist)
+    count = axis_count(SEQ)
+    if reach == 4 and count % 4 == 0:
+        row = (lax.axis_index(SEQ) // 2) % 2
+        later = [i for i in range(count) if (i // 2) % 2 == 1]
+        earlier = [i for i in range(count) if (i // 2) % 2 == 0 and i + 2 < count]
+        far = [shift_up(own[k], SEQ, 4) for k in range(2)]
+        near = []
+        for k in range(2):
+            direct = lax.ppermute(own[k], SEQ, [(i - 2, i) for i in later])
+            relayed = lax.ppermute(far[k], SEQ, [(i + 2, i) for i in earlier])
+            near.append(jnp.where(row == 1, direct, relayed))
+        evens[2] = jnp.stack(near)
+        evens[4] = jnp.stack(far)
+    else:
+        for dist in range(2, reach + 2, 2):
+            evens[dist] = shift_up(own, SEQ, dist)
     odds = list(range(1, reach + 1, 2))
     payload = [jnp.where(core == 0, evens[s - 1], evens[s + 1]) for s in odds]
     received = swap_partner(payload, SEQ)
@@ -76,17 +90,27 @@
         return carried
     odds = list(range(1, reach + 1, 2))
     received = swap_partner([parts[s] for s in odds], SEQ)
-    total = None
+    summed = {}
     for dist in range(0, reach + 2, 2):
         zero = jnp.zeros_like(parts[0])
         from_core1 = received[dist // 2] if dist // 2 < len(odds) else zero
         from_core0 = received[dist // 2 - 1] if dist >= 2 and dist // 2 - 1 < len(odds) else zero
         own = parts[dist] if dist <= reach else zero
-        summed = own + jnp.where(core == 0, from_core1, from_core0)
-        if dist == 0:
-            total = summed
-        else:
-            total = total + shift_up(summed.astype(jnp.bfloat16), SEQ, -dist).astype(jnp.float32)
+        summed[dist] = own + jnp.where(core == 0, from_core1, from_core0)
+    count = axis_count(SEQ)
+    if reach == 4 and count % 4 == 0:
+        row = (lax.axis_index(SEQ) // 2) % 2
+        later = [i for i in range(count) if (i // 2) % 2 == 1]
+        earlier = [i for i in range(count) if (i // 2) % 2 == 0 and i + 2 < count]
+        near = summed[2].astype(jnp.bfloat16)
+        direct = lax.ppermute(near, SEQ, [(i, i - 2) for i in later])
+        relayed = lax.ppermute(near, SEQ, [(i, i + 2) for i in earlier])
+        far = summed[4] + jnp.where(row == 1, relayed.astype(jnp.float32), 0.0)
+        total = summed[0] + jnp.where(row == 0, direct.astype(jnp.float32), 0.0)
+        return total + shift_up(far.astype(jnp.bfloat16), SEQ, -4).astype(jnp.float32)
+    total = summed[0]
+    for dist in range(2, reach + 2, 2):
+        total = total + shift_up(summed[dist].astype(jnp.bfloat16), SEQ, -dist).astype(jnp.float32)
     return total
 
 
@@ -102,8 +126,11 @@
     score_scale = HEAD_DIM ** (-0.5)
     utt_lengths = lengths[0]
 
-    weight_cols = lax.all_gather(out_weight, "dp", axis=1, tiled=True)
-    weight_full = lax.all_gather(weight_cols, SEQ, axis=0, tiled=True)
+    row_blocks, col_blocks = axis_count(SEQ), lax.axis_size("dp")
+    pieces = lax.all_gather(out_weight, SEQ + ("dp",), axis=0, tiled=False)
+    weight_full = jnp.transpose(
+        pieces.reshape((row_blocks, col_blocks) + out_weight.shape), (0, 2, 1, 3)
+    ).reshape(row_blocks * out_weight.shape[0], col_blocks * out_weight.shape[1])
 
     query_heads = head_major(query_rows[0], tok_rows)
     own_kv = jnp.stack([head_major(key_rows[0], tok_rows), head_major(value_rows[0], tok_rows)])
@@ -149,17 +176,18 @@
     attended = row_major(attended_heads, tok_rows)
     log_sum = top_score + jnp.log(row_sum)
 
+    upstream = out_grad[0]
+    partial_weight = lax.dot_general(
+        attended, upstream, (((0,), (0,)), ((), ())), preferred_element_type=jnp.float32
+    )
+    partial_weight, attended = lax.optimization_barrier((partial_weight, attended))
     mixed_out = jnp.dot(attended, weight_full, preferred_element_type=jnp.float32).astype(
         jnp.bfloat16
     )
-    upstream = out_grad[0]
     att_grad = lax.dot_general(
         upstream, weight_full, (((1,), (1,)), ((), ())), preferred_element_type=jnp.float32
     ).astype(jnp.bfloat16)
 
-    partial_weight = lax.dot_general(
-        attended, upstream, (((0,), (0,)), ((), ())), preferred_element_type=jnp.float32
-    )
     chip_count = lax.axis_size("chip")
     halves = partial_weight.reshape(chip_count, 2, -1, partial_weight.shape[1])
     keep = lax.dynamic_index_in_dim(halves, core, 1, keepdims=False)
@@ -183,8 +211,8 @@
     query_acc = None
     parts = [None] * (reach + 1)
     order = [d for d in range(reach, -1, -1) if d % 2 == 1] + [
-        d for d in range(reach, -1, -1) if d % 2 == 0
-    ]
+        d for d in range(2, reach + 1, 2)
+    ] + [0]
     for dist in order:
         key_block = held[dist][0]
         value_block = held[dist][1]

time: 188 us -> 172 us (0.915)
  waiting for transfers between devices: 77.3 us -> 44.7 us
  starting transfers between devices: 11.3 us -> 27 us
  local copies, waits for them, and re-layouts: 16.5 us -> 24 us
  blocking collectives: 5.14 us -> 0 us
    reduce_scatter x1, waiting for transfers between devices: 37.2 us -> 5.18 us  [local(): lax.psum_scatter(core_sum.reshape(-1, partial_weight.shape[1]).astype(jnp...]
    ppermute x0 -> x6, waiting for transfers between devices: none -> 23.5 us  [the longest x1 13.7 us: return_behind(): relayed = lax.ppermute(near, SEQ, [(i, i + 2) for i in earlier])]
    ppermute x4 -> x3, waiting for transfers between devices: 28.8 us -> 11.2 us  [shift_up(): return lax.ppermute(block, axis, route)]
    ppermute x0 -> x6, starting transfers between devices: none -> 17.2 us  [the longest x2 7.78 us: gather_behind(): relayed = lax.ppermute(far[k], SEQ, [(i + 2, i) for i in earlier])]
    reduce_scatter x1, waiting for transfers between devices: 6.42 us -> 0.01 us  [local(): lax.psum_scatter(row_share.astype(jnp.float32), 'dp', scatter_dimension=1...]
    all_gather x1 -> x0, blocking collectives: 5.14 us -> none  [local(): weight_cols = lax.all_gather(out_weight, 'dp', axis=1, tiled=True)]
    reshape x0 -> x1, local copies, waits for them, and re-layouts: none -> 3.93 us  [local(): pieces.reshape((row_blocks, col_blocks) + out_weight.shape)]
    unnamed x90 -> x107, local copies, waits for them, and re-layouts: 14.5 us -> 17.1 us
  transfers between devices with their start and end apart: 12 -> 17, of which waited for: 5 -> 7; matrix products, arithmetic and copies ran while one was open for 35% -> 42% of each run, Pallas kernels for 0% -> 0%
where the time goes in v15:
time: 172 us; the launch traced here: 170 us
  waiting for transfers between devices  44.7 us (26%)
  matrix products  36.9 us (21%)
  starting transfers between devices  27 us (16%)
  local copies, waits for them, and re-layouts  24 us (14%)
  other arithmetic  21.2 us (12%)
  between operations  16.4 us (10%)
    unnamed x107, local copies, waits for them, and re-layouts  17.1 us
    ppermute x1, waiting for transfers between devices, return_behind(): relayed = lax.ppermute(near, SEQ, [(i, i + 2) for i in earlier])  13.7 us
    ppermute x3, waiting for transfers between devices, shift_up(): return lax.ppermute(block, axis, route)  11.2 us
    ppermute x2, waiting for transfers between devices, gather_behind(): relayed = lax.ppermute(far[k], SEQ, [(i + 2, i) for i in earlier])  9.74 us
    ppermute x3, starting transfers between devices, shift_up(): return lax.ppermute(block, axis, route)  8.27 us
    ppermute x2, starting transfers between devices, gather_behind(): relayed = lax.ppermute(far[k], SEQ, [(i + 2, i) for i in earlier])  7.78 us
    dot_general x5, matrix products, local(): jnp.einsum('hqe,hke->hqk', grad_heads, value_block, preferred_element_typ...  6.63 us
    dot_general x5, matrix products, local(): jnp.einsum('hqe,hke->hqk', query_heads, held[dist][0], preferred_element_...  6.58 us
  transfers between devices with their start and end apart: 17, of which 7 were waited for; matrix products, arithmetic and copies ran while one was open for 42% of the time, Pallas kernels for 0%

profile of v15, /device:TPU:4, one launch (start us, length us, event | category | flops | bytes accessed | tf_op | source)
XLA Modules:
  0.0 170.2 jit_solution(13540292156350936666)
XLA Ops:
  8.1 1.2 copy.83
  9.3 3.5 %collective-permute-start.4 = (bf16[12,256,64]{1,2,0:T(8,128)(2,1)S(1)}, bf16[12,256,64]{1,2,0:T(8,128)(2,1)S(1)}, u32[]{:S(2)}, u32[]{:S(2)}) collective-permute-start(bf16[12,256,64]{1,2,0:T(8,128)(2,1)S(1)} %bitcast.252), channel_id=1, source_target_pairs={{0,8},{2,10},{4,12},{6,14},{8,16},{10,18},{12,20},{14,22},{16,24},... | collective-permute-start | bytes 1179656 | tf_op jit(solution)/shard_map/ppermute | solution.py:30
  12.8 1.3 collective-permute-start.3
  14.1 1.2 copy.81
  15.3 3.5 %collective-permute-start.1 = (bf16[12,256,64]{1,2,0:T(8,128)(2,1)S(1)}, bf16[12,256,64]{1,2,0:T(8,128)(2,1)S(1)}, u32[]{:S(2)}, u32[]{:S(2)}) collective-permute-start(bf16[12,256,64]{1,2,0:T(8,128)(2,1)S(1)} %bitcast.242), channel_id=1, source_target_pairs={{0,8},{2,10},{4,12},{6,14},{8,16},{10,18},{12,20},{14,22},{16,24},... | collective-permute-start | bytes 1179656 | tf_op jit(solution)/shard_map/ppermute | solution.py:30
  18.8 1.3 collective-permute-start
  21.2 1.2 copy.80
  22.4 5.4 %collective-permute-start.5 = (bf16[12,256,64]{1,2,0:T(8,128)(2,1)S(1)}, bf16[12,256,64]{1,2,0:T(8,128)(2,1)S(1)}, u32[]{:S(2)}, u32[]{:S(2)}) collective-permute-start(bf16[12,256,64]{1,2,0:T(8,128)(2,1)S(1)} %collective-permute-done.4), channel_id=1, source_target_pairs={{4,0},{6,2},{12,8},{14,10},{20,16},{22,18},{28,24},{30,26},{5,1},{... | collective-permute-start | bytes 1179656 | tf_op jit(solution)/shard_map/ppermute | solution.py:69
  27.8 1.8 %collective-permute-done.1 = bf16[12,256,64]{1,2,0:T(8,128)(2,1)S(1)} collective-permute-done((bf16[12,256,64]{1,2,0:T(8,128)(2,1)S(1)}, bf16[12,256,64]{1,2,0:T(8,128)(2,1)S(1)}, u32[]{:S(2)}, u32[]{:S(2)}) %collective-permute-start.1) | collective-permute-done | bytes 393248 | tf_op jit(solution)/shard_map/ppermute | solution.py:30
  29.6 2.4 %collective-permute-start.2 = (bf16[12,256,64]{1,2,0:T(8,128)(2,1)S(1)}, bf16[12,256,64]{1,2,0:T(8,128)(2,1)S(1)}, u32[]{:S(2)}, u32[]{:S(2)}) collective-permute-start(bf16[12,256,64]{1,2,0:T(8,128)(2,1)S(1)} %collective-permute-done.1), channel_id=1, source_target_pairs={{4,0},{6,2},{12,8},{14,10},{20,16},{22,18},{28,24},{30,26},{5,1},{... | collective-permute-start | bytes 1179656 | tf_op jit(solution)/shard_map/ppermute | solution.py:69
  33.4 4.4 %collective-permute-done.5 = bf16[12,256,64]{1,2,0:T(8,128)(2,1)S(1)} collective-permute-done((bf16[12,256,64]{1,2,0:T(8,128)(2,1)S(1)}, bf16[12,256,64]{1,2,0:T(8,128)(2,1)S(1)}, u32[]{:S(2)}, u32[]{:S(2)}) %collective-permute-start.5) | collective-permute-done | bytes 393248 | tf_op jit(solution)/shard_map/ppermute | solution.py:69
  38.9 5.3 %collective-permute-done.2 = bf16[12,256,64]{1,2,0:T(8,128)(2,1)S(1)} collective-permute-done((bf16[12,256,64]{1,2,0:T(8,128)(2,1)S(1)}, bf16[12,256,64]{1,2,0:T(8,128)(2,1)S(1)}, u32[]{:S(2)}, u32[]{:S(2)}) %collective-permute-start.2) | collective-permute-done | bytes 393248 | tf_op jit(solution)/shard_map/ppermute | solution.py:69
  45.3 2.5 %maximum_select_fusion = (bf16[2,12,256,64]{2,3,1,0:T(8,128)(2,1)}, bf16[2,12,256,64]{2,3,1,0:T(8,128)(2,1)}) fusion(bf16[1,12,256,64]{2,3,1,0:T(8,128)(2,1)S(1)} %bitcast.254, bf16[1,12,256,64]{2,3,1,0:T(8,128)(2,1)S(1)} %bitcast.244, pred[]{:T(512)S(6)} %eq.100, bf16[1,12,256,64]{2,3,1,0:T(8,128)(2,1)S(1)} %bitcast.257, ...), kind=kLoop, calls=%fused_computation.121 | loop fusion | flops 1966080 | bytes 3932161 | tf_op jit(solution)/shard_map/jit(_where)/select_n | solution.py:77
  47.8 2.4 %select_reduce_fusion.1 = (f32[12,256]{1,0:T(8,128)S(1)}, f32[12,256,256]{1,2,0:T(8,128)}) fusion(pred[256,256]{0,1:T(8,128)(4,1)S(1)} %get-tuple-element.44, bf16[12,256,64]{1,2,0:T(8,128)(2,1)S(1)} %bitcast.226, bf16[12,256,64]{1,2,0:T(8,128)(2,1)S(1)} %bitcast.245), kind=kOutput, calls=%fused_computation.28 | convolution fusion | flops 103019520 | bytes 4009984 | tf_op jit(solution)/shard_map/hqe,hke->hqk/dot_general | solution.py:153
  52.2 2.1 %fusion.8 = (f32[12,256]{1,0:T(8,128)S(1)}, f32[12,256,256]{2,1,0:T(8,128)S(1)}) fusion(pred[256,256]{0,1:T(8,128)(4,1)S(1)} %get-tuple-element.42, bf16[12,256,64]{1,2,0:T(8,128)(2,1)S(1)} %bitcast.229, bf16[2,12,256,64]{2,3,1,0:T(8,128)(2,1)} %collective-permute-done.7), kind=kOutput, calls=%fused_computation.26 | convolution fusion | flops 103019520 | bytes 4009984 | tf_op jit(solution)/shard_map/hqe,hke->hqk/dot_general | solution.py:153
  55.1 1.6 copy-done.3
  57.6 3.9 %fusion.18 = (f32[12,256]{1,0:T(8,128)S(1)}, f32[12,256]{1,0:T(8,128)S(1)}, f32[12,256]{1,0:T(8,128)S(1)}, f32[12,256]{1,0:T(8,128)S(1)}, f32[12,256]{1,0:T(8,128)S(1)}) fusion(f32[12,256,256]{2,1,0:T(8,128)S(1)} %get-tuple-element.54, f32[12,256]{1,0:T(8,128)S(1)} %maximum_maximum_fusion, pred[256,256]{0,1:T(8,128)(4,1)S(1)} %get-tuple-element.40, ...), kind=kLoop, calls=%fused_computation.41 | loop fusion | flops 19645440 | bytes 16130048 | tf_op jit(solution)/shard_map/reduce_sum | solution.py:166
  61.5 1.9 %fusion.59 = f32[12,256,64]{1,2,0:T(8,128)S(1)} fusion(f32[12,256,256]{2,1,0:T(8,128)S(1)} %get-tuple-element.48, f32[12,256]{1,0:T(8,128)S(1)} %maximum_maximum_fusion, pred[256,256]{0,1:T(8,128)(4,1)S(1)} %get-tuple-element.42, bf16[2,12,256,64]{2,3,1,0:T(8,128)(2,1)} %collective-permute-done.7), kind=kOutput, calls=%fused_computation.81 | convolution fusion | flops 104595456 | bytes 4403200 | tf_op jit(solution)/shard_map/hqk,hke->hqe/dot_general | solution.py:167
  65.8 1.8 %fusion.116 = (bf16[256,12,64]{0,2,1:T(8,128)(2,1)S(1)}, f32[12,256,64]{1,2,0:T(8,128)}) fusion(f32[256,12]{0,1:T(8,128)S(1)} %bitcast.273, f32[12,256,64]{1,2,0:T(8,128)S(1)} %fusion.57, f32[12,256,64]{1,2,0:T(8,128)S(1)} %fusion.59, f32[12,256,64]{1,2,0:T(8,128)S(1)} %fusion.100, bf16[12,256,64]{1,2,0:T(8,128)(2,1)S(1)} %broadcast_select_fusion, ...), kind=kOutput, calls=%fused_computation.128 | convolution fusion | flops 105578496 | bytes 7168000 | tf_op jit(solution)/shard_map/hqk,hke->hqe/dot_general | solution.py:167
  68.4 2.1 %copy-done.2 = f32[768,1536]{1,0:T(8,128)} copy-done((f32[768,1536]{1,0:T(8,128)}, f32[768,1536]{1,0:T(8,128)S(1)}, u32[]{:S(2)}) %copy-start.2) | copy-done | bytes 4718616
  70.6 1.7 %dynamic-slice_bitcast_fusion = f32[8,48,1536]{2,1,0:T(8,128)} fusion(f32[8,2,48,1536]{3,2,1,0:T(8,128)S(1)} %bitcast.236, s32[]{:T(128)S(6)} %select_n.243), kind=kLoop, calls=%fused_computation.38 | loop fusion | bytes 4718596 | tf_op jit(solution)/shard_map/jit(dynamic_index_in_dim)/squeeze | solution.py:194
  72.3 4.8 %collective-permute-done.13 = f32[8,48,1536]{2,1,0:T(8,128)S(1)} collective-permute-done((f32[8,48,1536]{2,1,0:T(8,128)}, f32[8,48,1536]{2,1,0:T(8,128)S(1)}, u32[]{:S(2)}, u32[]{:S(2)}) %collective-permute-start.13) | collective-permute-done | bytes 2359328 | tf_op jit(solution)/shard_map/ppermute | solution.py:34
  77.1 3.0 %fusion.15 = bf16[8,48,1536]{2,1,0:T(8,128)(2,1)} fusion(f32[8,48,1536]{2,1,0:T(8,128)S(1)} %collective-permute-done.13, f32[8,2,48,1536]{3,2,1,0:T(8,128)} %bitcast.237, s32[]{:T(128)S(6)} %select_n.242), kind=kLoop, calls=%fused_computation.37 | loop fusion | flops 1179648 | bytes 5898244 | tf_op jit(solution)/shard_map/convert_element_type | solution.py:197
  80.4 3.9 %copy.90 = bf16[16,2,48,768]{3,1,2,0:T(2,128)(2,1)S(1)} copy(bf16[16,2,48,768]{3,2,1,0:T(8,128)(2,1)} %bitcast.251) | data formatting | bytes 4718592 | tf_op jit(solution)/shard_map/reshape | solution.py:132
  84.8 1.5 convolution_convert_fusion.1
  86.3 1.2 copy.91
  87.5 2.8 %fusion.83 = f32[1,12,256,64]{2,3,1,0:T(8,128)S(1)} fusion(bf16[12,256,64]{1,2,0:T(8,128)(2,1)S(1)} %bitcast.259, f32[12,256,256]{2,1,0:T(8,128)} %copy-done.11, f32[12,256]{1,0:T(8,128)} %get-tuple-element.34, pred[256,256]{0,1:T(8,128)(4,1)} %copy-done.42), kind=kOutput, calls=%fused_computation.97 | convolution fusion | flops 103809024 | bytes 4403200 | tf_op jit(solution)/shard_map/hqk,hqe->hke/dot_general | solution.py:239
  91.3 1.2 copy-done.10
  94.7 1.1 multiply_convert_fusion
  96.8 1.1 multiply_convert_fusion.3
  98.5 2.2 %multiply_convert_fusion.4 = bf16[12,256,256]{1,2,0:T(8,128)(2,1)S(1)} fusion(f32[12,256,256]{2,1,0:T(8,128)S(1)} %copy-done.10, bf16[12,256,64]{1,2,0:T(8,128)(2,1)S(1)} %bitcast.265, f32[12,256]{1,0:T(8,128)S(1)} %multiply_reduce_fusion, f32[12,256]{1,0:T(8,128)S(1)} %copy-done.49, pred[256,256]{0,1:T(8,128)(4,1)S(1)} %copy-done.41, ...), kind=kOutput, calls=%fused_computation.18 | convolution fusion | flops 105381888 | bytes 5595136 | tf_op jit(solution)/shard_map/hqe,hke->hqk/dot_general | solution.py:227
  103.1 1.4 convolution_add_fusion.1
  104.5 1.1 multiply_convert_fusion.2
  106.5 1.1 multiply_convert_fusion.1
  108.9 1.4 fusion.39
  110.3 1.3 collective-permute-start.11
  112.9 1.6 fusion.80
  114.5 5.6 %collective-permute-start.10 = (bf16[2,12,256,64]{2,3,1,0:T(8,128)(2,1)}, bf16[2,12,256,64]{2,3,1,0:T(8,128)(2,1)}, u32[]{:S(2)}, u32[]{:S(2)}) collective-permute-start(bf16[2,12,256,64]{2,3,1,0:T(8,128)(2,1)} %fusion.39), channel_id=1, source_target_pairs={{4,0},{6,2},{12,8},{14,10},{20,16},{22,18},{28,24},{30,26},{5,1},{... | collective-permute-start | bytes 2359304 | tf_op jit(solution)/shard_map/ppermute | solution.py:106
  120.1 13.7 %collective-permute-done.11 = bf16[2,12,256,64]{2,3,1,0:T(8,128)(2,1)S(1)} collective-permute-done((bf16[2,12,256,64]{2,3,1,0:T(8,128)(2,1)}, bf16[2,12,256,64]{2,3,1,0:T(8,128)(2,1)S(1)}, u32[]{:S(2)}, u32[]{:S(2)}) %collective-permute-start.11) | collective-permute-done | bytes 786464 | tf_op jit(solution)/shard_map/ppermute | solution.py:107
  133.8 1.3 fusion.41
  135.1 1.3 collective-permute-start.12
  136.4 1.7 fusion.9
  138.1 1.2 fusion.112
  139.3 5.2 %reduce-scatter.3.cloned.1.call-done = bf16[48,1536]{1,0:T(8,128)(2,1)} async-done(((bf16[384,1536]{1,0:T(8,128)(2,1)}), bf16[48,1536]{1,0:T(8,128)(2,1)}) %reduce-scatter.3.cloned.1.call-update) | async-done | bytes 147472 | tf_op jit(solution)/shard_map/reduce_scatter | solution.py:196
  144.5 1.6 convert_element_type.191
  146.7 2.0 %copy.112 = bf16[1,256,768]{2,1,0:T(8,128)(2,1)} copy(bf16[1,256,768]{1,2,0:T(8,128)(2,1)} %bitcast.258) | data formatting | bytes 786432
  148.7 9.4 %collective-permute-done.12 = bf16[2,12,256,64]{2,3,1,0:T(8,128)(2,1)} collective-permute-done((bf16[2,12,256,64]{2,3,1,0:T(8,128)(2,1)}, bf16[2,12,256,64]{2,3,1,0:T(8,128)(2,1)}, u32[]{:S(2)}, u32[]{:S(2)}) %collective-permute-start.12) | collective-permute-done | bytes 786464 | tf_op jit(solution)/shard_map/ppermute | solution.py:30
  158.2 2.7 %fusion.38 = bf16[2,12,256,64]{2,3,1,0:T(8,128)(2,1)S(1)} fusion(f32[1,12,256,64]{2,3,1,0:T(8,128)} %fusion.80, f32[1,12,256,64]{2,3,1,0:T(8,128)S(1)} %fusion.97, bf16[2,12,256,64]{2,3,1,0:T(8,128)(2,1)} %collective-permute-done.12, bf16[2,12,256,64]{2,3,1,0:T(8,128)(2,1)} %collective-permute-done.10, f32[2,12,256,64]{2,3,1,0:T(8,128)} %copy-done.15, ...), kind=kLoop, calls=%fused_computation.57 | loop fusion | flops 3538944 | bytes 5505026 | tf_op jit(solution)/shard_map/convert.1
  (160 shorter events, 24.8 us)
Async XLA Ops:
  8.0 59.7 %copy-start = (bf16[1,256,1536]{2,1,0:T(8,128)(2,1)S(1)}, bf16[1,256,1536]{2,1,0:T(8,128)(2,1)}, u32[]{:S(2)}) copy-start(bf16[1,256,1536]{2,1,0:T(8,128)(2,1)} %param.9) | copy-start | bytes 2359300
  8.0 72.4 %all-gather.3.cloned.1.call-start = ((), (), s32[]{:S(2)}) async-start(), calls=%async_computation.4 | async-start | bytes 2433024 | tf_op jit(solution)/shard_map/all_gather | solution.py:130
  9.3 45.8 %copy-start.24 = (bf16[1,256,768]{1,2,0:T(8,128)(2,1)}, bf16[1,256,768]{1,2,0:T(8,128)(2,1)S(1)}, u32[]{:S(2)}) copy-start(bf16[1,256,768]{1,2,0:T(8,128)(2,1)S(1)} %copy.83) | copy-start | bytes 1179652
  9.3 13.1 %collective-permute-start.4 = (bf16[12,256,64]{1,2,0:T(8,128)(2,1)S(1)}, bf16[12,256,64]{1,2,0:T(8,128)(2,1)S(1)}, u32[]{:S(2)}, u32[]{:S(2)}) collective-permute-start(bf16[12,256,64]{1,2,0:T(8,128)(2,1)S(1)} %bitcast.252), channel_id=1, source_target_pairs={{0,8},{2,10},{4,12},{6,14},{8,16},{10,18},{12,20},{14,22},{16,24},... | collective-permute-start | bytes 1179656 | tf_op jit(solution)/shard_map/ppermute | solution.py:30
  12.8 19.8 %collective-permute-start.3 = (bf16[12,256,64]{1,2,0:T(8,128)(2,1)S(1)}, bf16[12,256,64]{1,2,0:T(8,128)(2,1)S(1)}, u32[]{:S(2)}, u32[]{:S(2)}) collective-permute-start(bf16[12,256,64]{1,2,0:T(8,128)(2,1)S(1)} %bitcast.253), channel_id=1, source_target_pairs={{0,4},{2,6},{8,12},{10,14},{16,20},{18,22},{24,28},{26,30},{1,5},{... | collective-permute-start | bytes 1179656 | tf_op jit(solution)/shard_map/ppermute | solution.py:68
  15.3 32.5 %copy-start.18 = (bf16[1,256,768]{1,2,0:T(8,128)(2,1)}, bf16[1,256,768]{1,2,0:T(8,128)(2,1)S(1)}, u32[]{:S(2)}) copy-start(bf16[1,256,768]{1,2,0:T(8,128)(2,1)S(1)} %copy.81) | copy-start | bytes 1179652
  15.3 14.3 %collective-permute-start.1 = (bf16[12,256,64]{1,2,0:T(8,128)(2,1)S(1)}, bf16[12,256,64]{1,2,0:T(8,128)(2,1)S(1)}, u32[]{:S(2)}, u32[]{:S(2)}) collective-permute-start(bf16[12,256,64]{1,2,0:T(8,128)(2,1)S(1)} %bitcast.242), channel_id=1, source_target_pairs={{0,8},{2,10},{4,12},{6,14},{8,16},{10,18},{12,20},{14,22},{16,24},... | collective-permute-start | bytes 1179656 | tf_op jit(solution)/shard_map/ppermute | solution.py:30
  18.8 20.1 %collective-permute-start = (bf16[12,256,64]{1,2,0:T(8,128)(2,1)S(1)}, bf16[12,256,64]{1,2,0:T(8,128)(2,1)}, u32[]{:S(2)}, u32[]{:S(2)}) collective-permute-start(bf16[12,256,64]{1,2,0:T(8,128)(2,1)S(1)} %bitcast.243), channel_id=1, source_target_pairs={{0,4},{2,6},{8,12},{10,14},{16,20},{18,22},{24,28},{26,30},{1,5},{... | collective-permute-start | bytes 1179656 | tf_op jit(solution)/shard_map/ppermute | solution.py:68
  20.1 124.3 %reduce-scatter.3.cloned.1.call-start = ((), (), s32[]{:S(2)}) async-start(), calls=%async_computation.2 | async-start | bytes 1327104 | tf_op jit(solution)/shard_map/reduce_scatter | solution.py:196
  22.4 16.5 %copy-start.44 = (bf16[12,256,64]{1,2,0:T(8,128)(2,1)}, bf16[12,256,64]{1,2,0:T(8,128)(2,1)S(1)}, u32[]{:S(2)}) copy-start(bf16[12,256,64]{1,2,0:T(8,128)(2,1)S(1)} %collective-permute-done.4) | copy-start | bytes 1179652
  22.4 15.4 %collective-permute-start.5 = (bf16[12,256,64]{1,2,0:T(8,128)(2,1)S(1)}, bf16[12,256,64]{1,2,0:T(8,128)(2,1)S(1)}, u32[]{:S(2)}, u32[]{:S(2)}) collective-permute-start(bf16[12,256,64]{1,2,0:T(8,128)(2,1)S(1)} %collective-permute-done.4), channel_id=1, source_target_pairs={{4,0},{6,2},{12,8},{14,10},{20,16},{22,18},{28,24},{30,26},{5,1},{... | collective-permute-start | bytes 1179656 | tf_op jit(solution)/shard_map/ppermute | solution.py:69
  29.6 21.2 %copy-start.20 = (bf16[12,256,64]{1,2,0:T(8,128)(2,1)}, bf16[12,256,64]{1,2,0:T(8,128)(2,1)S(1)}, u32[]{:S(2)}) copy-start(bf16[12,256,64]{1,2,0:T(8,128)(2,1)S(1)} %collective-permute-done.1) | copy-start | bytes 1179652
  29.6 14.7 %collective-permute-start.2 = (bf16[12,256,64]{1,2,0:T(8,128)(2,1)S(1)}, bf16[12,256,64]{1,2,0:T(8,128)(2,1)S(1)}, u32[]{:S(2)}, u32[]{:S(2)}) collective-permute-start(bf16[12,256,64]{1,2,0:T(8,128)(2,1)S(1)} %collective-permute-done.1), channel_id=1, source_target_pairs={{4,0},{6,2},{12,8},{14,10},{20,16},{22,18},{28,24},{30,26},{5,1},{... | collective-permute-start | bytes 1179656 | tf_op jit(solution)/shard_map/ppermute | solution.py:69
  32.6 25.0 %copy-start.33 = (pred[256,256]{0,1:T(8,128)(4,1)}, pred[256,256]{0,1:T(8,128)(4,1)S(1)}, u32[]{:S(2)}) copy-start(pred[256,256]{0,1:T(8,128)(4,1)S(1)} %get-tuple-element.44) | copy-start | bytes 196612
  32.6 28.9 %copy-start.40 = (pred[256,256]{0,1:T(8,128)(4,1)}, pred[256,256]{0,1:T(8,128)(4,1)S(1)}, u32[]{:S(2)}) copy-start(pred[256,256]{0,1:T(8,128)(4,1)S(1)} %get-tuple-element.42) | copy-start | bytes 196612
  32.6 30.8 %copy-start.35 = (pred[256,256]{0,1:T(8,128)(4,1)}, pred[256,256]{0,1:T(8,128)(4,1)S(1)}, u32[]{:S(2)}) copy-start(pred[256,256]{0,1:T(8,128)(4,1)S(1)} %get-tuple-element.43) | copy-start | bytes 196612
  32.6 32.3 %copy-start.42 = (pred[256,256]{0,1:T(8,128)(4,1)}, pred[256,256]{0,1:T(8,128)(4,1)S(1)}, u32[]{:S(2)}) copy-start(pred[256,256]{0,1:T(8,128)(4,1)S(1)} %get-tuple-element.40) | copy-start | bytes 196612
  32.6 33.2 %copy-start.37 = (pred[256,256]{0,1:T(8,128)(4,1)}, pred[256,256]{0,1:T(8,128)(4,1)S(1)}, u32[]{:S(2)}) copy-start(pred[256,256]{0,1:T(8,128)(4,1)S(1)} %get-tuple-element.41) | copy-start | bytes 196612
  38.9 26.9 %copy-start.26 = (bf16[12,256,64]{1,2,0:T(8,128)(2,1)}, bf16[12,256,64]{1,2,0:T(8,128)(2,1)S(1)}, u32[]{:S(2)}) copy-start(bf16[12,256,64]{1,2,0:T(8,128)(2,1)S(1)} %broadcast_select_fusion) | copy-start | bytes 1179652
  45.3 6.1 %copy-start.16 = (bf16[12,256,64]{1,2,0:T(8,128)(2,1)}, bf16[12,256,64]{1,2,0:T(8,128)(2,1)S(1)}, u32[]{:S(2)}) copy-start(bf16[12,256,64]{1,2,0:T(8,128)(2,1)S(1)} %broadcast_select_fusion.1) | copy-start | bytes 1179652
  47.8 4.3 %collective-permute-start.7 = (bf16[2,12,256,64]{2,3,1,0:T(8,128)(2,1)}, bf16[2,12,256,64]{2,3,1,0:T(8,128)(2,1)}, u32[]{:S(2)}, u32[]{:S(2)}) collective-permute-start(bf16[2,12,256,64]{2,3,1,0:T(8,128)(2,1)} %get-tuple-element.39), channel_id=1, source_target_pairs={{0,2},{2,0},{1,3},{3,1},{4,6},{6,4},{5,7},{7,5},{8,10},{10,8},{9,1... | collective-permute-start | bytes 2359304 | tf_op jit(solution)/shard_map/ppermute | solution.py:34
  50.2 4.1 %collective-permute-start.6 = (bf16[2,12,256,64]{2,3,1,0:T(8,128)(2,1)}, bf16[2,12,256,64]{2,3,1,0:T(8,128)(2,1)S(1)}, u32[]{:S(2)}, u32[]{:S(2)}) collective-permute-start(bf16[2,12,256,64]{2,3,1,0:T(8,128)(2,1)} %get-tuple-element.38), channel_id=1, source_target_pairs={{0,2},{2,0},{1,3},{3,1},{4,6},{6,4},{5,7},{7,5},{8,10},{10,8},{9,1... | collective-permute-start | bytes 2359304 | tf_op jit(solution)/shard_map/ppermute | solution.py:34
  51.4 12.0 %copy-start.5 = (f32[12,256,256]{1,2,0:T(8,128)}, f32[12,256,256]{1,2,0:T(8,128)S(1)}, u32[]{:S(2)}) copy-start(f32[12,256,256]{1,2,0:T(8,128)S(1)} %get-tuple-element.46) | copy-start | bytes 9437188
  52.1 13.7 %copy-start.7 = (f32[12,256,256]{2,1,0:T(8,128)}, f32[12,256,256]{2,1,0:T(8,128)S(1)}, u32[]{:S(2)}) copy-start(f32[12,256,256]{2,1,0:T(8,128)S(1)} %get-tuple-element.50) | copy-start | bytes 9437188
  52.2 4.5 %copy-start.3 = (f32[12,256,256]{1,2,0:T(8,128)S(1)}, f32[12,256,256]{1,2,0:T(8,128)}, u32[]{:S(2)}) copy-start(f32[12,256,256]{1,2,0:T(8,128)} %get-tuple-element.52) | copy-start | bytes 9437188
  54.3 7.2 %copy-start.9 = (f32[12,256,256]{2,1,0:T(8,128)}, f32[12,256,256]{2,1,0:T(8,128)S(1)}, u32[]{:S(2)}) copy-start(f32[12,256,256]{2,1,0:T(8,128)S(1)} %get-tuple-element.48) | copy-start | bytes 9437188
  54.3 10.6 %copy-start.31 = (bf16[2,12,256,64]{2,3,1,0:T(8,128)(2,1)}, bf16[2,12,256,64]{2,3,1,0:T(8,128)(2,1)S(1)}, u32[]{:S(2)}) copy-start(bf16[2,12,256,64]{2,3,1,0:T(8,128)(2,1)S(1)} %collective-permute-done.6) | copy-start | bytes 2359300
  55.0 9.9 %copy-start.11 = (f32[12,256,256]{2,1,0:T(8,128)}, f32[12,256,256]{2,1,0:T(8,128)S(1)}, u32[]{:S(2)}) copy-start(f32[12,256,256]{2,1,0:T(8,128)S(1)} %get-tuple-element.54) | copy-start | bytes 9437188
  72.3 4.8 %collective-permute-start.13 = (f32[8,48,1536]{2,1,0:T(8,128)}, f32[8,48,1536]{2,1,0:T(8,128)S(1)}, u32[]{:S(2)}, u32[]{:S(2)}) collective-permute-start(f32[8,48,1536]{2,1,0:T(8,128)} %dynamic-slice_bitcast_fusion), channel_id=1, source_target_pairs={{0,2},{2,0},{1,3},{3,1},{4,6},{6,4},{5,7},{7,5},{8,10},{10,8},{9,1... | collective-permute-start | bytes 7077896 | tf_op jit(solution)/shard_map/ppermute | solution.py:34
  80.1 82.6 %reduce-scatter.5.cloned.1.call-start = ((), (), s32[]{:S(2)}) async-start(), calls=%async_computation.3 | async-start | bytes 442368 | tf_op jit(solution)/shard_map/reduce_scatter | solution.py:202
  86.3 4.0 %copy-start.38 = (pred[256,256]{0,1:T(8,128)(4,1)S(1)}, pred[256,256]{0,1:T(8,128)(4,1)}, u32[]{:S(2)}) copy-start(pred[256,256]{0,1:T(8,128)(4,1)} %copy-done.37) | copy-start | bytes 196612
  86.3 4.0 %copy-start.48 = (f32[12,256]{1,0:T(8,128)S(1)}, f32[12,256]{1,0:T(8,128)}, u32[]{:S(2)}) copy-start(f32[12,256]{1,0:T(8,128)} %get-tuple-element.34) | copy-start | bytes 36868
  87.5 11.0 %copy-start.28 = (bf16[256,768]{0,1:T(8,128)(2,1)}, bf16[256,768]{0,1:T(8,128)(2,1)S(1)}, u32[]{:S(2)}) copy-start(bf16[256,768]{0,1:T(8,128)(2,1)S(1)} %copy.91) | copy-start | bytes 1179652
  87.5 3.0 %copy-start.8 = (f32[12,256,256]{2,1,0:T(8,128)S(1)}, f32[12,256,256]{2,1,0:T(8,128)}, u32[]{:S(2)}) copy-start(f32[12,256,256]{2,1,0:T(8,128)} %copy-done.7) | copy-start | bytes 9437188
  96.8 4.5 %copy-start.13 = (bf16[12,256,256]{1,2,0:T(8,128)(2,1)}, bf16[12,256,256]{1,2,0:T(8,128)(2,1)S(1)}, u32[]{:S(2)}) copy-start(bf16[12,256,256]{1,2,0:T(8,128)(2,1)S(1)} %multiply_convert_fusion) | copy-start | bytes 4718596
  98.5 2.8 %copy-start.19 = (bf16[1,256,768]{1,2,0:T(8,128)(2,1)S(1)}, bf16[1,256,768]{1,2,0:T(8,128)(2,1)}, u32[]{:S(2)}) copy-start(bf16[1,256,768]{1,2,0:T(8,128)(2,1)} %copy-done.18) | copy-start | bytes 1179652
  101.9 7.0 %collective-permute-start.8 = (f32[2,12,256,64]{2,3,1,0:T(8,128)S(1)}, f32[2,12,256,64]{2,3,1,0:T(8,128)S(1)}, u32[]{:S(2)}, u32[]{:S(2)}) collective-permute-start(f32[2,12,256,64]{2,3,1,0:T(8,128)S(1)} %pad_maximum_fusion), channel_id=1, source_target_pairs={{0,2},{2,0},{1,3},{3,1},{4,6},{6,4},{5,7},{7,5},{8,10},{10,8},{9,1... | collective-permute-start | bytes 4718600 | tf_op jit(solution)/shard_map/ppermute | solution.py:34
  102.2 2.3 %copy-start.27 = (bf16[12,256,64]{1,2,0:T(8,128)(2,1)S(1)}, bf16[12,256,64]{1,2,0:T(8,128)(2,1)}, u32[]{:S(2)}) copy-start(bf16[12,256,64]{1,2,0:T(8,128)(2,1)} %copy-done.26) | copy-start | bytes 1179652
  102.2 2.3 %copy-start.29 = (bf16[256,768]{0,1:T(8,128)(2,1)S(1)}, bf16[256,768]{0,1:T(8,128)(2,1)}, u32[]{:S(2)}) copy-start(bf16[256,768]{0,1:T(8,128)(2,1)} %copy-done.28) | copy-start | bytes 1179652
  102.2 6.7 %collective-permute-start.9 = (f32[2,12,256,64]{2,3,1,0:T(8,128)S(1)}, f32[2,12,256,64]{2,3,1,0:T(8,128)S(1)}, u32[]{:S(2)}, u32[]{:S(2)}) collective-permute-start(f32[2,12,256,64]{2,3,1,0:T(8,128)S(1)} %pad_maximum_fusion.1), channel_id=1, source_target_pairs={{0,2},{2,0},{1,3},{3,1},{4,6},{6,4},{5,7},{7,5},{8,10},{10,8},{9,1... | collective-permute-start | bytes 4718600 | tf_op jit(solution)/shard_map/ppermute | solution.py:34
  108.9 3.3 %copy-start.15 = (f32[2,12,256,64]{2,3,1,0:T(8,128)}, f32[2,12,256,64]{2,3,1,0:T(8,128)S(1)}, u32[]{:S(2)}) copy-start(f32[2,12,256,64]{2,3,1,0:T(8,128)S(1)} %collective-permute-done.8) | copy-start | bytes 4718596
  110.3 23.5 %collective-permute-start.11 = (bf16[2,12,256,64]{2,3,1,0:T(8,128)(2,1)}, bf16[2,12,256,64]{2,3,1,0:T(8,128)(2,1)S(1)}, u32[]{:S(2)}, u32[]{:S(2)}) collective-permute-start(bf16[2,12,256,64]{2,3,1,0:T(8,128)(2,1)} %fusion.39), channel_id=1, source_target_pairs={{0,4},{2,6},{8,12},{10,14},{16,20},{18,22},{24,28},{26,30},{1,5},{... | collective-permute-start | bytes 2359304 | tf_op jit(solution)/shard_map/ppermute | solution.py:107
  114.5 21.9 %copy-start.23 = (bf16[256,12,64]{0,2,1:T(8,128)(2,1)S(1)}, bf16[256,12,64]{0,2,1:T(8,128)(2,1)}, u32[]{:S(2)}) copy-start(bf16[256,12,64]{0,2,1:T(8,128)(2,1)} %copy-done.22) | copy-start | bytes 1179652
  114.5 23.6 %copy-start.17 = (bf16[12,256,64]{1,2,0:T(8,128)(2,1)S(1)}, bf16[12,256,64]{1,2,0:T(8,128)(2,1)}, u32[]{:S(2)}) copy-start(bf16[12,256,64]{1,2,0:T(8,128)(2,1)} %copy-done.16) | copy-start | bytes 1179652
  114.5 34.3 %collective-permute-start.10 = (bf16[2,12,256,64]{2,3,1,0:T(8,128)(2,1)}, bf16[2,12,256,64]{2,3,1,0:T(8,128)(2,1)}, u32[]{:S(2)}, u32[]{:S(2)}) collective-permute-start(bf16[2,12,256,64]{2,3,1,0:T(8,128)(2,1)} %fusion.39), channel_id=1, source_target_pairs={{4,0},{6,2},{12,8},{14,10},{20,16},{22,18},{28,24},{30,26},{5,1},{... | collective-permute-start | bytes 2359304 | tf_op jit(solution)/shard_map/ppermute | solution.py:106
  135.1 23.0 %collective-permute-start.12 = (bf16[2,12,256,64]{2,3,1,0:T(8,128)(2,1)}, bf16[2,12,256,64]{2,3,1,0:T(8,128)(2,1)}, u32[]{:S(2)}, u32[]{:S(2)}) collective-permute-start(bf16[2,12,256,64]{2,3,1,0:T(8,128)(2,1)} %fusion.41), channel_id=1, source_target_pairs={{8,0},{10,2},{12,4},{14,6},{16,8},{18,10},{20,12},{22,14},{24,16},... | collective-permute-start | bytes 2359304 | tf_op jit(solution)/shard_map/ppermute | solution.py:30
  138.1 8.0 %copy-start.14 = (bf16[12,256,256]{1,2,0:T(8,128)(2,1)S(1)}, bf16[12,256,256]{1,2,0:T(8,128)(2,1)}, u32[]{:S(2)}) copy-start(bf16[12,256,256]{1,2,0:T(8,128)(2,1)} %copy-done.13) | copy-start | bytes 4718596
  146.7 16.0 %copy-start.1 = (bf16[1,256,1536]{2,1,0:T(8,128)(2,1)S(1)}, bf16[1,256,1536]{2,1,0:T(8,128)(2,1)}, u32[]{:S(2)}) copy-start(bf16[1,256,1536]{2,1,0:T(8,128)(2,1)} %param.9) | copy-start | bytes 2359300
  (19 other events, 34.4 us)
Sparse Core Ops, SparseCore 0:
  20.2 58.5 all-gather.2
Sparse Core Ops, SparseCore 1:
  80.2 64.2 reduce-scatter.2
  147.1 12.1 reduce-scatter.4

commit v16 on v13

--- a/solution.py
+++ b/solution.py
@@ -51,14 +51,11 @@
         row = (lax.axis_index("seq") // 2) % 2
         later = [i for i in range(count) if (i // 2) % 2 == 1]
         earlier = [i for i in range(count) if (i // 2) % 2 == 0 and i + 2 < count]
-        far = [shift_up(own[k], "seq", 4) for k in range(2)]
-        near = []
-        for k in range(2):
-            direct = lax.ppermute(own[k], "seq", [(i - 2, i) for i in later])
-            relayed = lax.ppermute(far[k], "seq", [(i + 2, i) for i in earlier])
-            near.append(jnp.where(row == 1, direct, relayed))
-        evens[2] = jnp.stack(near)
-        evens[4] = jnp.stack(far)
+        far = shift_up(own, "seq", 4)
+        direct = lax.ppermute(own, "seq", [(i - 2, i) for i in later])
+        relayed = lax.ppermute(far, "seq", [(i + 2, i) for i in earlier])
+        evens[2] = jnp.where(row == 1, direct, relayed)
+        evens[4] = far
     else:
         for dist in range(2, reach + 2, 2):
             evens[dist] = shift_up(own, "seq", dist)

time: 167 us -> 172 us (1.030)
  waiting for transfers between devices: 44.5 us -> 54 us
  starting transfers between devices: 26.9 us -> 17.8 us
  local copies, waits for them, and re-layouts: 18.9 us -> 21.7 us
    ppermute x3 -> x2, waiting for transfers between devices: 13 us -> 22.9 us  [shift_up(): return lax.ppermute(block, axis, route)]
    all_gather x1, waiting for transfers between devices: 8 us -> 0.02 us  [local(): pieces = lax.all_gather(out_weight, ('seq', 'dp'), axis=0, tiled=False)]
    reduce_scatter x1, waiting for transfers between devices: 0.01 us -> 5.8 us  [local(): lax.psum_scatter(partial_weight.astype(jnp.bfloat16), 'seq', scatter_dime...]
    ppermute x4 -> x2, starting transfers between devices: 10.3 us -> 4.64 us  [the longest x1 3.35 us: gather_behind(): relayed = lax.ppermute(far, 'seq', [(i + 2, i) for i in earlier])]
    ppermute x3 -> x2, starting transfers between devices: 8.27 us -> 4.81 us  [shift_up(): return lax.ppermute(block, axis, route)]
    unnamed x101 -> x85, local copies, waits for them, and re-layouts: 13.6 us -> 16.5 us
    select_n x2 -> x0, other arithmetic: 2.11 us -> none  [gather_behind(): near.append(jnp.where(row == 1, direct, relayed))]
    select_n x5, other arithmetic: 0.06 us -> 1.97 us  [frame_labels(): return (jnp.where(outside, -1, utt_index), positions // STRETCH)]
  transfers between devices with their start and end apart: 16 -> 13, of which waited for: 6 -> 5; matrix products, arithmetic and copies ran while one was open for 43% -> 42% of each run, Pallas kernels for 0% -> 0%
where the time goes in v16:
time: 172 us; the launch traced here: 170 us
  waiting for transfers between devices  54 us (31%)
  matrix products  40.6 us (24%)
  local copies, waits for them, and re-layouts  21.7 us (13%)
  other arithmetic  19.4 us (11%)
  starting transfers between devices  17.8 us (10%)
  between operations  16.1 us (9%)
    ppermute x2, waiting for transfers between devices, shift_up(): return lax.ppermute(block, axis, route)  22.9 us
    unnamed x85, local copies, waits for them, and re-layouts  16.5 us
    ppermute x1, waiting for transfers between devices, return_behind(): relayed = lax.ppermute(near, 'seq', [(i, i + 2) for i in earlier])  14.4 us
    ppermute x1, waiting for transfers between devices, gather_behind(): relayed = lax.ppermute(far, 'seq', [(i + 2, i) for i in earlier])  10.8 us
    dot_general x5, matrix products, local(): jnp.einsum('hqe,hke->hqk', query_heads, held[dist][0], preferred_element_...  7.37 us
    dot_general x5, matrix products, local(): jnp.einsum('hqk,hqe->hke', prob_back, grad_heads, preferred_element_type=...  6.77 us
    dot_general x5, matrix products, local(): jnp.einsum('hqe,hke->hqk', grad_heads, value_block, preferred_element_typ...  6.58 us
    dot_general x5, matrix products, local(): jnp.einsum('hqk,hke->hqe', expo_full.astype(jnp.bfloat16), held[dist][1],...  6.26 us
  transfers between devices with their start and end apart: 13, of which 5 were waited for; matrix products, arithmetic and copies ran while one was open for 42% of the time, Pallas kernels for 0%

profile of v16, /device:TPU:4, one launch (start us, length us, event | category | flops | bytes accessed | tf_op | source)
XLA Modules:
  0.0 169.6 jit_solution(2271383260600595381)
XLA Ops:
  8.1 1.2 copy.81
  9.3 1.2 copy.79
  10.6 3.5 %collective-permute-start.1 = (bf16[2,12,256,64]{2,3,1,0:T(8,128)(2,1)S(1)}, bf16[2,12,256,64]{2,3,1,0:T(8,128)(2,1)S(1)}, u32[]{:S(2)}, u32[]{:S(2)}) collective-permute-start(bf16[2,12,256,64]{2,3,1,0:T(8,128)(2,1)S(1)} %pad_maximum_fusion.2), channel_id=1, source_target_pairs={{0,8},{2,10},{4,12},{6,14},{8,16},{10,18},{12,20},{14,22},{16,24},... | collective-permute-start | bytes 2359304 | tf_op jit(solution)/shard_map/ppermute | solution.py:18
  14.1 1.3 collective-permute-start
  16.4 15.2 %collective-permute-done.1 = bf16[2,12,256,64]{2,3,1,0:T(8,128)(2,1)S(1)} collective-permute-done((bf16[2,12,256,64]{2,3,1,0:T(8,128)(2,1)S(1)}, bf16[2,12,256,64]{2,3,1,0:T(8,128)(2,1)S(1)}, u32[]{:S(2)}, u32[]{:S(2)}) %collective-permute-start.1) | collective-permute-done | bytes 786464 | tf_op jit(solution)/shard_map/ppermute | solution.py:18
  31.6 3.4 %collective-permute-start.2 = (bf16[2,12,256,64]{2,3,1,0:T(8,128)(2,1)S(1)}, bf16[2,12,256,64]{2,3,1,0:T(8,128)(2,1)}, u32[]{:S(2)}, u32[]{:S(2)}) collective-permute-start(bf16[2,12,256,64]{2,3,1,0:T(8,128)(2,1)S(1)} %collective-permute-done.1), channel_id=1, source_target_pairs={{4,0},{6,2},{12,8},{14,10},{20,16},{22,18},{28,24},{30,26},{5,1},{... | collective-permute-start | bytes 2359304 | tf_op jit(solution)/shard_map/ppermute | solution.py:56
  35.5 1.2 copy.78
  38.1 1.9 %compare_and_fusion.3 = (pred[256,256]{0,1:T(8,128)(4,1)}, pred[256,256]{0,1:T(8,128)(4,1)}, pred[256,256]{0,1:T(8,128)(4,1)}, pred[256,256]{0,1:T(8,128)(4,1)}, pred[256,256]{0,1:T(8,128)(4,1)S(1)}) fusion(s32[256]{0:T(256)S(1)} %get-tuple-element.57, s32[256]{0:T(256)S(1)} %get-tuple-element.58, s32[256]{0:T(256)S(1)} %get-tuple-element.59, ...), kind=kLoop, calls=%fused_computation.149 | loop fusion | flops 983040 | bytes 337920 | tf_op jit(solution)/shard_map/and | solution.py:132
  40.0 10.8 %collective-permute-done.2 = bf16[2,12,256,64]{2,3,1,0:T(8,128)(2,1)} collective-permute-done((bf16[2,12,256,64]{2,3,1,0:T(8,128)(2,1)S(1)}, bf16[2,12,256,64]{2,3,1,0:T(8,128)(2,1)}, u32[]{:S(2)}, u32[]{:S(2)}) %collective-permute-start.2) | collective-permute-done | bytes 786464 | tf_op jit(solution)/shard_map/ppermute | solution.py:56
  50.8 2.1 %broadcast_select_fusion.2 = (bf16[2,12,256,64]{2,3,1,0:T(8,128)(2,1)}, bf16[2,12,256,64]{2,3,1,0:T(8,128)(2,1)S(1)}) fusion(pred[]{:T(512)S(6)} %eq.100, bf16[1,12,256,64]{2,3,1,0:T(8,128)(2,1)S(1)} %bitcast.269, bf16[1,12,256,64]{2,3,1,0:T(8,128)(2,1)S(1)} %bitcast.262, bf16[2,12,256,64]{2,3,1,0:T(8,128)(2,1)} %collective-permute-done, ...), kind=kLoop, calls=%fused_computation.131 | loop fusion | flops 1179648 | bytes 3932162 | tf_op jit(solution)/shard_map/jit(_where)/select_n | solution.py:63
  52.9 1.0 broadcast_select_fusion.1
  53.9 2.3 %select_reduce_fusion = (f32[12,256]{1,0:T(8,128)S(1)}, f32[12,256,256]{1,2,0:T(8,128)}) fusion(pred[256,256]{0,1:T(8,128)(4,1)S(1)} %get-tuple-element.44, bf16[12,256,64]{1,2,0:T(8,128)(2,1)S(1)} %bitcast.251, bf16[12,256,64]{1,2,0:T(8,128)(2,1)S(1)} %bitcast.263), kind=kOutput, calls=%fused_computation.31 | convolution fusion | flops 103019520 | bytes 4009984 | tf_op jit(solution)/shard_map/hqe,hke->hqk/dot_general | solution.py:139
  56.7 1.6 fusion.11
  59.1 2.1 %fusion.10 = (f32[12,256]{1,0:T(8,128)S(1)}, f32[12,256,256]{2,1,0:T(8,128)S(1)}) fusion(pred[256,256]{0,1:T(8,128)(4,1)S(1)} %copy-done.31, bf16[12,256,64]{1,2,0:T(8,128)(2,1)S(1)} %bitcast.254, bf16[2,12,256,64]{2,3,1,0:T(8,128)(2,1)} %collective-permute-done.4), kind=kOutput, calls=%fused_computation.29 | convolution fusion | flops 103019520 | bytes 4009984 | tf_op jit(solution)/shard_map/hqe,hke->hqk/dot_general | solution.py:139
  62.0 1.8 %copy-done.2 = f32[12,256,256]{1,2,0:T(8,128)S(1)} copy-done((f32[12,256,256]{1,2,0:T(8,128)S(1)}, f32[12,256,256]{1,2,0:T(8,128)}, u32[]{:S(2)}) %copy-start.2) | copy-done | bytes 3145752
  63.7 3.9 %fusion.20 = (f32[12,256]{1,0:T(8,128)S(1)}, f32[12,256]{1,0:T(8,128)S(1)}, f32[12,256]{1,0:T(8,128)S(1)}, f32[12,256]{1,0:T(8,128)S(1)}, f32[12,256]{1,0:T(8,128)S(1)}) fusion(f32[12,256,256]{2,1,0:T(8,128)S(1)} %get-tuple-element.54, f32[12,256]{1,0:T(8,128)S(1)} %maximum_maximum_fusion, pred[256,256]{0,1:T(8,128)(4,1)S(1)} %copy-done.34, ...), kind=kLoop, calls=%fused_computation.41 | loop fusion | flops 19645440 | bytes 16130048 | tf_op jit(solution)/shard_map/reduce_sum | solution.py:152
  69.1 1.9 %fusion.61 = f32[12,256,64]{1,2,0:T(8,128)S(1)} fusion(f32[12,256,256]{2,1,0:T(8,128)S(1)} %get-tuple-element.48, f32[12,256]{1,0:T(8,128)S(1)} %maximum_maximum_fusion, pred[256,256]{0,1:T(8,128)(4,1)S(1)} %copy-done.31, bf16[2,12,256,64]{2,3,1,0:T(8,128)(2,1)} %collective-permute-done.4), kind=kOutput, calls=%fused_computation.81 | convolution fusion | flops 104595456 | bytes 4403200 | tf_op jit(solution)/shard_map/hqk,hke->hqe/dot_general | solution.py:153
  72.8 1.8 %fusion.118 = (bf16[256,12,64]{0,2,1:T(8,128)(2,1)S(1)}, f32[12,256,64]{1,2,0:T(8,128)}) fusion(f32[256,12]{0,1:T(8,128)S(1)} %bitcast.289, f32[12,256,64]{1,2,0:T(8,128)S(1)} %fusion.59, f32[12,256,64]{1,2,0:T(8,128)S(1)} %fusion.61, f32[12,256,64]{1,2,0:T(8,128)S(1)} %fusion.102, f32[12,256,256]{2,1,0:T(8,128)S(1)} %get-tuple-element.50, ...), kind=kOutput, calls=%fused_computation.126 | convolution fusion | flops 105578496 | bytes 7176192 | tf_op jit(solution)/shard_map/hqk,hke->hqe/dot_general | solution.py:153
  75.3 2.2 %fusion.116 = bf16[768,1536]{1,0:T(8,128)(2,1)} fusion(bf16[256,768]{0,1:T(8,128)(2,1)S(1)} %bitcast.273, bf16[1,256,1536]{2,1,0:T(8,128)(2,1)S(1)} %copy-done), kind=kOutput, calls=%fused_computation.123 | convolution fusion | flops 603979776 | bytes 3538944 | tf_op jit(solution)/shard_map/dot_general | solution.py:166
  77.8 3.9 %copy.87 = bf16[16,2,48,768]{3,1,2,0:T(2,128)(2,1)S(1)} copy(bf16[16,2,48,768]{3,2,1,0:T(8,128)(2,1)} %bitcast.272) | data formatting | bytes 4718592 | tf_op jit(solution)/shard_map/reshape | solution.py:118
  82.2 1.4 copy-done.12
  83.6 1.6 convolution_convert_fusion.1
  85.2 1.2 copy.88
  86.4 2.9 %fusion.82 = f32[1,12,256,64]{2,3,1,0:T(8,128)S(1)} fusion(bf16[12,256,64]{1,2,0:T(8,128)(2,1)S(1)} %bitcast.276, f32[12,256,256]{2,1,0:T(8,128)} %copy-done.10, f32[12,256]{1,0:T(8,128)} %get-tuple-element.34, pred[256,256]{0,1:T(8,128)(4,1)} %get-tuple-element.40), kind=kOutput, calls=%fused_computation.96 | convolution fusion | flops 103809024 | bytes 4403200 | tf_op jit(solution)/shard_map/hqk,hqe->hke/dot_general | solution.py:217
  90.9 0.9 copy-done.7
  91.9 1.1 multiply_convert_fusion.2
  93.9 1.1 multiply_convert_fusion
  96.1 1.1 multiply_convert_fusion.3
  98.2 2.1 %multiply_convert_fusion.4 = bf16[12,256,256]{1,2,0:T(8,128)(2,1)S(1)} fusion(f32[12,256,256]{2,1,0:T(8,128)S(1)} %copy-done.9, bf16[12,256,64]{1,2,0:T(8,128)(2,1)S(1)} %bitcast.282, f32[12,256]{1,0:T(8,128)S(1)} %multiply_reduce_fusion, f32[12,256]{1,0:T(8,128)S(1)} %copy-done.37, pred[256,256]{0,1:T(8,128)(4,1)S(1)} %copy-done.33, ...), kind=kOutput, calls=%fused_computation.21 | convolution fusion | flops 105381888 | bytes 5595136 | tf_op jit(solution)/shard_map/hqe,hke->hqk/dot_general | solution.py:205
  103.8 1.1 multiply_convert_fusion.1
  105.3 1.4 convolution_add_fusion.1
  107.7 1.4 fusion.41
  109.1 1.3 collective-permute-start.8
  111.7 1.6 fusion.79
  113.3 5.7 %collective-permute-start.7 = (bf16[2,12,256,64]{2,3,1,0:T(8,128)(2,1)}, bf16[2,12,256,64]{2,3,1,0:T(8,128)(2,1)}, u32[]{:S(2)}, u32[]{:S(2)}) collective-permute-start(bf16[2,12,256,64]{2,3,1,0:T(8,128)(2,1)} %fusion.41), channel_id=1, source_target_pairs={{4,0},{6,2},{12,8},{14,10},{20,16},{22,18},{28,24},{30,26},{5,1},{... | collective-permute-start | bytes 2359304 | tf_op jit(solution)/shard_map/ppermute | solution.py:92
  119.0 14.4 %collective-permute-done.8 = bf16[2,12,256,64]{2,3,1,0:T(8,128)(2,1)S(1)} collective-permute-done((bf16[2,12,256,64]{2,3,1,0:T(8,128)(2,1)}, bf16[2,12,256,64]{2,3,1,0:T(8,128)(2,1)S(1)}, u32[]{:S(2)}, u32[]{:S(2)}) %collective-permute-start.8) | collective-permute-done | bytes 786464 | tf_op jit(solution)/shard_map/ppermute | solution.py:93
  133.4 1.3 fusion.43
  134.7 1.3 collective-permute-start.9
  136.0 1.7 fusion.12
  137.7 1.2 fusion.114
  138.9 5.8 %reduce-scatter.3.cloned.1.call-done = bf16[48,1536]{1,0:T(8,128)(2,1)} async-done(((bf16[768,1536]{1,0:T(8,128)(2,1)}), bf16[48,1536]{1,0:T(8,128)(2,1)}) %reduce-scatter.3.cloned.1.call-update) | async-done | bytes 147472 | tf_op jit(solution)/shard_map/reduce_scatter | solution.py:177
  144.7 1.6 convert_element_type.187
  146.4 2.0 %fusion.99 = f32[1,12,256,64]{2,3,1,0:T(8,128)S(1)} fusion(bf16[12,256,256]{1,2,0:T(8,128)(2,1)} %copy-done.16, bf16[12,256,64]{1,2,0:T(8,128)(2,1)S(1)} %bitcast.260), kind=kOutput, calls=%fused_computation.112 | convolution fusion | flops 100859904 | bytes 2752512 | tf_op jit(solution)/shard_map/hqk,hqe->hke/dot_general | solution.py:214
  148.4 2.0 %copy.109 = bf16[1,256,768]{2,1,0:T(8,128)(2,1)} copy(bf16[1,256,768]{1,2,0:T(8,128)(2,1)} %bitcast.275) | data formatting | bytes 786432
  150.4 7.7 %collective-permute-done.9 = bf16[2,12,256,64]{2,3,1,0:T(8,128)(2,1)} collective-permute-done((bf16[2,12,256,64]{2,3,1,0:T(8,128)(2,1)}, bf16[2,12,256,64]{2,3,1,0:T(8,128)(2,1)}, u32[]{:S(2)}, u32[]{:S(2)}) %collective-permute-start.9) | collective-permute-done | bytes 786464 | tf_op jit(solution)/shard_map/ppermute | solution.py:18
  158.1 2.1 %fusion.40 = bf16[2,12,256,64]{2,3,1,0:T(8,128)(2,1)S(1)} fusion(f32[1,12,256,64]{2,3,1,0:T(8,128)} %fusion.79, f32[1,12,256,64]{2,3,1,0:T(8,128)S(1)} %fusion.99, bf16[2,12,256,64]{2,3,1,0:T(8,128)(2,1)} %collective-permute-done.9, bf16[2,12,256,64]{2,3,1,0:T(8,128)(2,1)} %collective-permute-done.7, f32[2,12,256,64]{2,3,1,0:T(8,128)S(1)} %copy-done.15, ...), kind=kLoop, calls=%fused_computation.57 | loop fusion | flops 3538944 | bytes 5505026 | tf_op jit(solution)/shard_map/convert.1
  160.3 0.9 copy.110
  161.2 0.9 copy.111
  (128 shorter events, 20.3 us)
Async XLA Ops:
  8.0 67.3 %copy-start = (bf16[1,256,1536]{2,1,0:T(8,128)(2,1)S(1)}, bf16[1,256,1536]{2,1,0:T(8,128)(2,1)}, u32[]{:S(2)}) copy-start(bf16[1,256,1536]{2,1,0:T(8,128)(2,1)} %param.9) | copy-start | bytes 2359300
  8.0 7.5 %copy-start.38 = (s32[1,8]{1,0:T(1,128)S(1)}, s32[1,8]{1,0:T(1,128)}, u32[]{:S(2)}) copy-start(s32[1,8]{1,0:T(1,128)} %param.10) | copy-start | bytes 100
  8.0 69.8 %all-gather.3.cloned.1.call-start = ((), (), s32[]{:S(2)}) async-start(), calls=%async_computation.4 | async-start | bytes 2433024 | tf_op jit(solution)/shard_map/all_gather | solution.py:116
  10.6 21.0 %collective-permute-start.1 = (bf16[2,12,256,64]{2,3,1,0:T(8,128)(2,1)S(1)}, bf16[2,12,256,64]{2,3,1,0:T(8,128)(2,1)S(1)}, u32[]{:S(2)}, u32[]{:S(2)}) collective-permute-start(bf16[2,12,256,64]{2,3,1,0:T(8,128)(2,1)S(1)} %pad_maximum_fusion.2), channel_id=1, source_target_pairs={{0,8},{2,10},{4,12},{6,14},{8,16},{10,18},{12,20},{14,22},{16,24},... | collective-permute-start | bytes 2359304 | tf_op jit(solution)/shard_map/ppermute | solution.py:18
  14.1 25.9 %collective-permute-start = (bf16[2,12,256,64]{2,3,1,0:T(8,128)(2,1)S(1)}, bf16[2,12,256,64]{2,3,1,0:T(8,128)(2,1)}, u32[]{:S(2)}, u32[]{:S(2)}) collective-permute-start(bf16[2,12,256,64]{2,3,1,0:T(8,128)(2,1)S(1)} %pad_maximum_fusion.2), channel_id=1, source_target_pairs={{0,4},{2,6},{8,12},{10,14},{16,20},{18,22},{24,28},{26,30},{1,5},{... | collective-permute-start | bytes 2359304 | tf_op jit(solution)/shard_map/ppermute | solution.py:55
  15.4 129.3 %reduce-scatter.3.cloned.1.call-start = ((), (), s32[]{:S(2)}) async-start(), calls=%async_computation.2 | async-start | bytes 2506752 | tf_op jit(solution)/shard_map/reduce_scatter | solution.py:177
  31.6 19.2 %collective-permute-start.2 = (bf16[2,12,256,64]{2,3,1,0:T(8,128)(2,1)S(1)}, bf16[2,12,256,64]{2,3,1,0:T(8,128)(2,1)}, u32[]{:S(2)}, u32[]{:S(2)}) collective-permute-start(bf16[2,12,256,64]{2,3,1,0:T(8,128)(2,1)S(1)} %collective-permute-done.1), channel_id=1, source_target_pairs={{4,0},{6,2},{12,8},{14,10},{20,16},{22,18},{28,24},{30,26},{5,1},{... | collective-permute-start | bytes 2359304 | tf_op jit(solution)/shard_map/ppermute | solution.py:56
  39.9 13.9 %copy-start.24 = (pred[256,256]{0,1:T(8,128)(4,1)}, pred[256,256]{0,1:T(8,128)(4,1)S(1)}, u32[]{:S(2)}) copy-start(pred[256,256]{0,1:T(8,128)(4,1)S(1)} %get-tuple-element.44) | copy-start | bytes 196612
  53.9 5.2 %collective-permute-start.4 = (bf16[2,12,256,64]{2,3,1,0:T(8,128)(2,1)}, bf16[2,12,256,64]{2,3,1,0:T(8,128)(2,1)}, u32[]{:S(2)}, u32[]{:S(2)}) collective-permute-start(bf16[2,12,256,64]{2,3,1,0:T(8,128)(2,1)} %broadcast_select_fusion.1), channel_id=1, source_target_pairs={{0,2},{2,0},{4,6},{6,4},{8,10},{10,8},{12,14},{14,12},{16,18},{18,... | collective-permute-start | bytes 2359304 | tf_op jit(solution)/shard_map/ppermute | solution.py:23
  56.2 2.1 %copy-start.29 = (pred[256,256]{0,1:T(8,128)(4,1)S(1)}, pred[256,256]{0,1:T(8,128)(4,1)}, u32[]{:S(2)}) copy-start(pred[256,256]{0,1:T(8,128)(4,1)} %get-tuple-element.41) | copy-start | bytes 196612
  56.2 5.0 %collective-permute-start.3 = (bf16[2,12,256,64]{2,3,1,0:T(8,128)(2,1)}, bf16[2,12,256,64]{2,3,1,0:T(8,128)(2,1)S(1)}, u32[]{:S(2)}, u32[]{:S(2)}) collective-permute-start(bf16[2,12,256,64]{2,3,1,0:T(8,128)(2,1)} %get-tuple-element.36), channel_id=1, source_target_pairs={{0,2},{2,0},{4,6},{6,4},{8,10},{10,8},{12,14},{14,12},{16,18},{18,... | collective-permute-start | bytes 2359304 | tf_op jit(solution)/shard_map/ppermute | solution.py:23
  56.7 2.3 %copy-start.31 = (pred[256,256]{0,1:T(8,128)(4,1)S(1)}, pred[256,256]{0,1:T(8,128)(4,1)}, u32[]{:S(2)}) copy-start(pred[256,256]{0,1:T(8,128)(4,1)} %get-tuple-element.42) | copy-start | bytes 196612
  58.3 12.7 %copy-start.4 = (f32[12,256,256]{2,1,0:T(8,128)}, f32[12,256,256]{2,1,0:T(8,128)S(1)}, u32[]{:S(2)}) copy-start(f32[12,256,256]{2,1,0:T(8,128)S(1)} %get-tuple-element.46) | copy-start | bytes 9437188
  58.3 2.9 %copy-start.34 = (pred[256,256]{0,1:T(8,128)(4,1)S(1)}, pred[256,256]{0,1:T(8,128)(4,1)}, u32[]{:S(2)}) copy-start(pred[256,256]{0,1:T(8,128)(4,1)} %get-tuple-element.40) | copy-start | bytes 196612
  59.0 13.8 %copy-start.6 = (f32[12,256,256]{2,1,0:T(8,128)}, f32[12,256,256]{2,1,0:T(8,128)S(1)}, u32[]{:S(2)}) copy-start(f32[12,256,256]{2,1,0:T(8,128)S(1)} %get-tuple-element.50) | copy-start | bytes 9437188
  59.1 4.7 %copy-start.2 = (f32[12,256,256]{1,2,0:T(8,128)S(1)}, f32[12,256,256]{1,2,0:T(8,128)}, u32[]{:S(2)}) copy-start(f32[12,256,256]{1,2,0:T(8,128)} %get-tuple-element.52) | copy-start | bytes 9437188
  59.1 4.7 %copy-start.25 = (pred[256,256]{0,1:T(8,128)(4,1)S(1)}, pred[256,256]{0,1:T(8,128)(4,1)}, u32[]{:S(2)}) copy-start(pred[256,256]{0,1:T(8,128)(4,1)} %copy-done.24) | copy-start | bytes 196612
  59.1 4.7 %copy-start.27 = (pred[256,256]{0,1:T(8,128)(4,1)S(1)}, pred[256,256]{0,1:T(8,128)(4,1)}, u32[]{:S(2)}) copy-start(pred[256,256]{0,1:T(8,128)(4,1)} %get-tuple-element.43) | copy-start | bytes 196612
  61.2 7.9 %copy-start.8 = (f32[12,256,256]{2,1,0:T(8,128)}, f32[12,256,256]{2,1,0:T(8,128)S(1)}, u32[]{:S(2)}) copy-start(f32[12,256,256]{2,1,0:T(8,128)S(1)} %get-tuple-element.48) | copy-start | bytes 9437188
  61.2 10.6 %copy-start.22 = (bf16[2,12,256,64]{2,3,1,0:T(8,128)(2,1)}, bf16[2,12,256,64]{2,3,1,0:T(8,128)(2,1)S(1)}, u32[]{:S(2)}) copy-start(bf16[2,12,256,64]{2,3,1,0:T(8,128)(2,1)S(1)} %collective-permute-done.3) | copy-start | bytes 2359300
  61.9 9.9 %copy-start.10 = (f32[12,256,256]{2,1,0:T(8,128)}, f32[12,256,256]{2,1,0:T(8,128)S(1)}, u32[]{:S(2)}) copy-start(f32[12,256,256]{2,1,0:T(8,128)S(1)} %get-tuple-element.54) | copy-start | bytes 9437188
  77.6 84.6 %reduce-scatter.5.cloned.1.call-start = ((), (), s32[]{:S(2)}) async-start(), calls=%async_computation.3 | async-start | bytes 442368 | tf_op jit(solution)/shard_map/reduce_scatter | solution.py:180
  82.2 1.4 copy-start.12
  85.2 4.1 %copy-start.32 = (pred[256,256]{0,1:T(8,128)(4,1)S(1)}, pred[256,256]{0,1:T(8,128)(4,1)}, u32[]{:S(2)}) copy-start(pred[256,256]{0,1:T(8,128)(4,1)} %get-tuple-element.42) | copy-start | bytes 196612
  85.2 4.1 %copy-start.36 = (f32[12,256]{1,0:T(8,128)S(1)}, f32[12,256]{1,0:T(8,128)}, u32[]{:S(2)}) copy-start(f32[12,256]{1,0:T(8,128)} %get-tuple-element.34) | copy-start | bytes 36868
  86.4 8.6 %copy-start.19 = (bf16[256,768]{0,1:T(8,128)(2,1)}, bf16[256,768]{0,1:T(8,128)(2,1)S(1)}, u32[]{:S(2)}) copy-start(bf16[256,768]{0,1:T(8,128)(2,1)S(1)} %copy.88) | copy-start | bytes 1179652
  86.4 3.2 %copy-start.9 = (f32[12,256,256]{2,1,0:T(8,128)S(1)}, f32[12,256,256]{2,1,0:T(8,128)}, u32[]{:S(2)}) copy-start(f32[12,256,256]{2,1,0:T(8,128)} %copy-done.8) | copy-start | bytes 9437188
  89.6 1.2 copy-start.21
  89.6 2.3 %copy-start.7 = (f32[12,256,256]{2,1,0:T(8,128)S(1)}, f32[12,256,256]{2,1,0:T(8,128)}, u32[]{:S(2)}) copy-start(f32[12,256,256]{2,1,0:T(8,128)} %copy-done.6) | copy-start | bytes 9437188
  89.6 2.3 %copy-start.30 = (pred[256,256]{0,1:T(8,128)(4,1)S(1)}, pred[256,256]{0,1:T(8,128)(4,1)}, u32[]{:S(2)}) copy-start(pred[256,256]{0,1:T(8,128)(4,1)} %get-tuple-element.41) | copy-start | bytes 196612
  91.9 2.0 %copy-start.3 = (f32[12,256,256]{1,2,0:T(8,128)S(1)}, f32[12,256,256]{1,2,0:T(8,128)}, u32[]{:S(2)}) copy-start(f32[12,256,256]{1,2,0:T(8,128)} %get-tuple-element.52) | copy-start | bytes 9437188
  91.9 2.0 %copy-start.26 = (pred[256,256]{0,1:T(8,128)(4,1)S(1)}, pred[256,256]{0,1:T(8,128)(4,1)}, u32[]{:S(2)}) copy-start(pred[256,256]{0,1:T(8,128)(4,1)} %copy-done.24) | copy-start | bytes 196612
  93.9 2.0 %copy-start.11 = (f32[12,256,256]{2,1,0:T(8,128)S(1)}, f32[12,256,256]{2,1,0:T(8,128)}, u32[]{:S(2)}) copy-start(f32[12,256,256]{2,1,0:T(8,128)} %copy-done.10) | copy-start | bytes 9437188
  93.9 2.2 %copy-start.23 = (bf16[2,12,256,64]{2,3,1,0:T(8,128)(2,1)S(1)}, bf16[2,12,256,64]{2,3,1,0:T(8,128)(2,1)}, u32[]{:S(2)}) copy-start(bf16[2,12,256,64]{2,3,1,0:T(8,128)(2,1)} %copy-done.22) | copy-start | bytes 2359300
  93.9 2.2 %copy-start.35 = (pred[256,256]{0,1:T(8,128)(4,1)S(1)}, pred[256,256]{0,1:T(8,128)(4,1)}, u32[]{:S(2)}) copy-start(pred[256,256]{0,1:T(8,128)(4,1)} %get-tuple-element.40) | copy-start | bytes 196612
  96.1 5.4 %copy-start.16 = (bf16[12,256,256]{1,2,0:T(8,128)(2,1)}, bf16[12,256,256]{1,2,0:T(8,128)(2,1)S(1)}, u32[]{:S(2)}) copy-start(bf16[12,256,256]{1,2,0:T(8,128)(2,1)S(1)} %multiply_convert_fusion) | copy-start | bytes 4718596
  98.0 9.7 %collective-permute-start.5 = (f32[2,12,256,64]{2,3,1,0:T(8,128)S(1)}, f32[2,12,256,64]{2,3,1,0:T(8,128)S(1)}, u32[]{:S(2)}, u32[]{:S(2)}) collective-permute-start(f32[2,12,256,64]{2,3,1,0:T(8,128)S(1)} %pad_maximum_fusion), channel_id=1, source_target_pairs={{0,2},{2,0},{4,6},{6,4},{8,10},{10,8},{12,14},{14,12},{16,18},{18,... | collective-permute-start | bytes 4718600 | tf_op jit(solution)/shard_map/ppermute | solution.py:23
  101.1 6.6 %collective-permute-start.6 = (f32[2,12,256,64]{2,3,1,0:T(8,128)S(1)}, f32[2,12,256,64]{2,3,1,0:T(8,128)S(1)}, u32[]{:S(2)}, u32[]{:S(2)}) collective-permute-start(f32[2,12,256,64]{2,3,1,0:T(8,128)S(1)} %pad_maximum_fusion.1), channel_id=1, source_target_pairs={{0,2},{2,0},{4,6},{6,4},{8,10},{10,8},{12,14},{14,12},{16,18},{18,... | collective-permute-start | bytes 4718600 | tf_op jit(solution)/shard_map/ppermute | solution.py:23
  101.9 1.9 %copy-start.5 = (f32[12,256,256]{2,1,0:T(8,128)S(1)}, f32[12,256,256]{2,1,0:T(8,128)}, u32[]{:S(2)}) copy-start(f32[12,256,256]{2,1,0:T(8,128)} %copy-done.4) | copy-start | bytes 9437188
  101.9 1.9 %copy-start.28 = (pred[256,256]{0,1:T(8,128)(4,1)S(1)}, pred[256,256]{0,1:T(8,128)(4,1)}, u32[]{:S(2)}) copy-start(pred[256,256]{0,1:T(8,128)(4,1)} %get-tuple-element.43) | copy-start | bytes 196612
  107.7 3.3 %copy-start.14 = (f32[2,12,256,64]{2,3,1,0:T(8,128)}, f32[2,12,256,64]{2,3,1,0:T(8,128)S(1)}, u32[]{:S(2)}) copy-start(f32[2,12,256,64]{2,3,1,0:T(8,128)S(1)} %collective-permute-done.5) | copy-start | bytes 4718596
  109.1 24.3 %collective-permute-start.8 = (bf16[2,12,256,64]{2,3,1,0:T(8,128)(2,1)}, bf16[2,12,256,64]{2,3,1,0:T(8,128)(2,1)S(1)}, u32[]{:S(2)}, u32[]{:S(2)}) collective-permute-start(bf16[2,12,256,64]{2,3,1,0:T(8,128)(2,1)} %fusion.41), channel_id=1, source_target_pairs={{0,4},{2,6},{8,12},{10,14},{16,20},{18,22},{24,28},{26,30},{1,5},{... | collective-permute-start | bytes 2359304 | tf_op jit(solution)/shard_map/ppermute | solution.py:93
  113.3 22.7 %copy-start.13 = (bf16[96,8,2,768]{3,1,2,0:T(8,128)(2,1)S(1)}, bf16[96,8,2,768]{3,1,2,0:T(8,128)(2,1)}, u32[]{:S(2)}) copy-start(bf16[96,8,2,768]{3,1,2,0:T(8,128)(2,1)} %copy-done.12) | copy-start | bytes 7077892
  113.3 22.8 %copy-start.18 = (bf16[256,12,64]{0,2,1:T(8,128)(2,1)S(1)}, bf16[256,12,64]{0,2,1:T(8,128)(2,1)}, u32[]{:S(2)}) copy-start(bf16[256,12,64]{0,2,1:T(8,128)(2,1)} %copy-done.17) | copy-start | bytes 1179652
  113.3 37.1 %collective-permute-start.7 = (bf16[2,12,256,64]{2,3,1,0:T(8,128)(2,1)}, bf16[2,12,256,64]{2,3,1,0:T(8,128)(2,1)}, u32[]{:S(2)}, u32[]{:S(2)}) collective-permute-start(bf16[2,12,256,64]{2,3,1,0:T(8,128)(2,1)} %fusion.41), channel_id=1, source_target_pairs={{4,0},{6,2},{12,8},{14,10},{20,16},{22,18},{28,24},{30,26},{5,1},{... | collective-permute-start | bytes 2359304 | tf_op jit(solution)/shard_map/ppermute | solution.py:92
  134.7 23.4 %collective-permute-start.9 = (bf16[2,12,256,64]{2,3,1,0:T(8,128)(2,1)}, bf16[2,12,256,64]{2,3,1,0:T(8,128)(2,1)}, u32[]{:S(2)}, u32[]{:S(2)}) collective-permute-start(bf16[2,12,256,64]{2,3,1,0:T(8,128)(2,1)} %fusion.43), channel_id=1, source_target_pairs={{8,0},{10,2},{12,4},{14,6},{16,8},{18,10},{20,12},{22,14},{24,16},... | collective-permute-start | bytes 2359304 | tf_op jit(solution)/shard_map/ppermute | solution.py:18
  138.9 19.2 %copy-start.15 = (f32[2,12,256,64]{2,3,1,0:T(8,128)S(1)}, f32[2,12,256,64]{2,3,1,0:T(8,128)}, u32[]{:S(2)}) copy-start(f32[2,12,256,64]{2,3,1,0:T(8,128)} %copy-done.14) | copy-start | bytes 4718596
  148.4 13.8 %copy-start.1 = (bf16[1,256,1536]{2,1,0:T(8,128)(2,1)S(1)}, bf16[1,256,1536]{2,1,0:T(8,128)(2,1)}, u32[]{:S(2)}) copy-start(bf16[1,256,1536]{2,1,0:T(8,128)(2,1)} %param.9) | copy-start | bytes 2359300
  (4 other events, 3.7 us)
Sparse Core Ops, SparseCore 0:
  15.5 60.0 all-gather.2
Sparse Core Ops, SparseCore 1:
  77.6 67.0 reduce-scatter.2
  147.4 12.1 reduce-scatter.4

commit v17 on v14

--- a/solution.py
+++ b/solution.py
@@ -86,6 +86,20 @@
         from_core0 = received[dist // 2 - 1] if dist >= 2 and dist // 2 - 1 < len(odds) else zero
         own = parts[dist] if dist <= reach else zero
         summed[dist] = own + jnp.where(core == 0, from_core1, from_core0)
+    count = lax.axis_size("seq")
+    if reach == 4 and count % 4 == 0:
+        row = (lax.axis_index("seq") // 2) % 2
+        later = [i for i in range(count) if (i // 2) % 2 == 1]
+        earlier = [i for i in range(count) if (i // 2) % 2 == 0 and i + 2 < count]
+        pieces = []
+        for k in range(2):
+            near = summed[2][k].astype(jnp.bfloat16)
+            direct = lax.ppermute(near, "seq", [(i, i - 2) for i in later])
+            relayed = lax.ppermute(near, "seq", [(i, i + 2) for i in earlier])
+            far = summed[4][k] + jnp.where(row == 1, relayed.astype(jnp.float32), 0.0)
+            piece = summed[0][k] + jnp.where(row == 0, direct.astype(jnp.float32), 0.0)
+            pieces.append(piece + shift_up(far.astype(jnp.bfloat16), "seq", -4).astype(jnp.float32))
+        return jnp.stack(pieces)
     total = summed[0]
     for dist in range(2, reach + 2, 2):
         total = total + shift_up(summed[dist].astype(jnp.bfloat16), "seq", -dist).astype(jnp.float32)

time: 168 us -> 174 us (1.036)
  the two profiles are of different devices: /device:TPU:0 before, /device:TPU:4 now
where the time goes in v17:
time: 174 us; the launch traced here: 173 us
  waiting for transfers between devices  46.1 us (26%)
  matrix products  40.5 us (23%)
  starting transfers between devices  29.4 us (17%)
  local copies, waits for them, and re-layouts  20.8 us (12%)
  other arithmetic  20 us (11%)
  between operations  16.4 us (9%)
    reduce_scatter x1, waiting for transfers between devices, local(): lax.psum_scatter(partial_weight.astype(jnp.bfloat16), 'seq', scatter_dime...  15.5 us
    unnamed x103, local copies, waits for them, and re-layouts  14.7 us
    ppermute x4, waiting for transfers between devices, shift_up(): return lax.ppermute(block, axis, route)  11.4 us
    ppermute x2, waiting for transfers between devices, gather_behind(): relayed = lax.ppermute(far[k], 'seq', [(i + 2, i) for i in earlier])  9.75 us
    ppermute x4, starting transfers between devices, shift_up(): return lax.ppermute(block, axis, route)  9.56 us
    all_gather x1, waiting for transfers between devices, local(): pieces = lax.all_gather(out_weight, ('seq', 'dp'), axis=0, tiled=False)  8.09 us
    ppermute x2, starting transfers between devices, gather_behind(): relayed = lax.ppermute(far[k], 'seq', [(i + 2, i) for i in earlier])  7.76 us
    dot_general x5, matrix products, local(): jnp.einsum('hqe,hke->hqk', grad_heads, value_block, preferred_element_typ...  6.8 us
  transfers between devices with their start and end apart: 19, of which 8 were waited for; matrix products, arithmetic and copies ran while one was open for 42% of the time, Pallas kernels for 0%

profile of v17, /device:TPU:4, one launch (start us, length us, event | category | flops | bytes accessed | tf_op | source)
XLA Modules:
  0.0 173.2 jit_solution(9567825270967352009)
XLA Ops:
  8.1 1.2 copy.81
  9.3 3.5 %collective-permute-start.1 = (bf16[12,256,64]{1,2,0:T(8,128)(2,1)S(1)}, bf16[12,256,64]{1,2,0:T(8,128)(2,1)S(1)}, u32[]{:S(2)}, u32[]{:S(2)}) collective-permute-start(bf16[12,256,64]{1,2,0:T(8,128)(2,1)S(1)} %bitcast.260), channel_id=1, source_target_pairs={{0,8},{2,10},{4,12},{6,14},{8,16},{10,18},{12,20},{14,22},{16,24},... | collective-permute-start | bytes 1179656 | tf_op jit(solution)/shard_map/ppermute | solution.py:18
  12.8 1.3 collective-permute-start
  14.1 1.2 copy.83
  15.3 3.5 %collective-permute-start.4 = (bf16[12,256,64]{1,2,0:T(8,128)(2,1)S(1)}, bf16[12,256,64]{1,2,0:T(8,128)(2,1)S(1)}, u32[]{:S(2)}, u32[]{:S(2)}) collective-permute-start(bf16[12,256,64]{1,2,0:T(8,128)(2,1)S(1)} %bitcast.269), channel_id=1, source_target_pairs={{0,8},{2,10},{4,12},{6,14},{8,16},{10,18},{12,20},{14,22},{16,24},... | collective-permute-start | bytes 1179656 | tf_op jit(solution)/shard_map/ppermute | solution.py:18
  18.8 1.3 collective-permute-start.3
  21.2 1.2 copy.80
  22.5 5.3 %collective-permute-start.2 = (bf16[12,256,64]{1,2,0:T(8,128)(2,1)S(1)}, bf16[12,256,64]{1,2,0:T(8,128)(2,1)S(1)}, u32[]{:S(2)}, u32[]{:S(2)}) collective-permute-start(bf16[12,256,64]{1,2,0:T(8,128)(2,1)S(1)} %collective-permute-done.1), channel_id=1, source_target_pairs={{4,0},{6,2},{12,8},{14,10},{20,16},{22,18},{28,24},{30,26},{5,1},{... | collective-permute-start | bytes 1179656 | tf_op jit(solution)/shard_map/ppermute | solution.py:58
  27.8 1.7 %collective-permute-done.4 = bf16[12,256,64]{1,2,0:T(8,128)(2,1)S(1)} collective-permute-done((bf16[12,256,64]{1,2,0:T(8,128)(2,1)S(1)}, bf16[12,256,64]{1,2,0:T(8,128)(2,1)S(1)}, u32[]{:S(2)}, u32[]{:S(2)}) %collective-permute-start.4) | collective-permute-done | bytes 393248 | tf_op jit(solution)/shard_map/ppermute | solution.py:18
  29.6 2.4 %collective-permute-start.5 = (bf16[12,256,64]{1,2,0:T(8,128)(2,1)S(1)}, bf16[12,256,64]{1,2,0:T(8,128)(2,1)S(1)}, u32[]{:S(2)}, u32[]{:S(2)}) collective-permute-start(bf16[12,256,64]{1,2,0:T(8,128)(2,1)S(1)} %collective-permute-done.4), channel_id=1, source_target_pairs={{4,0},{6,2},{12,8},{14,10},{20,16},{22,18},{28,24},{30,26},{5,1},{... | collective-permute-start | bytes 1179656 | tf_op jit(solution)/shard_map/ppermute | solution.py:58
  33.4 4.4 %collective-permute-done.2 = bf16[12,256,64]{1,2,0:T(8,128)(2,1)S(1)} collective-permute-done((bf16[12,256,64]{1,2,0:T(8,128)(2,1)S(1)}, bf16[12,256,64]{1,2,0:T(8,128)(2,1)S(1)}, u32[]{:S(2)}, u32[]{:S(2)}) %collective-permute-start.2) | collective-permute-done | bytes 393248 | tf_op jit(solution)/shard_map/ppermute | solution.py:58
  39.0 5.3 %collective-permute-done.5 = bf16[12,256,64]{1,2,0:T(8,128)(2,1)S(1)} collective-permute-done((bf16[12,256,64]{1,2,0:T(8,128)(2,1)S(1)}, bf16[12,256,64]{1,2,0:T(8,128)(2,1)S(1)}, u32[]{:S(2)}, u32[]{:S(2)}) %collective-permute-start.5) | collective-permute-done | bytes 393248 | tf_op jit(solution)/shard_map/ppermute | solution.py:58
  45.3 2.5 %maximum_select_fusion = (bf16[2,12,256,64]{2,3,1,0:T(8,128)(2,1)}, bf16[2,12,256,64]{2,3,1,0:T(8,128)(2,1)}) fusion(bf16[1,12,256,64]{2,3,1,0:T(8,128)(2,1)S(1)} %bitcast.271, bf16[1,12,256,64]{2,3,1,0:T(8,128)(2,1)S(1)} %bitcast.262, pred[]{:T(512)S(6)} %eq.103, bf16[1,12,256,64]{2,3,1,0:T(8,128)(2,1)S(1)} %bitcast.274, ...), kind=kLoop, calls=%fused_computation.127 | loop fusion | flops 1966080 | bytes 3932161 | tf_op jit(solution)/shard_map/jit(_where)/select_n | solution.py:66
  47.8 2.3 %select_reduce_fusion.1 = (f32[12,256]{1,0:T(8,128)S(1)}, f32[12,256,256]{1,2,0:T(8,128)}) fusion(pred[256,256]{0,1:T(8,128)(4,1)S(1)} %get-tuple-element.51, bf16[12,256,64]{1,2,0:T(8,128)(2,1)S(1)} %bitcast.246, bf16[12,256,64]{1,2,0:T(8,128)(2,1)S(1)} %bitcast.263), kind=kOutput, calls=%fused_computation.28 | convolution fusion | flops 103019520 | bytes 4009984 | tf_op jit(solution)/shard_map/hqe,hke->hqk/dot_general | solution.py:145
  52.1 2.1 %fusion.6 = (f32[12,256]{1,0:T(8,128)S(1)}, f32[12,256,256]{2,1,0:T(8,128)S(1)}) fusion(pred[256,256]{0,1:T(8,128)(4,1)S(1)} %get-tuple-element.47, bf16[12,256,64]{1,2,0:T(8,128)(2,1)S(1)} %bitcast.249, bf16[2,12,256,64]{2,3,1,0:T(8,128)(2,1)} %collective-permute-done.6), kind=kOutput, calls=%fused_computation.24 | convolution fusion | flops 103019520 | bytes 4009984 | tf_op jit(solution)/shard_map/hqe,hke->hqk/dot_general | solution.py:145
  54.9 1.6 copy-done.2
  56.6 3.9 %fusion.17 = (f32[12,256]{1,0:T(8,128)S(1)}, f32[12,256]{1,0:T(8,128)S(1)}, f32[12,256]{1,0:T(8,128)S(1)}, f32[12,256]{1,0:T(8,128)S(1)}, f32[12,256]{1,0:T(8,128)S(1)}) fusion(f32[12,256,256]{2,1,0:T(8,128)S(1)} %get-tuple-element.61, f32[12,256]{1,0:T(8,128)S(1)} %maximum_maximum_fusion, pred[256,256]{0,1:T(8,128)(4,1)S(1)} %get-tuple-element.47, ...), kind=kLoop, calls=%fused_computation.38 | loop fusion | flops 19645440 | bytes 16130048 | tf_op jit(solution)/shard_map/reduce_sum | solution.py:158
  63.8 1.9 %fusion.94 = f32[12,256,64]{1,2,0:T(8,128)S(1)} fusion(f32[12,256,64]{1,2,0:T(8,128)S(1)} %fusion.59, f32[12,256,256]{2,1,0:T(8,128)S(1)} %get-tuple-element.61, f32[12,256]{1,0:T(8,128)S(1)} %maximum_maximum_fusion, pred[256,256]{0,1:T(8,128)(4,1)S(1)} %get-tuple-element.47, bf16[2,12,256,64]{2,3,1,0:T(8,128)(2,1)} %collective-permute-done.6), kind=kOutput, calls=%fused_computation.107 | convolution fusion | flops 104792064 | bytes 5189632 | tf_op jit(solution)/shard_map/hqk,hke->hqe/dot_general | solution.py:159
  65.7 1.8 %fusion.120 = (bf16[256,12,64]{0,2,1:T(8,128)(2,1)S(1)}, f32[12,256,64]{1,2,0:T(8,128)}) fusion(f32[256,12]{0,1:T(8,128)S(1)} %bitcast.290, f32[12,256,64]{1,2,0:T(8,128)S(1)} %fusion.51, f32[12,256,64]{1,2,0:T(8,128)S(1)} %fusion.53, f32[12,256,64]{1,2,0:T(8,128)S(1)} %fusion.94, bf16[12,256,64]{1,2,0:T(8,128)(2,1)S(1)} %broadcast_select_fusion, ...), kind=kOutput, calls=%fused_computation.134 | convolution fusion | flops 105578496 | bytes 7168000 | tf_op jit(solution)/shard_map/hqk,hke->hqe/dot_general | solution.py:159
  68.2 2.2 %fusion.118 = bf16[768,1536]{1,0:T(8,128)(2,1)} fusion(bf16[256,768]{0,1:T(8,128)(2,1)S(1)} %bitcast.267, bf16[1,256,1536]{2,1,0:T(8,128)(2,1)S(1)} %copy-done), kind=kOutput, calls=%fused_computation.131 | convolution fusion | flops 603979776 | bytes 3538944 | tf_op jit(solution)/shard_map/dot_general | solution.py:172
  70.7 8.1 %all-gather.3.cloned.1.call-done = bf16[1536,768]{1,0:T(8,128)(2,1)} async-done(((bf16[48,768]{1,0:T(8,128)(2,1)}), bf16[1536,768]{1,0:T(8,128)(2,1)}) %all-gather.3.cloned.1.call-update) | async-done | bytes 2359312 | tf_op jit(solution)/shard_map/all_gather | solution.py:122
  78.8 4.0 %copy.90 = bf16[16,2,48,768]{3,1,2,0:T(2,128)(2,1)S(1)} copy(bf16[16,2,48,768]{3,2,1,0:T(8,128)(2,1)} %bitcast.266) | data formatting | bytes 4718592 | tf_op jit(solution)/shard_map/reshape | solution.py:124
  83.2 1.6 convolution_convert_fusion.1
  84.8 1.2 copy.91
  86.0 2.9 %fusion.77 = f32[1,12,256,64]{2,3,1,0:T(8,128)S(1)} fusion(bf16[12,256,64]{1,2,0:T(8,128)(2,1)S(1)} %bitcast.278, f32[12,256,256]{2,1,0:T(8,128)} %copy-done.10, f32[12,256]{1,0:T(8,128)} %get-tuple-element.34, pred[256,256]{0,1:T(8,128)(4,1)} %copy-done.41), kind=kOutput, calls=%fused_computation.89 | convolution fusion | flops 103809024 | bytes 4403200 | tf_op jit(solution)/shard_map/hqk,hqe->hke/dot_general | solution.py:223
  91.4 1.1 multiply_convert_fusion.2
  93.3 2.4 %multiply_convert_fusion.3 = bf16[12,256,256]{1,2,0:T(8,128)(2,1)S(1)} fusion(f32[12,256,256]{2,1,0:T(8,128)S(1)} %copy-done.11, bf16[12,256,64]{1,2,0:T(8,128)(2,1)S(1)} %bitcast.282, f32[12,256]{1,0:T(8,128)S(1)} %multiply_reduce_fusion, f32[12,256]{1,0:T(8,128)S(1)} %copy-done.47, pred[256,256]{0,1:T(8,128)(4,1)S(1)} %copy-done.42, ...), kind=kOutput, calls=%fused_computation.17 | convolution fusion | flops 105381888 | bytes 5595136 | tf_op jit(solution)/shard_map/hqe,hke->hqk/dot_general | solution.py:211
  100.6 1.1 multiply_convert_fusion.1
  104.3 1.3 fusion.150
  105.6 1.4 fusion.121
  109.3 2.6 %fusion.35 = (bf16[2,12,256,64]{2,3,1,0:T(8,128)(2,1)S(1)}, f32[2,12,256,64]{2,3,1,0:T(8,128)}, f32[2,12,256,64]{2,3,1,0:T(8,128)}) fusion(f32[1,12,256,64]{2,3,1,0:T(8,128)S(1)} %fusion.80, f32[1,12,256,64]{2,3,1,0:T(8,128)S(1)} %fusion.89, f32[2,12,256,64]{2,3,1,0:T(8,128)S(1)} %collective-permute-done.9, ...), kind=kLoop, calls=%fused_computation.54 | loop fusion | flops 3932160 | bytes 11796481 | tf_op jit(solution)/shard_map/convert.1
  112.9 1.3 collective-permute-start.11
  114.2 1.3 collective-permute-start.14
  115.5 1.3 fusion.149
  117.1 15.5 %reduce-scatter.3.cloned.1.call-done = bf16[48,1536]{1,0:T(8,128)(2,1)} async-done(((bf16[768,1536]{1,0:T(8,128)(2,1)}), bf16[48,1536]{1,0:T(8,128)(2,1)}) %reduce-scatter.3.cloned.1.call-update) | async-done | bytes 147472 | tf_op jit(solution)/shard_map/reduce_scatter | solution.py:183
  132.7 1.7 convert_element_type.207
  134.4 3.4 %collective-permute-start.10 = (bf16[12,256,64]{1,2,0:T(8,128)(2,1)}, bf16[12,256,64]{1,2,0:T(8,128)(2,1)}, u32[]{:S(2)}, u32[]{:S(2)}) collective-permute-start(bf16[12,256,64]{1,2,0:T(8,128)(2,1)} %get-tuple-element.44), channel_id=1, source_target_pairs={{4,0},{6,2},{12,8},{14,10},{20,16},{22,18},{28,24},{30,26},{5,1},{... | collective-permute-start | bytes 1179656 | tf_op jit(solution)/shard_map/ppermute | solution.py:97
  137.8 2.0 %collective-permute-start.13 = (bf16[12,256,64]{1,2,0:T(8,128)(2,1)}, bf16[12,256,64]{1,2,0:T(8,128)(2,1)}, u32[]{:S(2)}, u32[]{:S(2)}) collective-permute-start(bf16[12,256,64]{1,2,0:T(8,128)(2,1)} %get-tuple-element.43), channel_id=1, source_target_pairs={{4,0},{6,2},{12,8},{14,10},{20,16},{22,18},{28,24},{30,26},{5,1},{... | collective-permute-start | bytes 1179656 | tf_op jit(solution)/shard_map/ppermute | solution.py:97
  139.9 2.8 %fusion.108 = (bf16[12,256,64]{1,2,0:T(8,128)(2,1)}, bf16[12,256,64]{1,2,0:T(8,128)(2,1)}) fusion(f32[2,12,256,64]{2,3,1,0:T(8,128)} %get-tuple-element.42, bf16[12,256,64]{1,2,0:T(8,128)(2,1)} %collective-permute-done.14, pred[]{:T(512)S(6)} %eq.104, bf16[12,256,64]{1,2,0:T(8,128)(2,1)} %collective-permute-done.11), kind=kLoop, calls=%fused_computation.115 | loop fusion | flops 1572864 | bytes 3145729 | tf_op jit(solution)/shard_map/convert_element_type | solution.py:101
  142.7 1.3 collective-permute-start.12
  144.0 1.3 collective-permute-start.15
  145.3 1.2 fusion.106
  146.5 1.9 %copy.112 = bf16[1,256,768]{2,1,0:T(8,128)(2,1)} copy(bf16[1,256,768]{1,2,0:T(8,128)(2,1)} %bitcast.277) | data formatting | bytes 786432
  148.4 2.8 %fusion.9 = bf16[1,256,1536]{2,1,0:T(8,128)(2,1)} fusion(bf16[256,768]{0,1:T(8,128)(2,1)} %bitcast.268, bf16[768,1536]{1,0:T(8,128)(2,1)S(1)} %bitcast.257), kind=kOutput, calls=%fused_computation.30 | convolution fusion | flops 604372992 | bytes 3538944 | tf_op jit(solution)/shard_map/dot_general | solution.py:176
  151.2 1.3 collective-permute-done.13
  152.5 4.5 %collective-permute-done.12 = bf16[12,256,64]{1,2,0:T(8,128)(2,1)} collective-permute-done((bf16[12,256,64]{1,2,0:T(8,128)(2,1)}, bf16[12,256,64]{1,2,0:T(8,128)(2,1)}, u32[]{:S(2)}, u32[]{:S(2)}) %collective-permute-start.12) | collective-permute-done | bytes 393248 | tf_op jit(solution)/shard_map/ppermute | solution.py:18
  156.9 5.2 %collective-permute-done.15 = bf16[12,256,64]{1,2,0:T(8,128)(2,1)} collective-permute-done((bf16[12,256,64]{1,2,0:T(8,128)(2,1)}, bf16[12,256,64]{1,2,0:T(8,128)(2,1)}, u32[]{:S(2)}, u32[]{:S(2)}) %collective-permute-start.15) | collective-permute-done | bytes 393248 | tf_op jit(solution)/shard_map/ppermute | solution.py:18
  162.2 1.8 %fusion.111 = (bf16[12,256,64]{1,2,0:T(8,128)(2,1)S(1)}, bf16[12,256,64]{1,2,0:T(8,128)(2,1)S(1)}) fusion(f32[2,12,256,64]{2,3,1,0:T(8,128)S(1)} %copy-done.16, bf16[12,256,64]{1,2,0:T(8,128)(2,1)} %collective-permute-done.15, bf16[12,256,64]{1,2,0:T(8,128)(2,1)} %collective-permute-done.13, pred[]{:T(512)S(6)} %eq.111, ...), kind=kLoop, calls=%fused_computation.119 | loop fusion | flops 2359296 | bytes 3932161 | tf_op jit(solution)/shard_map/convert_element_type | solution.py:231
  (158 shorter events, 28.1 us)
Async XLA Ops:
  8.0 60.2 %copy-start = (bf16[1,256,1536]{2,1,0:T(8,128)(2,1)S(1)}, bf16[1,256,1536]{2,1,0:T(8,128)(2,1)}, u32[]{:S(2)}) copy-start(bf16[1,256,1536]{2,1,0:T(8,128)(2,1)} %param.9) | copy-start | bytes 2359300
  8.0 70.7 %all-gather.3.cloned.1.call-start = ((), (), s32[]{:S(2)}) async-start(), calls=%async_computation.4 | async-start | bytes 2433024 | tf_op jit(solution)/shard_map/all_gather | solution.py:122
  9.3 38.5 %copy-start.17 = (bf16[1,256,768]{1,2,0:T(8,128)(2,1)}, bf16[1,256,768]{1,2,0:T(8,128)(2,1)S(1)}, u32[]{:S(2)}) copy-start(bf16[1,256,768]{1,2,0:T(8,128)(2,1)S(1)} %copy.81) | copy-start | bytes 1179652
  9.3 13.1 %collective-permute-start.1 = (bf16[12,256,64]{1,2,0:T(8,128)(2,1)S(1)}, bf16[12,256,64]{1,2,0:T(8,128)(2,1)S(1)}, u32[]{:S(2)}, u32[]{:S(2)}) collective-permute-start(bf16[12,256,64]{1,2,0:T(8,128)(2,1)S(1)} %bitcast.260), channel_id=1, source_target_pairs={{0,8},{2,10},{4,12},{6,14},{8,16},{10,18},{12,20},{14,22},{16,24},... | collective-permute-start | bytes 1179656 | tf_op jit(solution)/shard_map/ppermute | solution.py:18
  12.8 19.8 %collective-permute-start = (bf16[12,256,64]{1,2,0:T(8,128)(2,1)S(1)}, bf16[12,256,64]{1,2,0:T(8,128)(2,1)S(1)}, u32[]{:S(2)}, u32[]{:S(2)}) collective-permute-start(bf16[12,256,64]{1,2,0:T(8,128)(2,1)S(1)} %bitcast.261), channel_id=1, source_target_pairs={{0,4},{2,6},{8,12},{10,14},{16,20},{18,22},{24,28},{26,30},{1,5},{... | collective-permute-start | bytes 1179656 | tf_op jit(solution)/shard_map/ppermute | solution.py:57
  15.3 45.8 %copy-start.24 = (bf16[1,256,768]{1,2,0:T(8,128)(2,1)}, bf16[1,256,768]{1,2,0:T(8,128)(2,1)S(1)}, u32[]{:S(2)}) copy-start(bf16[1,256,768]{1,2,0:T(8,128)(2,1)S(1)} %copy.83) | copy-start | bytes 1179652
  15.3 14.3 %collective-permute-start.4 = (bf16[12,256,64]{1,2,0:T(8,128)(2,1)S(1)}, bf16[12,256,64]{1,2,0:T(8,128)(2,1)S(1)}, u32[]{:S(2)}, u32[]{:S(2)}) collective-permute-start(bf16[12,256,64]{1,2,0:T(8,128)(2,1)S(1)} %bitcast.269), channel_id=1, source_target_pairs={{0,8},{2,10},{4,12},{6,14},{8,16},{10,18},{12,20},{14,22},{16,24},... | collective-permute-start | bytes 1179656 | tf_op jit(solution)/shard_map/ppermute | solution.py:18
  18.8 20.1 %collective-permute-start.3 = (bf16[12,256,64]{1,2,0:T(8,128)(2,1)S(1)}, bf16[12,256,64]{1,2,0:T(8,128)(2,1)}, u32[]{:S(2)}, u32[]{:S(2)}) collective-permute-start(bf16[12,256,64]{1,2,0:T(8,128)(2,1)S(1)} %bitcast.270), channel_id=1, source_target_pairs={{0,4},{2,6},{8,12},{10,14},{16,20},{18,22},{24,28},{26,30},{1,5},{... | collective-permute-start | bytes 1179656 | tf_op jit(solution)/shard_map/ppermute | solution.py:57
  20.1 112.5 %reduce-scatter.3.cloned.1.call-start = ((), (), s32[]{:S(2)}) async-start(), calls=%async_computation.2 | async-start | bytes 2506752 | tf_op jit(solution)/shard_map/reduce_scatter | solution.py:183
  22.5 28.2 %copy-start.19 = (bf16[12,256,64]{1,2,0:T(8,128)(2,1)}, bf16[12,256,64]{1,2,0:T(8,128)(2,1)S(1)}, u32[]{:S(2)}) copy-start(bf16[12,256,64]{1,2,0:T(8,128)(2,1)S(1)} %collective-permute-done.1) | copy-start | bytes 1179652
  22.5 15.4 %collective-permute-start.2 = (bf16[12,256,64]{1,2,0:T(8,128)(2,1)S(1)}, bf16[12,256,64]{1,2,0:T(8,128)(2,1)S(1)}, u32[]{:S(2)}, u32[]{:S(2)}) collective-permute-start(bf16[12,256,64]{1,2,0:T(8,128)(2,1)S(1)} %collective-permute-done.1), channel_id=1, source_target_pairs={{4,0},{6,2},{12,8},{14,10},{20,16},{22,18},{28,24},{30,26},{5,1},{... | collective-permute-start | bytes 1179656 | tf_op jit(solution)/shard_map/ppermute | solution.py:58
  29.6 9.4 %copy-start.43 = (bf16[12,256,64]{1,2,0:T(8,128)(2,1)}, bf16[12,256,64]{1,2,0:T(8,128)(2,1)S(1)}, u32[]{:S(2)}) copy-start(bf16[12,256,64]{1,2,0:T(8,128)(2,1)S(1)} %collective-permute-done.4) | copy-start | bytes 1179652
  29.6 14.7 %collective-permute-start.5 = (bf16[12,256,64]{1,2,0:T(8,128)(2,1)S(1)}, bf16[12,256,64]{1,2,0:T(8,128)(2,1)S(1)}, u32[]{:S(2)}, u32[]{:S(2)}) collective-permute-start(bf16[12,256,64]{1,2,0:T(8,128)(2,1)S(1)} %collective-permute-done.4), channel_id=1, source_target_pairs={{4,0},{6,2},{12,8},{14,10},{20,16},{22,18},{28,24},{30,26},{5,1},{... | collective-permute-start | bytes 1179656 | tf_op jit(solution)/shard_map/ppermute | solution.py:58
  32.6 28.6 %copy-start.33 = (pred[256,256]{0,1:T(8,128)(4,1)}, pred[256,256]{0,1:T(8,128)(4,1)S(1)}, u32[]{:S(2)}) copy-start(pred[256,256]{0,1:T(8,128)(4,1)S(1)} %get-tuple-element.51) | copy-start | bytes 196612
  32.6 29.4 %copy-start.35 = (pred[256,256]{0,1:T(8,128)(4,1)}, pred[256,256]{0,1:T(8,128)(4,1)S(1)}, u32[]{:S(2)}) copy-start(pred[256,256]{0,1:T(8,128)(4,1)S(1)} %get-tuple-element.50) | copy-start | bytes 196612
  32.6 30.3 %copy-start.39 = (pred[256,256]{0,1:T(8,128)(4,1)}, pred[256,256]{0,1:T(8,128)(4,1)S(1)}, u32[]{:S(2)}) copy-start(pred[256,256]{0,1:T(8,128)(4,1)S(1)} %get-tuple-element.49) | copy-start | bytes 196612
  32.6 31.2 %copy-start.41 = (pred[256,256]{0,1:T(8,128)(4,1)}, pred[256,256]{0,1:T(8,128)(4,1)S(1)}, u32[]{:S(2)}) copy-start(pred[256,256]{0,1:T(8,128)(4,1)S(1)} %get-tuple-element.47) | copy-start | bytes 196612
  32.6 33.0 %copy-start.37 = (pred[256,256]{0,1:T(8,128)(4,1)}, pred[256,256]{0,1:T(8,128)(4,1)S(1)}, u32[]{:S(2)}) copy-start(pred[256,256]{0,1:T(8,128)(4,1)S(1)} %get-tuple-element.48) | copy-start | bytes 196612
  38.9 12.4 %copy-start.14 = (bf16[12,256,64]{1,2,0:T(8,128)(2,1)}, bf16[12,256,64]{1,2,0:T(8,128)(2,1)S(1)}, u32[]{:S(2)}) copy-start(bf16[12,256,64]{1,2,0:T(8,128)(2,1)S(1)} %broadcast_select_fusion.1) | copy-start | bytes 1179652
  45.3 20.4 %copy-start.26 = (bf16[12,256,64]{1,2,0:T(8,128)(2,1)}, bf16[12,256,64]{1,2,0:T(8,128)(2,1)S(1)}, u32[]{:S(2)}) copy-start(bf16[12,256,64]{1,2,0:T(8,128)(2,1)S(1)} %broadcast_select_fusion) | copy-start | bytes 1179652
  47.8 4.2 %collective-permute-start.6 = (bf16[2,12,256,64]{2,3,1,0:T(8,128)(2,1)}, bf16[2,12,256,64]{2,3,1,0:T(8,128)(2,1)}, u32[]{:S(2)}, u32[]{:S(2)}) collective-permute-start(bf16[2,12,256,64]{2,3,1,0:T(8,128)(2,1)} %get-tuple-element.45), channel_id=1, source_target_pairs={{0,2},{2,0},{4,6},{6,4},{8,10},{10,8},{12,14},{14,12},{16,18},{18,... | collective-permute-start | bytes 2359304 | tf_op jit(solution)/shard_map/ppermute | solution.py:23
  50.1 4.1 %collective-permute-start.7 = (bf16[2,12,256,64]{2,3,1,0:T(8,128)(2,1)}, bf16[2,12,256,64]{2,3,1,0:T(8,128)(2,1)S(1)}, u32[]{:S(2)}, u32[]{:S(2)}) collective-permute-start(bf16[2,12,256,64]{2,3,1,0:T(8,128)(2,1)} %get-tuple-element.46), channel_id=1, source_target_pairs={{0,2},{2,0},{4,6},{6,4},{8,10},{10,8},{12,14},{14,12},{16,18},{18,... | collective-permute-start | bytes 2359304 | tf_op jit(solution)/shard_map/ppermute | solution.py:23
  51.3 10.7 %copy-start.4 = (f32[12,256,256]{1,2,0:T(8,128)}, f32[12,256,256]{1,2,0:T(8,128)S(1)}, u32[]{:S(2)}) copy-start(f32[12,256,256]{1,2,0:T(8,128)S(1)} %get-tuple-element.53) | copy-start | bytes 9437188
  52.0 13.6 %copy-start.6 = (f32[12,256,256]{2,1,0:T(8,128)}, f32[12,256,256]{2,1,0:T(8,128)S(1)}, u32[]{:S(2)}) copy-start(f32[12,256,256]{2,1,0:T(8,128)S(1)} %get-tuple-element.57) | copy-start | bytes 9437188
  52.0 4.5 %copy-start.2 = (f32[12,256,256]{1,2,0:T(8,128)S(1)}, f32[12,256,256]{1,2,0:T(8,128)}, u32[]{:S(2)}) copy-start(f32[12,256,256]{1,2,0:T(8,128)} %get-tuple-element.59) | copy-start | bytes 9437188
  54.2 9.6 %copy-start.10 = (f32[12,256,256]{2,1,0:T(8,128)}, f32[12,256,256]{2,1,0:T(8,128)S(1)}, u32[]{:S(2)}) copy-start(f32[12,256,256]{2,1,0:T(8,128)S(1)} %get-tuple-element.61) | copy-start | bytes 9437188
  54.2 8.7 %copy-start.31 = (bf16[2,12,256,64]{2,3,1,0:T(8,128)(2,1)}, bf16[2,12,256,64]{2,3,1,0:T(8,128)(2,1)S(1)}, u32[]{:S(2)}) copy-start(bf16[2,12,256,64]{2,3,1,0:T(8,128)(2,1)S(1)} %collective-permute-done.7) | copy-start | bytes 2359300
  54.9 8.0 %copy-start.8 = (f32[12,256,256]{2,1,0:T(8,128)}, f32[12,256,256]{2,1,0:T(8,128)S(1)}, u32[]{:S(2)}) copy-start(f32[12,256,256]{2,1,0:T(8,128)S(1)} %get-tuple-element.55) | copy-start | bytes 9437188
  70.4 95.3 %reduce-scatter.5.cloned.1.call-start = ((), (), s32[]{:S(2)}) async-start(), calls=%async_computation.3 | async-start | bytes 442368 | tf_op jit(solution)/shard_map/reduce_scatter | solution.py:186
  86.0 6.6 %copy-start.28 = (bf16[256,768]{0,1:T(8,128)(2,1)}, bf16[256,768]{0,1:T(8,128)(2,1)S(1)}, u32[]{:S(2)}) copy-start(bf16[256,768]{0,1:T(8,128)(2,1)S(1)} %copy.91) | copy-start | bytes 1179652
  86.0 3.2 %copy-start.9 = (f32[12,256,256]{2,1,0:T(8,128)S(1)}, f32[12,256,256]{2,1,0:T(8,128)}, u32[]{:S(2)}) copy-start(f32[12,256,256]{2,1,0:T(8,128)} %copy-done.8) | copy-start | bytes 9437188
  86.0 3.2 %copy-start.40 = (pred[256,256]{0,1:T(8,128)(4,1)S(1)}, pred[256,256]{0,1:T(8,128)(4,1)}, u32[]{:S(2)}) copy-start(pred[256,256]{0,1:T(8,128)(4,1)} %copy-done.39) | copy-start | bytes 196612
  93.3 5.9 %copy-start.12 = (bf16[12,256,256]{1,2,0:T(8,128)(2,1)}, bf16[12,256,256]{1,2,0:T(8,128)(2,1)S(1)}, u32[]{:S(2)}) copy-start(bf16[12,256,256]{1,2,0:T(8,128)(2,1)S(1)} %multiply_convert_fusion.2) | copy-start | bytes 4718596
  96.5 12.8 %collective-permute-start.8 = (f32[2,12,256,64]{2,3,1,0:T(8,128)S(1)}, f32[2,12,256,64]{2,3,1,0:T(8,128)S(1)}, u32[]{:S(2)}, u32[]{:S(2)}) collective-permute-start(f32[2,12,256,64]{2,3,1,0:T(8,128)S(1)} %pad_maximum_fusion), channel_id=1, source_target_pairs={{0,2},{2,0},{4,6},{6,4},{8,10},{10,8},{12,14},{14,12},{16,18},{18,... | collective-permute-start | bytes 4718600 | tf_op jit(solution)/shard_map/ppermute | solution.py:23
  98.8 10.5 %collective-permute-start.9 = (f32[2,12,256,64]{2,3,1,0:T(8,128)S(1)}, f32[2,12,256,64]{2,3,1,0:T(8,128)S(1)}, u32[]{:S(2)}, u32[]{:S(2)}) collective-permute-start(f32[2,12,256,64]{2,3,1,0:T(8,128)S(1)} %pad_maximum_fusion.1), channel_id=1, source_target_pairs={{0,2},{2,0},{4,6},{6,4},{8,10},{10,8},{12,14},{14,12},{16,18},{18,... | collective-permute-start | bytes 4718600 | tf_op jit(solution)/shard_map/ppermute | solution.py:23
  109.3 6.2 %copy-start.20 = (bf16[12,256,64]{1,2,0:T(8,128)(2,1)S(1)}, bf16[12,256,64]{1,2,0:T(8,128)(2,1)}, u32[]{:S(2)}) copy-start(bf16[12,256,64]{1,2,0:T(8,128)(2,1)} %copy-done.19) | copy-start | bytes 1179652
  112.9 27.0 %collective-permute-start.11 = (bf16[12,256,64]{1,2,0:T(8,128)(2,1)}, bf16[12,256,64]{1,2,0:T(8,128)(2,1)}, u32[]{:S(2)}, u32[]{:S(2)}) collective-permute-start(bf16[12,256,64]{1,2,0:T(8,128)(2,1)} %get-tuple-element.44), channel_id=1, source_target_pairs={{0,4},{2,6},{8,12},{10,14},{16,20},{18,22},{24,28},{26,30},{1,5},{... | collective-permute-start | bytes 1179656 | tf_op jit(solution)/shard_map/ppermute | solution.py:98
  114.2 25.7 %collective-permute-start.14 = (bf16[12,256,64]{1,2,0:T(8,128)(2,1)}, bf16[12,256,64]{1,2,0:T(8,128)(2,1)}, u32[]{:S(2)}, u32[]{:S(2)}) collective-permute-start(bf16[12,256,64]{1,2,0:T(8,128)(2,1)} %get-tuple-element.43), channel_id=1, source_target_pairs={{0,4},{2,6},{8,12},{10,14},{16,20},{18,22},{24,28},{26,30},{1,5},{... | collective-permute-start | bytes 1179656 | tf_op jit(solution)/shard_map/ppermute | solution.py:98
  116.7 28.5 %copy-start.15 = (bf16[12,256,64]{1,2,0:T(8,128)(2,1)S(1)}, bf16[12,256,64]{1,2,0:T(8,128)(2,1)}, u32[]{:S(2)}) copy-start(bf16[12,256,64]{1,2,0:T(8,128)(2,1)} %copy-done.14) | copy-start | bytes 1179652
  134.4 10.9 %copy-start.13 = (bf16[12,256,256]{1,2,0:T(8,128)(2,1)S(1)}, bf16[12,256,256]{1,2,0:T(8,128)(2,1)}, u32[]{:S(2)}) copy-start(bf16[12,256,256]{1,2,0:T(8,128)(2,1)} %copy-done.12) | copy-start | bytes 4718596
  134.4 10.9 %copy-start.21 = (f32[12,256,64]{1,2,0:T(8,128)S(1)}, f32[12,256,64]{1,2,0:T(8,128)}, u32[]{:S(2)}) copy-start(f32[12,256,64]{1,2,0:T(8,128)} %fusion.150) | copy-start | bytes 2359300
  134.4 10.9 %copy-start.22 = (f32[12,256,64]{1,2,0:T(8,128)S(1)}, f32[12,256,64]{1,2,0:T(8,128)}, u32[]{:S(2)}) copy-start(f32[12,256,64]{1,2,0:T(8,128)} %fusion.149) | copy-start | bytes 2359300
  134.4 16.8 %collective-permute-start.10 = (bf16[12,256,64]{1,2,0:T(8,128)(2,1)}, bf16[12,256,64]{1,2,0:T(8,128)(2,1)}, u32[]{:S(2)}, u32[]{:S(2)}) collective-permute-start(bf16[12,256,64]{1,2,0:T(8,128)(2,1)} %get-tuple-element.44), channel_id=1, source_target_pairs={{4,0},{6,2},{12,8},{14,10},{20,16},{22,18},{28,24},{30,26},{5,1},{... | collective-permute-start | bytes 1179656 | tf_op jit(solution)/shard_map/ppermute | solution.py:97
  137.8 14.6 %collective-permute-start.13 = (bf16[12,256,64]{1,2,0:T(8,128)(2,1)}, bf16[12,256,64]{1,2,0:T(8,128)(2,1)}, u32[]{:S(2)}, u32[]{:S(2)}) collective-permute-start(bf16[12,256,64]{1,2,0:T(8,128)(2,1)} %get-tuple-element.43), channel_id=1, source_target_pairs={{4,0},{6,2},{12,8},{14,10},{20,16},{22,18},{28,24},{30,26},{5,1},{... | collective-permute-start | bytes 1179656 | tf_op jit(solution)/shard_map/ppermute | solution.py:97
  142.7 14.3 %collective-permute-start.12 = (bf16[12,256,64]{1,2,0:T(8,128)(2,1)}, bf16[12,256,64]{1,2,0:T(8,128)(2,1)}, u32[]{:S(2)}, u32[]{:S(2)}) collective-permute-start(bf16[12,256,64]{1,2,0:T(8,128)(2,1)} %get-tuple-element.39), channel_id=1, source_target_pairs={{8,0},{10,2},{12,4},{14,6},{16,8},{18,10},{20,12},{22,14},{24,16},... | collective-permute-start | bytes 1179656 | tf_op jit(solution)/shard_map/ppermute | solution.py:18
  144.0 18.2 %collective-permute-start.15 = (bf16[12,256,64]{1,2,0:T(8,128)(2,1)}, bf16[12,256,64]{1,2,0:T(8,128)(2,1)}, u32[]{:S(2)}, u32[]{:S(2)}) collective-permute-start(bf16[12,256,64]{1,2,0:T(8,128)(2,1)} %get-tuple-element.38), channel_id=1, source_target_pairs={{8,0},{10,2},{12,4},{14,6},{16,8},{18,10},{20,12},{22,14},{24,16},... | collective-permute-start | bytes 1179656 | tf_op jit(solution)/shard_map/ppermute | solution.py:18
  148.4 13.8 %copy-start.16 = (f32[2,12,256,64]{2,3,1,0:T(8,128)S(1)}, f32[2,12,256,64]{2,3,1,0:T(8,128)}, u32[]{:S(2)}) copy-start(f32[2,12,256,64]{2,3,1,0:T(8,128)} %get-tuple-element.41) | copy-start | bytes 4718596
  148.4 17.4 %copy-start.1 = (bf16[1,256,1536]{2,1,0:T(8,128)(2,1)S(1)}, bf16[1,256,1536]{2,1,0:T(8,128)(2,1)}, u32[]{:S(2)}) copy-start(bf16[1,256,1536]{2,1,0:T(8,128)(2,1)} %param.9) | copy-start | bytes 2359300
  (19 other events, 33.3 us)
Sparse Core Ops, SparseCore 0:
  20.2 58.4 all-gather.2
Sparse Core Ops, SparseCore 1:
  70.5 62.1 reduce-scatter.2
  135.4 11.8 reduce-scatter.4

commit v18 on v13

--- a/solution.py
+++ b/solution.py
@@ -170,9 +170,6 @@
         attended, upstream, (((0,), (0,)), ((), ())), preferred_element_type=jnp.float32
     )
     partial_weight, attended = lax.optimization_barrier((partial_weight, attended))
-    mixed_out = jnp.dot(attended, weight_full, preferred_element_type=jnp.float32).astype(
-        jnp.bfloat16
-    )
     att_grad = lax.dot_general(
         upstream, weight_full, (((1,), (1,)), ((), ())), preferred_element_type=jnp.float32
     ).astype(jnp.bfloat16)
@@ -222,7 +219,11 @@
         )
         parts[dist] = jnp.stack([key_part, value_part])
 
+    attended, parts = lax.optimization_barrier((attended, parts))
     kv_grad = return_behind(parts, reach, paired, core)
+    mixed_out = jnp.dot(attended, weight_full, preferred_element_type=jnp.float32).astype(
+        jnp.bfloat16
+    )
     query_grad = row_major(query_acc * score_scale, tok_rows).astype(jnp.bfloat16)
     key_grad = row_major(kv_grad[0], tok_rows).astype(jnp.bfloat16)
     value_grad = row_major(kv_grad[1], tok_rows).astype(jnp.bfloat16)

time: 167 us -> 206 us (1.23)
  waiting for transfers between devices: 44.5 us -> 86.1 us
  matrix products: 41.2 us -> 31.6 us
  other arithmetic: 17.7 us -> 25.2 us
    reduce_scatter x1, waiting for transfers between devices: 0.01 us -> 28.6 us  [local(): lax.psum_scatter(partial_weight.astype(jnp.bfloat16), 'seq', scatter_dime...]
    ppermute x3, waiting for transfers between devices: 13 us -> 0.01 us  [shift_up(): return lax.ppermute(block, axis, route)]
    reduce_scatter x1, waiting for transfers between devices: 0.01 us -> 7.44 us  [local(): lax.psum_scatter(row_share.astype(jnp.float32), 'dp', scatter_dimension=1...]
    all_gather x1, waiting for transfers between devices: 8 us -> 15.1 us  [local(): pieces = lax.all_gather(out_weight, ('seq', 'dp'), axis=0, tiled=False)]
    another operation x2 -> x5, other arithmetic: 0.29 us -> 6.64 us  [local(): parts[dist] = jnp.stack([key_part, value_part])]
    ppermute x4, waiting for transfers between devices: 0.01 us -> 5.37 us  [swap_partner(): return lax.ppermute(block, axis, [(i, i ^ 1) for i in range(count)])]
    ppermute x1, waiting for transfers between devices: 13.6 us -> 16.8 us  [return_behind(): relayed = lax.ppermute(near, 'seq', [(i, i + 2) for i in earlier])]
    dot_general x5, matrix products: 6.51 us -> 3.4 us  [local(): jnp.einsum('hqe,hke->hqk', query_heads, held[dist][0], preferred_element_...]
  transfers between devices with their start and end apart: 16 -> 16, of which waited for: 6 -> 8; matrix products, arithmetic and copies ran while one was open for 43% -> 19% of each run, Pallas kernels for 0% -> 0%
where the time goes in v18:
time: 206 us; the launch traced here: 204 us
  waiting for transfers between devices  86.1 us (42%)
  matrix products  31.6 us (15%)
  starting transfers between devices  26.3 us (13%)
  other arithmetic  25.2 us (12%)
  local copies, waits for them, and re-layouts  18.2 us (9%)
  between operations  16.6 us (8%)
    reduce_scatter x1, waiting for transfers between devices, local(): lax.psum_scatter(partial_weight.astype(jnp.bfloat16), 'seq', scatter_dime...  28.6 us
    ppermute x1, waiting for transfers between devices, return_behind(): relayed = lax.ppermute(near, 'seq', [(i, i + 2) for i in earlier])  16.8 us
    all_gather x1, waiting for transfers between devices, local(): pieces = lax.all_gather(out_weight, ('seq', 'dp'), axis=0, tiled=False)  15.1 us
    unnamed x125, local copies, waits for them, and re-layouts  13 us
    ppermute x2, waiting for transfers between devices, gather_behind(): relayed = lax.ppermute(far[k], 'seq', [(i + 2, i) for i in earlier])  12.7 us
    ppermute x3, starting transfers between devices, shift_up(): return lax.ppermute(block, axis, route)  8.27 us
    reduce_scatter x1, waiting for transfers between devices, local(): lax.psum_scatter(row_share.astype(jnp.float32), 'dp', scatter_dimension=1...  7.44 us
    dot_general x5, matrix products, local(): jnp.einsum('hqe,hke->hqk', grad_heads, value_block, preferred_element_typ...  6.94 us
  transfers between devices with their start and end apart: 16, of which 8 were waited for; matrix products, arithmetic and copies ran while one was open for 19% of the time, Pallas kernels for 0%

profile of v18, /device:TPU:4, one launch (start us, length us, event | category | flops | bytes accessed | tf_op | source)
XLA Modules:
  0.0 204.0 jit_solution(6292886510369758924)
XLA Ops:
  8.1 1.2 copy.81
  9.3 3.5 %collective-permute-start.1 = (bf16[12,256,64]{1,2,0:T(8,128)(2,1)S(1)}, bf16[12,256,64]{1,2,0:T(8,128)(2,1)S(1)}, u32[]{:S(2)}, u32[]{:S(2)}) collective-permute-start(bf16[12,256,64]{1,2,0:T(8,128)(2,1)S(1)} %bitcast.232), channel_id=1, source_target_pairs={{0,8},{2,10},{4,12},{6,14},{8,16},{10,18},{12,20},{14,22},{16,24},... | collective-permute-start | bytes 1179656 | tf_op jit(solution)/shard_map/ppermute | solution.py:18
  12.8 1.3 collective-permute-start
  14.1 1.2 copy.83
  15.3 3.5 %collective-permute-start.4 = (bf16[12,256,64]{1,2,0:T(8,128)(2,1)S(1)}, bf16[12,256,64]{1,2,0:T(8,128)(2,1)S(1)}, u32[]{:S(2)}, u32[]{:S(2)}) collective-permute-start(bf16[12,256,64]{1,2,0:T(8,128)(2,1)S(1)} %bitcast.241), channel_id=1, source_target_pairs={{0,8},{2,10},{4,12},{6,14},{8,16},{10,18},{12,20},{14,22},{16,24},... | collective-permute-start | bytes 1179656 | tf_op jit(solution)/shard_map/ppermute | solution.py:18
  18.8 1.3 collective-permute-start.3
  21.8 1.2 copy.80
  24.4 4.6 %collective-permute-start.2 = (bf16[12,256,64]{1,2,0:T(8,128)(2,1)S(1)}, bf16[12,256,64]{1,2,0:T(8,128)(2,1)S(1)}, u32[]{:S(2)}, u32[]{:S(2)}) collective-permute-start(bf16[12,256,64]{1,2,0:T(8,128)(2,1)S(1)} %collective-permute-done.1), channel_id=1, source_target_pairs={{4,0},{6,2},{12,8},{14,10},{20,16},{22,18},{28,24},{30,26},{5,1},{... | collective-permute-start | bytes 1179656 | tf_op jit(solution)/shard_map/ppermute | solution.py:58
  29.7 2.3 %collective-permute-start.5 = (bf16[12,256,64]{1,2,0:T(8,128)(2,1)S(1)}, bf16[12,256,64]{1,2,0:T(8,128)(2,1)S(1)}, u32[]{:S(2)}, u32[]{:S(2)}) collective-permute-start(bf16[12,256,64]{1,2,0:T(8,128)(2,1)S(1)} %collective-permute-done.4), channel_id=1, source_target_pairs={{4,0},{6,2},{12,8},{14,10},{20,16},{22,18},{28,24},{30,26},{5,1},{... | collective-permute-start | bytes 1179656 | tf_op jit(solution)/shard_map/ppermute | solution.py:58
  32.6 6.3 %collective-permute-done.2 = bf16[12,256,64]{1,2,0:T(8,128)(2,1)S(1)} collective-permute-done((bf16[12,256,64]{1,2,0:T(8,128)(2,1)S(1)}, bf16[12,256,64]{1,2,0:T(8,128)(2,1)S(1)}, u32[]{:S(2)}, u32[]{:S(2)}) %collective-permute-start.2) | collective-permute-done | bytes 393248 | tf_op jit(solution)/shard_map/ppermute | solution.py:58
  39.0 6.4 %collective-permute-done.5 = bf16[12,256,64]{1,2,0:T(8,128)(2,1)S(1)} collective-permute-done((bf16[12,256,64]{1,2,0:T(8,128)(2,1)S(1)}, bf16[12,256,64]{1,2,0:T(8,128)(2,1)S(1)}, u32[]{:S(2)}, u32[]{:S(2)}) %collective-permute-start.5) | collective-permute-done | bytes 393248 | tf_op jit(solution)/shard_map/ppermute | solution.py:58
  49.9 4.1 %fusion.17 = (f32[12,256]{1,0:T(8,128)S(1)}, f32[12,256]{1,0:T(8,128)S(1)}, f32[12,256]{1,0:T(8,128)S(1)}, f32[12,256]{1,0:T(8,128)S(1)}, f32[12,256]{1,0:T(8,128)S(1)}) fusion(f32[12,256,256]{2,1,0:T(8,128)S(1)} %get-tuple-element.66, f32[12,256]{1,0:T(8,128)S(1)} %maximum_maximum_fusion, pred[256,256]{0,1:T(8,128)(4,1)S(1)} %get-tuple-element.52, ...), kind=kLoop, calls=%fused_computation.38 | loop fusion | flops 19645440 | bytes 16130048 | tf_op jit(solution)/shard_map/reduce_sum | solution.py:155
  58.2 1.8 fusion.109
  60.8 2.2 %fusion.107 = bf16[768,1536]{1,0:T(8,128)(2,1)} fusion(bf16[256,768]{0,1:T(8,128)(2,1)S(1)} %bitcast.239, bf16[1,256,1536]{2,1,0:T(8,128)(2,1)S(1)} %copy-done), kind=kOutput, calls=%fused_computation.119 | convolution fusion | flops 603979776 | bytes 3538944 | tf_op jit(solution)/shard_map/dot_general | solution.py:169
  62.9 15.1 %all-gather.3.cloned.1.call-done = bf16[1536,768]{1,0:T(8,128)(2,1)} async-done(((bf16[48,768]{1,0:T(8,128)(2,1)}), bf16[1536,768]{1,0:T(8,128)(2,1)}) %all-gather.3.cloned.1.call-update) | async-done | bytes 2359312 | tf_op jit(solution)/shard_map/all_gather | solution.py:119
  78.0 3.9 %copy.90 = bf16[16,2,48,768]{3,1,2,0:T(2,128)(2,1)S(1)} copy(bf16[16,2,48,768]{3,2,1,0:T(8,128)(2,1)} %bitcast.238) | data formatting | bytes 4718592 | tf_op jit(solution)/shard_map/reshape | solution.py:121
  82.4 1.6 convolution_convert_fusion.1
  84.0 1.2 copy.91
  85.2 2.8 %fusion.73 = f32[1,12,256,64]{2,3,1,0:T(8,128)S(1)} fusion(bf16[12,256,64]{1,2,0:T(8,128)(2,1)S(1)} %bitcast.248, f32[12,256,256]{1,2,0:T(8,128)} %copy-done.4, f32[12,256]{1,0:T(8,128)} %get-tuple-element.46, pred[256,256]{0,1:T(8,128)(4,1)} %copy-done.49), kind=kOutput, calls=%fused_computation.90 | convolution fusion | flops 103809024 | bytes 4403200 | tf_op jit(solution)/shard_map/hqk,hqe->hke/dot_general | solution.py:217
  88.9 1.2 copy-done.9
  90.8 1.2 copy-done.7
  93.3 2.3 %multiply_convert_fusion.2 = bf16[12,256,256]{1,2,0:T(8,128)(2,1)S(1)} fusion(f32[12,256,256]{2,1,0:T(8,128)S(1)} %copy-done.9, bf16[12,256,64]{1,2,0:T(8,128)(2,1)} %bitcast.253, bf16[12,256,64]{1,2,0:T(8,128)(2,1)S(1)} %copy-done.34, f32[12,256]{1,0:T(8,128)S(1)} %multiply_reduce_fusion, f32[12,256]{1,0:T(8,128)S(1)} %copy-done.58, ...), kind=kOutput, calls=%fused_computation.15 | convolution fusion | flops 105381888 | bytes 5595136 | tf_op jit(solution)/shard_map/hqe,hke->hqk/dot_general | solution.py:205
  95.7 1.3 multiply_convert_fusion.4
  97.7 1.7 copy-done.5
  99.5 1.1 multiply_convert_fusion
  101.3 1.1 multiply_convert_fusion.1
  104.1 1.1 multiply_convert_fusion.3
  106.5 1.4 pad_maximum_fusion.4
  107.9 1.3 pad_maximum_fusion.3
  109.2 1.3 pad_maximum_fusion.2
  110.5 1.3 pad_maximum_fusion.1
  111.8 1.3 pad_maximum_fusion
  113.8 3.1 %collective-permute-done.8 = f32[2,12,256,64]{2,3,1,0:T(8,128)} collective-permute-done((f32[2,12,256,64]{2,3,1,0:T(8,128)}, f32[2,12,256,64]{2,3,1,0:T(8,128)}, u32[]{:S(2)}, u32[]{:S(2)}) %collective-permute-start.8) | collective-permute-done | bytes 1572896 | tf_op jit(solution)/shard_map/ppermute | solution.py:23
  116.9 2.2 %collective-permute-done.9 = f32[2,12,256,64]{2,3,1,0:T(8,128)} collective-permute-done((f32[2,12,256,64]{2,3,1,0:T(8,128)}, f32[2,12,256,64]{2,3,1,0:T(8,128)}, u32[]{:S(2)}, u32[]{:S(2)}) %collective-permute-start.9) | collective-permute-done | bytes 1572896 | tf_op jit(solution)/shard_map/ppermute | solution.py:23
  119.1 3.3 %add_convert_fusion.2 = bf16[2,12,256,64]{2,3,1,0:T(8,128)(2,1)} fusion(f32[2,12,256,64]{2,3,1,0:T(8,128)} %pad_maximum_fusion.2, f32[2,12,256,64]{2,3,1,0:T(8,128)} %collective-permute-done.9, f32[2,12,256,64]{2,3,1,0:T(8,128)} %collective-permute-done.8, pred[]{:T(512)S(6)} %eq.101), kind=kLoop, calls=%fused_computation.60 | loop fusion | flops 1179648 | bytes 5505025 | tf_op jit(solution)/shard_map/convert_element_type | solution.py:94
  122.4 1.5 collective-permute-start.11
  125.3 5.7 %collective-permute-start.10 = (bf16[2,12,256,64]{2,3,1,0:T(8,128)(2,1)}, bf16[2,12,256,64]{2,3,1,0:T(8,128)(2,1)}, u32[]{:S(2)}, u32[]{:S(2)}) collective-permute-start(bf16[2,12,256,64]{2,3,1,0:T(8,128)(2,1)} %add_convert_fusion.2), channel_id=1, source_target_pairs={{4,0},{6,2},{12,8},{14,10},{20,16},{22,18},{28,24},{30,26},{5,1},{... | collective-permute-start | bytes 2359304 | tf_op jit(solution)/shard_map/ppermute | solution.py:95
  131.0 16.8 %collective-permute-done.11 = bf16[2,12,256,64]{2,3,1,0:T(8,128)(2,1)S(1)} collective-permute-done((bf16[2,12,256,64]{2,3,1,0:T(8,128)(2,1)}, bf16[2,12,256,64]{2,3,1,0:T(8,128)(2,1)S(1)}, u32[]{:S(2)}, u32[]{:S(2)}) %collective-permute-start.11) | collective-permute-done | bytes 786464 | tf_op jit(solution)/shard_map/ppermute | solution.py:96
  147.8 1.3 add_convert_fusion.1
  149.2 1.3 collective-permute-start.12
  151.4 0.9 copy.112
  152.3 1.7 fusion.9
  154.0 28.6 %reduce-scatter.3.cloned.1.call-done = bf16[48,1536]{1,0:T(8,128)(2,1)} async-done(((bf16[768,1536]{1,0:T(8,128)(2,1)}), bf16[48,1536]{1,0:T(8,128)(2,1)}) %reduce-scatter.3.cloned.1.call-update) | async-done | bytes 147472 | tf_op jit(solution)/shard_map/reduce_scatter | solution.py:177
  182.5 1.6 convert_element_type.187
  184.2 2.9 %add_convert_fusion = bf16[2,12,256,64]{2,3,1,0:T(8,128)(2,1)S(1)} fusion(bf16[2,12,256,64]{2,3,1,0:T(8,128)(2,1)} %collective-permute-done.12, bf16[2,12,256,64]{2,3,1,0:T(8,128)(2,1)} %collective-permute-done.10, f32[2,12,256,64]{2,3,1,0:T(8,128)} %pad_maximum_fusion, f32[2,12,256,64]{2,3,1,0:T(8,128)} %collective-permute-done.8, pred[]{:T(512)S(6)} %eq.109, ...), kind=kLoop, calls=%fused_computation.58 | loop fusion | flops 3145728 | bytes 5505026 | tf_op jit(solution)/shard_map/convert.1
  187.2 0.9 copy.113
  188.2 0.9 copy.114
  189.1 7.4 %reduce-scatter.5.cloned.1.call-done = f32[48,768]{1,0:T(8,128)} async-done(((f32[48,1536]{1,0:T(8,128)}), f32[48,768]{1,0:T(8,128)}) %reduce-scatter.5.cloned.1.call-update) | async-done | bytes 147472 | tf_op jit(solution)/shard_map/reduce_scatter | solution.py:180
  (177 shorter events, 23.9 us)
Async XLA Ops:
  8.0 52.8 %copy-start = (bf16[1,256,1536]{2,1,0:T(8,128)(2,1)S(1)}, bf16[1,256,1536]{2,1,0:T(8,128)(2,1)}, u32[]{:S(2)}) copy-start(bf16[1,256,1536]{2,1,0:T(8,128)(2,1)} %param.9) | copy-start | bytes 2359300
  8.0 70.0 %all-gather.3.cloned.1.call-start = ((), (), s32[]{:S(2)}) async-start(), calls=%async_computation.4 | async-start | bytes 2433024 | tf_op jit(solution)/shard_map/all_gather | solution.py:119
  9.3 36.5 %copy-start.25 = (bf16[1,256,768]{1,2,0:T(8,128)(2,1)}, bf16[1,256,768]{1,2,0:T(8,128)(2,1)S(1)}, u32[]{:S(2)}) copy-start(bf16[1,256,768]{1,2,0:T(8,128)(2,1)S(1)} %copy.81) | copy-start | bytes 1179652
  9.3 15.0 %collective-permute-start.1 = (bf16[12,256,64]{1,2,0:T(8,128)(2,1)S(1)}, bf16[12,256,64]{1,2,0:T(8,128)(2,1)S(1)}, u32[]{:S(2)}, u32[]{:S(2)}) collective-permute-start(bf16[12,256,64]{1,2,0:T(8,128)(2,1)S(1)} %bitcast.232), channel_id=1, source_target_pairs={{0,8},{2,10},{4,12},{6,14},{8,16},{10,18},{12,20},{14,22},{16,24},... | collective-permute-start | bytes 1179656 | tf_op jit(solution)/shard_map/ppermute | solution.py:18
  12.8 19.8 %collective-permute-start = (bf16[12,256,64]{1,2,0:T(8,128)(2,1)S(1)}, bf16[12,256,64]{1,2,0:T(8,128)(2,1)S(1)}, u32[]{:S(2)}, u32[]{:S(2)}) collective-permute-start(bf16[12,256,64]{1,2,0:T(8,128)(2,1)S(1)} %bitcast.233), channel_id=1, source_target_pairs={{0,4},{2,6},{8,12},{10,14},{16,20},{18,22},{24,28},{26,30},{1,5},{... | collective-permute-start | bytes 1179656 | tf_op jit(solution)/shard_map/ppermute | solution.py:57
  15.3 39.4 %copy-start.31 = (bf16[1,256,768]{1,2,0:T(8,128)(2,1)}, bf16[1,256,768]{1,2,0:T(8,128)(2,1)S(1)}, u32[]{:S(2)}) copy-start(bf16[1,256,768]{1,2,0:T(8,128)(2,1)S(1)} %copy.83) | copy-start | bytes 1179652
  15.3 14.4 %collective-permute-start.4 = (bf16[12,256,64]{1,2,0:T(8,128)(2,1)S(1)}, bf16[12,256,64]{1,2,0:T(8,128)(2,1)S(1)}, u32[]{:S(2)}, u32[]{:S(2)}) collective-permute-start(bf16[12,256,64]{1,2,0:T(8,128)(2,1)S(1)} %bitcast.241), channel_id=1, source_target_pairs={{0,8},{2,10},{4,12},{6,14},{8,16},{10,18},{12,20},{14,22},{16,24},... | collective-permute-start | bytes 1179656 | tf_op jit(solution)/shard_map/ppermute | solution.py:18
  18.8 20.2 %collective-permute-start.3 = (bf16[12,256,64]{1,2,0:T(8,128)(2,1)S(1)}, bf16[12,256,64]{1,2,0:T(8,128)(2,1)S(1)}, u32[]{:S(2)}, u32[]{:S(2)}) collective-permute-start(bf16[12,256,64]{1,2,0:T(8,128)(2,1)S(1)} %bitcast.242), channel_id=1, source_target_pairs={{0,4},{2,6},{8,12},{10,14},{16,20},{18,22},{24,28},{26,30},{1,5},{... | collective-permute-start | bytes 1179656 | tf_op jit(solution)/shard_map/ppermute | solution.py:57
  20.1 162.4 %reduce-scatter.3.cloned.1.call-start = ((), (), s32[]{:S(2)}) async-start(), calls=%async_computation.2 | async-start | bytes 2506752 | tf_op jit(solution)/shard_map/reduce_scatter | solution.py:177
  24.3 22.7 %copy-start.27 = (bf16[12,256,64]{1,2,0:T(8,128)(2,1)}, bf16[12,256,64]{1,2,0:T(8,128)(2,1)S(1)}, u32[]{:S(2)}) copy-start(bf16[12,256,64]{1,2,0:T(8,128)(2,1)S(1)} %collective-permute-done.1) | copy-start | bytes 1179652
  24.4 14.5 %collective-permute-start.2 = (bf16[12,256,64]{1,2,0:T(8,128)(2,1)S(1)}, bf16[12,256,64]{1,2,0:T(8,128)(2,1)S(1)}, u32[]{:S(2)}, u32[]{:S(2)}) collective-permute-start(bf16[12,256,64]{1,2,0:T(8,128)(2,1)S(1)} %collective-permute-done.1), channel_id=1, source_target_pairs={{4,0},{6,2},{12,8},{14,10},{20,16},{22,18},{28,24},{30,26},{5,1},{... | collective-permute-start | bytes 1179656 | tf_op jit(solution)/shard_map/ppermute | solution.py:58
  29.7 25.8 %copy-start.55 = (bf16[12,256,64]{1,2,0:T(8,128)(2,1)}, bf16[12,256,64]{1,2,0:T(8,128)(2,1)S(1)}, u32[]{:S(2)}) copy-start(bf16[12,256,64]{1,2,0:T(8,128)(2,1)S(1)} %collective-permute-done.4) | copy-start | bytes 1179652
  29.7 15.7 %collective-permute-start.5 = (bf16[12,256,64]{1,2,0:T(8,128)(2,1)S(1)}, bf16[12,256,64]{1,2,0:T(8,128)(2,1)S(1)}, u32[]{:S(2)}, u32[]{:S(2)}) collective-permute-start(bf16[12,256,64]{1,2,0:T(8,128)(2,1)S(1)} %collective-permute-done.4), channel_id=1, source_target_pairs={{4,0},{6,2},{12,8},{14,10},{20,16},{22,18},{28,24},{30,26},{5,1},{... | collective-permute-start | bytes 1179656 | tf_op jit(solution)/shard_map/ppermute | solution.py:58
  32.6 22.1 %copy-start.51 = (pred[256,256]{0,1:T(8,128)(4,1)}, pred[256,256]{0,1:T(8,128)(4,1)S(1)}, u32[]{:S(2)}) copy-start(pred[256,256]{0,1:T(8,128)(4,1)S(1)} %get-tuple-element.56) | copy-start | bytes 196612
  32.6 22.9 %copy-start.49 = (pred[256,256]{0,1:T(8,128)(4,1)}, pred[256,256]{0,1:T(8,128)(4,1)S(1)}, u32[]{:S(2)}) copy-start(pred[256,256]{0,1:T(8,128)(4,1)S(1)} %get-tuple-element.55) | copy-start | bytes 196612
  32.6 23.8 %copy-start.46 = (pred[256,256]{0,1:T(8,128)(4,1)}, pred[256,256]{0,1:T(8,128)(4,1)S(1)}, u32[]{:S(2)}) copy-start(pred[256,256]{0,1:T(8,128)(4,1)S(1)} %get-tuple-element.54) | copy-start | bytes 196612
  32.6 24.7 %copy-start.44 = (pred[256,256]{0,1:T(8,128)(4,1)}, pred[256,256]{0,1:T(8,128)(4,1)S(1)}, u32[]{:S(2)}) copy-start(pred[256,256]{0,1:T(8,128)(4,1)S(1)} %get-tuple-element.52) | copy-start | bytes 196612
  32.6 25.6 %copy-start.53 = (pred[256,256]{0,1:T(8,128)(4,1)}, pred[256,256]{0,1:T(8,128)(4,1)S(1)}, u32[]{:S(2)}) copy-start(pred[256,256]{0,1:T(8,128)(4,1)S(1)} %get-tuple-element.53) | copy-start | bytes 196612
  39.0 8.8 %copy-start.23 = (bf16[12,256,64]{1,2,0:T(8,128)(2,1)}, bf16[12,256,64]{1,2,0:T(8,128)(2,1)S(1)}, u32[]{:S(2)}) copy-start(bf16[12,256,64]{1,2,0:T(8,128)(2,1)S(1)} %broadcast_select_fusion.1) | copy-start | bytes 1179652
  45.5 12.7 %copy-start.33 = (bf16[12,256,64]{1,2,0:T(8,128)(2,1)}, bf16[12,256,64]{1,2,0:T(8,128)(2,1)S(1)}, u32[]{:S(2)}) copy-start(bf16[12,256,64]{1,2,0:T(8,128)(2,1)S(1)} %broadcast_select_fusion) | copy-start | bytes 1179652
  45.7 2.8 %collective-permute-start.6 = (bf16[2,12,256,64]{2,3,1,0:T(8,128)(2,1)S(1)}, bf16[2,12,256,64]{2,3,1,0:T(8,128)(2,1)S(1)}, u32[]{:S(2)}, u32[]{:S(2)}) collective-permute-start(bf16[2,12,256,64]{2,3,1,0:T(8,128)(2,1)S(1)} %get-tuple-element.50), channel_id=1, source_target_pairs={{0,2},{2,0},{4,6},{6,4},{8,10},{10,8},{12,14},{14,12},{16,18},{18,... | collective-permute-start | bytes 2359304 | tf_op jit(solution)/shard_map/ppermute | solution.py:23
  46.5 8.2 %copy-start.2 = (f32[12,256,256]{1,2,0:T(8,128)}, f32[12,256,256]{1,2,0:T(8,128)S(1)}, u32[]{:S(2)}) copy-start(f32[12,256,256]{1,2,0:T(8,128)S(1)} %get-tuple-element.64) | copy-start | bytes 9437188
  46.5 2.7 %collective-permute-start.7 = (bf16[2,12,256,64]{2,3,1,0:T(8,128)(2,1)S(1)}, bf16[2,12,256,64]{2,3,1,0:T(8,128)(2,1)S(1)}, u32[]{:S(2)}, u32[]{:S(2)}) collective-permute-start(bf16[2,12,256,64]{2,3,1,0:T(8,128)(2,1)S(1)} %get-tuple-element.51), channel_id=1, source_target_pairs={{0,2},{2,0},{4,6},{6,4},{8,10},{10,8},{12,14},{14,12},{16,18},{18,... | collective-permute-start | bytes 2359304 | tf_op jit(solution)/shard_map/ppermute | solution.py:23
  47.7 7.8 %copy-start.4 = (f32[12,256,256]{1,2,0:T(8,128)}, f32[12,256,256]{1,2,0:T(8,128)S(1)}, u32[]{:S(2)}) copy-start(f32[12,256,256]{1,2,0:T(8,128)S(1)} %get-tuple-element.58) | copy-start | bytes 9437188
  48.5 9.8 %copy-start.8 = (f32[12,256,256]{2,1,0:T(8,128)}, f32[12,256,256]{2,1,0:T(8,128)S(1)}, u32[]{:S(2)}) copy-start(f32[12,256,256]{2,1,0:T(8,128)S(1)} %get-tuple-element.62) | copy-start | bytes 9437188
  48.5 8.8 %copy-start.41 = (bf16[2,12,256,64]{2,3,1,0:T(8,128)(2,1)}, bf16[2,12,256,64]{2,3,1,0:T(8,128)(2,1)S(1)}, u32[]{:S(2)}) copy-start(bf16[2,12,256,64]{2,3,1,0:T(8,128)(2,1)S(1)} %collective-permute-done.6) | copy-start | bytes 2359300
  49.2 8.1 %copy-start.6 = (f32[12,256,256]{2,1,0:T(8,128)}, f32[12,256,256]{2,1,0:T(8,128)S(1)}, u32[]{:S(2)}) copy-start(f32[12,256,256]{2,1,0:T(8,128)S(1)} %get-tuple-element.66) | copy-start | bytes 9437188
  49.2 7.2 %copy-start.38 = (bf16[2,12,256,64]{2,3,1,0:T(8,128)(2,1)}, bf16[2,12,256,64]{2,3,1,0:T(8,128)(2,1)S(1)}, u32[]{:S(2)}) copy-start(bf16[2,12,256,64]{2,3,1,0:T(8,128)(2,1)S(1)} %collective-permute-done.7) | copy-start | bytes 2359300
  49.9 6.5 %copy-start.10 = (f32[12,256,256]{2,1,0:T(8,128)}, f32[12,256,256]{2,1,0:T(8,128)S(1)}, u32[]{:S(2)}) copy-start(f32[12,256,256]{2,1,0:T(8,128)S(1)} %get-tuple-element.60) | copy-start | bytes 9437188
  85.2 7.5 %copy-start.35 = (bf16[256,768]{0,1:T(8,128)(2,1)}, bf16[256,768]{0,1:T(8,128)(2,1)S(1)}, u32[]{:S(2)}) copy-start(bf16[256,768]{0,1:T(8,128)(2,1)S(1)} %copy.91) | copy-start | bytes 1179652
  95.7 7.4 %copy-start.15 = (bf16[12,256,256]{1,2,0:T(8,128)(2,1)}, bf16[12,256,256]{1,2,0:T(8,128)(2,1)S(1)}, u32[]{:S(2)}) copy-start(bf16[12,256,256]{1,2,0:T(8,128)(2,1)S(1)} %multiply_convert_fusion.2) | copy-start | bytes 4718596
  97.0 8.9 %copy-start.19 = (bf16[12,256,256]{1,2,0:T(8,128)(2,1)}, bf16[12,256,256]{1,2,0:T(8,128)(2,1)S(1)}, u32[]{:S(2)}) copy-start(bf16[12,256,256]{1,2,0:T(8,128)(2,1)S(1)} %multiply_convert_fusion.4) | copy-start | bytes 4718596
  113.1 3.8 %collective-permute-start.8 = (f32[2,12,256,64]{2,3,1,0:T(8,128)}, f32[2,12,256,64]{2,3,1,0:T(8,128)}, u32[]{:S(2)}, u32[]{:S(2)}) collective-permute-start(f32[2,12,256,64]{2,3,1,0:T(8,128)} %pad_maximum_fusion.1), channel_id=1, source_target_pairs={{0,2},{2,0},{4,6},{6,4},{8,10},{10,8},{12,14},{14,12},{16,18},{18,... | collective-permute-start | bytes 4718600 | tf_op jit(solution)/shard_map/ppermute | solution.py:23
  113.4 5.7 %collective-permute-start.9 = (f32[2,12,256,64]{2,3,1,0:T(8,128)}, f32[2,12,256,64]{2,3,1,0:T(8,128)}, u32[]{:S(2)}, u32[]{:S(2)}) collective-permute-start(f32[2,12,256,64]{2,3,1,0:T(8,128)} %pad_maximum_fusion.3), channel_id=1, source_target_pairs={{0,2},{2,0},{4,6},{6,4},{8,10},{10,8},{12,14},{14,12},{16,18},{18,... | collective-permute-start | bytes 4718600 | tf_op jit(solution)/shard_map/ppermute | solution.py:23
  113.7 10.3 %copy-start.26 = (bf16[1,256,768]{1,2,0:T(8,128)(2,1)S(1)}, bf16[1,256,768]{1,2,0:T(8,128)(2,1)}, u32[]{:S(2)}) copy-start(bf16[1,256,768]{1,2,0:T(8,128)(2,1)} %copy-done.25) | copy-start | bytes 1179652
  113.7 82.8 %reduce-scatter.5.cloned.1.call-start = ((), (), s32[]{:S(2)}) async-start(), calls=%async_computation.3 | async-start | bytes 442368 | tf_op jit(solution)/shard_map/reduce_scatter | solution.py:180
  113.7 10.2 %copy-start.20 = (bf16[12,256,256]{1,2,0:T(8,128)(2,1)S(1)}, bf16[12,256,256]{1,2,0:T(8,128)(2,1)}, u32[]{:S(2)}) copy-start(bf16[12,256,256]{1,2,0:T(8,128)(2,1)} %copy-done.19) | copy-start | bytes 4718596
  113.8 10.6 %copy-start.22 = (bf16[12,256,256]{1,2,0:T(8,128)(2,1)S(1)}, bf16[12,256,256]{1,2,0:T(8,128)(2,1)}, u32[]{:S(2)}) copy-start(bf16[12,256,256]{1,2,0:T(8,128)(2,1)} %copy-done.21) | copy-start | bytes 4718596
  113.8 10.6 %copy-start.43 = (bf16[2,12,256,64]{2,3,1,0:T(8,128)(2,1)S(1)}, bf16[2,12,256,64]{2,3,1,0:T(8,128)(2,1)}, u32[]{:S(2)}) copy-start(bf16[2,12,256,64]{2,3,1,0:T(8,128)(2,1)} %copy-done.41) | copy-start | bytes 2359300
  122.4 25.4 %collective-permute-start.11 = (bf16[2,12,256,64]{2,3,1,0:T(8,128)(2,1)}, bf16[2,12,256,64]{2,3,1,0:T(8,128)(2,1)S(1)}, u32[]{:S(2)}, u32[]{:S(2)}) collective-permute-start(bf16[2,12,256,64]{2,3,1,0:T(8,128)(2,1)} %add_convert_fusion.2), channel_id=1, source_target_pairs={{0,4},{2,6},{8,12},{10,14},{16,20},{18,22},{24,28},{26,30},{1,5},{... | collective-permute-start | bytes 2359304 | tf_op jit(solution)/shard_map/ppermute | solution.py:96
  124.4 23.4 %copy-start.14 = (f32[2,12,256,64]{2,3,1,0:T(8,128)S(1)}, f32[2,12,256,64]{2,3,1,0:T(8,128)}, u32[]{:S(2)}) copy-start(f32[2,12,256,64]{2,3,1,0:T(8,128)} %pad_maximum_fusion.4) | copy-start | bytes 4718596
  125.2 25.3 %copy-start.18 = (bf16[12,256,256]{1,2,0:T(8,128)(2,1)S(1)}, bf16[12,256,256]{1,2,0:T(8,128)(2,1)}, u32[]{:S(2)}) copy-start(bf16[12,256,256]{1,2,0:T(8,128)(2,1)} %copy-done.17) | copy-start | bytes 4718596
  125.2 25.3 %copy-start.28 = (bf16[12,256,64]{1,2,0:T(8,128)(2,1)S(1)}, bf16[12,256,64]{1,2,0:T(8,128)(2,1)}, u32[]{:S(2)}) copy-start(bf16[12,256,64]{1,2,0:T(8,128)(2,1)} %copy-done.27) | copy-start | bytes 1179652
  125.2 25.7 %copy-start.16 = (bf16[12,256,256]{1,2,0:T(8,128)(2,1)S(1)}, bf16[12,256,256]{1,2,0:T(8,128)(2,1)}, u32[]{:S(2)}) copy-start(bf16[12,256,256]{1,2,0:T(8,128)(2,1)} %copy-done.15) | copy-start | bytes 4718596
  125.2 25.7 %copy-start.24 = (bf16[12,256,64]{1,2,0:T(8,128)(2,1)S(1)}, bf16[12,256,64]{1,2,0:T(8,128)(2,1)}, u32[]{:S(2)}) copy-start(bf16[12,256,64]{1,2,0:T(8,128)(2,1)} %copy-done.23) | copy-start | bytes 1179652
  125.3 59.0 %collective-permute-start.10 = (bf16[2,12,256,64]{2,3,1,0:T(8,128)(2,1)}, bf16[2,12,256,64]{2,3,1,0:T(8,128)(2,1)}, u32[]{:S(2)}, u32[]{:S(2)}) collective-permute-start(bf16[2,12,256,64]{2,3,1,0:T(8,128)(2,1)} %add_convert_fusion.2), channel_id=1, source_target_pairs={{4,0},{6,2},{12,8},{14,10},{20,16},{22,18},{28,24},{30,26},{5,1},{... | collective-permute-start | bytes 2359304 | tf_op jit(solution)/shard_map/ppermute | solution.py:95
  149.2 35.0 %collective-permute-start.12 = (bf16[2,12,256,64]{2,3,1,0:T(8,128)(2,1)}, bf16[2,12,256,64]{2,3,1,0:T(8,128)(2,1)}, u32[]{:S(2)}, u32[]{:S(2)}) collective-permute-start(bf16[2,12,256,64]{2,3,1,0:T(8,128)(2,1)} %add_convert_fusion.1), channel_id=1, source_target_pairs={{8,0},{10,2},{12,4},{14,6},{16,8},{18,10},{20,12},{22,14},{24,16},... | collective-permute-start | bytes 2359304 | tf_op jit(solution)/shard_map/ppermute | solution.py:18
  184.2 12.3 %copy-start.1 = (bf16[1,256,1536]{2,1,0:T(8,128)(2,1)S(1)}, bf16[1,256,1536]{2,1,0:T(8,128)(2,1)}, u32[]{:S(2)}) copy-start(bf16[1,256,1536]{2,1,0:T(8,128)(2,1)} %param.9) | copy-start | bytes 2359300
  (27 other events, 58.9 us)
Sparse Core Ops, SparseCore 0:
  20.2 57.7 all-gather.2
Sparse Core Ops, SparseCore 1:
  113.8 68.7 reduce-scatter.2
  185.3 11.2 reduce-scatter.4
